TPU v7x, 32 devices: a whole 2x2x4 slice. The times are simulated.
32 devices in a mesh: group: 2 (over x), ctx: 16 (over z, y, core).
Axes of the slice: x: 2, y: 2, z: 4, core: 2. Of those that a mesh axis runs over, the one named last changes fastest.
Arguments:
- xbc: bfloat16 [16384, 5120], P(('group', 'ctx')), parts along dimension 0, may hold values from -6 to 6
- z_gate: bfloat16 [16384, 4096], P(('group', 'ctx')), parts along dimension 0, may hold values from -6 to 6
- dt_raw: bfloat16 [16384, 64], P(('group', 'ctx')), parts along dimension 0, may hold values from -4 to 4
- lengths: int32 [8], P('group'), parts along dimension 0, may hold values from 1 to 6144, 8192 in all
- conv_weight: float32 [4, 5120], replicated, may hold values from -3 to 3
- conv_bias: float32 [5120], replicated, may hold values from -3 to 3
- dt_bias: float32 [64], replicated, may hold values from -3 to -1
- a_log: float32 [64], replicated, may hold values from -14 to 0
- d_skip: float32 [64], replicated, may hold values from 0.5 to 2
- norm_gain: float32 [4096], replicated, may hold values from 0.5 to 1.5
Outputs:
- mixed: bfloat16 [16384, 4096], P(('group', 'ctx')), parts along dimension 0
There are 2 independent parts, one for each index of `group`. A program takes and returns all parts, laid end to end along the dimension named above; an argument that names none is the same for every part. Nothing has to cross between parts.
Inputs may be any that keep to these rules, and one draw needn't show every extreme that they name: `lengths`: the 4 prompts lie one after another and fill all 8192 positions; the longest has exactly 6144 tokens.
All inputs are finite; a program needn't handle non-finite values.
Results may differ from a plain program's by a relative error of at most 0.0035.
Values may be sent and summed in bfloat16 or wider, within the bound.
No kernel may reach another device: no remote copies, remote signals or barrier semaphores. Data moves between devices by JAX's collectives and lax.ppermute only.
A program may use at most 128 MiB of HBM per device.

v0:
```python
import jax
import jax.numpy as jnp
from jax import lax
from jax.sharding import PartitionSpec as P

HEADS = 64
HEAD_DIM = 64
STATE = 256
GROUPS = 2
CONV = 4
STRETCH = 256
CHANNELS = 5120


def shifted(value, axis, by):
    peers = lax.axis_size(axis)
    pairs = [(i, i + by) for i in range(peers) if 0 <= i + by < peers]
    return lax.ppermute(value, axis, pairs)


def segment_of(positions, lengths):
    prompt_ends = jnp.cumsum(lengths)
    hits = (prompt_ends[None, :] <= positions[:, None]).astype(jnp.int32)
    return jnp.sum(hits, axis=1)


def causal_conv(extended, positions, lengths, conv_weight, conv_bias):
    out_rows = extended.shape[0] - (CONV - 1)
    segments = segment_of(positions, lengths)
    inside = positions >= 0
    target = segments[CONV - 1 :]
    summed = jnp.zeros((out_rows, extended.shape[1]), jnp.float32)
    for tap in range(CONV):
        kept = inside[tap : tap + out_rows] & (segments[tap : tap + out_rows] == target)
        term = extended[tap : tap + out_rows].astype(jnp.float32) * conv_weight[tap][None, :]
        summed = summed + jnp.where(kept[:, None], term, 0.0)
    return jax.nn.silu(summed + conv_bias[None, :]).astype(jnp.bfloat16)


def stretch_local(block, step_size, segments, seg_before, decay_rate, d_skip):
    span = block.shape[0]
    inner = HEADS * HEAD_DIM
    bc_width = GROUPS * STATE
    per_group = HEADS // GROUPS
    values = block[:, :inner]
    b_rows = block[:, inner : inner + bc_width].reshape(span, GROUPS, STATE)
    c_rows = block[:, inner + bc_width :].reshape(span, GROUPS, STATE)
    log_cum = jnp.cumsum(-step_size * decay_rate[None, :], axis=0)
    scaled = (
        values.astype(jnp.float32).reshape(span, HEADS, HEAD_DIM) * step_size[:, :, None]
    ).astype(jnp.bfloat16)
    scaled_groups = scaled.reshape(span, GROUPS, per_group, HEAD_DIM)
    order = jnp.arange(span)
    kept = (segments[:, None] == segments[None, :]) & (order[:, None] >= order[None, :])
    gaps = jnp.where(kept[:, :, None], log_cum[:, None, :] - log_cum[None, :, :], 0.0)
    decay = jnp.where(kept[:, :, None], jnp.exp(gaps), 0.0)
    scores = jnp.einsum("tgn,sgn->tsg", c_rows, b_rows, preferred_element_type=jnp.float32)
    weights = (decay.reshape(span, span, GROUPS, per_group) * scores[:, :, :, None]).astype(
        jnp.bfloat16
    )
    intra = jnp.einsum(
        "tsgk,sgkp->tgkp", weights, scaled_groups, preferred_element_type=jnp.float32
    ).reshape(span, inner)
    end_seg = segments[span - 1]
    end_weight = jnp.where(
        (segments == end_seg)[:, None], jnp.exp(log_cum[span - 1][None, :] - log_cum), 0.0
    )
    weighted_b = (
        b_rows.astype(jnp.float32)[:, :, None, :]
        * end_weight.reshape(span, GROUPS, per_group)[:, :, :, None]
    ).astype(jnp.bfloat16)
    state_end = jnp.einsum(
        "sgkp,sgkn->gkpn", scaled_groups, weighted_b, preferred_element_type=jnp.float32
    ).reshape(HEADS, HEAD_DIM, STATE)
    decay_stretch = jnp.where(end_seg == seg_before, jnp.exp(log_cum[span - 1]), 0.0)
    in_weight = jnp.where((segments == seg_before)[:, None], jnp.exp(log_cum), 0.0)
    skip = values.astype(jnp.float32).reshape(span, HEADS, HEAD_DIM) * d_skip[None, :, None]
    local_out = intra + skip.reshape(span, inner)
    return (local_out, in_weight, decay_stretch, state_end, c_rows)


def from_state(state, c_rows, in_weight):
    span = c_rows.shape[0]
    per_group = HEADS // GROUPS
    state_low = state.astype(jnp.bfloat16).reshape(GROUPS, per_group, HEAD_DIM, STATE)
    term = jnp.einsum("tgn,gkpn->tgkp", c_rows, state_low, preferred_element_type=jnp.float32)
    term = term * in_weight.reshape(span, GROUPS, per_group)[:, :, :, None]
    return term.reshape(span, HEADS * HEAD_DIM)


def finish(mixed_out, z_block, norm_gain):
    span = mixed_out.shape[0]
    inner = HEADS * HEAD_DIM
    gated = mixed_out * jax.nn.silu(z_block.astype(jnp.float32))
    grouped = gated.reshape(span, GROUPS, inner // GROUPS)
    mean_square = jnp.mean(grouped * grouped, axis=2, keepdims=True) + 1e-05
    normed = (grouped * lax.rsqrt(mean_square)).reshape(span, inner)
    return (normed * norm_gain[None, :]).astype(jnp.bfloat16)


def compose_flat(earlier, later):
    return (earlier[0] * later[0], later[0] * earlier[1] + later[1])


def local(xbc, z_gate, dt_raw, lengths, conv_weight, conv_bias, dt_bias, a_log, d_skip, norm_gain):
    tok_rows = xbc.shape[0]
    first_pos = lax.axis_index("ctx") * tok_rows
    rim_rows = shifted(xbc[tok_rows - (CONV - 1) :], "ctx", 1)
    extended = jnp.concatenate([rim_rows, xbc], axis=0)
    positions = first_pos - (CONV - 1) + jnp.arange(tok_rows + CONV - 1)
    conv_out = causal_conv(extended, positions, lengths, conv_weight, conv_bias)
    step_size = jax.nn.softplus(dt_raw.astype(jnp.float32) + dt_bias[None, :])
    decay_rate = jnp.exp(a_log)
    segments = segment_of(first_pos + jnp.arange(tok_rows), lengths)
    stretch_count = tok_rows // STRETCH
    seg_before = segment_of(first_pos + jnp.arange(stretch_count) * STRETCH - 1, lengths)
    inputs = (
        conv_out.reshape(stretch_count, STRETCH, CHANNELS),
        step_size.reshape(stretch_count, STRETCH, HEADS),
        segments.reshape(stretch_count, STRETCH),
        seg_before,
    )

    def first_pass(carry, item):
        decay_acc, state_acc = carry
        block, step_block, seg_block, seg_prev = item
        local_out, in_weight, decay_stretch, state_end, c_rows = stretch_local(
            block, step_block, seg_block, seg_prev, decay_rate, d_skip
        )
        new_carry = (
            decay_acc * decay_stretch,
            decay_stretch[:, None, None] * state_acc + state_end,
        )
        return (new_carry, (local_out, in_weight, decay_acc, state_acc, c_rows))

    start_carry = (
        jnp.ones((HEADS,), jnp.float32),
        jnp.zeros((HEADS, HEAD_DIM, STATE), jnp.float32),
    )
    (decay_dev, state_dev), stacked = lax.scan(first_pass, start_carry, inputs)
    device_count = lax.axis_size("ctx")
    head_size = HEAD_DIM * STATE
    piece_len = HEADS * head_size // device_count
    heads_span = max(1, piece_len // head_size)
    decay_table = lax.all_gather(decay_dev[None, :], "ctx", axis=0, tiled=True)
    received = lax.all_to_all(
        state_dev.reshape(device_count, piece_len), "ctx", split_axis=0, concat_axis=0, tiled=True
    )
    first_head = lax.axis_index("ctx") * piece_len // head_size
    picked = lax.dynamic_slice_in_dim(decay_table, first_head, heads_span, 1)
    factors = jnp.repeat(picked, piece_len // heads_span, axis=1)
    inclusive = lax.associative_scan(compose_flat, (factors, received), axis=0)
    exclusive = jnp.concatenate([jnp.zeros((1, piece_len), jnp.float32), inclusive[1][:-1]], axis=0)
    returned = lax.all_to_all(
        exclusive.astype(jnp.bfloat16), "ctx", split_axis=0, concat_axis=0, tiled=True
    ).astype(exclusive.dtype)
    state_in = returned.reshape(HEADS, HEAD_DIM, STATE)

    def second_pass(unused, item):
        local_out, in_weight, decay_acc, state_acc, c_rows, z_block = item
        state = decay_acc[:, None, None] * state_in + state_acc
        mixed_out = local_out + from_state(state, c_rows, in_weight)
        return (unused, finish(mixed_out, z_block, norm_gain))

    _, outputs = lax.scan(
        second_pass, 0, stacked + (z_gate.reshape(stretch_count, STRETCH, HEADS * HEAD_DIM),)
    )
    return outputs.reshape(tok_rows, HEADS * HEAD_DIM)


def solution(mesh):
    return jax.shard_map(
        local,
        mesh=mesh,
        in_specs=(
            P(("group", "ctx"), None),
            P(("group", "ctx"), None),
            P(("group", "ctx"), None),
            P("group"),
            P(),
            P(),
            P(),
            P(),
            P(),
            P(),
        ),
        out_specs=P(("group", "ctx"), None),
        check_vma=False,
    )
```

profile of v0, /device:TPU:13, one launch (start us, length us, event | category | flops | bytes accessed | tf_op | source)
XLA Modules:
  0.0 653.7 jit_solution(6796162996965464087)
XLA Ops:
  10.0 18.8 %multiply_convert_fusion.7 = bf16[512,5120]{1,0:T(8,128)(2,1)} fusion(bf16[512,5120]{1,0:T(8,128)(2,1)} %param.14, bf16[3,5120]{1,0:T(4,128)(2,1)S(1)} %collective-permute-done, f32[5120]{0:T(1024)} %param.19, f32[5120]{0:T(1024)S(1)} %bitcast.219, f32[5120]{0:T(1024)S(1)} %bitcast.220, f32[5120]{0:T(1024)S(1)} %bitcast.218, f32[5120]{0:T(1024)S(1)} %bitcast.217, ...), kind=kLoop, calls=%fused_computation.62 | loop fusion | flops 78643200 | bytes 10620928 | tf_op jit(solution)/shard_map/convert_element_type | solution.py:37
  28.8 87.8 %while.34 = (s32[]{:T(128)}, f32[64]{0:T(128)}, f32[64,64,256]{2,1,0:T(8,128)}, f32[2,256,4096]{1,2,0:T(8,128)}, f32[2,256,64]{1,2,0:T(8,128)}, /*index=5*/f32[2...) while((s32[]{:T(128)}, f32[64]{0:T(128)}, ...), condition=%wide.region_7.8_spmd.clone, body=%wide.region_4.7_spmd.clone.sunk | while | flops 1185203072 | bytes 112872720 | solution.py:140
  41.4 6.3 fusion.68
  55.4 5.8 fusion.66
  83.3 6.3 fusion.68
  97.4 5.8 fusion.66
  105.8 4.8 bitcast_dynamic-update-slice_fusion.8
  110.7 5.0 bitcast_add_fusion.4
  116.6 11.9 %all_to_all.14 = f32[16,1,65536]{2,1,0:T(1,128)} reshape(f32[64,64,256]{2,1,0:T(8,128)} %get-tuple-element.137) | data formatting | bytes 8388608 | tf_op jit(solution)/shard_map/all_to_all | solution.py:146
  128.6 5.2 all-to-all-start
  135.9 117.9 %all-reduce.10 = f32[16,64]{1,0:T(8,128)S(1)} all-reduce(f32[16,64]{1,0:T(8,128)S(1)} %reshape.249), channel_id=2, replica_groups=mesh['group'=2,'ctx'=16] {'ctx'}, use_global_device_ids=true, to_apply=%add.9 | all-reduce | flops 1024 | bytes 8192
  254.4 4.4 copy.83
  258.9 11.2 %slice.185 = f32[8,65536]{1,0:T(8,128)} slice(f32[16,65536]{1,0:T(8,128)} %bitcast.206), slice={[1:16:2], [0:65536:1]} | slice | bytes 4194304 | tf_op jit(solution)/shard_map/slice | solution.py:152
  270.1 11.2 %slice.189 = f32[8,65536]{1,0:T(8,128)} slice(f32[16,65536]{1,0:T(8,128)} %bitcast.207), slice={[0:15:2], [0:65536:1]} | slice | bytes 4194304 | tf_op jit(solution)/shard_map/slice | solution.py:152
  281.3 11.3 %slice.184 = f32[7,65536]{1,0:T(8,128)} slice(f32[16,65536]{1,0:T(8,128)} %bitcast.208), slice={[2:16:2], [0:65536:1]} | slice | bytes 3670016 | tf_op jit(solution)/shard_map/slice | solution.py:152
  292.6 6.6 %copy.95 = f32[16,1,65536]{2,0,1:T(8,128)} copy(f32[16,1,65536]{2,1,0:T(1,128)} %all-to-all-done) | data formatting | bytes 8388608
  299.2 11.2 %slice.186 = f32[8,65536]{1,0:T(8,128)} slice(f32[16,65536]{1,0:T(8,128)} %bitcast.203), slice={[0:15:2], [0:65536:1]} | slice | bytes 4194304 | tf_op jit(solution)/shard_map/slice | solution.py:152
  310.4 11.2 %slice.187 = f32[8,65536]{1,0:T(8,128)} slice(f32[16,65536]{1,0:T(8,128)} %bitcast.204), slice={[1:16:2], [0:65536:1]} | slice | bytes 4194304 | tf_op jit(solution)/shard_map/slice | solution.py:152
  321.6 5.2 fusion.37
  326.9 7.6 %slice.192 = f32[4,65536]{1,0:T(4,128)} slice(f32[8,65536]{1,0:T(8,128)S(1)} %get-tuple-element.376), slice={[0:7:2], [0:65536:1]} | slice | bytes 2097152 | tf_op jit(solution)/shard_map/slice | solution.py:152
  334.5 7.9 %slice.193 = f32[4,65536]{1,0:T(4,128)} slice(f32[8,65536]{1,0:T(8,128)S(1)} %get-tuple-element.376), slice={[1:8:2], [0:65536:1]} | slice | bytes 2097152 | tf_op jit(solution)/shard_map/slice | solution.py:152
  342.4 10.7 %slice.191 = f32[4,65536]{1,0:T(4,128)} slice(f32[8,65536]{1,0:T(8,128)} %get-tuple-element.375), slice={[1:8:2], [0:65536:1]} | slice | bytes 2097152 | tf_op jit(solution)/shard_map/slice | solution.py:152
  353.0 10.7 %slice.195 = f32[4,65536]{1,0:T(4,128)} slice(f32[8,65536]{1,0:T(8,128)} %get-tuple-element.375), slice={[0:7:2], [0:65536:1]} | slice | bytes 2097152 | tf_op jit(solution)/shard_map/slice | solution.py:152
  367.4 6.9 %slice.198 = f32[2,65536]{1,0:T(2,128)} slice(f32[4,65536]{1,0:T(4,128)S(1)} %get-tuple-element.380), slice={[0:3:2], [0:65536:1]} | slice | bytes 1048576 | tf_op jit(solution)/shard_map/slice | solution.py:152
  374.4 6.9 %slice.199 = f32[2,65536]{1,0:T(2,128)} slice(f32[4,65536]{1,0:T(4,128)S(1)} %get-tuple-element.380), slice={[1:4:2], [0:65536:1]} | slice | bytes 1048576 | tf_op jit(solution)/shard_map/slice | solution.py:152
  381.3 10.1 %slice.197 = f32[2,65536]{1,0:T(2,128)} slice(f32[4,65536]{1,0:T(4,128)} %get-tuple-element.379), slice={[1:4:2], [0:65536:1]} | slice | bytes 1048576 | tf_op jit(solution)/shard_map/slice | solution.py:152
  391.4 10.1 %slice.201 = f32[2,65536]{1,0:T(2,128)} slice(f32[4,65536]{1,0:T(4,128)} %get-tuple-element.379), slice={[0:3:2], [0:65536:1]} | slice | bytes 1048576 | tf_op jit(solution)/shard_map/slice | solution.py:152
  409.4 10.1 %slice.190 = f32[3,65536]{1,0:T(4,128)S(1)} slice(f32[8,65536]{1,0:T(8,128)} %get-tuple-element.375), slice={[2:8:2], [0:65536:1]} | slice | bytes 1572864 | tf_op jit(solution)/shard_map/slice | solution.py:152
  419.5 8.0 %slice.207 = f32[3,65536]{1,0:T(4,128)} slice(f32[8,65536]{1,0:T(8,128)S(1)} %get-tuple-element.376), slice={[2:8:2], [0:65536:1]} | slice | bytes 1572864 | tf_op jit(solution)/shard_map/slice | solution.py:152
  427.6 11.3 %slice.209 = f32[7,65536]{1,0:T(8,128)} slice(f32[16,65536]{1,0:T(8,128)} %bitcast.205), slice={[2:16:2], [0:65536:1]} | slice | bytes 3670016 | tf_op jit(solution)/shard_map/slice | solution.py:152
  442.0 4.4 pad.29
  450.8 4.4 pad.31
  455.3 5.0 pad.32
  463.4 17.4 %pad.83 = f32[16,65536]{1,0:T(8,128)} pad(f32[8,65536]{1,0:T(8,128)} %add.197, f32[]{:T(128)} %constant.102.clone.1), padding=1_0_1x0_0_0 | pad | bytes 6291460
  485.4 9.0 %pad.46 = f32[15,65536]{1,0:T(8,128)} pad(f32[8,65536]{1,0:T(8,128)S(1)} %pad_maximum_fusion.1, f32[]{:T(128)} %constant.102.clone.1), padding=0_0_1x0_0_0 | pad | bytes 6029316 | tf_op jit(solution)/shard_map/slice | solution.py:153
  506.1 6.3 all-to-all-start.1
  512.5 47.3 %all-to-all-done.1 = bf16[16,2,32768]{2,1,0:T(2,128)(2,1)S(1)} async-done(((bf16[16,2,32768]{2,1,0:T(2,128)(2,1)}), bf16[16,2,32768]{2,1,0:T(2,128)(2,1)S(1)}, u32[]{:S(2)}, u32[]{:S(2)}) %all-to-all-start.1) | async-done | bytes 2097184 | tf_op jit(solution)/shard_map/all_to_all | solution.py:154
  559.8 6.8 %reshape.274 = bf16[16,1,65536]{2,1,0:T(2,128)(2,1)} reshape(bf16[16,2,32768]{2,1,0:T(2,128)(2,1)S(1)} %all-to-all-done.1) | data formatting | bytes 4194304
  566.6 14.9 %convert_reduce_fusion = f32[16,65536]{1,0:T(8,128)} fusion(bf16[16,1,65536]{2,1,0:T(2,128)(2,1)} %reshape.274), kind=kLoop, calls=%fused_computation.69 | loop fusion | flops 1048576 | bytes 6291456 | tf_op jit(solution)/shard_map/convert_element_type | solution.py:156
  585.4 67.8 %while.33 = (s32[]{:T(128)}, bf16[2,256,4096]{2,1,0:T(8,128)(2,1)}, f32[2,256,4096]{1,2,0:T(8,128)}, f32[2,64]{1,0:T(2,128)S(1)}, f32[64,64,256]{2,1,0:T(8,128)}...) while((s32[]{:T(128)}, bf16[2,256,4096]{2,1,0:T(8,128)(2,1)}, ...), condition=%wide.region_10.11_spmd, body=%wide.region_8.10_spmd.sunk | while | flops 560988672 | bytes 136800976 | solution.py:165
  585.4 4.7 constant_dynamic-slice_fusion.16
  590.2 6.3 bitcast_multiply_fusion.4
  605.7 5.0 fusion.59
  610.8 4.2 fusion.60
  619.4 4.7 constant_dynamic-slice_fusion.16
  624.1 6.3 bitcast_multiply_fusion.4
  639.6 5.0 fusion.59
  644.7 4.2 fusion.60
  (195 shorter events, 132.6 us)
Async XLA Ops:
  0.9 9.1 %collective-permute-start = (bf16[3,5120]{1,0:T(4,128)(2,1)S(1)}, bf16[3,5120]{1,0:T(4,128)(2,1)S(1)}, u32[]{:S(2)}, u32[]{:S(2)}) collective-permute-start(bf16[3,5120]{1,0:T(4,128)(2,1)S(1)} %slice.169), channel_id=1, source_target_pairs={{0,1},{1,2},{2,3},{3,4},{4,5},{5,6},{6,7},{7,8},{8,9},{9,10},{10,1... | collective-permute-start | bytes 92168 | tf_op jit(solution)/shard_map/ppermute | solution.py:18
  10.0 18.8 %copy-start.15 = (f32[64]{0:T(128)S(1)}, f32[64]{0:T(128)}, u32[]{:S(2)}) copy-start(f32[64]{0:T(128)} %param.22) | copy-start | bytes 772
  40.4 1.0 copy-start.5
  40.7 7.0 %copy-start.3 = (f32[256,4096]{0,1:T(8,128)}, f32[256,4096]{0,1:T(8,128)S(1)}, u32[]{:S(2)}) copy-start(f32[256,4096]{0,1:T(8,128)S(1)} %slice_convert_fusion.2) | copy-start | bytes 12582916 | tf_op jit(solution)/shard_map/while
  63.2 3.7 copy-start.2
  66.9 2.8 copy-start.11
  66.9 2.9 copy-start.16
  66.9 2.9 copy-start.7
  69.8 0.6 copy-start.12
  69.9 0.6 copy-start.17
  69.9 0.8 copy-start.8
  82.2 1.0 copy-start.5
  82.6 7.0 %copy-start.3 = (f32[256,4096]{0,1:T(8,128)}, f32[256,4096]{0,1:T(8,128)S(1)}, u32[]{:S(2)}) copy-start(f32[256,4096]{0,1:T(8,128)S(1)} %slice_convert_fusion.2) | copy-start | bytes 12582916 | tf_op jit(solution)/shard_map/while
  105.8 4.8 copy-start.2
  110.6 5.0 copy-start.11
  110.6 5.1 copy-start.16
  110.6 5.1 copy-start.7
  115.7 0.6 copy-start.12
  115.8 0.6 copy-start.17
  115.8 0.8 copy-start.8
  128.6 5.2 copy-start.19
  128.6 164.0 %all-to-all-start = ((f32[16,1,65536]{2,1,0:T(1,128)}), f32[16,1,65536]{2,1,0:T(1,128)}, u32[]{:S(2)}, u32[]{:S(2)}) async-start(f32[16,1,65536]{2,1,0:T(1,128)} %all_to_all.14), calls=%async_computation | async-start | bytes 8388608 | tf_op jit(solution)/shard_map/all_to_all | solution.py:146
  427.6 11.4 %copy-start.10 = (f32[2,65536]{1,0:T(2,128)S(1)}, f32[2,65536]{1,0:T(2,128)}, u32[]{:S(2)}) copy-start(f32[2,65536]{1,0:T(2,128)} %pad_add_fusion) | copy-start | bytes 1572868
  449.3 5.9 copy-start.6
  506.1 53.6 %all-to-all-start.1 = ((bf16[16,2,32768]{2,1,0:T(2,128)(2,1)}), bf16[16,2,32768]{2,1,0:T(2,128)(2,1)S(1)}, u32[]{:S(2)}, u32[]{:S(2)}) async-start(bf16[16,2,32768]{2,1,0:T(2,128)(2,1)} %reshape.273), calls=%async_computation.1 | async-start | bytes 4194304 | tf_op jit(solution)/shard_map/all_to_all | solution.py:154
  581.5 3.9 copy-start.9
  581.5 3.9 copy-start.13
  581.5 3.9 copy-start.14
  581.5 3.9 copy-start.18
  590.2 7.0 %copy-start.1 = (f32[2,256,4096]{1,2,0:T(8,128)S(1)}, f32[2,256,4096]{1,2,0:T(8,128)}, u32[]{:S(2)}) copy-start(f32[2,256,4096]{1,2,0:T(8,128)} %get-tuple-element.633) | copy-start | bytes 25165828 | tf_op jit(solution)/shard_map/while
  597.2 3.7 copy-start.4
  605.7 5.1 copy-start
  624.1 7.0 %copy-start.1 = (f32[2,256,4096]{1,2,0:T(8,128)S(1)}, f32[2,256,4096]{1,2,0:T(8,128)}, u32[]{:S(2)}) copy-start(f32[2,256,4096]{1,2,0:T(8,128)} %get-tuple-element.633) | copy-start | bytes 25165828 | tf_op jit(solution)/shard_map/while
  631.1 3.7 copy-start.4
  639.6 5.1 copy-start
where the time goes:
time: 663 us; the launch traced here: 654 us
  local copies, waits for them, and re-layouts  307 us (46%)
  other arithmetic  122 us (18%)
  blocking collectives  118 us (18%)
  waiting for transfers between devices  47.3 us (7%)
  matrix products  39.1 us (6%)
  starting transfers between devices  15.2 us (2%)
    slice x18, local copies, waits for them, and re-layouts, local(): inclusive = lax.associative_scan(compose_flat, (factors, received), axis=0)  158 us
    unnamed x1, blocking collectives  118 us
    all_to_all x1, waiting for transfers between devices, local(): lax.all_to_all(exclusive.astype(jnp.bfloat16), 'ctx', split_axis=0, conca...  47.3 us
    unnamed x24, local copies, waits for them, and re-layouts  40.8 us
    dynamic_slice x10, local copies, waits for them, and re-layouts, local(): lax.scan(second_pass, 0, stacked + (z_gate.reshape(stretch_count, STRETCH...  23.7 us
    convert_element_type x1, other arithmetic, causal_conv(): return jax.nn.silu(summed + conv_bias[None, :]).astype(jnp.bfloat16)  18.8 us
    dynamic_slice x14, local copies, waits for them, and re-layouts, local(): (decay_dev, state_dev), stacked = lax.scan(first_pass, start_carry, inputs)  17.3 us
    dynamic_update_slice x6, other arithmetic, local(): (decay_dev, state_dev), stacked = lax.scan(first_pass, start_carry, inputs)  15.5 us
  transfers between devices with their start and end apart: 3, of which 1 were waited for; matrix products, arithmetic and copies ran while one was open for 7% of the time, Pallas kernels for 0%

commit v1 on v0

v1 whole, which is shorter than its diff:
```python
import jax
import jax.numpy as jnp
from jax import lax
from jax.experimental import pallas as pl
from jax.experimental.pallas import tpu as pltpu
from jax.sharding import PartitionSpec as P

HEADS = 64
HEAD_DIM = 64
STATE = 256
GROUPS = 2
CONV = 4
STRETCH = 256
CHANNELS = 5120
INNER = HEADS * HEAD_DIM
PER_GROUP = HEADS // GROUPS
GROUP_COLS = INNER // GROUPS


def shifted(value, axis, by):
    peers = lax.axis_size(axis)
    pairs = [(i, i + by) for i in range(peers) if 0 <= i + by < peers]
    return lax.ppermute(value, axis, pairs)


def segment_of(positions, lengths):
    prompt_ends = jnp.cumsum(lengths)
    hits = (prompt_ends[None, :] <= positions[:, None]).astype(jnp.int32)
    return jnp.sum(hits, axis=1)


def causal_conv(extended, positions, lengths, conv_weight, conv_bias):
    out_rows = extended.shape[0] - (CONV - 1)
    segments = segment_of(positions, lengths)
    inside = positions >= 0
    target = segments[CONV - 1 :]
    summed = jnp.zeros((out_rows, extended.shape[1]), jnp.float32)
    for tap in range(CONV):
        kept = inside[tap : tap + out_rows] & (segments[tap : tap + out_rows] == target)
        term = extended[tap : tap + out_rows].astype(jnp.float32) * conv_weight[tap][None, :]
        summed = summed + jnp.where(kept[:, None], term, 0.0)
    return jax.nn.silu(summed + conv_bias[None, :]).astype(jnp.bfloat16)


def state_kernel(bt_ref, u_ref, cum_ref, segc_ref, out_ref, uw_ref):
    cum = cum_ref[0]
    segc = segc_ref[:, 0:1]
    last = cum[STRETCH - 1 : STRETCH, :]
    seg_last = segc[STRETCH - 1 : STRETCH, :]
    w = jnp.where(segc == seg_last, jnp.exp(last - cum), 0.0)
    for j in range(PER_GROUP):
        cols = slice(j * HEAD_DIM, (j + 1) * HEAD_DIM)
        uw_ref[:, cols] = (u_ref[:, cols].astype(jnp.float32) * w[:, j : j + 1]).astype(jnp.bfloat16)
    out_ref[0] = jnp.dot(bt_ref[...], uw_ref[...], preferred_element_type=jnp.float32)


def block_states(bt, u, cum_g, segc):
    tok = u.shape[0]
    nb = tok // STRETCH
    return pl.pallas_call(
        state_kernel,
        grid=(nb, GROUPS),
        in_specs=[
            pl.BlockSpec((STATE, STRETCH), lambda b, g: (g, b)),
            pl.BlockSpec((STRETCH, GROUP_COLS), lambda b, g: (b, g)),
            pl.BlockSpec((1, STRETCH, PER_GROUP), lambda b, g: (g, b, 0)),
            pl.BlockSpec((STRETCH, 128), lambda b, g: (b, 0)),
        ],
        out_specs=pl.BlockSpec((1, STATE, GROUP_COLS), lambda b, g: (b, 0, g)),
        out_shape=jax.ShapeDtypeStruct((nb, STATE, INNER), jnp.float32),
        scratch_shapes=[pltpu.VMEM((STRETCH, GROUP_COLS), jnp.bfloat16)],
    )(bt, u, cum_g, segc)


def mix_kernel(
    c_ref, b_ref, x_ref, u_ref, z_ref, hbt_ref, cum_ref, cumt_ref, segc_ref, segr_ref, eb_ref,
    dsk_ref, gain_ref, out_ref, y_ref,
):
    cmat = c_ref[...]
    gram = lax.dot_general(
        cmat, b_ref[...], (((1,), (1,)), ((), ())), preferred_element_type=jnp.float32
    )
    segc = segc_ref[:, 0:1]
    segr = segr_ref[0:1, :]
    rows = lax.broadcasted_iota(jnp.int32, (STRETCH, STRETCH), 0)
    cols = lax.broadcasted_iota(jnp.int32, (STRETCH, STRETCH), 1)
    gram = jnp.where((segc == segr) & (cols <= rows), gram, 0.0)
    cum = cum_ref[0]
    cumt = cumt_ref[0]
    entry = eb_ref[0:1, 0:1]
    in_weight = jnp.where(segc == entry, jnp.exp(cum), 0.0)
    inter = jnp.dot(cmat, hbt_ref[0], preferred_element_type=jnp.float32)
    for j in range(PER_GROUP):
        hc = slice(j * HEAD_DIM, (j + 1) * HEAD_DIM)
        gap = jnp.minimum(cum[:, j : j + 1] - cumt[j : j + 1, :], 0.0)
        weights = (gram * jnp.exp(gap)).astype(jnp.bfloat16)
        intra = jnp.dot(weights, u_ref[:, hc], preferred_element_type=jnp.float32)
        y_ref[:, hc] = intra + inter[:, hc] * in_weight[:, j : j + 1]
    y = y_ref[...] + dsk_ref[...] * x_ref[...].astype(jnp.float32)
    zf = z_ref[...].astype(jnp.float32)
    gated = y * (zf * jax.nn.sigmoid(zf))
    mean_square = jnp.mean(gated * gated, axis=1, keepdims=True) + 1e-05
    out_ref[...] = (gated * lax.rsqrt(mean_square) * gain_ref[...]).astype(jnp.bfloat16)


def mix(conv, u, z_gate, hbt, cum_g, cumt_g, segc, segr, eb, dsk, gain):
    tok = u.shape[0]
    nb = tok // STRETCH
    b_col = INNER // STATE
    c_col = b_col + GROUPS
    return pl.pallas_call(
        mix_kernel,
        grid=(nb, GROUPS),
        in_specs=[
            pl.BlockSpec((STRETCH, STATE), lambda b, g: (b, c_col + g)),
            pl.BlockSpec((STRETCH, STATE), lambda b, g: (b, b_col + g)),
            pl.BlockSpec((STRETCH, GROUP_COLS), lambda b, g: (b, g)),
            pl.BlockSpec((STRETCH, GROUP_COLS), lambda b, g: (b, g)),
            pl.BlockSpec((STRETCH, GROUP_COLS), lambda b, g: (b, g)),
            pl.BlockSpec((1, STATE, GROUP_COLS), lambda b, g: (b, 0, g)),
            pl.BlockSpec((1, STRETCH, PER_GROUP), lambda b, g: (g, b, 0)),
            pl.BlockSpec((1, PER_GROUP, STRETCH), lambda b, g: (g, 0, b)),
            pl.BlockSpec((STRETCH, 128), lambda b, g: (b, 0)),
            pl.BlockSpec((8, STRETCH), lambda b, g: (0, b)),
            pl.BlockSpec((8, 128), lambda b, g: (b, 0)),
            pl.BlockSpec((1, GROUP_COLS), lambda b, g: (0, g)),
            pl.BlockSpec((1, GROUP_COLS), lambda b, g: (0, g)),
        ],
        out_specs=pl.BlockSpec((STRETCH, GROUP_COLS), lambda b, g: (b, g)),
        out_shape=jax.ShapeDtypeStruct((tok, INNER), jnp.bfloat16),
        scratch_shapes=[pltpu.VMEM((STRETCH, GROUP_COLS), jnp.float32)],
    )(conv, conv, conv, u, z_gate, hbt, cum_g, cumt_g, segc, segr, eb, dsk, gain)


def compose(state_dev, decay_dev):
    peers = lax.axis_size("ctx")
    width = INNER // peers
    pieces = state_dev.reshape(STATE, peers, width).transpose(1, 0, 2)
    payload = jnp.concatenate([pieces, decay_dev.reshape(peers, 1, width)], axis=1)
    got = lax.all_to_all(payload, "ctx", split_axis=0, concat_axis=0, tiled=True)
    states = got[:, :STATE, :]
    span = max(1, width // HEAD_DIM)
    sub = width // span
    decays = got[:, STATE, :].reshape(peers, span, sub)[:, :, 0].T
    dest = lax.broadcasted_iota(jnp.int32, (peers, peers, peers), 0)
    src = lax.broadcasted_iota(jnp.int32, (peers, peers, peers), 1)
    mid = lax.broadcasted_iota(jnp.int32, (peers, peers, peers), 2)
    between = (mid > src) & (mid < dest)
    factors = jnp.where(between[None], decays[:, None, None, :], 1.0)
    links = jnp.prod(factors, axis=3)
    links = jnp.where((src[:, :, 0] < dest[:, :, 0])[None], links, 0.0)
    entering = jnp.einsum(
        "hdj,jnhp->dnhp",
        links,
        states.reshape(peers, STATE, span, sub),
        precision=lax.Precision.HIGHEST,
    ).reshape(peers, STATE, width)
    back = lax.all_to_all(
        entering.astype(jnp.bfloat16), "ctx", split_axis=0, concat_axis=0, tiled=True
    )
    return back.transpose(1, 0, 2).reshape(STATE, INNER).astype(jnp.float32)


def local(xbc, z_gate, dt_raw, lengths, conv_weight, conv_bias, dt_bias, a_log, d_skip, norm_gain):
    tok = xbc.shape[0]
    nb = tok // STRETCH
    first_pos = lax.axis_index("ctx") * tok
    rim_rows = shifted(xbc[tok - (CONV - 1) :], "ctx", 1)
    extended = jnp.concatenate([rim_rows, xbc], axis=0)
    positions = first_pos - (CONV - 1) + jnp.arange(tok + CONV - 1)
    conv = causal_conv(extended, positions, lengths, conv_weight, conv_bias)
    step = jax.nn.softplus(dt_raw.astype(jnp.float32) + dt_bias[None, :])
    log_decay = -step * jnp.exp(a_log)[None, :]
    cum = jnp.cumsum(log_decay.reshape(nb, STRETCH, HEADS), axis=1).reshape(tok, HEADS)
    u = (
        conv[:, :INNER].astype(jnp.float32).reshape(tok, HEADS, HEAD_DIM) * step[:, :, None]
    ).astype(jnp.bfloat16).reshape(tok, INNER)
    segments = segment_of(first_pos + jnp.arange(tok), lengths)
    seg_before = segment_of(first_pos + jnp.arange(nb) * STRETCH - 1, lengths)
    seg_last = segments.reshape(nb, STRETCH)[:, -1]
    cum_last = cum.reshape(nb, STRETCH, HEADS)[:, -1, :]
    block_decay = jnp.where((seg_last == seg_before)[:, None], jnp.exp(cum_last), 0.0)

    cum_g = cum.reshape(tok, GROUPS, PER_GROUP).transpose(1, 0, 2)
    cumt_g = cum.T.reshape(GROUPS, PER_GROUP, tok)
    segc = jnp.broadcast_to(segments[:, None], (tok, 128)).astype(jnp.int32)
    segr = jnp.broadcast_to(segments[None, :], (8, tok)).astype(jnp.int32)
    eb = jnp.broadcast_to(seg_before[:, None, None], (nb, 8, 128)).reshape(nb * 8, 128)
    eb = eb.astype(jnp.int32)
    bt = conv[:, INNER : INNER + GROUPS * STATE].T

    ends = block_states(bt, u, cum_g, segc)
    col_decay = jnp.repeat(block_decay, HEAD_DIM, axis=1)
    state_dev = ends[0]
    decay_dev = col_decay[0]
    for b in range(1, nb):
        state_dev = col_decay[b][None, :] * state_dev + ends[b]
        decay_dev = decay_dev * col_decay[b]
    state_in = compose(state_dev, decay_dev)
    entering = [state_in]
    for b in range(1, nb):
        entering.append(col_decay[b - 1][None, :] * entering[-1] + ends[b - 1])
    hbt = jnp.stack(entering).astype(jnp.bfloat16)

    dsk = jnp.repeat(d_skip, HEAD_DIM)[None, :]
    gain = norm_gain[None, :]
    return mix(conv, u, z_gate, hbt, cum_g, cumt_g, segc, segr, eb, dsk, gain)


def solution(mesh):
    return jax.shard_map(
        local,
        mesh=mesh,
        in_specs=(
            P(("group", "ctx"), None),
            P(("group", "ctx"), None),
            P(("group", "ctx"), None),
            P("group"),
            P(),
            P(),
            P(),
            P(),
            P(),
            P(),
        ),
        out_specs=P(("group", "ctx"), None),
        check_vma=False,
    )
```

time: 663 us -> 297 us (0.45)
  the two profiles are of different devices: /device:TPU:13 before, /device:TPU:15 now
where the time goes in v1:
time: 297 us; the launch traced here: 296 us
  waiting for transfers between devices  141 us (47%)
  local copies, waits for them, and re-layouts  52.2 us (18%)
  other arithmetic  41.7 us (14%)
  Pallas kernels  41.1 us (14%)
  starting transfers between devices  13.7 us (5%)
  matrix products  5.88 us (2%)
    all_to_all x1, waiting for transfers between devices, compose(): lax.all_to_all(payload, 'ctx', split_axis=0, concat_axis=0, tiled=True)  95.2 us
    all_to_all x1, waiting for transfers between devices, compose(): lax.all_to_all(entering.astype(jnp.bfloat16), 'ctx', split_axis=0, concat...  45.7 us
    pallas_call x1, Pallas kernels, mix(): pl.pallas_call(mix_kernel, grid=(nb, GROUPS), in_specs=[pl.BlockSpec((STR...  31.2 us
    convert_element_type x1, other arithmetic, causal_conv(): return jax.nn.silu(summed + conv_bias[None, :]).astype(jnp.bfloat16)  16.4 us
    mul x2, local copies, waits for them, and re-layouts, local(): conv[:, :INNER].astype(jnp.float32).reshape(tok, HEADS, HEAD_DIM)  13.2 us
    slice x2, local copies, waits for them, and re-layouts, compose(): states = got[:, :STATE, :]  10.1 us
    pallas_call x1, Pallas kernels, block_states(): pl.pallas_call(state_kernel, grid=(nb, GROUPS), in_specs=[pl.BlockSpec((S...  9.94 us
    convert_element_type x1, other arithmetic, local(): u = (conv[:, :INNER].astype(jnp.float32).reshape(tok, HEADS, HEAD_DIM) *...  8.02 us
  transfers between devices with their start and end apart: 3, of which 2 were waited for; matrix products, arithmetic and copies ran while one was open for 8% of the time, Pallas kernels for 0%

profile of v1, /device:TPU:15, one launch (start us, length us, event | category | flops | bytes accessed | tf_op | source)
XLA Modules:
  0.0 295.7 jit_solution(6221361048581560629)
XLA Ops:
  0.0 0.9 slice.106
  0.9 3.7 %collective-permute-start = (bf16[3,5120]{1,0:T(4,128)(2,1)S(1)}, bf16[3,5120]{1,0:T(4,128)(2,1)S(1)}, u32[]{:S(2)}, u32[]{:S(2)}) collective-permute-start(bf16[3,5120]{1,0:T(4,128)(2,1)S(1)} %slice.106), channel_id=1, source_target_pairs={{0,1},{1,2},{2,3},{3,4},{4,5},{5,6},{6,7},{7,8},{8,9},{9,10},{10,1... | collective-permute-start | bytes 92168 | tf_op jit(solution)/shard_map/ppermute | solution.py:23
  4.7 0.7 exp.19
  5.3 0.8 reduce-window.18
  6.2 0.2 fusion.13
  6.6 1.2 fusion.16
  7.8 1.0 negate_multiply_fusion
  8.8 1.2 reduce-window.19
  10.1 0.2 slice_reduce_fusion
  10.3 0.1 bitcast_bitcast_fusion
  10.4 0.2 fusion.4
  10.6 0.2 compare_reduce_fusion
  10.9 0.1 copy.59
  11.1 0.1 reshape_reshape.3
  11.6 0.1 mul.136
  11.7 1.0 copy.60
  12.7 4.3 %mul.127 = f32[512,64,64]{0,2,1:T(8,128)} broadcast(f32[512,64]{0,1:T(8,128)S(1)} %get-tuple-element.16), dimensions={0,1} | broadcast | bytes 8519680 | tf_op jit(solution)/shard_map/mul | solution.py:176
  17.0 8.9 %copy.54 = f32[512,4096]{1,0:T(8,128)} copy(f32[512,4096]{0,1:T(8,128)} %bitcast.66) | data formatting | bytes 16777216 | tf_op jit(solution)/shard_map/mul | solution.py:176
  26.0 16.4 %multiply_convert_fusion.c_ref.b_ref.x_ref = bf16[512,5120]{1,0:T(8,128)(2,1)S(1)} fusion(bf16[512,5120]{1,0:T(8,128)(2,1)} %param.10, bf16[3,5120]{1,0:T(4,128)(2,1)S(1)} %collective-permute-done, f32[5120]{0:T(1024)S(1)} %copy-done.1, f32[5120]{0:T(1024)S(1)} %bitcast.81, f32[5120]{0:T(1024)S(1)} %bitcast.82, f32[5120]{0:T(1024)S(1)} %bitcast.80, ...), kind=kLoop, calls=%fused_computation | loop fusion | flops 78643200 | bytes 10620928 | tf_op jit(solution)/shard_map/convert_element_type | solution.py:42
  42.4 2.4 copy-done
  44.8 1.0 copy.61.bt_ref
  45.8 8.0 %multiply_convert_fusion.1.u_ref = bf16[512,4096]{1,0:T(8,128)(2,1)} fusion(f32[512,4096]{1,0:T(8,128)} %copy.54, bf16[512,5120]{1,0:T(8,128)(2,1)} %copy-done), kind=kLoop, calls=%fused_computation.1 | loop fusion | flops 6291456 | bytes 16777216 | tf_op jit(solution)/shard_map/convert_element_type | solution.py:177
  53.8 0.8 broadcast_in_dim.146.segc_ref
  54.7 9.9 %shard_map.100 = f32[2,256,4096]{2,1,0:T(8,128)} custom-call(bf16[512,512]{1,0:T(8,128)(2,1)} %copy.61.bt_ref, bf16[512,4096]{1,0:T(8,128)(2,1)} %multiply_convert_fusion.1.u_ref, f32[2,512,32]{2,1,0:T(8,128)} %bitcast.74, s32[512,128]{1,0:T(8,128)} %broadcast_in_dim.146.segc_ref), custom_call_target="tpu_custom_call" | custom-call | tf_op jit(solution)/shard_map/pallas_call | solution.py:60
  64.6 4.0 %fusion.15 = (f32[1,256,4096]{2,1,0:T(8,128)S(1)}, f32[1,256,4096]{2,1,0:T(8,128)S(1)}) fusion(f32[2,256,4096]{2,1,0:T(8,128)} %shard_map.100), kind=kLoop, calls=%fused_computation.56 | loop fusion | bytes 16777216 | tf_op jit(solution)/shard_map/slice | solution.py:194
  68.6 1.7 copy.74
  70.4 1.7 copy.75
  72.1 4.6 %fusion.2 = f32[16,256,256]{2,1,0:T(8,128)S(1)} fusion(f32[256,16,256]{2,1,0:T(8,128)S(1)} %bitcast.69, f32[256,16,256]{2,1,0:T(8,128)S(1)} %bitcast.68, f32[16,256]{1,0:T(8,128)S(1)} %broadcast_in_dim.145), kind=kLoop, calls=%fused_computation.10 | loop fusion | flops 2097152 | bytes 12599296 | tf_op jit(solution)/shard_map/transpose | solution.py:138
  76.7 2.5 pad_maximum_fusion.1
  79.2 5.0 %all-to-all-start = ((f32[16,257,256]{2,1,0:T(8,128)}), f32[16,257,256]{2,1,0:T(8,128)}, u32[]{:S(2)}, u32[]{:S(2)}) async-start(f32[16,257,256]{2,1,0:T(8,128)} %pad_maximum_fusion.1), calls=%async_computation | async-start | bytes 8650752 | tf_op jit(solution)/shard_map/all_to_all | solution.py:140
  84.2 95.2 %all-to-all-done = f32[16,257,256]{2,1,0:T(8,128)} async-done(((f32[16,257,256]{2,1,0:T(8,128)}), f32[16,257,256]{2,1,0:T(8,128)}, u32[]{:S(2)}, u32[]{:S(2)}) %all-to-all-start) | async-done | bytes 4210720 | tf_op jit(solution)/shard_map/all_to_all | solution.py:140
  179.5 4.6 %slice.147 = f32[16,256,256]{2,1,0:T(8,128)} slice(f32[16,257,256]{2,1,0:T(8,128)} %all-to-all-done), slice={[0:16], [0:256], [0:256]} | slice | bytes 8388608 | tf_op jit(solution)/shard_map/slice | solution.py:141
  184.1 5.5 %copy.64 = f32[16,256,256]{1,0,2:T(8,128)} copy(f32[16,256,256]{2,1,0:T(8,128)} %slice.147) | data formatting | bytes 8388608 | tf_op jit(solution)/shard_map/slice | solution.py:141
  189.5 0.9 slice_reduce_fusion.1
  190.7 1.2 select_reduce_fusion
  191.8 5.9 %convolution_convert_fusion = bf16[4,256,64,16]{1,3,2,0:T(8,128)(2,1)S(1)} fusion(f32[16,256,4,64]{1,0,3,2:T(8,128)} %bitcast.67, f32[4,16,16]{2,1,0:T(8,128)S(1)} %select_reduce_fusion, pred[16,16]{1,0:T(8,128)(4,1)S(1)} %fusion.9), kind=kOutput, calls=%fused_computation.13 | convolution fusion | flops 202376192 | bytes 6295808 | tf_op jit(solution)/shard_map/hdj,jnhp->dnhp/dot_general | solution.py:152
  197.7 2.7 copy.66
  200.5 4.9 %all-to-all-start.1 = ((bf16[16,256,256]{2,1,0:T(8,128)(2,1)}), bf16[16,256,256]{2,1,0:T(8,128)(2,1)S(1)}, u32[]{:S(2)}, u32[]{:S(2)}) async-start(bf16[16,256,256]{2,1,0:T(8,128)(2,1)} %copy.66), calls=%async_computation.1 | async-start | bytes 4194304 | tf_op jit(solution)/shard_map/all_to_all | solution.py:158
  205.6 0.7 broadcast_in_dim_reshape.3.dsk_ref
  206.3 0.7 copy.73
  207.1 45.7 %all-to-all-done.1 = bf16[16,256,256]{2,1,0:T(8,128)(2,1)S(1)} async-done(((bf16[16,256,256]{2,1,0:T(8,128)(2,1)}), bf16[16,256,256]{2,1,0:T(8,128)(2,1)S(1)}, u32[]{:S(2)}, u32[]{:S(2)}) %all-to-all-start.1) | async-done | bytes 2097184 | tf_op jit(solution)/shard_map/all_to_all | solution.py:158
  252.8 2.5 copy.67
  255.3 2.9 convert_element_type.79
  258.2 2.8 add_convert_fusion
  261.0 2.3 pad_maximum_fusion.2.hbt_ref
  263.3 0.7 broadcast_in_dim.158.eb_ref
  263.9 0.6 broadcast_in_dim.155.segr_ref
  264.5 31.2 %shard_map.101 = bf16[512,4096]{1,0:T(8,128)(2,1)} custom-call(bf16[512,5120]{1,0:T(8,128)(2,1)} %copy-done, bf16[512,5120]{1,0:T(8,128)(2,1)} %copy-done, bf16[512,5120]{1,0:T(8,128)(2,1)} %copy-done, bf16[512,4096]{1,0:T(8,128)(2,1)} %multiply_convert_fusion.1.u_ref, bf16[512,4096]{1,0:T(8,128)(2,1)} %z_ref.1, ...), custom_call_target="tpu_custom_call" | custom-call | tf_op jit(solution)/shard_map/pallas_call | solution.py:111
  (36 shorter events, 1.6 us)
Async XLA Ops:
  0.9 25.0 %collective-permute-start = (bf16[3,5120]{1,0:T(4,128)(2,1)S(1)}, bf16[3,5120]{1,0:T(4,128)(2,1)S(1)}, u32[]{:S(2)}, u32[]{:S(2)}) collective-permute-start(bf16[3,5120]{1,0:T(4,128)(2,1)S(1)} %slice.106), channel_id=1, source_target_pairs={{0,1},{1,2},{2,3},{3,4},{4,5},{5,6},{6,7},{7,8},{8,9},{9,10},{10,1... | collective-permute-start | bytes 92168 | tf_op jit(solution)/shard_map/ppermute | solution.py:23
  17.0 9.0 %copy-start.1 = (f32[5120]{0:T(1024)S(1)}, f32[5120]{0:T(1024)}, u32[]{:S(2)}) copy-start(f32[5120]{0:T(1024)} %param.15) | copy-start | bytes 61444
  42.4 2.4 copy-start
  79.2 100.3 %all-to-all-start = ((f32[16,257,256]{2,1,0:T(8,128)}), f32[16,257,256]{2,1,0:T(8,128)}, u32[]{:S(2)}, u32[]{:S(2)}) async-start(f32[16,257,256]{2,1,0:T(8,128)} %pad_maximum_fusion.1), calls=%async_computation | async-start | bytes 8650752 | tf_op jit(solution)/shard_map/all_to_all | solution.py:140
  197.7 7.8 %copy-start.2 = (f32[64]{0:T(128)S(1)}, f32[64]{0:T(128)}, u32[]{:S(2)}) copy-start(f32[64]{0:T(128)} %param.18) | copy-start | bytes 772
  200.5 52.3 %all-to-all-start.1 = ((bf16[16,256,256]{2,1,0:T(8,128)(2,1)}), bf16[16,256,256]{2,1,0:T(8,128)(2,1)S(1)}, u32[]{:S(2)}, u32[]{:S(2)}) async-start(bf16[16,256,256]{2,1,0:T(8,128)(2,1)} %copy.66), calls=%async_computation.1 | async-start | bytes 4194304 | tf_op jit(solution)/shard_map/all_to_all | solution.py:158

commit v2 on v1

--- a/solution.py
+++ b/solution.py
@@ -42,20 +42,22 @@
     return jax.nn.silu(summed + conv_bias[None, :]).astype(jnp.bfloat16)
 
 
-def state_kernel(bt_ref, u_ref, cum_ref, segc_ref, out_ref, uw_ref):
+def state_kernel(bt_ref, x_ref, dt_ref, cum_ref, segc_ref, out_ref, uw_ref):
     cum = cum_ref[0]
+    step = dt_ref[0]
     segc = segc_ref[:, 0:1]
     last = cum[STRETCH - 1 : STRETCH, :]
     seg_last = segc[STRETCH - 1 : STRETCH, :]
     w = jnp.where(segc == seg_last, jnp.exp(last - cum), 0.0)
     for j in range(PER_GROUP):
         cols = slice(j * HEAD_DIM, (j + 1) * HEAD_DIM)
-        uw_ref[:, cols] = (u_ref[:, cols].astype(jnp.float32) * w[:, j : j + 1]).astype(jnp.bfloat16)
+        scaled = (x_ref[:, cols].astype(jnp.float32) * step[:, j : j + 1]).astype(jnp.bfloat16)
+        uw_ref[:, cols] = (scaled.astype(jnp.float32) * w[:, j : j + 1]).astype(jnp.bfloat16)
     out_ref[0] = jnp.dot(bt_ref[...], uw_ref[...], preferred_element_type=jnp.float32)
 
 
-def block_states(bt, u, cum_g, segc):
-    tok = u.shape[0]
+def block_states(bt, conv, dt_g, cum_g, segc):
+    tok = conv.shape[0]
     nb = tok // STRETCH
     return pl.pallas_call(
         state_kernel,
@@ -64,16 +66,17 @@
             pl.BlockSpec((STATE, STRETCH), lambda b, g: (g, b)),
             pl.BlockSpec((STRETCH, GROUP_COLS), lambda b, g: (b, g)),
             pl.BlockSpec((1, STRETCH, PER_GROUP), lambda b, g: (g, b, 0)),
+            pl.BlockSpec((1, STRETCH, PER_GROUP), lambda b, g: (g, b, 0)),
             pl.BlockSpec((STRETCH, 128), lambda b, g: (b, 0)),
         ],
         out_specs=pl.BlockSpec((1, STATE, GROUP_COLS), lambda b, g: (b, 0, g)),
         out_shape=jax.ShapeDtypeStruct((nb, STATE, INNER), jnp.float32),
         scratch_shapes=[pltpu.VMEM((STRETCH, GROUP_COLS), jnp.bfloat16)],
-    )(bt, u, cum_g, segc)
+    )(bt, conv, dt_g, cum_g, segc)
 
 
 def mix_kernel(
-    c_ref, b_ref, x_ref, u_ref, z_ref, hbt_ref, cum_ref, cumt_ref, segc_ref, segr_ref, eb_ref,
+    c_ref, b_ref, x_ref, dt_ref, z_ref, hbt_ref, cum_ref, cumt_ref, segc_ref, segr_ref, eb_ref,
     dsk_ref, gain_ref, out_ref, y_ref,
 ):
     cmat = c_ref[...]
@@ -87,6 +90,7 @@
     gram = jnp.where((segc == segr) & (cols <= rows), gram, 0.0)
     cum = cum_ref[0]
     cumt = cumt_ref[0]
+    step = dt_ref[0]
     entry = eb_ref[0:1, 0:1]
     in_weight = jnp.where(segc == entry, jnp.exp(cum), 0.0)
     inter = jnp.dot(cmat, hbt_ref[0], preferred_element_type=jnp.float32)
@@ -94,7 +98,8 @@
         hc = slice(j * HEAD_DIM, (j + 1) * HEAD_DIM)
         gap = jnp.minimum(cum[:, j : j + 1] - cumt[j : j + 1, :], 0.0)
         weights = (gram * jnp.exp(gap)).astype(jnp.bfloat16)
-        intra = jnp.dot(weights, u_ref[:, hc], preferred_element_type=jnp.float32)
+        scaled = (x_ref[:, hc].astype(jnp.float32) * step[:, j : j + 1]).astype(jnp.bfloat16)
+        intra = jnp.dot(weights, scaled, preferred_element_type=jnp.float32)
         y_ref[:, hc] = intra + inter[:, hc] * in_weight[:, j : j + 1]
     y = y_ref[...] + dsk_ref[...] * x_ref[...].astype(jnp.float32)
     zf = z_ref[...].astype(jnp.float32)
@@ -103,8 +108,8 @@
     out_ref[...] = (gated * lax.rsqrt(mean_square) * gain_ref[...]).astype(jnp.bfloat16)
 
 
-def mix(conv, u, z_gate, hbt, cum_g, cumt_g, segc, segr, eb, dsk, gain):
-    tok = u.shape[0]
+def mix(conv, dt_g, z_gate, hbt, cum_g, cumt_g, segc, segr, eb, dsk, gain):
+    tok = conv.shape[0]
     nb = tok // STRETCH
     b_col = INNER // STATE
     c_col = b_col + GROUPS
@@ -115,7 +120,7 @@
             pl.BlockSpec((STRETCH, STATE), lambda b, g: (b, c_col + g)),
             pl.BlockSpec((STRETCH, STATE), lambda b, g: (b, b_col + g)),
             pl.BlockSpec((STRETCH, GROUP_COLS), lambda b, g: (b, g)),
-            pl.BlockSpec((STRETCH, GROUP_COLS), lambda b, g: (b, g)),
+            pl.BlockSpec((1, STRETCH, PER_GROUP), lambda b, g: (g, b, 0)),
             pl.BlockSpec((STRETCH, GROUP_COLS), lambda b, g: (b, g)),
             pl.BlockSpec((1, STATE, GROUP_COLS), lambda b, g: (b, 0, g)),
             pl.BlockSpec((1, STRETCH, PER_GROUP), lambda b, g: (g, b, 0)),
@@ -129,19 +134,29 @@
         out_specs=pl.BlockSpec((STRETCH, GROUP_COLS), lambda b, g: (b, g)),
         out_shape=jax.ShapeDtypeStruct((tok, INNER), jnp.bfloat16),
         scratch_shapes=[pltpu.VMEM((STRETCH, GROUP_COLS), jnp.float32)],
-    )(conv, conv, conv, u, z_gate, hbt, cum_g, cumt_g, segc, segr, eb, dsk, gain)
+    )(conv, conv, conv, dt_g, z_gate, hbt, cum_g, cumt_g, segc, segr, eb, dsk, gain)
 
 
 def compose(state_dev, decay_dev):
     peers = lax.axis_size("ctx")
     width = INNER // peers
     pieces = state_dev.reshape(STATE, peers, width).transpose(1, 0, 2)
-    payload = jnp.concatenate([pieces, decay_dev.reshape(peers, 1, width)], axis=1)
+    decay_hi = decay_dev.astype(jnp.bfloat16)
+    decay_lo = (decay_dev - decay_hi.astype(jnp.float32)).astype(jnp.bfloat16)
+    payload = jnp.concatenate(
+        [
+            pieces.astype(jnp.bfloat16),
+            decay_hi.reshape(peers, 1, width),
+            decay_lo.reshape(peers, 1, width),
+        ],
+        axis=1,
+    )
     got = lax.all_to_all(payload, "ctx", split_axis=0, concat_axis=0, tiled=True)
-    states = got[:, :STATE, :]
+    states = got[:, :STATE, :].astype(jnp.float32)
     span = max(1, width // HEAD_DIM)
     sub = width // span
-    decays = got[:, STATE, :].reshape(peers, span, sub)[:, :, 0].T
+    decay_rows = got[:, STATE, :].astype(jnp.float32) + got[:, STATE + 1, :].astype(jnp.float32)
+    decays = decay_rows.reshape(peers, span, sub)[:, :, 0].T
     dest = lax.broadcasted_iota(jnp.int32, (peers, peers, peers), 0)
     src = lax.broadcasted_iota(jnp.int32, (peers, peers, peers), 1)
     mid = lax.broadcasted_iota(jnp.int32, (peers, peers, peers), 2)
@@ -172,9 +187,6 @@
     step = jax.nn.softplus(dt_raw.astype(jnp.float32) + dt_bias[None, :])
     log_decay = -step * jnp.exp(a_log)[None, :]
     cum = jnp.cumsum(log_decay.reshape(nb, STRETCH, HEADS), axis=1).reshape(tok, HEADS)
-    u = (
-        conv[:, :INNER].astype(jnp.float32).reshape(tok, HEADS, HEAD_DIM) * step[:, :, None]
-    ).astype(jnp.bfloat16).reshape(tok, INNER)
     segments = segment_of(first_pos + jnp.arange(tok), lengths)
     seg_before = segment_of(first_pos + jnp.arange(nb) * STRETCH - 1, lengths)
     seg_last = segments.reshape(nb, STRETCH)[:, -1]
@@ -182,6 +194,7 @@
     block_decay = jnp.where((seg_last == seg_before)[:, None], jnp.exp(cum_last), 0.0)
 
     cum_g = cum.reshape(tok, GROUPS, PER_GROUP).transpose(1, 0, 2)
+    dt_g = step.reshape(tok, GROUPS, PER_GROUP).transpose(1, 0, 2)
     cumt_g = cum.T.reshape(GROUPS, PER_GROUP, tok)
     segc = jnp.broadcast_to(segments[:, None], (tok, 128)).astype(jnp.int32)
     segr = jnp.broadcast_to(segments[None, :], (8, tok)).astype(jnp.int32)
@@ -189,7 +202,7 @@
     eb = eb.astype(jnp.int32)
     bt = conv[:, INNER : INNER + GROUPS * STATE].T
 
-    ends = block_states(bt, u, cum_g, segc)
+    ends = block_states(bt, conv, dt_g, cum_g, segc)
     col_decay = jnp.repeat(block_decay, HEAD_DIM, axis=1)
     state_dev = ends[0]
     decay_dev = col_decay[0]
@@ -204,7 +217,7 @@
 
     dsk = jnp.repeat(d_skip, HEAD_DIM)[None, :]
     gain = norm_gain[None, :]
-    return mix(conv, u, z_gate, hbt, cum_g, cumt_g, segc, segr, eb, dsk, gain)
+    return mix(conv, dt_g, z_gate, hbt, cum_g, cumt_g, segc, segr, eb, dsk, gain)
 
 
 def solution(mesh):

time: 297 us -> 232 us (0.78)
  waiting for transfers between devices: 141 us -> 94.5 us
  local copies, waits for them, and re-layouts: 52.2 us -> 35.1 us
  Pallas kernels: 41.1 us -> 50.4 us
  other arithmetic: 41.7 us -> 34 us
    all_to_all x1, waiting for transfers between devices: 95.2 us -> 48.8 us  [compose(): lax.all_to_all(payload, 'ctx', split_axis=0, concat_axis=0, tiled=True)]
    mul x2 -> x0, local copies, waits for them, and re-layouts: 13.2 us -> none  [local(): conv[:, :INNER].astype(jnp.float32).reshape(tok, HEADS, HEAD_DIM)]
    pallas_call x1, Pallas kernels: 31.2 us -> 36.5 us  [mix(): pl.pallas_call(mix_kernel, grid=(nb, GROUPS), in_specs=[pl.BlockSpec((STR...]
    slice x5 -> x4, local copies, waits for them, and re-layouts: 11.3 us -> 6.4 us  [the longest x2 6.12 us: compose(): states = got[:, :STATE, :].astype(jnp.float32)]
    transpose x1 -> x0, other arithmetic: 4.59 us -> none  [compose(): pieces = state_dev.reshape(STATE, peers, width).transpose(1, 0, 2)]
    pallas_call x1, Pallas kernels: 9.94 us -> 13.9 us  [block_states(): pl.pallas_call(state_kernel, grid=(nb, GROUPS), in_specs=[pl.BlockSpec((S...]
    convert_element_type x1 -> x2, other arithmetic: 8.02 us -> 4.92 us  [the longest x1 4.9 us: compose(): pieces.astype(jnp.bfloat16)]
  transfers between devices with their start and end apart: 3 -> 3, of which waited for: 2 -> 2; matrix products, arithmetic and copies ran while one was open for 8% -> 5% of each run, Pallas kernels for 0% -> 0%
where the time goes in v2:
time: 232 us; the launch traced here: 231 us
  waiting for transfers between devices  94.5 us (41%)
  Pallas kernels  50.4 us (22%)
  local copies, waits for them, and re-layouts  35.1 us (15%)
  other arithmetic  34 us (15%)
  starting transfers between devices  13.7 us (6%)
  matrix products  3.37 us (1%)
    all_to_all x1, waiting for transfers between devices, compose(): lax.all_to_all(payload, 'ctx', split_axis=0, concat_axis=0, tiled=True)  48.8 us
    all_to_all x1, waiting for transfers between devices, compose(): lax.all_to_all(entering.astype(jnp.bfloat16), 'ctx', split_axis=0, concat...  45.7 us
    pallas_call x1, Pallas kernels, mix(): pl.pallas_call(mix_kernel, grid=(nb, GROUPS), in_specs=[pl.BlockSpec((STR...  36.5 us
    convert_element_type x1, other arithmetic, causal_conv(): return jax.nn.silu(summed + conv_bias[None, :]).astype(jnp.bfloat16)  17.4 us
    pallas_call x1, Pallas kernels, block_states(): pl.pallas_call(state_kernel, grid=(nb, GROUPS), in_specs=[pl.BlockSpec((S...  13.9 us
    slice x2, local copies, waits for them, and re-layouts, compose(): states = got[:, :STATE, :].astype(jnp.float32)  6.12 us
    unnamed x6, local copies, waits for them, and re-layouts  5.86 us
    convert_element_type x2, local copies, waits for them, and re-layouts, compose(): return back.transpose(1, 0, 2).reshape(STATE, INNER).astype(jnp.float32)  5.37 us
  transfers between devices with their start and end apart: 3, of which 2 were waited for; matrix products, arithmetic and copies ran while one was open for 5% of the time, Pallas kernels for 0%

profile of v2, /device:TPU:15, one launch (start us, length us, event | category | flops | bytes accessed | tf_op | source)
XLA Modules:
  0.0 231.2 jit_solution(1635869954511169313)
XLA Ops:
  0.0 0.9 slice.106
  0.9 3.7 %collective-permute-start = (bf16[3,5120]{1,0:T(4,128)(2,1)S(1)}, bf16[3,5120]{1,0:T(4,128)(2,1)S(1)}, u32[]{:S(2)}, u32[]{:S(2)}) collective-permute-start(bf16[3,5120]{1,0:T(4,128)(2,1)S(1)} %slice.106), channel_id=1, source_target_pairs={{0,1},{1,2},{2,3},{3,4},{4,5},{5,6},{6,7},{7,8},{8,9},{9,10},{10,1... | collective-permute-start | bytes 92168 | tf_op jit(solution)/shard_map/ppermute | solution.py:23
  4.7 1.2 fusion.19
  5.8 0.7 exp.19
  6.5 1.0 negate_multiply_fusion
  7.5 1.2 reduce-window.19
  8.8 0.2 slice_reduce_fusion
  9.0 0.1 bitcast_bitcast_fusion
  9.1 0.2 fusion.5
  9.3 0.8 reduce-window.18
  10.2 0.2 fusion.16
  10.4 0.1 copy.54
  10.6 0.2 compare_reduce_fusion
  11.1 0.1 mul.126
  11.4 0.1 copy.58
  11.5 1.0 copy.53
  12.5 0.1 reshape_reshape.3
  12.6 1.0 copy.59
  13.6 0.1 broadcast_in_dim.144
  13.7 17.4 %multiply_convert_fusion.x_ref.c_ref.b_ref = bf16[512,5120]{1,0:T(8,128)(2,1)S(1)} fusion(bf16[512,5120]{1,0:T(8,128)(2,1)} %param.10, bf16[3,5120]{1,0:T(4,128)(2,1)S(1)} %collective-permute-done, f32[5120]{0:T(1024)} %param.15, f32[5120]{0:T(1024)S(1)} %bitcast.84, f32[5120]{0:T(1024)S(1)} %bitcast.85, f32[5120]{0:T(1024)S(1)} %bitcast.83, ...), kind=kLoop, calls=%fused_computation | loop fusion | flops 78643200 | bytes 10620928 | tf_op jit(solution)/shard_map/convert_element_type | solution.py:42
  31.1 2.4 %copy-done = bf16[512,5120]{1,0:T(8,128)(2,1)} copy-done((bf16[512,5120]{1,0:T(8,128)(2,1)}, bf16[512,5120]{1,0:T(8,128)(2,1)S(1)}, u32[]{:S(2)}) %copy-start) | copy-done | bytes 5242904
  33.6 1.0 copy.60.bt_ref
  34.6 0.8 broadcast_in_dim.145.segc_ref
  35.4 13.9 %shard_map.100 = f32[2,256,4096]{2,1,0:T(8,128)} custom-call(bf16[512,512]{1,0:T(8,128)(2,1)} %copy.60.bt_ref, bf16[512,5120]{1,0:T(8,128)(2,1)} %copy-done, f32[2,512,32]{2,1,0:T(8,128)} %bitcast.74, f32[2,512,32]{2,1,0:T(8,128)} %bitcast.76, s32[512,128]{1,0:T(8,128)} %broadcast_in_dim.145.segc_ref), custom_call_target="tpu_custom_call" | custom-call | tf_op jit(solution)/shard_map/pallas_call | solution.py:62
  49.3 4.0 %fusion.18 = (f32[1,256,4096]{2,1,0:T(8,128)S(1)}, f32[1,256,4096]{2,1,0:T(8,128)S(1)}) fusion(f32[2,256,4096]{2,1,0:T(8,128)} %shard_map.100), kind=kLoop, calls=%fused_computation.60 | loop fusion | bytes 16777216 | tf_op jit(solution)/shard_map/slice | solution.py:207
  53.3 1.7 copy.74
  55.0 1.7 copy.73
  56.8 4.9 %fusion.3 = bf16[16,256,256]{2,1,0:T(8,128)(2,1)S(1)} fusion(f32[256,16,256]{2,1,0:T(8,128)S(1)} %bitcast.67, f32[256,16,256]{2,1,0:T(8,128)S(1)} %bitcast.68, f32[16,256]{1,0:T(8,128)S(1)} %broadcast_in_dim.144), kind=kLoop, calls=%fused_computation.12 | loop fusion | flops 3145728 | bytes 10502144 | tf_op jit(solution)/shard_map/convert_element_type | solution.py:148
  61.7 1.5 pad_maximum_fusion.2
  63.2 5.0 %all-to-all-start = ((bf16[16,258,256]{2,1,0:T(8,128)(2,1)}), bf16[16,258,256]{2,1,0:T(8,128)(2,1)S(1)}, u32[]{:S(2)}, u32[]{:S(2)}) async-start(bf16[16,258,256]{2,1,0:T(8,128)(2,1)} %pad_maximum_fusion.2), calls=%async_computation | async-start | bytes 4325376 | tf_op jit(solution)/shard_map/all_to_all | solution.py:154
  68.2 48.8 %all-to-all-done = bf16[16,258,256]{2,1,0:T(8,128)(2,1)S(1)} async-done(((bf16[16,258,256]{2,1,0:T(8,128)(2,1)}), bf16[16,258,256]{2,1,0:T(8,128)(2,1)S(1)}, u32[]{:S(2)}, u32[]{:S(2)}) %all-to-all-start) | async-done | bytes 2113568 | tf_op jit(solution)/shard_map/all_to_all | solution.py:154
  117.0 1.5 slice.146
  118.6 4.6 %copy.63 = bf16[16,256,256]{1,0,2:T(8,128)(2,1)} copy(bf16[16,256,256]{2,1,0:T(8,128)(2,1)} %slice.146) | data formatting | bytes 4194304 | tf_op jit(solution)/shard_map/slice | solution.py:155
  123.3 0.1 copy.64
  123.4 1.2 select_reduce_fusion
  124.5 3.4 %convolution_convert_fusion = bf16[4,256,64,16]{1,3,2,0:T(8,128)(2,1)S(1)} fusion(bf16[16,256,4,64]{1,0,3,2:T(8,128)(2,1)} %bitcast.72, f32[4,16,16]{2,1,0:T(8,128)S(1)} %select_reduce_fusion, pred[16,16]{1,0:T(8,128)(4,1)S(1)} %fusion.12), kind=kOutput, calls=%fused_computation.13 | convolution fusion | flops 202376192 | bytes 4198656 | tf_op jit(solution)/shard_map/hdj,jnhp->dnhp/dot_general | solution.py:167
  127.9 2.7 %copy.65 = bf16[16,256,256]{2,1,0:T(8,128)(2,1)} copy(bf16[16,256,256]{1,0,2:T(8,128)(2,1)S(1)} %bitcast.73) | data formatting | bytes 4194304 | tf_op jit(solution)/shard_map/convert_element_type | solution.py:174
  130.7 4.9 %all-to-all-start.1 = ((bf16[16,256,256]{2,1,0:T(8,128)(2,1)}), bf16[16,256,256]{2,1,0:T(8,128)(2,1)S(1)}, u32[]{:S(2)}, u32[]{:S(2)}) async-start(bf16[16,256,256]{2,1,0:T(8,128)(2,1)} %copy.65), calls=%async_computation.1 | async-start | bytes 4194304 | tf_op jit(solution)/shard_map/all_to_all | solution.py:173
  135.7 0.7 copy.72
  136.6 0.7 broadcast_in_dim_reshape.3.dsk_ref
  137.3 45.7 %all-to-all-done.1 = bf16[16,256,256]{2,1,0:T(8,128)(2,1)S(1)} async-done(((bf16[16,256,256]{2,1,0:T(8,128)(2,1)}), bf16[16,256,256]{2,1,0:T(8,128)(2,1)S(1)}, u32[]{:S(2)}, u32[]{:S(2)}) %all-to-all-start.1) | async-done | bytes 2097184 | tf_op jit(solution)/shard_map/all_to_all | solution.py:173
  183.0 2.5 %copy.66 = bf16[256,16,256]{2,1,0:T(8,128)(2,1)} copy(bf16[256,16,256]{2,0,1:T(8,128)(2,1)S(1)} %bitcast.71) | data formatting | bytes 4194304 | tf_op jit(solution)/shard_map/convert_element_type | solution.py:176
  185.5 2.9 %convert_element_type.128 = bf16[1,256,4096]{2,1,0:T(8,128)(2,1)S(1)} reshape(bf16[256,16,256]{2,1,0:T(8,128)(2,1)} %copy.66) | data formatting | bytes 4194304 | tf_op jit(solution)/shard_map/convert_element_type | solution.py:176
  188.4 2.8 %add_convert_fusion = bf16[1,256,4096]{2,1,0:T(8,128)(2,1)S(1)} fusion(bf16[1,256,4096]{2,1,0:T(8,128)(2,1)S(1)} %convert_element_type.128, f32[4096]{0:T(1024)S(1)} %mul.127, f32[2,256,4096]{2,1,0:T(8,128)} %shard_map.100), kind=kLoop, calls=%fused_computation.10 | loop fusion | flops 4194304 | bytes 8404992 | tf_op jit(solution)/shard_map/convert.3
  191.2 2.3 pad_maximum_fusion.1.hbt_ref
  193.5 0.6 broadcast_in_dim.154.segr_ref
  194.1 0.7 broadcast_in_dim.157.eb_ref
  194.7 36.5 %shard_map.101 = bf16[512,4096]{1,0:T(8,128)(2,1)} custom-call(bf16[512,5120]{1,0:T(8,128)(2,1)} %copy-done, bf16[512,5120]{1,0:T(8,128)(2,1)} %copy-done, bf16[512,5120]{1,0:T(8,128)(2,1)} %copy-done, f32[2,512,32]{2,1,0:T(8,128)} %bitcast.75, bf16[512,4096]{1,0:T(8,128)(2,1)} %z_ref.1, bf16[2,256,4096]{2,1,0:T(8,128)(2,1)} %pad_maximum_fusion.1.hbt_ref, ...), custom_call_target="tpu_custom_call" | custom-call | tf_op jit(solution)/shard_map/pallas_call | solution.py:116
  (33 shorter events, 1.4 us)
Async XLA Ops:
  0.9 12.8 %collective-permute-start = (bf16[3,5120]{1,0:T(4,128)(2,1)S(1)}, bf16[3,5120]{1,0:T(4,128)(2,1)S(1)}, u32[]{:S(2)}, u32[]{:S(2)}) collective-permute-start(bf16[3,5120]{1,0:T(4,128)(2,1)S(1)} %slice.106), channel_id=1, source_target_pairs={{0,1},{1,2},{2,3},{3,4},{4,5},{5,6},{6,7},{7,8},{8,9},{9,10},{10,1... | collective-permute-start | bytes 92168 | tf_op jit(solution)/shard_map/ppermute | solution.py:23
  31.1 2.4 %copy-start = (bf16[512,5120]{1,0:T(8,128)(2,1)}, bf16[512,5120]{1,0:T(8,128)(2,1)S(1)}, u32[]{:S(2)}) copy-start(bf16[512,5120]{1,0:T(8,128)(2,1)S(1)} %multiply_convert_fusion.x_ref.c_ref.b_ref) | copy-start | bytes 15728644
  63.2 53.9 %all-to-all-start = ((bf16[16,258,256]{2,1,0:T(8,128)(2,1)}), bf16[16,258,256]{2,1,0:T(8,128)(2,1)S(1)}, u32[]{:S(2)}, u32[]{:S(2)}) async-start(bf16[16,258,256]{2,1,0:T(8,128)(2,1)} %pad_maximum_fusion.2), calls=%async_computation | async-start | bytes 4325376 | tf_op jit(solution)/shard_map/all_to_all | solution.py:154
  127.9 8.6 %copy-start.1 = (f32[64]{0:T(128)S(1)}, f32[64]{0:T(128)}, u32[]{:S(2)}) copy-start(f32[64]{0:T(128)} %param.18) | copy-start | bytes 772
  130.7 52.3 %all-to-all-start.1 = ((bf16[16,256,256]{2,1,0:T(8,128)(2,1)}), bf16[16,256,256]{2,1,0:T(8,128)(2,1)S(1)}, u32[]{:S(2)}, u32[]{:S(2)}) async-start(bf16[16,256,256]{2,1,0:T(8,128)(2,1)} %copy.65), calls=%async_computation.1 | async-start | bytes 4194304 | tf_op jit(solution)/shard_map/all_to_all | solution.py:173

commit v3 on v2

--- a/solution.py
+++ b/solution.py
@@ -75,13 +75,11 @@
     )(bt, conv, dt_g, cum_g, segc)
 
 
-def mix_kernel(
-    c_ref, b_ref, x_ref, dt_ref, z_ref, hbt_ref, cum_ref, cumt_ref, segc_ref, segr_ref, eb_ref,
-    dsk_ref, gain_ref, out_ref, y_ref,
+def intra_kernel(
+    c_ref, b_ref, x_ref, dt_ref, cum_ref, cumt_ref, segc_ref, segr_ref, dsk_ref, out_ref
 ):
-    cmat = c_ref[...]
     gram = lax.dot_general(
-        cmat, b_ref[...], (((1,), (1,)), ((), ())), preferred_element_type=jnp.float32
+        c_ref[...], b_ref[...], (((1,), (1,)), ((), ())), preferred_element_type=jnp.float32
     )
     segc = segc_ref[:, 0:1]
     segr = segr_ref[0:1, :]
@@ -91,50 +89,78 @@
     cum = cum_ref[0]
     cumt = cumt_ref[0]
     step = dt_ref[0]
-    entry = eb_ref[0:1, 0:1]
-    in_weight = jnp.where(segc == entry, jnp.exp(cum), 0.0)
-    inter = jnp.dot(cmat, hbt_ref[0], preferred_element_type=jnp.float32)
     for j in range(PER_GROUP):
         hc = slice(j * HEAD_DIM, (j + 1) * HEAD_DIM)
         gap = jnp.minimum(cum[:, j : j + 1] - cumt[j : j + 1, :], 0.0)
         weights = (gram * jnp.exp(gap)).astype(jnp.bfloat16)
-        scaled = (x_ref[:, hc].astype(jnp.float32) * step[:, j : j + 1]).astype(jnp.bfloat16)
+        xf = x_ref[:, hc].astype(jnp.float32)
+        scaled = (xf * step[:, j : j + 1]).astype(jnp.bfloat16)
         intra = jnp.dot(weights, scaled, preferred_element_type=jnp.float32)
-        y_ref[:, hc] = intra + inter[:, hc] * in_weight[:, j : j + 1]
-    y = y_ref[...] + dsk_ref[...] * x_ref[...].astype(jnp.float32)
+        out_ref[:, hc] = intra + dsk_ref[:, hc] * xf
+
+
+def intra_part(conv, dt_g, cum_g, cumt_g, segc, segr, dsk):
+    tok = conv.shape[0]
+    nb = tok // STRETCH
+    b_col = INNER // STATE
+    c_col = b_col + GROUPS
+    return pl.pallas_call(
+        intra_kernel,
+        grid=(nb, GROUPS),
+        in_specs=[
+            pl.BlockSpec((STRETCH, STATE), lambda b, g: (b, c_col + g)),
+            pl.BlockSpec((STRETCH, STATE), lambda b, g: (b, b_col + g)),
+            pl.BlockSpec((STRETCH, GROUP_COLS), lambda b, g: (b, g)),
+            pl.BlockSpec((1, STRETCH, PER_GROUP), lambda b, g: (g, b, 0)),
+            pl.BlockSpec((1, STRETCH, PER_GROUP), lambda b, g: (g, b, 0)),
+            pl.BlockSpec((1, PER_GROUP, STRETCH), lambda b, g: (g, 0, b)),
+            pl.BlockSpec((STRETCH, 128), lambda b, g: (b, 0)),
+            pl.BlockSpec((8, STRETCH), lambda b, g: (0, b)),
+            pl.BlockSpec((1, GROUP_COLS), lambda b, g: (0, g)),
+        ],
+        out_specs=pl.BlockSpec((STRETCH, GROUP_COLS), lambda b, g: (b, g)),
+        out_shape=jax.ShapeDtypeStruct((tok, INNER), jnp.float32),
+    )(conv, conv, conv, dt_g, cum_g, cumt_g, segc, segr, dsk)
+
+
+def mix_kernel(
+    c_ref, y_ref, z_ref, hbt_ref, cum_ref, segc_ref, eb_ref, gain_ref, out_ref, acc_ref
+):
+    segc = segc_ref[:, 0:1]
+    entry = eb_ref[0:1, 0:1]
+    in_weight = jnp.where(segc == entry, jnp.exp(cum_ref[0]), 0.0)
+    inter = jnp.dot(c_ref[...], hbt_ref[0], preferred_element_type=jnp.float32)
+    for j in range(PER_GROUP):
+        hc = slice(j * HEAD_DIM, (j + 1) * HEAD_DIM)
+        acc_ref[:, hc] = inter[:, hc] * in_weight[:, j : j + 1]
+    y = y_ref[...] + acc_ref[...]
     zf = z_ref[...].astype(jnp.float32)
     gated = y * (zf * jax.nn.sigmoid(zf))
     mean_square = jnp.mean(gated * gated, axis=1, keepdims=True) + 1e-05
     out_ref[...] = (gated * lax.rsqrt(mean_square) * gain_ref[...]).astype(jnp.bfloat16)
 
 
-def mix(conv, dt_g, z_gate, hbt, cum_g, cumt_g, segc, segr, eb, dsk, gain):
+def mix(conv, y_local, z_gate, hbt, cum_g, segc, eb, gain):
     tok = conv.shape[0]
     nb = tok // STRETCH
-    b_col = INNER // STATE
-    c_col = b_col + GROUPS
+    c_col = INNER // STATE + GROUPS
     return pl.pallas_call(
         mix_kernel,
         grid=(nb, GROUPS),
         in_specs=[
             pl.BlockSpec((STRETCH, STATE), lambda b, g: (b, c_col + g)),
-            pl.BlockSpec((STRETCH, STATE), lambda b, g: (b, b_col + g)),
-            pl.BlockSpec((STRETCH, GROUP_COLS), lambda b, g: (b, g)),
-            pl.BlockSpec((1, STRETCH, PER_GROUP), lambda b, g: (g, b, 0)),
+            pl.BlockSpec((STRETCH, GROUP_COLS), lambda b, g: (b, g)),
             pl.BlockSpec((STRETCH, GROUP_COLS), lambda b, g: (b, g)),
             pl.BlockSpec((1, STATE, GROUP_COLS), lambda b, g: (b, 0, g)),
             pl.BlockSpec((1, STRETCH, PER_GROUP), lambda b, g: (g, b, 0)),
-            pl.BlockSpec((1, PER_GROUP, STRETCH), lambda b, g: (g, 0, b)),
             pl.BlockSpec((STRETCH, 128), lambda b, g: (b, 0)),
-            pl.BlockSpec((8, STRETCH), lambda b, g: (0, b)),
             pl.BlockSpec((8, 128), lambda b, g: (b, 0)),
-            pl.BlockSpec((1, GROUP_COLS), lambda b, g: (0, g)),
             pl.BlockSpec((1, GROUP_COLS), lambda b, g: (0, g)),
         ],
         out_specs=pl.BlockSpec((STRETCH, GROUP_COLS), lambda b, g: (b, g)),
         out_shape=jax.ShapeDtypeStruct((tok, INNER), jnp.bfloat16),
         scratch_shapes=[pltpu.VMEM((STRETCH, GROUP_COLS), jnp.float32)],
-    )(conv, conv, conv, dt_g, z_gate, hbt, cum_g, cumt_g, segc, segr, eb, dsk, gain)
+    )(conv, y_local, z_gate, hbt, cum_g, segc, eb, gain)
 
 
 def compose(state_dev, decay_dev):
@@ -203,6 +229,8 @@
     bt = conv[:, INNER : INNER + GROUPS * STATE].T
 
     ends = block_states(bt, conv, dt_g, cum_g, segc)
+    dsk = jnp.repeat(d_skip, HEAD_DIM)[None, :]
+    y_local = intra_part(conv, dt_g, cum_g, cumt_g, segc, segr, dsk)
     col_decay = jnp.repeat(block_decay, HEAD_DIM, axis=1)
     state_dev = ends[0]
     decay_dev = col_decay[0]
@@ -214,10 +242,8 @@
     for b in range(1, nb):
         entering.append(col_decay[b - 1][None, :] * entering[-1] + ends[b - 1])
     hbt = jnp.stack(entering).astype(jnp.bfloat16)
-
-    dsk = jnp.repeat(d_skip, HEAD_DIM)[None, :]
     gain = norm_gain[None, :]
-    return mix(conv, dt_g, z_gate, hbt, cum_g, cumt_g, segc, segr, eb, dsk, gain)
+    return mix(conv, y_local, z_gate, hbt, cum_g, segc, eb, gain)
 
 
 def solution(mesh):

time: 232 us -> 205 us (0.88)
  waiting for transfers between devices: 94.5 us -> 61.7 us
  Pallas kernels: 50.4 us -> 57.3 us
    all_to_all x1, waiting for transfers between devices: 45.7 us -> 12.9 us  [compose(): lax.all_to_all(entering.astype(jnp.bfloat16), 'ctx', split_axis=0, concat...]
    pallas_call x0 -> x1, Pallas kernels: none -> 32.2 us  [intra_part(): pl.pallas_call(intra_kernel, grid=(nb, GROUPS), in_specs=[pl.BlockSpec((S...]
    pallas_call x1, Pallas kernels: 36.5 us -> 11.3 us  [mix(): pl.pallas_call(mix_kernel, grid=(nb, GROUPS), in_specs=[pl.BlockSpec((STR...]
  transfers between devices with their start and end apart: 3 -> 3, of which waited for: 2 -> 2; matrix products, arithmetic and copies ran while one was open for 5% -> 6% of each run, Pallas kernels for 0% -> 16%
where the time goes in v3:
time: 205 us
  waiting for transfers between devices  61.7 us (30%)
  Pallas kernels  57.3 us (28%)
  local copies, waits for them, and re-layouts  35 us (17%)
  other arithmetic  33.4 us (16%)
  starting transfers between devices  13.7 us (7%)
  matrix products  3.37 us (2%)
    all_to_all x1, waiting for transfers between devices, compose(): lax.all_to_all(payload, 'ctx', split_axis=0, concat_axis=0, tiled=True)  48.8 us
    pallas_call x1, Pallas kernels, intra_part(): pl.pallas_call(intra_kernel, grid=(nb, GROUPS), in_specs=[pl.BlockSpec((S...  32.2 us
    convert_element_type x1, other arithmetic, causal_conv(): return jax.nn.silu(summed + conv_bias[None, :]).astype(jnp.bfloat16)  16.7 us
    pallas_call x1, Pallas kernels, block_states(): pl.pallas_call(state_kernel, grid=(nb, GROUPS), in_specs=[pl.BlockSpec((S...  13.7 us
    all_to_all x1, waiting for transfers between devices, compose(): lax.all_to_all(entering.astype(jnp.bfloat16), 'ctx', split_axis=0, concat...  12.9 us
    pallas_call x1, Pallas kernels, mix(): pl.pallas_call(mix_kernel, grid=(nb, GROUPS), in_specs=[pl.BlockSpec((STR...  11.3 us
    slice x2, local copies, waits for them, and re-layouts, compose(): states = got[:, :STATE, :].astype(jnp.float32)  6.07 us
    unnamed x6, local copies, waits for them, and re-layouts  5.78 us
  transfers between devices with their start and end apart: 3, of which 2 were waited for; matrix products, arithmetic and copies ran while one was open for 6% of the time, Pallas kernels for 16%

profile of v3, /device:TPU:15, one launch (start us, length us, event | category | flops | bytes accessed | tf_op | source)
XLA Modules:
  0.0 204.6 jit_solution(12279812242025133806)
XLA Ops:
  0.0 0.9 slice.106
  0.9 3.7 %collective-permute-start = (bf16[3,5120]{1,0:T(4,128)(2,1)S(1)}, bf16[3,5120]{1,0:T(4,128)(2,1)S(1)}, u32[]{:S(2)}, u32[]{:S(2)}) collective-permute-start(bf16[3,5120]{1,0:T(4,128)(2,1)S(1)} %slice.106), channel_id=1, source_target_pairs={{0,1},{1,2},{2,3},{3,4},{4,5},{5,6},{6,7},{7,8},{8,9},{9,10},{10,1... | collective-permute-start | bytes 92168 | tf_op jit(solution)/shard_map/ppermute | solution.py:23
  4.7 1.2 fusion.19
  5.8 0.7 exp.19
  6.5 1.0 negate_multiply_fusion
  7.5 1.2 reduce-window.19
  8.8 0.2 slice_reduce_fusion
  9.0 0.1 bitcast_bitcast_fusion
  9.1 0.8 reduce-window.18
  10.1 0.2 fusion.16
  10.3 0.1 copy.60
  10.4 0.2 fusion.5
  10.6 0.2 compare_reduce_fusion
  11.1 0.1 mul.126
  11.4 0.1 copy.57
  11.5 0.1 reshape_reshape.3
  11.6 1.0 copy.58
  12.6 1.0 copy.53
  13.8 16.7 %multiply_convert_fusion.c_ref.b_ref.x_ref = bf16[512,5120]{1,0:T(8,128)(2,1)S(1)} fusion(bf16[512,5120]{1,0:T(8,128)(2,1)} %param.10, bf16[3,5120]{1,0:T(4,128)(2,1)S(1)} %collective-permute-done, f32[5120]{0:T(1024)} %param.15, f32[5120]{0:T(1024)S(1)} %bitcast.85, f32[5120]{0:T(1024)S(1)} %bitcast.86, f32[5120]{0:T(1024)S(1)} %bitcast.84, ...), kind=kLoop, calls=%fused_computation | loop fusion | flops 78643200 | bytes 10620928 | tf_op jit(solution)/shard_map/convert_element_type | solution.py:42
  30.5 2.3 %copy-done = bf16[512,5120]{1,0:T(8,128)(2,1)} copy-done((bf16[512,5120]{1,0:T(8,128)(2,1)}, bf16[512,5120]{1,0:T(8,128)(2,1)S(1)}, u32[]{:S(2)}) %copy-start) | copy-done | bytes 5242904
  32.8 1.0 copy.61.bt_ref
  33.8 0.8 broadcast_in_dim.139.segc_ref
  34.7 13.7 %shard_map.101 = f32[2,256,4096]{2,1,0:T(8,128)} custom-call(bf16[512,512]{1,0:T(8,128)(2,1)} %copy.61.bt_ref, bf16[512,5120]{1,0:T(8,128)(2,1)} %copy-done, f32[2,512,32]{2,1,0:T(8,128)} %bitcast.77, f32[2,512,32]{2,1,0:T(8,128)} %bitcast.74, s32[512,128]{1,0:T(8,128)} %broadcast_in_dim.139.segc_ref), custom_call_target="tpu_custom_call" | custom-call | tf_op jit(solution)/shard_map/pallas_call | solution.py:62
  48.4 4.0 %fusion.18 = (f32[1,256,4096]{2,1,0:T(8,128)S(1)}, f32[1,256,4096]{2,1,0:T(8,128)S(1)}) fusion(f32[2,256,4096]{2,1,0:T(8,128)} %shard_map.101), kind=kLoop, calls=%fused_computation.60 | loop fusion | bytes 16777216 | tf_op jit(solution)/shard_map/slice | solution.py:235
  52.4 1.7 copy.73
  54.2 1.7 copy.74
  55.9 4.9 %fusion.3 = bf16[16,256,256]{2,1,0:T(8,128)(2,1)S(1)} fusion(f32[256,16,256]{2,1,0:T(8,128)S(1)} %bitcast.68, f32[256,16,256]{2,1,0:T(8,128)S(1)} %bitcast.67, f32[16,256]{1,0:T(8,128)S(1)} %broadcast_in_dim.147), kind=kLoop, calls=%fused_computation.12 | loop fusion | flops 3145728 | bytes 10502144 | tf_op jit(solution)/shard_map/convert_element_type | solution.py:174
  60.8 1.5 pad_maximum_fusion.2
  62.3 5.1 %all-to-all-start = ((bf16[16,258,256]{2,1,0:T(8,128)(2,1)}), bf16[16,258,256]{2,1,0:T(8,128)(2,1)S(1)}, u32[]{:S(2)}, u32[]{:S(2)}) async-start(bf16[16,258,256]{2,1,0:T(8,128)(2,1)} %pad_maximum_fusion.2), calls=%async_computation | async-start | bytes 4325376 | tf_op jit(solution)/shard_map/all_to_all | solution.py:180
  67.4 48.8 %all-to-all-done = bf16[16,258,256]{2,1,0:T(8,128)(2,1)S(1)} async-done(((bf16[16,258,256]{2,1,0:T(8,128)(2,1)}), bf16[16,258,256]{2,1,0:T(8,128)(2,1)S(1)}, u32[]{:S(2)}, u32[]{:S(2)}) %all-to-all-start) | async-done | bytes 2113568 | tf_op jit(solution)/shard_map/all_to_all | solution.py:180
  116.2 1.5 slice.146
  117.7 4.6 %copy.64 = bf16[16,256,256]{1,0,2:T(8,128)(2,1)} copy(bf16[16,256,256]{2,1,0:T(8,128)(2,1)} %slice.146) | data formatting | bytes 4194304 | tf_op jit(solution)/shard_map/slice | solution.py:181
  122.4 0.1 copy.65
  122.5 1.2 select_reduce_fusion
  123.7 3.4 %convolution_convert_fusion = bf16[4,256,64,16]{1,3,2,0:T(8,128)(2,1)S(1)} fusion(bf16[16,256,4,64]{1,0,3,2:T(8,128)(2,1)} %bitcast.72, f32[4,16,16]{2,1,0:T(8,128)S(1)} %select_reduce_fusion, pred[16,16]{1,0:T(8,128)(4,1)S(1)} %fusion.12), kind=kOutput, calls=%fused_computation.13 | convolution fusion | flops 202376192 | bytes 4198656 | tf_op jit(solution)/shard_map/hdj,jnhp->dnhp/dot_general | solution.py:193
  127.0 2.7 %copy.66 = bf16[16,256,256]{2,1,0:T(8,128)(2,1)} copy(bf16[16,256,256]{1,0,2:T(8,128)(2,1)S(1)} %bitcast.73) | data formatting | bytes 4194304 | tf_op jit(solution)/shard_map/convert_element_type | solution.py:200
  129.8 4.9 %all-to-all-start.1 = ((bf16[16,256,256]{2,1,0:T(8,128)(2,1)}), bf16[16,256,256]{2,1,0:T(8,128)(2,1)S(1)}, u32[]{:S(2)}, u32[]{:S(2)}) async-start(bf16[16,256,256]{2,1,0:T(8,128)(2,1)} %copy.66), calls=%async_computation.1 | async-start | bytes 4194304 | tf_op jit(solution)/shard_map/all_to_all | solution.py:199
  134.8 0.7 copy.72
  135.6 0.7 broadcast_in_dim_reshape.3.dsk_ref
  136.4 0.6 broadcast_in_dim.140.segr_ref
  137.0 32.2 %shard_map.100.y_ref = f32[512,4096]{1,0:T(8,128)} custom-call(bf16[512,5120]{1,0:T(8,128)(2,1)} %copy-done, bf16[512,5120]{1,0:T(8,128)(2,1)} %copy-done, bf16[512,5120]{1,0:T(8,128)(2,1)} %copy-done, f32[2,512,32]{2,1,0:T(8,128)} %bitcast.78, f32[2,512,32]{2,1,0:T(8,128)} %bitcast.75, f32[2,32,512]{2,1,0:T(8,128)} %bitcast.79, ...), custom_call_target="tpu_custom_call" | custom-call | tf_op jit(solution)/shard_map/pallas_call | solution.py:107
  169.2 12.9 %all-to-all-done.1 = bf16[16,256,256]{2,1,0:T(8,128)(2,1)S(1)} async-done(((bf16[16,256,256]{2,1,0:T(8,128)(2,1)}), bf16[16,256,256]{2,1,0:T(8,128)(2,1)S(1)}, u32[]{:S(2)}, u32[]{:S(2)}) %all-to-all-start.1) | async-done | bytes 2097184 | tf_op jit(solution)/shard_map/all_to_all | solution.py:199
  182.1 2.5 %copy.67 = bf16[256,16,256]{2,1,0:T(8,128)(2,1)} copy(bf16[256,16,256]{2,0,1:T(8,128)(2,1)S(1)} %bitcast.71) | data formatting | bytes 4194304 | tf_op jit(solution)/shard_map/convert_element_type | solution.py:202
  184.6 2.9 %convert_element_type.128 = bf16[1,256,4096]{2,1,0:T(8,128)(2,1)S(1)} reshape(bf16[256,16,256]{2,1,0:T(8,128)(2,1)} %copy.67) | data formatting | bytes 4194304 | tf_op jit(solution)/shard_map/convert_element_type | solution.py:202
  187.5 2.8 %add_convert_fusion = bf16[1,256,4096]{2,1,0:T(8,128)(2,1)S(1)} fusion(bf16[1,256,4096]{2,1,0:T(8,128)(2,1)S(1)} %convert_element_type.128, f32[4096]{0:T(1024)S(1)} %mul.127, f32[2,256,4096]{2,1,0:T(8,128)} %shard_map.101), kind=kLoop, calls=%fused_computation.10 | loop fusion | flops 4194304 | bytes 8404992 | tf_op jit(solution)/shard_map/convert.3
  190.3 2.3 %pad_maximum_fusion.1.hbt_ref = bf16[2,256,4096]{2,1,0:T(8,128)(2,1)} fusion(bf16[1,256,4096]{2,1,0:T(8,128)(2,1)S(1)} %add_convert_fusion, bf16[1,256,4096]{2,1,0:T(8,128)(2,1)S(1)} %convert_element_type.128), kind=kLoop, calls=%fused_computation.6 | loop fusion | flops 2097152 | bytes 8388608 | tf_op jit(solution)/shard_map/stack | solution.py:244
  192.6 0.7 broadcast_in_dim.158.eb_ref
  193.3 11.3 %shard_map.102 = bf16[512,4096]{1,0:T(8,128)(2,1)} custom-call(bf16[512,5120]{1,0:T(8,128)(2,1)} %copy-done, f32[512,4096]{1,0:T(8,128)} %shard_map.100.y_ref, bf16[512,4096]{1,0:T(8,128)(2,1)} %z_ref.1, bf16[2,256,4096]{2,1,0:T(8,128)(2,1)} %pad_maximum_fusion.1.hbt_ref, f32[2,512,32]{2,1,0:T(8,128)} %bitcast.76, s32[512,128]{1,0:T(8,128)} %broadcast_in_dim.139.segc_ref, ...), custom_call_target="tpu_custom_call" | custom-call | tf_op jit(solution)/shard_map/pallas_call | solution.py:147
  (34 shorter events, 1.5 us)
Async XLA Ops:
  0.9 12.9 %collective-permute-start = (bf16[3,5120]{1,0:T(4,128)(2,1)S(1)}, bf16[3,5120]{1,0:T(4,128)(2,1)S(1)}, u32[]{:S(2)}, u32[]{:S(2)}) collective-permute-start(bf16[3,5120]{1,0:T(4,128)(2,1)S(1)} %slice.106), channel_id=1, source_target_pairs={{0,1},{1,2},{2,3},{3,4},{4,5},{5,6},{6,7},{7,8},{8,9},{9,10},{10,1... | collective-permute-start | bytes 92168 | tf_op jit(solution)/shard_map/ppermute | solution.py:23
  30.5 2.3 %copy-start = (bf16[512,5120]{1,0:T(8,128)(2,1)}, bf16[512,5120]{1,0:T(8,128)(2,1)S(1)}, u32[]{:S(2)}) copy-start(bf16[512,5120]{1,0:T(8,128)(2,1)S(1)} %multiply_convert_fusion.c_ref.b_ref.x_ref) | copy-start | bytes 15728644
  62.3 53.9 %all-to-all-start = ((bf16[16,258,256]{2,1,0:T(8,128)(2,1)}), bf16[16,258,256]{2,1,0:T(8,128)(2,1)S(1)}, u32[]{:S(2)}, u32[]{:S(2)}) async-start(bf16[16,258,256]{2,1,0:T(8,128)(2,1)} %pad_maximum_fusion.2), calls=%async_computation | async-start | bytes 4325376 | tf_op jit(solution)/shard_map/all_to_all | solution.py:180
  127.0 8.5 %copy-start.1 = (f32[64]{0:T(128)S(1)}, f32[64]{0:T(128)}, u32[]{:S(2)}) copy-start(f32[64]{0:T(128)} %param.18) | copy-start | bytes 772
  129.8 52.3 %all-to-all-start.1 = ((bf16[16,256,256]{2,1,0:T(8,128)(2,1)}), bf16[16,256,256]{2,1,0:T(8,128)(2,1)S(1)}, u32[]{:S(2)}, u32[]{:S(2)}) async-start(bf16[16,256,256]{2,1,0:T(8,128)(2,1)} %copy.66), calls=%async_computation.1 | async-start | bytes 4194304 | tf_op jit(solution)/shard_map/all_to_all | solution.py:199

commit v4 on v3

--- a/solution.py
+++ b/solution.py
@@ -56,21 +56,21 @@
     out_ref[0] = jnp.dot(bt_ref[...], uw_ref[...], preferred_element_type=jnp.float32)
 
 
-def block_states(bt, conv, dt_g, cum_g, segc):
+def block_states(bt, conv, dt_g, cum_g, segc, g):
     tok = conv.shape[0]
     nb = tok // STRETCH
     return pl.pallas_call(
         state_kernel,
-        grid=(nb, GROUPS),
+        grid=(nb,),
         in_specs=[
-            pl.BlockSpec((STATE, STRETCH), lambda b, g: (g, b)),
-            pl.BlockSpec((STRETCH, GROUP_COLS), lambda b, g: (b, g)),
-            pl.BlockSpec((1, STRETCH, PER_GROUP), lambda b, g: (g, b, 0)),
-            pl.BlockSpec((1, STRETCH, PER_GROUP), lambda b, g: (g, b, 0)),
-            pl.BlockSpec((STRETCH, 128), lambda b, g: (b, 0)),
-        ],
-        out_specs=pl.BlockSpec((1, STATE, GROUP_COLS), lambda b, g: (b, 0, g)),
-        out_shape=jax.ShapeDtypeStruct((nb, STATE, INNER), jnp.float32),
+            pl.BlockSpec((STATE, STRETCH), lambda b: (g, b)),
+            pl.BlockSpec((STRETCH, GROUP_COLS), lambda b: (b, g)),
+            pl.BlockSpec((1, STRETCH, PER_GROUP), lambda b: (g, b, 0)),
+            pl.BlockSpec((1, STRETCH, PER_GROUP), lambda b: (g, b, 0)),
+            pl.BlockSpec((STRETCH, 128), lambda b: (b, 0)),
+        ],
+        out_specs=pl.BlockSpec((1, STATE, GROUP_COLS), lambda b: (b, 0, 0)),
+        out_shape=jax.ShapeDtypeStruct((nb, STATE, GROUP_COLS), jnp.float32),
         scratch_shapes=[pltpu.VMEM((STRETCH, GROUP_COLS), jnp.bfloat16)],
     )(bt, conv, dt_g, cum_g, segc)
 
@@ -140,32 +140,33 @@
     out_ref[...] = (gated * lax.rsqrt(mean_square) * gain_ref[...]).astype(jnp.bfloat16)
 
 
-def mix(conv, y_local, z_gate, hbt, cum_g, segc, eb, gain):
+def mix(conv, y_local, z_gate, hbt, cum_g, segc, eb, gain, g):
     tok = conv.shape[0]
     nb = tok // STRETCH
     c_col = INNER // STATE + GROUPS
     return pl.pallas_call(
         mix_kernel,
-        grid=(nb, GROUPS),
+        grid=(nb,),
         in_specs=[
-            pl.BlockSpec((STRETCH, STATE), lambda b, g: (b, c_col + g)),
-            pl.BlockSpec((STRETCH, GROUP_COLS), lambda b, g: (b, g)),
-            pl.BlockSpec((STRETCH, GROUP_COLS), lambda b, g: (b, g)),
-            pl.BlockSpec((1, STATE, GROUP_COLS), lambda b, g: (b, 0, g)),
-            pl.BlockSpec((1, STRETCH, PER_GROUP), lambda b, g: (g, b, 0)),
-            pl.BlockSpec((STRETCH, 128), lambda b, g: (b, 0)),
-            pl.BlockSpec((8, 128), lambda b, g: (b, 0)),
-            pl.BlockSpec((1, GROUP_COLS), lambda b, g: (0, g)),
-        ],
-        out_specs=pl.BlockSpec((STRETCH, GROUP_COLS), lambda b, g: (b, g)),
-        out_shape=jax.ShapeDtypeStruct((tok, INNER), jnp.bfloat16),
+            pl.BlockSpec((STRETCH, STATE), lambda b: (b, c_col + g)),
+            pl.BlockSpec((STRETCH, GROUP_COLS), lambda b: (b, g)),
+            pl.BlockSpec((STRETCH, GROUP_COLS), lambda b: (b, g)),
+            pl.BlockSpec((1, STATE, GROUP_COLS), lambda b: (b, 0, 0)),
+            pl.BlockSpec((1, STRETCH, PER_GROUP), lambda b: (g, b, 0)),
+            pl.BlockSpec((STRETCH, 128), lambda b: (b, 0)),
+            pl.BlockSpec((8, 128), lambda b: (b, 0)),
+            pl.BlockSpec((1, GROUP_COLS), lambda b: (0, g)),
+        ],
+        out_specs=pl.BlockSpec((STRETCH, GROUP_COLS), lambda b: (b, 0)),
+        out_shape=jax.ShapeDtypeStruct((tok, GROUP_COLS), jnp.bfloat16),
         scratch_shapes=[pltpu.VMEM((STRETCH, GROUP_COLS), jnp.float32)],
     )(conv, y_local, z_gate, hbt, cum_g, segc, eb, gain)
 
 
 def compose(state_dev, decay_dev):
     peers = lax.axis_size("ctx")
-    width = INNER // peers
+    total = state_dev.shape[1]
+    width = total // peers
     pieces = state_dev.reshape(STATE, peers, width).transpose(1, 0, 2)
     decay_hi = decay_dev.astype(jnp.bfloat16)
     decay_lo = (decay_dev - decay_hi.astype(jnp.float32)).astype(jnp.bfloat16)
@@ -199,7 +200,7 @@
     back = lax.all_to_all(
         entering.astype(jnp.bfloat16), "ctx", split_axis=0, concat_axis=0, tiled=True
     )
-    return back.transpose(1, 0, 2).reshape(STATE, INNER).astype(jnp.float32)
+    return back.transpose(1, 0, 2).reshape(STATE, total).astype(jnp.float32)
 
 
 def local(xbc, z_gate, dt_raw, lengths, conv_weight, conv_bias, dt_bias, a_log, d_skip, norm_gain):
@@ -228,22 +229,25 @@
     eb = eb.astype(jnp.int32)
     bt = conv[:, INNER : INNER + GROUPS * STATE].T
 
-    ends = block_states(bt, conv, dt_g, cum_g, segc)
     dsk = jnp.repeat(d_skip, HEAD_DIM)[None, :]
+    gain = norm_gain[None, :]
+    col_decay = jnp.repeat(block_decay, HEAD_DIM, axis=1).reshape(nb, GROUPS, GROUP_COLS)
     y_local = intra_part(conv, dt_g, cum_g, cumt_g, segc, segr, dsk)
-    col_decay = jnp.repeat(block_decay, HEAD_DIM, axis=1)
-    state_dev = ends[0]
-    decay_dev = col_decay[0]
-    for b in range(1, nb):
-        state_dev = col_decay[b][None, :] * state_dev + ends[b]
-        decay_dev = decay_dev * col_decay[b]
-    state_in = compose(state_dev, decay_dev)
-    entering = [state_in]
-    for b in range(1, nb):
-        entering.append(col_decay[b - 1][None, :] * entering[-1] + ends[b - 1])
-    hbt = jnp.stack(entering).astype(jnp.bfloat16)
-    gain = norm_gain[None, :]
-    return mix(conv, y_local, z_gate, hbt, cum_g, segc, eb, gain)
+    outs = []
+    for g in range(GROUPS):
+        ends = block_states(bt, conv, dt_g, cum_g, segc, g)
+        state_dev = ends[0]
+        decay_dev = col_decay[0, g]
+        for b in range(1, nb):
+            state_dev = col_decay[b, g][None, :] * state_dev + ends[b]
+            decay_dev = decay_dev * col_decay[b, g]
+        state_in = compose(state_dev, decay_dev)
+        entering = [state_in]
+        for b in range(1, nb):
+            entering.append(col_decay[b - 1, g][None, :] * entering[-1] + ends[b - 1])
+        hbt = jnp.stack(entering).astype(jnp.bfloat16)
+        outs.append(mix(conv, y_local, z_gate, hbt, cum_g, segc, eb, gain, g))
+    return jnp.concatenate(outs, axis=1)
 
 
 def solution(mesh):

time: 205 us -> 214 us (1.044)
  the two profiles are of different devices: /device:TPU:15 before, /device:TPU:1 now
where the time goes in v4:
time: 214 us; the launch traced here: 213 us
  Pallas kernels  63.8 us (30%)
  waiting for transfers between devices  50.1 us (23%)
  other arithmetic  38.1 us (18%)
  starting transfers between devices  29.7 us (14%)
  local copies, waits for them, and re-layouts  29.4 us (14%)
    pallas_call x1, Pallas kernels, intra_part(): pl.pallas_call(intra_kernel, grid=(nb, GROUPS), in_specs=[pl.BlockSpec((S...  32.2 us
    all_to_all x2, waiting for transfers between devices, compose(): lax.all_to_all(payload, 'ctx', split_axis=0, concat_axis=0, tiled=True)  30.7 us
    all_to_all x2, waiting for transfers between devices, compose(): lax.all_to_all(entering.astype(jnp.bfloat16), 'ctx', split_axis=0, concat...  19.4 us
    convert_element_type x1, other arithmetic, causal_conv(): return jax.nn.silu(summed + conv_bias[None, :]).astype(jnp.bfloat16)  17.4 us
    pallas_call x2, Pallas kernels, block_states(): pl.pallas_call(state_kernel, grid=(nb,), in_specs=[pl.BlockSpec((STATE, S...  16.3 us
    pallas_call x2, Pallas kernels, mix(): pl.pallas_call(mix_kernel, grid=(nb,), in_specs=[pl.BlockSpec((STRETCH, S...  15.3 us
    all_to_all x2, starting transfers between devices, compose(): lax.all_to_all(entering.astype(jnp.bfloat16), 'ctx', split_axis=0, concat...  13.4 us
    all_to_all x2, starting transfers between devices, compose(): lax.all_to_all(payload, 'ctx', split_axis=0, concat_axis=0, tiled=True)  11.7 us
  transfers between devices with their start and end apart: 5, of which 3 were waited for; matrix products, arithmetic and copies ran while one was open for 13% of the time, Pallas kernels for 19%

profile of v4, /device:TPU:1, one launch (start us, length us, event | category | flops | bytes accessed | tf_op | source)
XLA Modules:
  0.0 213.3 jit_solution(14328028783543476825)
XLA Ops:
  0.0 0.9 slice.133
  0.9 4.5 %collective-permute-start = (bf16[3,5120]{1,0:T(4,128)(2,1)S(1)}, bf16[3,5120]{1,0:T(4,128)(2,1)S(1)}, u32[]{:S(2)}, u32[]{:S(2)}) collective-permute-start(bf16[3,5120]{1,0:T(4,128)(2,1)S(1)} %slice.133), channel_id=1, source_target_pairs={{0,1},{1,2},{2,3},{3,4},{4,5},{5,6},{6,7},{7,8},{8,9},{9,10},{10,1... | collective-permute-start | bytes 92168 | tf_op jit(solution)/shard_map/ppermute | solution.py:23
  5.5 0.7 exp.19
  6.2 0.8 reduce-window.18
  7.4 1.0 negate_multiply_fusion
  8.4 1.2 reduce-window.19
  10.8 1.2 fusion.29
  12.2 1.0 copy.76
  13.2 1.0 copy.71
  14.2 17.4 %multiply_convert_fusion.c_ref.b_ref.x_ref = bf16[512,5120]{1,0:T(8,128)(2,1)S(1)} fusion(bf16[512,5120]{1,0:T(8,128)(2,1)} %param.10, bf16[3,5120]{1,0:T(4,128)(2,1)S(1)} %collective-permute-done, f32[5120]{0:T(1024)S(1)} %copy-done.2, f32[5120]{0:T(1024)S(1)} %bitcast.133, f32[5120]{0:T(1024)S(1)} %bitcast.134, f32[5120]{0:T(1024)S(1)} %bitcast.132, ...), kind=kLoop, calls=%fused_computation | loop fusion | flops 78643200 | bytes 10620928 | tf_op jit(solution)/shard_map/convert_element_type | solution.py:42
  31.6 2.4 %copy-done = bf16[512,5120]{1,0:T(8,128)(2,1)} copy-done((bf16[512,5120]{1,0:T(8,128)(2,1)}, bf16[512,5120]{1,0:T(8,128)(2,1)S(1)}, u32[]{:S(2)}) %copy-start) | copy-done | bytes 5242904
  34.0 1.0 copy.79.bt_ref
  35.1 0.8 broadcast_in_dim.149.segc_ref
  35.9 8.1 %shard_map.101 = f32[2,256,2048]{2,1,0:T(8,128)} custom-call(bf16[512,512]{1,0:T(8,128)(2,1)} %copy.79.bt_ref, bf16[512,5120]{1,0:T(8,128)(2,1)} %copy-done, f32[2,512,32]{2,1,0:T(8,128)} %bitcast.115, f32[2,512,32]{2,1,0:T(8,128)} %bitcast.110, s32[512,128]{1,0:T(8,128)} %broadcast_in_dim.149.segc_ref), custom_call_target="tpu_custom_call" | custom-call | tf_op jit(solution)/shard_map/pallas_call | solution.py:62
  44.0 2.5 %slice_bitcast_fusion.3 = (f32[32,8,16,128]{3,1,2,0:T(8,128)S(1)}, f32[32,8,16,128]{3,1,2,0:T(8,128)S(1)}) fusion(f32[2,256,2048]{2,1,0:T(8,128)} %shard_map.101), kind=kLoop, calls=%fused_computation.20 | loop fusion | bytes 8388608
  47.3 1.3 fusion.4
  48.6 1.1 pad_maximum_fusion.4
  49.7 5.0 %all-to-all-start = ((bf16[16,258,128]{2,1,0:T(8,128)(2,1)}), bf16[16,258,128]{2,1,0:T(8,128)(2,1)S(1)}, u32[]{:S(2)}, u32[]{:S(2)}) async-start(bf16[16,258,128]{2,1,0:T(8,128)(2,1)} %pad_maximum_fusion.4), calls=%async_computation | async-start | bytes 2162688 | tf_op jit(solution)/shard_map/all_to_all | solution.py:181
  54.7 8.2 %shard_map.103 = f32[2,256,2048]{2,1,0:T(8,128)} custom-call(bf16[512,512]{1,0:T(8,128)(2,1)} %copy.79.bt_ref, bf16[512,5120]{1,0:T(8,128)(2,1)} %copy-done, f32[2,512,32]{2,1,0:T(8,128)} %bitcast.116, f32[2,512,32]{2,1,0:T(8,128)} %bitcast.111, s32[512,128]{1,0:T(8,128)} %broadcast_in_dim.149.segc_ref), custom_call_target="tpu_custom_call" | custom-call | tf_op jit(solution)/shard_map/pallas_call | solution.py:62
  62.9 2.5 %slice_bitcast_fusion.2 = (f32[32,8,16,128]{3,1,2,0:T(8,128)S(1)}, f32[32,8,16,128]{3,1,2,0:T(8,128)S(1)}) fusion(f32[2,256,2048]{2,1,0:T(8,128)} %shard_map.103), kind=kLoop, calls=%fused_computation.19 | loop fusion | bytes 8388608
  66.2 1.3 fusion.5
  67.5 1.1 pad_maximum_fusion.5
  68.5 10.0 %all-to-all-done = bf16[16,258,128]{2,1,0:T(8,128)(2,1)S(1)} async-done(((bf16[16,258,128]{2,1,0:T(8,128)(2,1)}), bf16[16,258,128]{2,1,0:T(8,128)(2,1)S(1)}, u32[]{:S(2)}, u32[]{:S(2)}) %all-to-all-start) | async-done | bytes 1056800 | tf_op jit(solution)/shard_map/all_to_all | solution.py:181
  78.5 6.7 %all-to-all-start.2 = ((bf16[16,258,128]{2,1,0:T(8,128)(2,1)}), bf16[16,258,128]{2,1,0:T(8,128)(2,1)S(1)}, u32[]{:S(2)}, u32[]{:S(2)}) async-start(bf16[16,258,128]{2,1,0:T(8,128)(2,1)} %pad_maximum_fusion.5), calls=%async_computation.2 | async-start | bytes 2162688 | tf_op jit(solution)/shard_map/all_to_all | solution.py:181
  85.3 1.1 slice.182
  86.4 1.9 copy.82
  88.3 20.8 %all-to-all-done.2 = bf16[16,258,128]{2,1,0:T(8,128)(2,1)S(1)} async-done(((bf16[16,258,128]{2,1,0:T(8,128)(2,1)}), bf16[16,258,128]{2,1,0:T(8,128)(2,1)S(1)}, u32[]{:S(2)}, u32[]{:S(2)}) %all-to-all-start.2) | async-done | bytes 1056800 | tf_op jit(solution)/shard_map/all_to_all | solution.py:181
  109.4 1.2 select_reduce_fusion.1
  110.6 1.0 convolution_convert_fusion.1
  111.6 1.7 copy.84
  113.3 6.7 %all-to-all-start.1 = ((bf16[16,256,128]{2,1,0:T(8,128)(2,1)}), bf16[16,256,128]{2,1,0:T(8,128)(2,1)S(1)}, u32[]{:S(2)}, u32[]{:S(2)}) async-start(bf16[16,256,128]{2,1,0:T(8,128)(2,1)} %copy.84), calls=%async_computation.1 | async-start | bytes 2097152 | tf_op jit(solution)/shard_map/all_to_all | solution.py:200
  120.1 0.9 copy.89
  121.0 1.0 convolution_convert_fusion
  122.0 1.7 copy.91
  123.8 19.4 %all-to-all-done.1 = bf16[16,256,128]{2,1,0:T(8,128)(2,1)S(1)} async-done(((bf16[16,256,128]{2,1,0:T(8,128)(2,1)}), bf16[16,256,128]{2,1,0:T(8,128)(2,1)S(1)}, u32[]{:S(2)}, u32[]{:S(2)}) %all-to-all-start.1) | async-done | bytes 1048608 | tf_op jit(solution)/shard_map/all_to_all | solution.py:200
  143.2 6.7 %all-to-all-start.3 = ((bf16[16,256,128]{2,1,0:T(8,128)(2,1)}), bf16[16,256,128]{2,1,0:T(8,128)(2,1)S(1)}, u32[]{:S(2)}, u32[]{:S(2)}) async-start(bf16[16,256,128]{2,1,0:T(8,128)(2,1)} %copy.91), calls=%async_computation.3 | async-start | bytes 2097152 | tf_op jit(solution)/shard_map/all_to_all | solution.py:200
  150.1 0.7 broadcast_in_dim_reshape.3.dsk_ref
  152.0 32.2 %shard_map.100.y_ref = f32[512,4096]{1,0:T(8,128)} custom-call(bf16[512,5120]{1,0:T(8,128)(2,1)} %copy-done, bf16[512,5120]{1,0:T(8,128)(2,1)} %copy-done, bf16[512,5120]{1,0:T(8,128)(2,1)} %copy-done, f32[2,512,32]{2,1,0:T(8,128)} %bitcast.117, f32[2,512,32]{2,1,0:T(8,128)} %bitcast.112, f32[2,32,512]{2,1,0:T(8,128)} %bitcast.128, ...), custom_call_target="tpu_custom_call" | custom-call | tf_op jit(solution)/shard_map/pallas_call | solution.py:107
  184.2 0.7 copy.85
  185.4 1.9 add_convert_fusion.1
  187.3 1.5 pad_maximum_fusion.2.hbt_ref
  188.8 0.7 copy.92
  190.0 1.9 add_convert_fusion
  191.9 1.5 pad_maximum_fusion.3.hbt_ref
  193.4 0.7 broadcast_in_dim.163.eb_ref
  194.0 7.6 %shard_map.104 = bf16[512,2048]{1,0:T(8,128)(2,1)} custom-call(bf16[512,5120]{1,0:T(8,128)(2,1)} %copy-done, f32[512,4096]{1,0:T(8,128)} %shard_map.100.y_ref, bf16[512,4096]{1,0:T(8,128)(2,1)} %z_ref.3, bf16[2,256,2048]{2,1,0:T(8,128)(2,1)} %pad_maximum_fusion.3.hbt_ref, f32[2,512,32]{2,1,0:T(8,128)} %bitcast.113, s32[512,128]{1,0:T(8,128)} %broadcast_in_dim.149.segc_ref, ...), custom_call_target="tpu_custom_call" | custom-call | tf_op jit(solution)/shard_map/pallas_call | solution.py:147
  201.6 7.7 %shard_map.102 = bf16[512,2048]{1,0:T(8,128)(2,1)} custom-call(bf16[512,5120]{1,0:T(8,128)(2,1)} %copy-done, f32[512,4096]{1,0:T(8,128)} %shard_map.100.y_ref, bf16[512,4096]{1,0:T(8,128)(2,1)} %z_ref.3, bf16[2,256,2048]{2,1,0:T(8,128)(2,1)} %pad_maximum_fusion.2.hbt_ref, f32[2,512,32]{2,1,0:T(8,128)} %bitcast.114, s32[512,128]{1,0:T(8,128)} %broadcast_in_dim.149.segc_ref, ...), custom_call_target="tpu_custom_call" | custom-call | tf_op jit(solution)/shard_map/pallas_call | solution.py:147
  209.3 4.0 %pad_maximum_fusion.1 = bf16[512,4096]{1,0:T(8,128)(2,1)} fusion(bf16[512,2048]{1,0:T(8,128)(2,1)S(1)} %copy-done.1, bf16[512,2048]{1,0:T(8,128)(2,1)} %shard_map.102), kind=kLoop, calls=%fused_computation.6 | loop fusion | flops 8388608 | bytes 8388608 | tf_op jit(solution)/shard_map/concatenate | solution.py:250
  (53 shorter events, 6.4 us)
Async XLA Ops:
  0.0 14.2 %copy-start.2 = (f32[5120]{0:T(1024)S(1)}, f32[5120]{0:T(1024)}, u32[]{:S(2)}) copy-start(f32[5120]{0:T(1024)} %param.15) | copy-start | bytes 61444
  0.9 13.3 %collective-permute-start = (bf16[3,5120]{1,0:T(4,128)(2,1)S(1)}, bf16[3,5120]{1,0:T(4,128)(2,1)S(1)}, u32[]{:S(2)}, u32[]{:S(2)}) collective-permute-start(bf16[3,5120]{1,0:T(4,128)(2,1)S(1)} %slice.133), channel_id=1, source_target_pairs={{0,1},{1,2},{2,3},{3,4},{4,5},{5,6},{6,7},{7,8},{8,9},{9,10},{10,1... | collective-permute-start | bytes 92168 | tf_op jit(solution)/shard_map/ppermute | solution.py:23
  31.6 2.4 %copy-start = (bf16[512,5120]{1,0:T(8,128)(2,1)}, bf16[512,5120]{1,0:T(8,128)(2,1)S(1)}, u32[]{:S(2)}) copy-start(bf16[512,5120]{1,0:T(8,128)(2,1)S(1)} %multiply_convert_fusion.c_ref.b_ref.x_ref) | copy-start | bytes 15728644
  49.7 28.8 %all-to-all-start = ((bf16[16,258,128]{2,1,0:T(8,128)(2,1)}), bf16[16,258,128]{2,1,0:T(8,128)(2,1)S(1)}, u32[]{:S(2)}, u32[]{:S(2)}) async-start(bf16[16,258,128]{2,1,0:T(8,128)(2,1)} %pad_maximum_fusion.4), calls=%async_computation | async-start | bytes 2162688 | tf_op jit(solution)/shard_map/all_to_all | solution.py:181
  78.5 30.5 %all-to-all-start.2 = ((bf16[16,258,128]{2,1,0:T(8,128)(2,1)}), bf16[16,258,128]{2,1,0:T(8,128)(2,1)S(1)}, u32[]{:S(2)}, u32[]{:S(2)}) async-start(bf16[16,258,128]{2,1,0:T(8,128)(2,1)} %pad_maximum_fusion.5), calls=%async_computation.2 | async-start | bytes 2162688 | tf_op jit(solution)/shard_map/all_to_all | solution.py:181
  113.3 29.9 %all-to-all-start.1 = ((bf16[16,256,128]{2,1,0:T(8,128)(2,1)}), bf16[16,256,128]{2,1,0:T(8,128)(2,1)S(1)}, u32[]{:S(2)}, u32[]{:S(2)}) async-start(bf16[16,256,128]{2,1,0:T(8,128)(2,1)} %copy.84), calls=%async_computation.1 | async-start | bytes 2097152 | tf_op jit(solution)/shard_map/all_to_all | solution.py:200
  122.0 28.0 %copy-start.3 = (f32[64]{0:T(128)S(1)}, f32[64]{0:T(128)}, u32[]{:S(2)}) copy-start(f32[64]{0:T(128)} %param.18) | copy-start | bytes 772
  143.2 45.6 %all-to-all-start.3 = ((bf16[16,256,128]{2,1,0:T(8,128)(2,1)}), bf16[16,256,128]{2,1,0:T(8,128)(2,1)S(1)}, u32[]{:S(2)}, u32[]{:S(2)}) async-start(bf16[16,256,128]{2,1,0:T(8,128)(2,1)} %copy.91), calls=%async_computation.3 | async-start | bytes 2097152 | tf_op jit(solution)/shard_map/all_to_all | solution.py:200
  201.6 7.7 %copy-start.1 = (bf16[512,2048]{1,0:T(8,128)(2,1)S(1)}, bf16[512,2048]{1,0:T(8,128)(2,1)}, u32[]{:S(2)}) copy-start(bf16[512,2048]{1,0:T(8,128)(2,1)} %shard_map.104) | copy-start | bytes 6291460

commit v5 on v3

v5 whole, which is shorter than its diff:
```python
import jax
import jax.numpy as jnp
from jax import lax
from jax.experimental import pallas as pl
from jax.experimental.pallas import tpu as pltpu
from jax.sharding import PartitionSpec as P

HEADS = 64
HEAD_DIM = 64
STATE = 256
GROUPS = 2
CONV = 4
STRETCH = 256
CHANNELS = 5120
INNER = HEADS * HEAD_DIM
PER_GROUP = HEADS // GROUPS
GROUP_COLS = INNER // GROUPS


def shifted(value, axis, by):
    peers = lax.axis_size(axis)
    pairs = [(i, i + by) for i in range(peers) if 0 <= i + by < peers]
    return lax.ppermute(value, axis, pairs)


def segment_of(positions, lengths):
    prompt_ends = jnp.cumsum(lengths)
    hits = (prompt_ends[None, :] <= positions[:, None]).astype(jnp.int32)
    return jnp.sum(hits, axis=1)


CONV_COLS = 640


def conv_kernel(x_ref, rim_ref, w_ref, bias_ref, m_ref, out_ref):
    x = x_ref[...].astype(jnp.float32)
    rim = rim_ref[...].astype(jnp.float32)
    rows8 = lax.broadcasted_iota(jnp.int32, rim.shape, 0)
    summed = jnp.zeros(x.shape, jnp.float32)
    top = jnp.zeros(rim.shape, jnp.float32)
    for tap in range(CONV):
        by = CONV - 1 - tap
        wk = w_ref[tap : tap + 1, :]
        kept = m_ref[:, tap : tap + 1] > 0.0
        if by == 0:
            term = x
            top_term = x[0:8]
        else:
            term = pltpu.roll(x, by, 0)
            top_term = jnp.where(rows8 < by, pltpu.roll(rim, by, 0), term[0:8])
        summed = summed + jnp.where(kept, term * wk, 0.0)
        top = top + jnp.where(kept[0:8], top_term * wk, 0.0)
    out_ref[...] = jax.nn.silu(summed + bias_ref[...]).astype(jnp.bfloat16)
    out_ref[0:8, :] = jax.nn.silu(top + bias_ref[...]).astype(jnp.bfloat16)


def conv_part(xbc, rim8, w8, bias, masks):
    tok, chans = xbc.shape
    return pl.pallas_call(
        conv_kernel,
        grid=(chans // CONV_COLS,),
        in_specs=[
            pl.BlockSpec((tok, CONV_COLS), lambda c: (0, c)),
            pl.BlockSpec((8, CONV_COLS), lambda c: (0, c)),
            pl.BlockSpec((8, CONV_COLS), lambda c: (0, c)),
            pl.BlockSpec((1, CONV_COLS), lambda c: (0, c)),
            pl.BlockSpec((tok, 128), lambda c: (0, 0)),
        ],
        out_specs=pl.BlockSpec((tok, CONV_COLS), lambda c: (0, c)),
        out_shape=jax.ShapeDtypeStruct((tok, chans), jnp.bfloat16),
    )(xbc, rim8, w8, bias, masks)


def state_kernel(
    bt_ref, x_ref, dt_ref, cum_ref, segc_ref, bdec_ref, local_ref, cdec_ref, pay_ref,
    uw_ref, acc_ref, dec_ref,
):
    b = pl.program_id(1)

    @pl.when(b == 0)
    def _():
        acc_ref[...] = jnp.zeros(acc_ref.shape, jnp.float32)
        dec_ref[...] = jnp.ones(dec_ref.shape, jnp.float32)

    local_ref[0] = acc_ref[...]
    cdec_ref[0] = dec_ref[...]
    cum = cum_ref[0]
    step = dt_ref[0]
    segc = segc_ref[:, 0:1]
    last = cum[STRETCH - 1 : STRETCH, :]
    seg_last = segc[STRETCH - 1 : STRETCH, :]
    w = jnp.where(segc == seg_last, jnp.exp(last - cum), 0.0)
    for j in range(PER_GROUP):
        cols = slice(j * HEAD_DIM, (j + 1) * HEAD_DIM)
        scaled = (x_ref[:, cols].astype(jnp.float32) * step[:, j : j + 1]).astype(jnp.bfloat16)
        uw_ref[:, cols] = (scaled.astype(jnp.float32) * w[:, j : j + 1]).astype(jnp.bfloat16)
    block_state = jnp.dot(bt_ref[...], uw_ref[...], preferred_element_type=jnp.float32)
    decay = bdec_ref[0]
    acc_ref[...] = decay * acc_ref[...] + block_state
    dec_ref[...] = dec_ref[...] * decay

    @pl.when(b == pl.num_programs(1) - 1)
    def _():
        pieces, _, width = pay_ref.shape
        total = acc_ref[...]
        dec = dec_ref[...]
        hi = dec.astype(jnp.bfloat16)
        lo = (dec - hi.astype(jnp.float32)).astype(jnp.bfloat16)
        for k in range(pieces):
            cols = slice(k * width, (k + 1) * width)
            pay_ref[k, 0:STATE, :] = total[:, cols].astype(jnp.bfloat16)
            pay_ref[k, STATE : STATE + 1, :] = hi[:, cols]
            pay_ref[k, STATE + 1 : STATE + 2, :] = lo[:, cols]


def block_states(bt, conv, dt_g, cum_g, segc, bdec, peers):
    tok = conv.shape[0]
    nb = tok // STRETCH
    width = INNER // peers
    per = peers // GROUPS
    return pl.pallas_call(
        state_kernel,
        grid=(GROUPS, nb),
        in_specs=[
            pl.BlockSpec((STATE, STRETCH), lambda g, b: (g, b)),
            pl.BlockSpec((STRETCH, GROUP_COLS), lambda g, b: (b, g)),
            pl.BlockSpec((1, STRETCH, PER_GROUP), lambda g, b: (g, b, 0)),
            pl.BlockSpec((1, STRETCH, PER_GROUP), lambda g, b: (g, b, 0)),
            pl.BlockSpec((STRETCH, 128), lambda g, b: (b, 0)),
            pl.BlockSpec((1, 1, GROUP_COLS), lambda g, b: (b, 0, g)),
        ],
        out_specs=[
            pl.BlockSpec((1, STATE, GROUP_COLS), lambda g, b: (b, 0, g)),
            pl.BlockSpec((1, 1, GROUP_COLS), lambda g, b: (b, 0, g)),
            pl.BlockSpec((per, STATE + 2, width), lambda g, b: (g, 0, 0)),
        ],
        out_shape=[
            jax.ShapeDtypeStruct((nb, STATE, INNER), jnp.float32),
            jax.ShapeDtypeStruct((nb, 1, INNER), jnp.float32),
            jax.ShapeDtypeStruct((peers, STATE + 2, width), jnp.bfloat16),
        ],
        scratch_shapes=[
            pltpu.VMEM((STRETCH, GROUP_COLS), jnp.bfloat16),
            pltpu.VMEM((STATE, GROUP_COLS), jnp.float32),
            pltpu.VMEM((1, GROUP_COLS), jnp.float32),
        ],
    )(bt, conv, dt_g, cum_g, segc, bdec)


def intra_kernel(
    c_ref, b_ref, x_ref, dt_ref, cum_ref, cumt_ref, segc_ref, segr_ref, dsk_ref, out_ref
):
    gram = lax.dot_general(
        c_ref[...], b_ref[...], (((1,), (1,)), ((), ())), preferred_element_type=jnp.float32
    )
    segc = segc_ref[:, 0:1]
    segr = segr_ref[0:1, :]
    rows = lax.broadcasted_iota(jnp.int32, (STRETCH, STRETCH), 0)
    cols = lax.broadcasted_iota(jnp.int32, (STRETCH, STRETCH), 1)
    gram = jnp.where((segc == segr) & (cols <= rows), gram, 0.0)
    cum = cum_ref[0]
    cumt = cumt_ref[0]
    step = dt_ref[0]
    for j in range(PER_GROUP):
        hc = slice(j * HEAD_DIM, (j + 1) * HEAD_DIM)
        gap = jnp.minimum(cum[:, j : j + 1] - cumt[j : j + 1, :], 0.0)
        weights = (gram * jnp.exp(gap)).astype(jnp.bfloat16)
        xf = x_ref[:, hc].astype(jnp.float32)
        scaled = (xf * step[:, j : j + 1]).astype(jnp.bfloat16)
        intra = jnp.dot(weights, scaled, preferred_element_type=jnp.float32)
        out_ref[:, hc] = intra + dsk_ref[:, hc] * xf


def intra_part(conv, dt_g, cum_g, cumt_g, segc, segr, dsk):
    tok = conv.shape[0]
    nb = tok // STRETCH
    b_col = INNER // STATE
    c_col = b_col + GROUPS
    return pl.pallas_call(
        intra_kernel,
        grid=(nb, GROUPS),
        in_specs=[
            pl.BlockSpec((STRETCH, STATE), lambda b, g: (b, c_col + g)),
            pl.BlockSpec((STRETCH, STATE), lambda b, g: (b, b_col + g)),
            pl.BlockSpec((STRETCH, GROUP_COLS), lambda b, g: (b, g)),
            pl.BlockSpec((1, STRETCH, PER_GROUP), lambda b, g: (g, b, 0)),
            pl.BlockSpec((1, STRETCH, PER_GROUP), lambda b, g: (g, b, 0)),
            pl.BlockSpec((1, PER_GROUP, STRETCH), lambda b, g: (g, 0, b)),
            pl.BlockSpec((STRETCH, 128), lambda b, g: (b, 0)),
            pl.BlockSpec((8, STRETCH), lambda b, g: (0, b)),
            pl.BlockSpec((1, GROUP_COLS), lambda b, g: (0, g)),
        ],
        out_specs=pl.BlockSpec((STRETCH, GROUP_COLS), lambda b, g: (b, g)),
        out_shape=jax.ShapeDtypeStruct((tok, INNER), jnp.float32),
    )(conv, conv, conv, dt_g, cum_g, cumt_g, segc, segr, dsk)


def mix_kernel(
    c_ref, y_ref, z_ref, back_ref, local_ref, cdec_ref, cum_ref, segc_ref, eb_ref, gain_ref,
    out_ref, hin_ref, acc_ref,
):
    pieces, _, width = back_ref.shape
    for k in range(pieces):
        hin_ref[:, k * width : (k + 1) * width] = back_ref[k].astype(jnp.float32)
    state = cdec_ref[0] * hin_ref[...] + local_ref[0]
    segc = segc_ref[:, 0:1]
    entry = eb_ref[0:1, 0:1]
    in_weight = jnp.where(segc == entry, jnp.exp(cum_ref[0]), 0.0)
    inter = jnp.dot(c_ref[...], state.astype(jnp.bfloat16), preferred_element_type=jnp.float32)
    for j in range(PER_GROUP):
        hc = slice(j * HEAD_DIM, (j + 1) * HEAD_DIM)
        acc_ref[:, hc] = inter[:, hc] * in_weight[:, j : j + 1]
    y = y_ref[...] + acc_ref[...]
    zf = z_ref[...].astype(jnp.float32)
    gated = y * (zf * jax.nn.sigmoid(zf))
    mean_square = jnp.mean(gated * gated, axis=1, keepdims=True) + 1e-05
    out_ref[...] = (gated * lax.rsqrt(mean_square) * gain_ref[...]).astype(jnp.bfloat16)


def mix(conv, y_local, z_gate, back, local_states, cdec, cum_g, segc, eb, gain):
    tok = conv.shape[0]
    nb = tok // STRETCH
    c_col = INNER // STATE + GROUPS
    peers, _, width = back.shape
    per = peers // GROUPS
    return pl.pallas_call(
        mix_kernel,
        grid=(nb, GROUPS),
        in_specs=[
            pl.BlockSpec((STRETCH, STATE), lambda b, g: (b, c_col + g)),
            pl.BlockSpec((STRETCH, GROUP_COLS), lambda b, g: (b, g)),
            pl.BlockSpec((STRETCH, GROUP_COLS), lambda b, g: (b, g)),
            pl.BlockSpec((per, STATE, width), lambda b, g: (g, 0, 0)),
            pl.BlockSpec((1, STATE, GROUP_COLS), lambda b, g: (b, 0, g)),
            pl.BlockSpec((1, 1, GROUP_COLS), lambda b, g: (b, 0, g)),
            pl.BlockSpec((1, STRETCH, PER_GROUP), lambda b, g: (g, b, 0)),
            pl.BlockSpec((STRETCH, 128), lambda b, g: (b, 0)),
            pl.BlockSpec((8, 128), lambda b, g: (b, 0)),
            pl.BlockSpec((1, GROUP_COLS), lambda b, g: (0, g)),
        ],
        out_specs=pl.BlockSpec((STRETCH, GROUP_COLS), lambda b, g: (b, g)),
        out_shape=jax.ShapeDtypeStruct((tok, INNER), jnp.bfloat16),
        scratch_shapes=[
            pltpu.VMEM((STATE, GROUP_COLS), jnp.float32),
            pltpu.VMEM((STRETCH, GROUP_COLS), jnp.float32),
        ],
    )(conv, y_local, z_gate, back, local_states, cdec, cum_g, segc, eb, gain)


def scan_kernel(got_ref, out_ref):
    peers = got_ref.shape[0]

    def body(d, carry):
        out_ref[d] = carry.astype(jnp.bfloat16)
        decay = got_ref[d, STATE : STATE + 1, :].astype(jnp.float32) + got_ref[
            d, STATE + 1 : STATE + 2, :
        ].astype(jnp.float32)
        return decay * carry + got_ref[d, 0:STATE, :].astype(jnp.float32)

    lax.fori_loop(0, peers, body, jnp.zeros(out_ref.shape[1:], jnp.float32))


def compose(payload):
    peers, _, width = payload.shape
    got = lax.all_to_all(payload, "ctx", split_axis=0, concat_axis=0, tiled=True)
    entering = pl.pallas_call(
        scan_kernel,
        out_shape=jax.ShapeDtypeStruct((peers, STATE, width), jnp.bfloat16),
    )(got)
    return lax.all_to_all(entering, "ctx", split_axis=0, concat_axis=0, tiled=True)


def local(xbc, z_gate, dt_raw, lengths, conv_weight, conv_bias, dt_bias, a_log, d_skip, norm_gain):
    tok = xbc.shape[0]
    nb = tok // STRETCH
    peers = lax.axis_size("ctx")
    first_pos = lax.axis_index("ctx") * tok
    rim_rows = shifted(xbc[tok - (CONV - 1) :], "ctx", 1)
    rim8 = jnp.concatenate([jnp.zeros((8 - (CONV - 1), CHANNELS), xbc.dtype), rim_rows], axis=0)
    ext_pos = first_pos - (CONV - 1) + jnp.arange(tok + CONV - 1)
    ext_seg = segment_of(ext_pos, lengths)
    target = ext_seg[CONV - 1 :]
    kept = [
        (ext_pos[tap : tap + tok] >= 0) & (ext_seg[tap : tap + tok] == target) for tap in range(CONV)
    ]
    masks = jnp.stack(kept, axis=1).astype(jnp.float32)
    masks = jnp.concatenate([masks, jnp.zeros((tok, 128 - CONV), jnp.float32)], axis=1)
    w8 = jnp.concatenate([conv_weight, jnp.zeros((8 - CONV, CHANNELS), jnp.float32)], axis=0)
    conv = conv_part(xbc, rim8, w8, conv_bias[None, :], masks)
    step = jax.nn.softplus(dt_raw.astype(jnp.float32) + dt_bias[None, :])
    log_decay = -step * jnp.exp(a_log)[None, :]
    cum = jnp.cumsum(log_decay.reshape(nb, STRETCH, HEADS), axis=1).reshape(tok, HEADS)
    segments = segment_of(first_pos + jnp.arange(tok), lengths)
    seg_before = segment_of(first_pos + jnp.arange(nb) * STRETCH - 1, lengths)
    seg_last = segments.reshape(nb, STRETCH)[:, -1]
    cum_last = cum.reshape(nb, STRETCH, HEADS)[:, -1, :]
    block_decay = jnp.where((seg_last == seg_before)[:, None], jnp.exp(cum_last), 0.0)

    cum_g = cum.reshape(tok, GROUPS, PER_GROUP).transpose(1, 0, 2)
    dt_g = step.reshape(tok, GROUPS, PER_GROUP).transpose(1, 0, 2)
    cumt_g = cum.T.reshape(GROUPS, PER_GROUP, tok)
    segc = jnp.broadcast_to(segments[:, None], (tok, 128)).astype(jnp.int32)
    segr = jnp.broadcast_to(segments[None, :], (8, tok)).astype(jnp.int32)
    eb = jnp.broadcast_to(seg_before[:, None, None], (nb, 8, 128)).reshape(nb * 8, 128)
    eb = eb.astype(jnp.int32)
    bt = conv[:, INNER : INNER + GROUPS * STATE].T
    bdec = jnp.repeat(block_decay, HEAD_DIM, axis=1)[:, None, :]

    local_states, cdec, payload = block_states(bt, conv, dt_g, cum_g, segc, bdec, peers)
    dsk = jnp.repeat(d_skip, HEAD_DIM)[None, :]
    y_local = intra_part(conv, dt_g, cum_g, cumt_g, segc, segr, dsk)
    back = compose(payload)
    gain = norm_gain[None, :]
    return mix(conv, y_local, z_gate, back, local_states, cdec, cum_g, segc, eb, gain)


def solution(mesh):
    return jax.shard_map(
        local,
        mesh=mesh,
        in_specs=(
            P(("group", "ctx"), None),
            P(("group", "ctx"), None),
            P(("group", "ctx"), None),
            P("group"),
            P(),
            P(),
            P(),
            P(),
            P(),
            P(),
        ),
        out_specs=P(("group", "ctx"), None),
        check_vma=False,
    )
```

time: 205 us -> 172 us (0.84)
  the two profiles are of different devices: /device:TPU:15 before, /device:TPU:13 now
where the time goes in v5:
time: 172 us; the launch traced here: 171 us
  Pallas kernels  75.4 us (44%)
  blocking collectives  54 us (31%)
  local copies, waits for them, and re-layouts  14 us (8%)
  waiting for transfers between devices  13.2 us (8%)
  starting transfers between devices  9.51 us (6%)
  other arithmetic  4.66 us (3%)
    all_to_all x1, blocking collectives, compose(): lax.all_to_all(payload, 'ctx', split_axis=0, concat_axis=0, tiled=True)  54 us
    pallas_call x1, Pallas kernels, intra_part(): pl.pallas_call(intra_kernel, grid=(nb, GROUPS), in_specs=[pl.BlockSpec((S...  32.1 us
    pallas_call x1, Pallas kernels, block_states(): pl.pallas_call(state_kernel, grid=(GROUPS, nb), in_specs=[pl.BlockSpec((S...  14.8 us
    all_to_all x1, waiting for transfers between devices, compose(): lax.all_to_all(entering, 'ctx', split_axis=0, concat_axis=0, tiled=True)  13.2 us
    pallas_call x1, Pallas kernels, mix(): pl.pallas_call(mix_kernel, grid=(nb, GROUPS), in_specs=[pl.BlockSpec((STR...  13.1 us
    pallas_call x1, Pallas kernels, conv_part(): pl.pallas_call(conv_kernel, grid=(chans // CONV_COLS,), in_specs=[pl.Bloc...  11.8 us
    all_to_all x1, starting transfers between devices, compose(): lax.all_to_all(entering, 'ctx', split_axis=0, concat_axis=0, tiled=True)  5.81 us
    ppermute x1, starting transfers between devices, shifted(): return lax.ppermute(value, axis, pairs)  3.71 us
  transfers between devices with their start and end apart: 2, of which 1 were waited for; matrix products, arithmetic and copies ran while one was open for 7% of the time, Pallas kernels for 19%

profile of v5, /device:TPU:13, one launch (start us, length us, event | category | flops | bytes accessed | tf_op | source)
XLA Modules:
  0.0 170.9 jit_solution(12813331284912189305)
XLA Ops:
  0.0 0.9 slice.43
  0.9 3.7 %collective-permute-start = (bf16[3,5120]{1,0:T(4,128)(2,1)S(1)}, bf16[3,5120]{1,0:T(4,128)(2,1)S(1)}, u32[]{:S(2)}, u32[]{:S(2)}) collective-permute-start(bf16[3,5120]{1,0:T(4,128)(2,1)S(1)} %slice.43), channel_id=1, source_target_pairs={{0,1},{1,2},{2,3},{3,4},{4,5},{5,6},{6,7},{7,8},{8,9},{9,10},{10,1... | collective-permute-start | bytes 92168 | tf_op jit(solution)/shard_map/ppermute | solution.py:23
  4.7 0.7 exp.14
  5.3 0.8 reduce-window.18
  6.2 0.2 fusion.4
  6.3 0.1 copy.57
  6.4 0.1 convert_reduce_fusion.1
  6.5 0.1 convert_reduce_fusion
  6.6 0.1 fusion.1
  6.8 0.2 copy.48
  7.0 1.0 negate_multiply_fusion
  8.0 1.2 reduce-window.19
  9.2 0.2 slice_reduce_fusion
  9.5 0.1 bitcast_bitcast_fusion
  9.6 0.2 fusion
  9.7 0.2 compare_reduce_fusion
  9.9 0.1 broadcast_select_fusion
  10.0 0.7 pad_convert_fusion.m_ref
  10.7 0.1 copy.53
  10.8 1.6 concatenate.12.w_ref
  12.4 0.1 reshape_reshape.3
  12.5 0.1 broadcast_in_dim.67
  12.6 0.7 broadcast_in_dim_reshape.7.bdec_ref
  13.3 1.0 copy.54
  14.3 1.0 copy.49
  15.3 0.0 collective-permute-done
  15.3 0.7 concatenate.11.rim_ref
  16.0 11.8 %shard_map.100.c_ref.b_ref.x_ref = bf16[512,5120]{1,0:T(8,128)(2,1)} custom-call(bf16[512,5120]{1,0:T(8,128)(2,1)} %x_ref.1, bf16[8,5120]{1,0:T(8,128)(2,1)} %concatenate.11.rim_ref, f32[8,5120]{1,0:T(8,128)} %concatenate.12.w_ref, f32[1,5120]{1,0:T(1,128)} %bitcast.45, f32[512,128]{1,0:T(8,128)} %pad_convert_fusion.m_ref), custom_call_target="tpu_custom_call" | custom-call | tf_op jit(solution)/shard_map/pallas_call | solution.py:59
  27.8 1.1 slice.59
  28.9 1.0 copy.58
  29.9 0.8 broadcast_in_dim.33.segc_ref
  30.7 14.8 %shard_map.102 = (f32[2,256,4096]{2,1,0:T(8,128)}, f32[2,1,4096]{2,1,0:T(1,128)}, bf16[16,258,256]{2,1,0:T(8,128)(2,1)}) custom-call(bf16[512,512]{1,0:T(8,128)(2,1)} %bitcast.41, bf16[512,5120]{1,0:T(8,128)(2,1)} %shard_map.100.c_ref.b_ref.x_ref, f32[2,512,32]{2,1,0:T(8,128)} %bitcast.39, f32[2,512,32]{2,1,0:T(8,128)} %bitcast.36, ...), custom_call_target="tpu_custom_call" | custom-call | tf_op jit(solution)/shard_map/pallas_call | solution.py:121
  45.6 54.0 %all_to_all.10.got_ref = bf16[16,258,256]{2,1,0:T(8,128)(2,1)} all-to-all(bf16[16,258,256]{2,1,0:T(8,128)(2,1)} %get-tuple-element.8), channel_id=1, replica_groups=mesh['group'=2,'ctx'=16] {'ctx'}, dimensions={0} | all-to-all | bytes 4227072 | tf_op jit(solution)/shard_map/all_to_all | solution.py:265
  99.6 0.0 copy-start.1
  99.6 3.6 %shard_map.103 = bf16[16,256,256]{2,1,0:T(8,128)(2,1)} custom-call(bf16[16,258,256]{2,1,0:T(8,128)(2,1)} %all_to_all.10.got_ref), custom_call_target="tpu_custom_call" | custom-call | tf_op jit(solution)/shard_map/pallas_call | solution.py:266
  103.1 5.8 %all-to-all-start.1 = ((bf16[16,256,256]{2,1,0:T(8,128)(2,1)}), bf16[16,256,256]{2,1,0:T(8,128)(2,1)S(1)}, u32[]{:S(2)}, u32[]{:S(2)}) async-start(bf16[16,256,256]{2,1,0:T(8,128)(2,1)} %shard_map.103), calls=%async_computation.1 | async-start | bytes 4194304 | tf_op jit(solution)/shard_map/all_to_all | solution.py:270
  108.9 0.1 broadcast_in_dim.68
  109.0 0.1 broadcast_in_dim.69
  109.1 0.0 copy-done.1
  109.1 0.1 broadcast_in_dim.35
  109.2 0.7 broadcast_in_dim_reshape.6.dsk_ref
  109.8 0.7 copy.62
  110.5 0.6 broadcast_in_dim.34.segr_ref
  111.1 32.1 %shard_map.101.y_ref = f32[512,4096]{1,0:T(8,128)} custom-call(bf16[512,5120]{1,0:T(8,128)(2,1)} %shard_map.100.c_ref.b_ref.x_ref, bf16[512,5120]{1,0:T(8,128)(2,1)} %shard_map.100.c_ref.b_ref.x_ref, bf16[512,5120]{1,0:T(8,128)(2,1)} %shard_map.100.c_ref.b_ref.x_ref, f32[2,512,32]{2,1,0:T(8,128)} %bitcast.40, f32[2,512,32]{2,1,0:T(8,128)} %bitcast.37, ...), custom_call_target="tpu_custom_call" | custom-call | tf_op jit(solution)/shard_map/pallas_call | solution.py:179
  143.2 13.2 %all-to-all-done.1.back_ref = bf16[16,256,256]{2,1,0:T(8,128)(2,1)S(1)} async-done(((bf16[16,256,256]{2,1,0:T(8,128)(2,1)}), bf16[16,256,256]{2,1,0:T(8,128)(2,1)S(1)}, u32[]{:S(2)}, u32[]{:S(2)}) %all-to-all-start.1) | async-done | bytes 2097184 | tf_op jit(solution)/shard_map/all_to_all | solution.py:270
  156.4 0.8 broadcast_in_dim.70.eb_ref
  157.2 0.6 copy-done
  157.7 13.1 %shard_map.104 = bf16[512,4096]{1,0:T(8,128)(2,1)} custom-call(bf16[512,5120]{1,0:T(8,128)(2,1)} %shard_map.100.c_ref.b_ref.x_ref, f32[512,4096]{1,0:T(8,128)} %shard_map.101.y_ref, bf16[512,4096]{1,0:T(8,128)(2,1)} %z_ref.1, bf16[16,256,256]{2,1,0:T(8,128)(2,1)} %copy-done, f32[2,256,4096]{2,1,0:T(8,128)} %get-tuple-element.9.local_ref, ...), custom_call_target="tpu_custom_call" | custom-call | tf_op jit(solution)/shard_map/pallas_call | solution.py:226
  (13 shorter events, 0.1 us)
Async XLA Ops:
  0.9 14.4 %collective-permute-start = (bf16[3,5120]{1,0:T(4,128)(2,1)S(1)}, bf16[3,5120]{1,0:T(4,128)(2,1)S(1)}, u32[]{:S(2)}, u32[]{:S(2)}) collective-permute-start(bf16[3,5120]{1,0:T(4,128)(2,1)S(1)} %slice.43), channel_id=1, source_target_pairs={{0,1},{1,2},{2,3},{3,4},{4,5},{5,6},{6,7},{7,8},{8,9},{9,10},{10,1... | collective-permute-start | bytes 92168 | tf_op jit(solution)/shard_map/ppermute | solution.py:23
  99.6 9.5 %copy-start.1 = (f32[64]{0:T(128)S(1)}, f32[64]{0:T(128)}, u32[]{:S(2)}) copy-start(f32[64]{0:T(128)} %param.18) | copy-start | bytes 772
  103.1 53.2 %all-to-all-start.1 = ((bf16[16,256,256]{2,1,0:T(8,128)(2,1)}), bf16[16,256,256]{2,1,0:T(8,128)(2,1)S(1)}, u32[]{:S(2)}, u32[]{:S(2)}) async-start(bf16[16,256,256]{2,1,0:T(8,128)(2,1)} %shard_map.103), calls=%async_computation.1 | async-start | bytes 4194304 | tf_op jit(solution)/shard_map/all_to_all | solution.py:270
  156.4 1.4 copy-start

commit v6 on v5

--- a/solution.py
+++ b/solution.py
@@ -27,6 +27,19 @@
     prompt_ends = jnp.cumsum(lengths)
     hits = (prompt_ends[None, :] <= positions[:, None]).astype(jnp.int32)
     return jnp.sum(hits, axis=1)
+
+
+def expand_heads(v):
+    heads = lax.broadcasted_iota(jnp.int32, (PER_GROUP, GROUP_COLS), 0)
+    cols = lax.broadcasted_iota(jnp.int32, (PER_GROUP, GROUP_COLS), 1)
+    spread = (cols // HEAD_DIM == heads).astype(jnp.bfloat16)
+    hi = v.astype(jnp.bfloat16)
+    rest = v - hi.astype(jnp.float32)
+    mid = rest.astype(jnp.bfloat16)
+    lo = (rest - mid.astype(jnp.float32)).astype(jnp.bfloat16)
+    out = jnp.dot(hi, spread, preferred_element_type=jnp.float32)
+    out = out + jnp.dot(mid, spread, preferred_element_type=jnp.float32)
+    return out + jnp.dot(lo, spread, preferred_element_type=jnp.float32)
 
 
 CONV_COLS = 640
@@ -73,7 +86,7 @@
 
 def state_kernel(
     bt_ref, x_ref, dt_ref, cum_ref, segc_ref, bdec_ref, local_ref, cdec_ref, pay_ref,
-    uw_ref, acc_ref, dec_ref,
+    acc_ref, dec_ref,
 ):
     b = pl.program_id(1)
 
@@ -90,11 +103,9 @@
     last = cum[STRETCH - 1 : STRETCH, :]
     seg_last = segc[STRETCH - 1 : STRETCH, :]
     w = jnp.where(segc == seg_last, jnp.exp(last - cum), 0.0)
-    for j in range(PER_GROUP):
-        cols = slice(j * HEAD_DIM, (j + 1) * HEAD_DIM)
-        scaled = (x_ref[:, cols].astype(jnp.float32) * step[:, j : j + 1]).astype(jnp.bfloat16)
-        uw_ref[:, cols] = (scaled.astype(jnp.float32) * w[:, j : j + 1]).astype(jnp.bfloat16)
-    block_state = jnp.dot(bt_ref[...], uw_ref[...], preferred_element_type=jnp.float32)
+    scaled = (x_ref[...].astype(jnp.float32) * expand_heads(step)).astype(jnp.bfloat16)
+    weighted = (scaled.astype(jnp.float32) * expand_heads(w)).astype(jnp.bfloat16)
+    block_state = jnp.dot(bt_ref[...], weighted, preferred_element_type=jnp.float32)
     decay = bdec_ref[0]
     acc_ref[...] = decay * acc_ref[...] + block_state
     dec_ref[...] = dec_ref[...] * decay
@@ -140,7 +151,6 @@
             jax.ShapeDtypeStruct((peers, STATE + 2, width), jnp.bfloat16),
         ],
         scratch_shapes=[
-            pltpu.VMEM((STRETCH, GROUP_COLS), jnp.bfloat16),
             pltpu.VMEM((STATE, GROUP_COLS), jnp.float32),
             pltpu.VMEM((1, GROUP_COLS), jnp.float32),
         ],
@@ -171,33 +181,33 @@
         out_ref[:, hc] = intra + dsk_ref[:, hc] * xf
 
 
-def intra_part(conv, dt_g, cum_g, cumt_g, segc, segr, dsk):
+def intra_part(conv, dt_g, cum_g, cumt_g, segc, segr, dsk, g):
     tok = conv.shape[0]
     nb = tok // STRETCH
     b_col = INNER // STATE
     c_col = b_col + GROUPS
     return pl.pallas_call(
         intra_kernel,
-        grid=(nb, GROUPS),
+        grid=(nb,),
         in_specs=[
-            pl.BlockSpec((STRETCH, STATE), lambda b, g: (b, c_col + g)),
-            pl.BlockSpec((STRETCH, STATE), lambda b, g: (b, b_col + g)),
-            pl.BlockSpec((STRETCH, GROUP_COLS), lambda b, g: (b, g)),
-            pl.BlockSpec((1, STRETCH, PER_GROUP), lambda b, g: (g, b, 0)),
-            pl.BlockSpec((1, STRETCH, PER_GROUP), lambda b, g: (g, b, 0)),
-            pl.BlockSpec((1, PER_GROUP, STRETCH), lambda b, g: (g, 0, b)),
-            pl.BlockSpec((STRETCH, 128), lambda b, g: (b, 0)),
-            pl.BlockSpec((8, STRETCH), lambda b, g: (0, b)),
-            pl.BlockSpec((1, GROUP_COLS), lambda b, g: (0, g)),
-        ],
-        out_specs=pl.BlockSpec((STRETCH, GROUP_COLS), lambda b, g: (b, g)),
-        out_shape=jax.ShapeDtypeStruct((tok, INNER), jnp.float32),
+            pl.BlockSpec((STRETCH, STATE), lambda b: (b, c_col + g)),
+            pl.BlockSpec((STRETCH, STATE), lambda b: (b, b_col + g)),
+            pl.BlockSpec((STRETCH, GROUP_COLS), lambda b: (b, g)),
+            pl.BlockSpec((1, STRETCH, PER_GROUP), lambda b: (g, b, 0)),
+            pl.BlockSpec((1, STRETCH, PER_GROUP), lambda b: (g, b, 0)),
+            pl.BlockSpec((1, PER_GROUP, STRETCH), lambda b: (g, 0, b)),
+            pl.BlockSpec((STRETCH, 128), lambda b: (b, 0)),
+            pl.BlockSpec((8, STRETCH), lambda b: (0, b)),
+            pl.BlockSpec((1, GROUP_COLS), lambda b: (0, g)),
+        ],
+        out_specs=pl.BlockSpec((STRETCH, GROUP_COLS), lambda b: (b, 0)),
+        out_shape=jax.ShapeDtypeStruct((tok, GROUP_COLS), jnp.float32),
     )(conv, conv, conv, dt_g, cum_g, cumt_g, segc, segr, dsk)
 
 
 def mix_kernel(
     c_ref, y_ref, z_ref, back_ref, local_ref, cdec_ref, cum_ref, segc_ref, eb_ref, gain_ref,
-    out_ref, hin_ref, acc_ref,
+    out_ref, hin_ref,
 ):
     pieces, _, width = back_ref.shape
     for k in range(pieces):
@@ -207,10 +217,7 @@
     entry = eb_ref[0:1, 0:1]
     in_weight = jnp.where(segc == entry, jnp.exp(cum_ref[0]), 0.0)
     inter = jnp.dot(c_ref[...], state.astype(jnp.bfloat16), preferred_element_type=jnp.float32)
-    for j in range(PER_GROUP):
-        hc = slice(j * HEAD_DIM, (j + 1) * HEAD_DIM)
-        acc_ref[:, hc] = inter[:, hc] * in_weight[:, j : j + 1]
-    y = y_ref[...] + acc_ref[...]
+    y = y_ref[...] + inter * expand_heads(in_weight)
     zf = z_ref[...].astype(jnp.float32)
     gated = y * (zf * jax.nn.sigmoid(zf))
     mean_square = jnp.mean(gated * gated, axis=1, keepdims=True) + 1e-05
@@ -240,10 +247,7 @@
         ],
         out_specs=pl.BlockSpec((STRETCH, GROUP_COLS), lambda b, g: (b, g)),
         out_shape=jax.ShapeDtypeStruct((tok, INNER), jnp.bfloat16),
-        scratch_shapes=[
-            pltpu.VMEM((STATE, GROUP_COLS), jnp.float32),
-            pltpu.VMEM((STRETCH, GROUP_COLS), jnp.float32),
-        ],
+        scratch_shapes=[pltpu.VMEM((STATE, GROUP_COLS), jnp.float32)],
     )(conv, y_local, z_gate, back, local_states, cdec, cum_g, segc, eb, gain)
 
 
@@ -308,7 +312,9 @@
 
     local_states, cdec, payload = block_states(bt, conv, dt_g, cum_g, segc, bdec, peers)
     dsk = jnp.repeat(d_skip, HEAD_DIM)[None, :]
-    y_local = intra_part(conv, dt_g, cum_g, cumt_g, segc, segr, dsk)
+    y_local = jnp.concatenate(
+        [intra_part(conv, dt_g, cum_g, cumt_g, segc, segr, dsk, g) for g in range(GROUPS)], axis=1
+    )
     back = compose(payload)
     gain = norm_gain[None, :]
     return mix(conv, y_local, z_gate, back, local_states, cdec, cum_g, segc, eb, gain)

time: 172 us -> 169 us (0.983)
  the two profiles are of different devices: /device:TPU:13 before, /device:TPU:1 now
where the time goes in v6:
time: 169 us; the launch traced here: 167 us
  Pallas kernels  76 us (45%)
  blocking collectives  55.8 us (33%)
  local copies, waits for them, and re-layouts  14 us (8%)
  other arithmetic  12.3 us (7%)
  starting transfers between devices  8.44 us (5%)
    all_to_all x1, blocking collectives, compose(): lax.all_to_all(payload, 'ctx', split_axis=0, concat_axis=0, tiled=True)  55.8 us
    pallas_call x2, Pallas kernels, intra_part(): pl.pallas_call(intra_kernel, grid=(nb,), in_specs=[pl.BlockSpec((STRETCH,...  34.8 us
    pallas_call x1, Pallas kernels, mix(): pl.pallas_call(mix_kernel, grid=(nb, GROUPS), in_specs=[pl.BlockSpec((STR...  13.4 us
    pallas_call x1, Pallas kernels, block_states(): pl.pallas_call(state_kernel, grid=(GROUPS, nb), in_specs=[pl.BlockSpec((S...  12.3 us
    pallas_call x1, Pallas kernels, conv_part(): pl.pallas_call(conv_kernel, grid=(chans // CONV_COLS,), in_specs=[pl.Bloc...  11.8 us
    concatenate x1, other arithmetic, local(): jnp.concatenate([intra_part(conv, dt_g, cum_g, cumt_g, segc, segr, dsk, g...  7.67 us
    ppermute x1, starting transfers between devices, shifted(): return lax.ppermute(value, axis, pairs)  4.54 us
    all_to_all x1, starting transfers between devices, compose(): lax.all_to_all(entering, 'ctx', split_axis=0, concat_axis=0, tiled=True)  3.9 us
  transfers between devices with their start and end apart: 2, of which 0 were waited for; matrix products, arithmetic and copies ran while one was open for 12% of the time, Pallas kernels for 21%

profile of v6, /device:TPU:1, one launch (start us, length us, event | category | flops | bytes accessed | tf_op | source)
XLA Modules:
  0.0 166.7 jit_solution(236270705539852671)
XLA Ops:
  0.0 0.9 slice.43
  0.9 4.5 %collective-permute-start = (bf16[3,5120]{1,0:T(4,128)(2,1)S(1)}, bf16[3,5120]{1,0:T(4,128)(2,1)S(1)}, u32[]{:S(2)}, u32[]{:S(2)}) collective-permute-start(bf16[3,5120]{1,0:T(4,128)(2,1)S(1)} %slice.43), channel_id=1, source_target_pairs={{0,1},{1,2},{2,3},{3,4},{4,5},{5,6},{6,7},{7,8},{8,9},{9,10},{10,1... | collective-permute-start | bytes 92168 | tf_op jit(solution)/shard_map/ppermute | solution.py:23
  5.5 0.7 exp.14
  6.1 0.8 reduce-window.18
  7.0 0.2 fusion.4
  7.2 0.1 copy.57
  7.3 0.1 convert_reduce_fusion.1
  7.4 0.1 convert_reduce_fusion
  7.5 0.1 fusion.1
  7.6 0.2 copy.48
  7.8 1.0 negate_multiply_fusion
  8.8 1.2 reduce-window.19
  10.0 0.2 slice_reduce_fusion
  10.3 0.1 bitcast_bitcast_fusion
  10.4 0.2 fusion
  10.6 0.2 compare_reduce_fusion
  10.8 0.1 broadcast_select_fusion
  10.8 0.7 pad_convert_fusion.m_ref
  11.6 0.1 copy.53
  11.7 1.6 concatenate.15.w_ref
  13.2 0.1 reshape_reshape.3
  13.4 0.1 broadcast_in_dim.67
  13.4 0.7 broadcast_in_dim_reshape.7.bdec_ref
  14.1 1.0 copy.54
  15.1 1.0 copy.49
  16.1 0.0 collective-permute-done
  16.2 0.6 concatenate.14.rim_ref
  16.8 11.8 %shard_map.100.c_ref.b_ref.x_ref = bf16[512,5120]{1,0:T(8,128)(2,1)} custom-call(bf16[512,5120]{1,0:T(8,128)(2,1)} %x_ref.1, bf16[8,5120]{1,0:T(8,128)(2,1)} %concatenate.14.rim_ref, f32[8,5120]{1,0:T(8,128)} %concatenate.15.w_ref, f32[1,5120]{1,0:T(1,128)} %bitcast.48, f32[512,128]{1,0:T(8,128)} %pad_convert_fusion.m_ref), custom_call_target="tpu_custom_call" | custom-call | tf_op jit(solution)/shard_map/pallas_call | solution.py:72
  28.6 1.1 slice.59
  29.7 1.1 copy.58
  30.8 0.8 broadcast_in_dim.33.segc_ref
  31.6 12.3 %shard_map.103 = (f32[2,256,4096]{2,1,0:T(8,128)}, f32[2,1,4096]{2,1,0:T(1,128)}, bf16[16,258,256]{2,1,0:T(8,128)(2,1)}) custom-call(bf16[512,512]{1,0:T(8,128)(2,1)} %bitcast.43, bf16[512,5120]{1,0:T(8,128)(2,1)} %shard_map.100.c_ref.b_ref.x_ref, f32[2,512,32]{2,1,0:T(8,128)} %bitcast.40, f32[2,512,32]{2,1,0:T(8,128)} %bitcast.36, ...), custom_call_target="tpu_custom_call" | custom-call | tf_op jit(solution)/shard_map/pallas_call | solution.py:132
  43.9 55.8 %all_to_all.10.got_ref = bf16[16,258,256]{2,1,0:T(8,128)(2,1)} all-to-all(bf16[16,258,256]{2,1,0:T(8,128)(2,1)} %get-tuple-element.8), channel_id=1, replica_groups=mesh['group'=2,'ctx'=16] {'ctx'}, dimensions={0} | all-to-all | bytes 4227072 | tf_op jit(solution)/shard_map/all_to_all | solution.py:269
  99.7 3.6 %shard_map.104 = bf16[16,256,256]{2,1,0:T(8,128)(2,1)} custom-call(bf16[16,258,256]{2,1,0:T(8,128)(2,1)} %all_to_all.10.got_ref), custom_call_target="tpu_custom_call" | custom-call | tf_op jit(solution)/shard_map/pallas_call | solution.py:270
  103.3 3.9 %all-to-all-start.1 = ((bf16[16,256,256]{2,1,0:T(8,128)(2,1)}), bf16[16,256,256]{2,1,0:T(8,128)(2,1)S(1)}, u32[]{:S(2)}, u32[]{:S(2)}) async-start(bf16[16,256,256]{2,1,0:T(8,128)(2,1)} %shard_map.104), calls=%async_computation.1 | async-start | bytes 4194304 | tf_op jit(solution)/shard_map/all_to_all | solution.py:274
  107.2 0.1 broadcast_in_dim.68
  107.3 0.1 broadcast_in_dim.69
  107.4 0.1 broadcast_in_dim.35
  107.4 0.7 broadcast_in_dim_reshape.6.dsk_ref
  108.1 0.7 copy.62
  108.8 0.6 broadcast_in_dim.34.segr_ref
  109.4 17.4 %shard_map.102 = f32[512,2048]{1,0:T(8,128)} custom-call(bf16[512,5120]{1,0:T(8,128)(2,1)} %shard_map.100.c_ref.b_ref.x_ref, bf16[512,5120]{1,0:T(8,128)(2,1)} %shard_map.100.c_ref.b_ref.x_ref, bf16[512,5120]{1,0:T(8,128)(2,1)} %shard_map.100.c_ref.b_ref.x_ref, f32[2,512,32]{2,1,0:T(8,128)} %bitcast.41, f32[2,512,32]{2,1,0:T(8,128)} %bitcast.37, ...), custom_call_target="tpu_custom_call" | custom-call | tf_op jit(solution)/shard_map/pallas_call | solution.py:189
  126.8 17.4 %shard_map.101 = f32[512,2048]{1,0:T(8,128)} custom-call(bf16[512,5120]{1,0:T(8,128)(2,1)} %shard_map.100.c_ref.b_ref.x_ref, bf16[512,5120]{1,0:T(8,128)(2,1)} %shard_map.100.c_ref.b_ref.x_ref, bf16[512,5120]{1,0:T(8,128)(2,1)} %shard_map.100.c_ref.b_ref.x_ref, f32[2,512,32]{2,1,0:T(8,128)} %bitcast.42, f32[2,512,32]{2,1,0:T(8,128)} %bitcast.38, ...), custom_call_target="tpu_custom_call" | custom-call | tf_op jit(solution)/shard_map/pallas_call | solution.py:189
  144.2 7.7 %pad_maximum_fusion.y_ref = f32[512,4096]{1,0:T(8,128)} fusion(f32[512,2048]{1,0:T(8,128)} %shard_map.102, f32[512,2048]{1,0:T(8,128)} %shard_map.101), kind=kLoop, calls=%fused_computation | loop fusion | flops 2097152 | bytes 16777216 | tf_op jit(solution)/shard_map/concatenate | solution.py:315
  151.9 0.0 all-to-all-done.1.back_ref
  151.9 0.7 broadcast_in_dim.70.eb_ref
  152.6 0.6 copy-done
  153.2 13.4 %shard_map.105 = bf16[512,4096]{1,0:T(8,128)(2,1)} custom-call(bf16[512,5120]{1,0:T(8,128)(2,1)} %shard_map.100.c_ref.b_ref.x_ref, f32[512,4096]{1,0:T(8,128)} %pad_maximum_fusion.y_ref, bf16[512,4096]{1,0:T(8,128)(2,1)} %z_ref.1, bf16[16,256,256]{2,1,0:T(8,128)(2,1)} %copy-done, f32[2,256,4096]{2,1,0:T(8,128)} %get-tuple-element.9.local_ref, ...), custom_call_target="tpu_custom_call" | custom-call | tf_op jit(solution)/shard_map/pallas_call | solution.py:233
  (15 shorter events, 0.1 us)
Async XLA Ops:
  0.9 15.2 %collective-permute-start = (bf16[3,5120]{1,0:T(4,128)(2,1)S(1)}, bf16[3,5120]{1,0:T(4,128)(2,1)S(1)}, u32[]{:S(2)}, u32[]{:S(2)}) collective-permute-start(bf16[3,5120]{1,0:T(4,128)(2,1)S(1)} %slice.43), channel_id=1, source_target_pairs={{0,1},{1,2},{2,3},{3,4},{4,5},{5,6},{6,7},{7,8},{8,9},{9,10},{10,1... | collective-permute-start | bytes 92168 | tf_op jit(solution)/shard_map/ppermute | solution.py:23
  99.7 7.6 %copy-start.1 = (f32[64]{0:T(128)S(1)}, f32[64]{0:T(128)}, u32[]{:S(2)}) copy-start(f32[64]{0:T(128)} %param.18) | copy-start | bytes 772
  103.3 48.6 %all-to-all-start.1 = ((bf16[16,256,256]{2,1,0:T(8,128)(2,1)}), bf16[16,256,256]{2,1,0:T(8,128)(2,1)S(1)}, u32[]{:S(2)}, u32[]{:S(2)}) async-start(bf16[16,256,256]{2,1,0:T(8,128)(2,1)} %shard_map.104), calls=%async_computation.1 | async-start | bytes 4194304 | tf_op jit(solution)/shard_map/all_to_all | solution.py:274
  151.9 1.4 copy-start

commit v7 on v6

--- a/solution.py
+++ b/solution.py
@@ -3,7 +3,7 @@
 from jax import lax
 from jax.experimental import pallas as pl
 from jax.experimental.pallas import tpu as pltpu
-from jax.sharding import PartitionSpec as P
+from jax.sharding import Mesh, PartitionSpec as P
 
 HEADS = 64
 HEAD_DIM = 64
@@ -85,7 +85,7 @@
 
 
 def state_kernel(
-    bt_ref, x_ref, dt_ref, cum_ref, segc_ref, bdec_ref, local_ref, cdec_ref, pay_ref,
+    bt_ref, x_ref, dt_ref, cum_ref, segc_ref, bdec_ref, local_ref, cdec_ref, tot_ref, tdec_ref,
     acc_ref, dec_ref,
 ):
     b = pl.program_id(1)
@@ -112,23 +112,13 @@
 
     @pl.when(b == pl.num_programs(1) - 1)
     def _():
-        pieces, _, width = pay_ref.shape
-        total = acc_ref[...]
-        dec = dec_ref[...]
-        hi = dec.astype(jnp.bfloat16)
-        lo = (dec - hi.astype(jnp.float32)).astype(jnp.bfloat16)
-        for k in range(pieces):
-            cols = slice(k * width, (k + 1) * width)
-            pay_ref[k, 0:STATE, :] = total[:, cols].astype(jnp.bfloat16)
-            pay_ref[k, STATE : STATE + 1, :] = hi[:, cols]
-            pay_ref[k, STATE + 1 : STATE + 2, :] = lo[:, cols]
-
-
-def block_states(bt, conv, dt_g, cum_g, segc, bdec, peers):
+        tot_ref[...] = acc_ref[...]
+        tdec_ref[...] = dec_ref[...]
+
+
+def block_states(bt, conv, dt_g, cum_g, segc, bdec):
     tok = conv.shape[0]
     nb = tok // STRETCH
-    width = INNER // peers
-    per = peers // GROUPS
     return pl.pallas_call(
         state_kernel,
         grid=(GROUPS, nb),
@@ -143,12 +133,14 @@
         out_specs=[
             pl.BlockSpec((1, STATE, GROUP_COLS), lambda g, b: (b, 0, g)),
             pl.BlockSpec((1, 1, GROUP_COLS), lambda g, b: (b, 0, g)),
-            pl.BlockSpec((per, STATE + 2, width), lambda g, b: (g, 0, 0)),
+            pl.BlockSpec((STATE, GROUP_COLS), lambda g, b: (0, g)),
+            pl.BlockSpec((1, GROUP_COLS), lambda g, b: (0, g)),
         ],
         out_shape=[
             jax.ShapeDtypeStruct((nb, STATE, INNER), jnp.float32),
             jax.ShapeDtypeStruct((nb, 1, INNER), jnp.float32),
-            jax.ShapeDtypeStruct((peers, STATE + 2, width), jnp.bfloat16),
+            jax.ShapeDtypeStruct((STATE, INNER), jnp.float32),
+            jax.ShapeDtypeStruct((1, INNER), jnp.float32),
         ],
         scratch_shapes=[
             pltpu.VMEM((STATE, GROUP_COLS), jnp.float32),
@@ -181,38 +173,48 @@
         out_ref[:, hc] = intra + dsk_ref[:, hc] * xf
 
 
-def intra_part(conv, dt_g, cum_g, cumt_g, segc, segr, dsk, g):
+def intra_part(conv, dt_g, cum_g, cumt_g, segc, segr, dsk, g, into=None):
     tok = conv.shape[0]
     nb = tok // STRETCH
     b_col = INNER // STATE
     c_col = b_col + GROUPS
+    operands = [conv, conv, conv, dt_g, cum_g, cumt_g, segc, segr, dsk]
+    specs = [
+        pl.BlockSpec((STRETCH, STATE), lambda b: (b, c_col + g)),
+        pl.BlockSpec((STRETCH, STATE), lambda b: (b, b_col + g)),
+        pl.BlockSpec((STRETCH, GROUP_COLS), lambda b: (b, g)),
+        pl.BlockSpec((1, STRETCH, PER_GROUP), lambda b: (g, b, 0)),
+        pl.BlockSpec((1, STRETCH, PER_GROUP), lambda b: (g, b, 0)),
+        pl.BlockSpec((1, PER_GROUP, STRETCH), lambda b: (g, 0, b)),
+        pl.BlockSpec((STRETCH, 128), lambda b: (b, 0)),
+        pl.BlockSpec((8, STRETCH), lambda b: (0, b)),
+        pl.BlockSpec((1, GROUP_COLS), lambda b: (0, g)),
+    ]
+    kernel = intra_kernel
+    aliases = {}
+    if into is not None:
+        operands.append(into)
+        specs.append(pl.BlockSpec(memory_space=pl.ANY))
+        aliases = {len(operands) - 1: 0}
+
+        def kernel(*refs):
+            intra_kernel(*refs[:-2], refs[-1])
+
     return pl.pallas_call(
-        intra_kernel,
+        kernel,
         grid=(nb,),
-        in_specs=[
-            pl.BlockSpec((STRETCH, STATE), lambda b: (b, c_col + g)),
-            pl.BlockSpec((STRETCH, STATE), lambda b: (b, b_col + g)),
-            pl.BlockSpec((STRETCH, GROUP_COLS), lambda b: (b, g)),
-            pl.BlockSpec((1, STRETCH, PER_GROUP), lambda b: (g, b, 0)),
-            pl.BlockSpec((1, STRETCH, PER_GROUP), lambda b: (g, b, 0)),
-            pl.BlockSpec((1, PER_GROUP, STRETCH), lambda b: (g, 0, b)),
-            pl.BlockSpec((STRETCH, 128), lambda b: (b, 0)),
-            pl.BlockSpec((8, STRETCH), lambda b: (0, b)),
-            pl.BlockSpec((1, GROUP_COLS), lambda b: (0, g)),
-        ],
-        out_specs=pl.BlockSpec((STRETCH, GROUP_COLS), lambda b: (b, 0)),
-        out_shape=jax.ShapeDtypeStruct((tok, GROUP_COLS), jnp.float32),
-    )(conv, conv, conv, dt_g, cum_g, cumt_g, segc, segr, dsk)
+        in_specs=specs,
+        out_specs=pl.BlockSpec((STRETCH, GROUP_COLS), lambda b: (b, g)),
+        out_shape=jax.ShapeDtypeStruct((tok, INNER), jnp.float32),
+        input_output_aliases=aliases,
+    )(*operands)
 
 
 def mix_kernel(
-    c_ref, y_ref, z_ref, back_ref, local_ref, cdec_ref, cum_ref, segc_ref, eb_ref, gain_ref,
-    out_ref, hin_ref,
+    c_ref, y_ref, z_ref, hin_ref, local_ref, cdec_ref, cum_ref, segc_ref, eb_ref, gain_ref,
+    out_ref,
 ):
-    pieces, _, width = back_ref.shape
-    for k in range(pieces):
-        hin_ref[:, k * width : (k + 1) * width] = back_ref[k].astype(jnp.float32)
-    state = cdec_ref[0] * hin_ref[...] + local_ref[0]
+    state = cdec_ref[0] * hin_ref[...].astype(jnp.float32) + local_ref[0]
     segc = segc_ref[:, 0:1]
     entry = eb_ref[0:1, 0:1]
     in_weight = jnp.where(segc == entry, jnp.exp(cum_ref[0]), 0.0)
@@ -228,8 +230,6 @@
     tok = conv.shape[0]
     nb = tok // STRETCH
     c_col = INNER // STATE + GROUPS
-    peers, _, width = back.shape
-    per = peers // GROUPS
     return pl.pallas_call(
         mix_kernel,
         grid=(nb, GROUPS),
@@ -237,7 +237,7 @@
             pl.BlockSpec((STRETCH, STATE), lambda b, g: (b, c_col + g)),
             pl.BlockSpec((STRETCH, GROUP_COLS), lambda b, g: (b, g)),
             pl.BlockSpec((STRETCH, GROUP_COLS), lambda b, g: (b, g)),
-            pl.BlockSpec((per, STATE, width), lambda b, g: (g, 0, 0)),
+            pl.BlockSpec((STATE, GROUP_COLS), lambda b, g: (0, g)),
             pl.BlockSpec((1, STATE, GROUP_COLS), lambda b, g: (b, 0, g)),
             pl.BlockSpec((1, 1, GROUP_COLS), lambda b, g: (b, 0, g)),
             pl.BlockSpec((1, STRETCH, PER_GROUP), lambda b, g: (g, b, 0)),
@@ -247,7 +247,6 @@
         ],
         out_specs=pl.BlockSpec((STRETCH, GROUP_COLS), lambda b, g: (b, g)),
         out_shape=jax.ShapeDtypeStruct((tok, INNER), jnp.bfloat16),
-        scratch_shapes=[pltpu.VMEM((STATE, GROUP_COLS), jnp.float32)],
     )(conv, y_local, z_gate, back, local_states, cdec, cum_g, segc, eb, gain)
 
 
@@ -264,22 +263,50 @@
     lax.fori_loop(0, peers, body, jnp.zeros(out_ref.shape[1:], jnp.float32))
 
 
-def compose(payload):
-    peers, _, width = payload.shape
-    got = lax.all_to_all(payload, "ctx", split_axis=0, concat_axis=0, tiled=True)
+def swap_cores(value):
+    return lax.ppermute(value, "core", [(0, 1), (1, 0)])
+
+
+def compose(total, total_decay):
+    core = lax.axis_index("core")
+    chips = lax.axis_size("chip")
+    half = INNER // 2
+    width = half // chips
+    both = jnp.concatenate([total, total_decay], axis=0)
+    mine = lax.dynamic_slice_in_dim(both, core * half, half, axis=1)
+    theirs = swap_cores(lax.dynamic_slice_in_dim(both, (1 - core) * half, half, axis=1))
+    first = jnp.where(core == 0, mine, theirs)
+    second = jnp.where(core == 0, theirs, mine)
+    first_decay = first[STATE:]
+    chip_state = second[STATE:] * first[:STATE] + second[:STATE]
+    chip_decay = first_decay * second[STATE:]
+    decay_hi = chip_decay.astype(jnp.bfloat16)
+    decay_lo = (chip_decay - decay_hi.astype(jnp.float32)).astype(jnp.bfloat16)
+    payload = jnp.concatenate(
+        [chip_state.astype(jnp.bfloat16), decay_hi, decay_lo], axis=0
+    ).reshape(STATE + 2, chips, width).transpose(1, 0, 2)
+    got = lax.all_to_all(payload, "chip", split_axis=0, concat_axis=0, tiled=True)
     entering = pl.pallas_call(
         scan_kernel,
-        out_shape=jax.ShapeDtypeStruct((peers, STATE, width), jnp.bfloat16),
+        out_shape=jax.ShapeDtypeStruct((chips, STATE, width), jnp.bfloat16),
     )(got)
-    return lax.all_to_all(entering, "ctx", split_axis=0, concat_axis=0, tiled=True)
+    back = lax.all_to_all(entering, "chip", split_axis=0, concat_axis=0, tiled=True)
+    chip_in = back.transpose(1, 0, 2).reshape(STATE, half).astype(jnp.float32)
+    later_in = first_decay * chip_in + first[:STATE]
+    keep = jnp.where(core == 0, chip_in, later_in).astype(jnp.bfloat16)
+    other = swap_cores(jnp.where(core == 0, later_in, chip_in).astype(jnp.bfloat16))
+    return jnp.where(
+        core == 0,
+        jnp.concatenate([keep, other], axis=1),
+        jnp.concatenate([other, keep], axis=1),
+    )
 
 
 def local(xbc, z_gate, dt_raw, lengths, conv_weight, conv_bias, dt_bias, a_log, d_skip, norm_gain):
     tok = xbc.shape[0]
     nb = tok // STRETCH
-    peers = lax.axis_size("ctx")
-    first_pos = lax.axis_index("ctx") * tok
-    rim_rows = shifted(xbc[tok - (CONV - 1) :], "ctx", 1)
+    first_pos = (lax.axis_index("chip") * lax.axis_size("core") + lax.axis_index("core")) * tok
+    rim_rows = shifted(xbc[tok - (CONV - 1) :], ("chip", "core"), 1)
     rim8 = jnp.concatenate([jnp.zeros((8 - (CONV - 1), CHANNELS), xbc.dtype), rim_rows], axis=0)
     ext_pos = first_pos - (CONV - 1) + jnp.arange(tok + CONV - 1)
     ext_seg = segment_of(ext_pos, lengths)
@@ -310,32 +337,24 @@
     bt = conv[:, INNER : INNER + GROUPS * STATE].T
     bdec = jnp.repeat(block_decay, HEAD_DIM, axis=1)[:, None, :]
 
-    local_states, cdec, payload = block_states(bt, conv, dt_g, cum_g, segc, bdec, peers)
+    local_states, cdec, total, total_decay = block_states(bt, conv, dt_g, cum_g, segc, bdec)
     dsk = jnp.repeat(d_skip, HEAD_DIM)[None, :]
-    y_local = jnp.concatenate(
-        [intra_part(conv, dt_g, cum_g, cumt_g, segc, segr, dsk, g) for g in range(GROUPS)], axis=1
-    )
-    back = compose(payload)
+    y_local = None
+    for g in range(GROUPS):
+        y_local = intra_part(conv, dt_g, cum_g, cumt_g, segc, segr, dsk, g, y_local)
+    back = compose(total, total_decay)
     gain = norm_gain[None, :]
     return mix(conv, y_local, z_gate, back, local_states, cdec, cum_g, segc, eb, gain)
 
 
 def solution(mesh):
+    groups, peers = mesh.devices.shape
+    split = Mesh(mesh.devices.reshape(groups, peers // 2, 2), ("group", "chip", "core"))
+    rows = P(("group", "chip", "core"), None)
     return jax.shard_map(
         local,
-        mesh=mesh,
-        in_specs=(
-            P(("group", "ctx"), None),
-            P(("group", "ctx"), None),
-            P(("group", "ctx"), None),
-            P("group"),
-            P(),
-            P(),
-            P(),
-            P(),
-            P(),
-            P(),
-        ),
-        out_specs=P(("group", "ctx"), None),
+        mesh=split,
+        in_specs=(rows, rows, rows, P("group"), P(), P(), P(), P(), P(), P()),
+        out_specs=rows,
         check_vma=False,
     )

time: 169 us -> 180 us (1.065)
  local copies, waits for them, and re-layouts: 14 us -> 21.3 us
  waiting for transfers between devices: 0.01 us -> 4.37 us
  blocking collectives: 55.8 us -> 59.4 us
  starting transfers between devices: 8.44 us -> 6.6 us
    concatenate x1, other arithmetic: 7.67 us -> 0.09 us  [compose(): jnp.concatenate([chip_state.astype(jnp.bfloat16), decay_hi, decay_lo], ax...]
    select_n x0 -> x2, other arithmetic: none -> 4.77 us  [the longest x1 2.6 us: compose(): second = jnp.where(core == 0, theirs, mine)]
    ppermute x0 -> x2, waiting for transfers between devices: none -> 4.37 us  [swap_cores(): return lax.ppermute(value, 'core', [(0, 1), (1, 0)])]
    unnamed x5 -> x9, local copies, waits for them, and re-layouts: 1.69 us -> 5.97 us
    all_to_all x1 -> x0, starting transfers between devices: 3.9 us -> none  [compose(): lax.all_to_all(entering, 'ctx', split_axis=0, concat_axis=0, tiled=True)]
    all_to_all x1 -> x2, blocking collectives: 55.8 us -> 59.4 us  [the longest x1 30.9 us: compose(): lax.all_to_all(payload, 'chip', split_axis=0, concat_axis=0, tiled=True)]
    ppermute x0 -> x2, starting transfers between devices: none -> 2.06 us  [swap_cores(): return lax.ppermute(value, 'core', [(0, 1), (1, 0)])]
    convert_element_type x0 -> x3, other arithmetic: none -> 1.95 us  [the longest x1 1.54 us: compose(): keep = jnp.where(core == 0, chip_in, later_in).astype(jnp.bfloat16)]
  transfers between devices with their start and end apart: 2 -> 3, of which waited for: 0 -> 1; matrix products, arithmetic and copies ran while one was open for 12% -> 7% of each run, Pallas kernels for 21% -> 20%
where the time goes in v7:
time: 180 us; the launch traced here: 179 us
  Pallas kernels  75.6 us (42%)
  blocking collectives  59.4 us (33%)
  local copies, waits for them, and re-layouts  21.3 us (12%)
  other arithmetic  11.6 us (6%)
  starting transfers between devices  6.6 us (4%)
  waiting for transfers between devices  4.37 us (2%)
    pallas_call x2, Pallas kernels, intra_part(): pl.pallas_call(kernel, grid=(nb,), in_specs=specs, out_specs=pl.BlockSpec...  34.9 us
    all_to_all x1, blocking collectives, compose(): lax.all_to_all(payload, 'chip', split_axis=0, concat_axis=0, tiled=True)  30.9 us
    all_to_all x1, blocking collectives, compose(): lax.all_to_all(entering, 'chip', split_axis=0, concat_axis=0, tiled=True)  28.5 us
    pallas_call x1, Pallas kernels, mix(): pl.pallas_call(mix_kernel, grid=(nb, GROUPS), in_specs=[pl.BlockSpec((STR...  13.5 us
    pallas_call x1, Pallas kernels, block_states(): pl.pallas_call(state_kernel, grid=(GROUPS, nb), in_specs=[pl.BlockSpec((S...  12.9 us
    pallas_call x1, Pallas kernels, conv_part(): pl.pallas_call(conv_kernel, grid=(chans // CONV_COLS,), in_specs=[pl.Bloc...  11.8 us
    unnamed x9, local copies, waits for them, and re-layouts  5.97 us
    ppermute x1, starting transfers between devices, shifted(): return lax.ppermute(value, axis, pairs)  4.54 us
  transfers between devices with their start and end apart: 3, of which 1 were waited for; matrix products, arithmetic and copies ran while one was open for 7% of the time, Pallas kernels for 20%

profile of v7, /device:TPU:1, one launch (start us, length us, event | category | flops | bytes accessed | tf_op | source)
XLA Modules:
  0.0 179.1 jit_solution(15751904753096747122)
XLA Ops:
  0.0 0.9 slice.57
  0.9 4.5 %collective-permute-start = (bf16[3,5120]{1,0:T(4,128)(2,1)S(1)}, bf16[3,5120]{1,0:T(4,128)(2,1)S(1)}, u32[]{:S(2)}, u32[]{:S(2)}) collective-permute-start(bf16[3,5120]{1,0:T(4,128)(2,1)S(1)} %slice.57), channel_id=1, source_target_pairs={{0,1},{1,2},{2,3},{3,4},{4,5},{5,6},{6,7},{7,8},{8,9},{9,10},{10,1... | collective-permute-start | bytes 92168 | tf_op jit(solution)/shard_map/ppermute | solution.py:23
  5.5 0.8 reduce-window.18
  6.6 0.2 copy.57
  6.8 0.7 exp.14
  7.5 1.0 negate_multiply_fusion
  8.5 1.2 reduce-window.19
  9.7 0.2 slice_reduce_fusion
  9.9 0.1 bitcast_bitcast_fusion
  10.1 0.2 fusion.1
  10.3 0.2 fusion.5
  10.6 0.2 compare_reduce_fusion
  10.9 0.7 pad_convert_fusion.m_ref
  11.6 0.1 copy.62
  11.7 0.7 concatenate.24.w_ref
  12.4 1.0 copy.58
  13.4 0.1 reshape_reshape.3
  13.5 1.0 copy.63
  14.6 0.7 broadcast_in_dim_reshape.7.bdec_ref
  15.3 0.7 concatenate.23.rim_ref
  16.0 11.8 %shard_map.100.c_ref.b_ref.x_ref.refs_0_.refs_1_.refs_2_ = bf16[512,5120]{1,0:T(8,128)(2,1)} custom-call(bf16[512,5120]{1,0:T(8,128)(2,1)} %x_ref.1, bf16[8,5120]{1,0:T(8,128)(2,1)} %concatenate.23.rim_ref, f32[8,5120]{1,0:T(8,128)} %concatenate.24.w_ref, f32[1,5120]{1,0:T(1,128)} %bitcast.66, f32[512,128]{1,0:T(8,128)} %pad_convert_fusion.m_ref), custom_call_target="tpu_custom_call" | custom-call | tf_op jit(solution)/shard_map/pallas_call | solution.py:72
  27.8 1.1 slice.77
  28.9 1.0 copy.69
  29.9 0.8 broadcast_in_dim.33.segc_ref.refs_6_
  30.7 12.9 %shard_map.103 = (f32[2,256,4096]{2,1,0:T(8,128)}, f32[2,1,4096]{2,1,0:T(1,128)}, f32[256,4096]{1,0:T(8,128)}, f32[1,4096]{1,0:T(1,128)}) custom-call(bf16[512,512]{1,0:T(8,128)(2,1)} %bitcast.59, bf16[512,5120]{1,0:T(8,128)(2,1)} %shard_map.100.c_ref.b_ref.x_ref.refs_0_.refs_1_.refs_2_, f32[2,512,32]{2,1,0:T(8,128)} %bitcast.52, f32[2,512,32]{2,1,0:T(8,128)} %bitcast.48, ...), custom_call_target="tpu_custom_call" | custom-call | tf_op jit(solution)/shard_map/pallas_call | solution.py:122
  43.6 4.6 %constant_dynamic-update-slice_fusion = f32[257,4096]{1,0:T(8,128)} fusion(f32[256,4096]{1,0:T(8,128)} %get-tuple-element.9), kind=kLoop, calls=%fused_computation.27 | loop fusion | bytes 8388608
  48.2 1.6 dynamic-update-slice.1
  49.8 1.7 constant_dynamic-slice_fusion
  51.7 4.4 %collective-permute-done.1 = f32[257,2048]{1,0:T(8,128)} collective-permute-done((f32[257,2048]{1,0:T(8,128)S(1)}, f32[257,2048]{1,0:T(8,128)}, u32[]{:S(2)}, u32[]{:S(2)}) %collective-permute-start.1) | collective-permute-done | bytes 2105376 | tf_op jit(solution)/shard_map/ppermute | solution.py:267
  56.0 2.6 %dynamic-slice_select_fusion.1 = (f32[257,2048]{1,0:T(8,128)S(1)}, f32[257,2048]{1,0:T(8,128)S(1)}) fusion(f32[257,2048]{1,0:T(8,128)} %collective-permute-done.1, f32[257,4096]{1,0:T(8,128)} %dynamic-update-slice.1, s32[]{:T(128)S(6)} %select_n.52, pred[]{:T(512)S(6)} %eq.24), kind=kLoop, calls=%fused_computation.8 | loop fusion | flops 1052672 | bytes 8421381 | tf_op jit(solution)/shard_map/jit(_where)/select_n | solution.py:279
  58.7 0.4 fusion
  59.2 0.3 copy.75
  59.6 0.2 copy.82
  59.8 30.9 %all_to_all.10.got_ref = bf16[8,258,256]{2,1,0:T(8,128)(2,1)} all-to-all(bf16[8,258,256]{2,1,0:T(8,128)(2,1)S(1)} %bitcast.57), channel_id=1, replica_groups=mesh['group'=2,'chip'=8,'core'=2] {'chip'}, dimensions={0} | all-to-all | bytes 2113536 | tf_op jit(solution)/shard_map/all_to_all | solution.py:288
  90.7 2.5 %shard_map.104 = bf16[8,256,256]{2,1,0:T(8,128)(2,1)} custom-call(bf16[8,258,256]{2,1,0:T(8,128)(2,1)} %all_to_all.10.got_ref), custom_call_target="tpu_custom_call" | custom-call | tf_op jit(solution)/shard_map/pallas_call | solution.py:289
  93.2 28.5 %all_to_all.11 = bf16[8,256,256]{2,1,0:T(8,128)(2,1)S(1)} all-to-all(bf16[8,256,256]{2,1,0:T(8,128)(2,1)} %shard_map.104), channel_id=1, replica_groups=mesh['group'=2,'chip'=8,'core'=2] {'chip'}, dimensions={0} | all-to-all | bytes 2097152 | tf_op jit(solution)/shard_map/all_to_all | solution.py:293
  121.7 0.2 convert_bitcast_fusion
  121.9 0.3 copy.74
  122.2 1.5 select_convert_fusion.1
  123.7 2.0 %collective-permute-start.2 = (bf16[256,2048]{1,0:T(8,128)(2,1)}, bf16[256,2048]{1,0:T(8,128)(2,1)S(1)}, u32[]{:S(2)}, u32[]{:S(2)}) collective-permute-start(bf16[256,2048]{1,0:T(8,128)(2,1)} %get-tuple-element.18), channel_id=1, source_target_pairs={{0,1},{1,0},{2,3},{3,2},{4,5},{5,4},{6,7},{7,6},{8,9},{9,8},{10,11... | collective-permute-start | bytes 3145736 | tf_op jit(solution)/shard_map/ppermute | solution.py:267
  125.7 0.7 copy.73
  126.5 0.7 broadcast_in_dim_reshape.6.dsk_ref.refs_8_
  127.3 0.6 broadcast_in_dim.34.segr_ref.refs_7_
  127.9 17.4 %shard_map.101.refs_9_ = f32[512,4096]{1,0:T(8,128)} custom-call(bf16[512,5120]{1,0:T(8,128)(2,1)} %shard_map.100.c_ref.b_ref.x_ref.refs_0_.refs_1_.refs_2_, bf16[512,5120]{1,0:T(8,128)(2,1)} %shard_map.100.c_ref.b_ref.x_ref.refs_0_.refs_1_.refs_2_, bf16[512,5120]{1,0:T(8,128)(2,1)} %shard_map.100.c_ref.b_ref.x_ref.refs_0_.refs_1_.refs_2_, ...), custom_call_target="tpu_custom_call" | custom-call | tf_op jit(solution)/shard_map/pallas_call | solution.py:203
  145.3 17.6 %shard_map.102.y_ref = f32[512,4096]{1,0:T(8,128)} custom-call(bf16[512,5120]{1,0:T(8,128)(2,1)} %shard_map.100.c_ref.b_ref.x_ref.refs_0_.refs_1_.refs_2_, bf16[512,5120]{1,0:T(8,128)(2,1)} %shard_map.100.c_ref.b_ref.x_ref.refs_0_.refs_1_.refs_2_, ...), custom_call_target="tpu_custom_call", output_to_operand_aliasing={{}: (9, {})} | custom-call | tf_op jit(solution)/shard_map/pallas_call | solution.py:203
  162.8 2.2 %maximum_select_fusion.hin_ref = bf16[256,4096]{1,0:T(8,128)(2,1)} fusion(bf16[256,2048]{1,0:T(8,128)(2,1)S(1)} %collective-permute-done.2, bf16[256,2048]{1,0:T(8,128)(2,1)S(1)} %get-tuple-element.17, pred[]{:T(512)S(6)} %eq.24), kind=kLoop, calls=%fused_computation.2 | loop fusion | flops 9437184 | bytes 4194305 | tf_op jit(solution)/shard_map/jit(_where)/select_n | solution.py:298
  165.0 0.7 broadcast_in_dim.70.eb_ref
  165.7 13.5 %shard_map.105 = bf16[512,4096]{1,0:T(8,128)(2,1)} custom-call(bf16[512,5120]{1,0:T(8,128)(2,1)} %shard_map.100.c_ref.b_ref.x_ref.refs_0_.refs_1_.refs_2_, f32[512,4096]{1,0:T(8,128)} %shard_map.102.y_ref, bf16[512,4096]{1,0:T(8,128)(2,1)} %z_ref.1, bf16[256,4096]{1,0:T(8,128)(2,1)} %maximum_select_fusion.hin_ref, ...), custom_call_target="tpu_custom_call" | custom-call | tf_op jit(solution)/shard_map/pallas_call | solution.py:233
  (33 shorter events, 1.1 us)
Async XLA Ops:
  0.0 11.7 %copy-start = (f32[4,5120]{1,0:T(4,128)S(1)}, f32[4,5120]{1,0:T(4,128)}, u32[]{:S(2)}) copy-start(f32[4,5120]{1,0:T(4,128)} %param.14) | copy-start | bytes 245764
  0.9 14.4 %collective-permute-start = (bf16[3,5120]{1,0:T(4,128)(2,1)S(1)}, bf16[3,5120]{1,0:T(4,128)(2,1)S(1)}, u32[]{:S(2)}, u32[]{:S(2)}) collective-permute-start(bf16[3,5120]{1,0:T(4,128)(2,1)S(1)} %slice.57), channel_id=1, source_target_pairs={{0,1},{1,2},{2,3},{3,4},{4,5},{5,6},{6,7},{7,8},{8,9},{9,10},{10,1... | collective-permute-start | bytes 92168 | tf_op jit(solution)/shard_map/ppermute | solution.py:23
  43.6 4.6 %copy-start.1 = (f32[1,4096]{1,0:T(1,128)S(1)}, f32[1,4096]{1,0:T(1,128)}, u32[]{:S(2)}) copy-start(f32[1,4096]{1,0:T(1,128)} %get-tuple-element.10) | copy-start | bytes 49156
  51.6 4.5 %collective-permute-start.1 = (f32[257,2048]{1,0:T(8,128)S(1)}, f32[257,2048]{1,0:T(8,128)}, u32[]{:S(2)}, u32[]{:S(2)}) collective-permute-start(f32[257,2048]{1,0:T(8,128)S(1)} %constant_dynamic-slice_fusion), channel_id=1, source_target_pairs={{0,1},{1,0},{2,3},{3,2},{4,5},{5,4},{6,7},{7,6},{8,9},{9,8},{10,11... | collective-permute-start | bytes 6316040 | tf_op jit(solution)/shard_map/ppermute | solution.py:267
  122.2 4.2 %copy-start.2 = (f32[64]{0:T(128)S(1)}, f32[64]{0:T(128)}, u32[]{:S(2)}) copy-start(f32[64]{0:T(128)} %param.18) | copy-start | bytes 772
  123.7 39.1 %collective-permute-start.2 = (bf16[256,2048]{1,0:T(8,128)(2,1)}, bf16[256,2048]{1,0:T(8,128)(2,1)S(1)}, u32[]{:S(2)}, u32[]{:S(2)}) collective-permute-start(bf16[256,2048]{1,0:T(8,128)(2,1)} %get-tuple-element.18), channel_id=1, source_target_pairs={{0,1},{1,0},{2,3},{3,2},{4,5},{5,4},{6,7},{7,6},{8,9},{9,8},{10,11... | collective-permute-start | bytes 3145736 | tf_op jit(solution)/shard_map/ppermute | solution.py:267

commit v8 on v6

--- a/solution.py
+++ b/solution.py
@@ -181,28 +181,41 @@
         out_ref[:, hc] = intra + dsk_ref[:, hc] * xf
 
 
-def intra_part(conv, dt_g, cum_g, cumt_g, segc, segr, dsk, g):
+def intra_part(conv, dt_g, cum_g, cumt_g, segc, segr, dsk, g, into=None):
     tok = conv.shape[0]
     nb = tok // STRETCH
     b_col = INNER // STATE
     c_col = b_col + GROUPS
+    operands = [conv, conv, conv, dt_g, cum_g, cumt_g, segc, segr, dsk]
+    specs = [
+        pl.BlockSpec((STRETCH, STATE), lambda b: (b, c_col + g)),
+        pl.BlockSpec((STRETCH, STATE), lambda b: (b, b_col + g)),
+        pl.BlockSpec((STRETCH, GROUP_COLS), lambda b: (b, g)),
+        pl.BlockSpec((1, STRETCH, PER_GROUP), lambda b: (g, b, 0)),
+        pl.BlockSpec((1, STRETCH, PER_GROUP), lambda b: (g, b, 0)),
+        pl.BlockSpec((1, PER_GROUP, STRETCH), lambda b: (g, 0, b)),
+        pl.BlockSpec((STRETCH, 128), lambda b: (b, 0)),
+        pl.BlockSpec((8, STRETCH), lambda b: (0, b)),
+        pl.BlockSpec((1, GROUP_COLS), lambda b: (0, g)),
+    ]
+    kernel = intra_kernel
+    aliases = {}
+    if into is not None:
+        operands.append(into)
+        specs.append(pl.BlockSpec(memory_space=pl.ANY))
+        aliases = {len(operands) - 1: 0}
+
+        def kernel(*refs):
+            intra_kernel(*refs[:-2], refs[-1])
+
     return pl.pallas_call(
-        intra_kernel,
+        kernel,
         grid=(nb,),
-        in_specs=[
-            pl.BlockSpec((STRETCH, STATE), lambda b: (b, c_col + g)),
-            pl.BlockSpec((STRETCH, STATE), lambda b: (b, b_col + g)),
-            pl.BlockSpec((STRETCH, GROUP_COLS), lambda b: (b, g)),
-            pl.BlockSpec((1, STRETCH, PER_GROUP), lambda b: (g, b, 0)),
-            pl.BlockSpec((1, STRETCH, PER_GROUP), lambda b: (g, b, 0)),
-            pl.BlockSpec((1, PER_GROUP, STRETCH), lambda b: (g, 0, b)),
-            pl.BlockSpec((STRETCH, 128), lambda b: (b, 0)),
-            pl.BlockSpec((8, STRETCH), lambda b: (0, b)),
-            pl.BlockSpec((1, GROUP_COLS), lambda b: (0, g)),
-        ],
-        out_specs=pl.BlockSpec((STRETCH, GROUP_COLS), lambda b: (b, 0)),
-        out_shape=jax.ShapeDtypeStruct((tok, GROUP_COLS), jnp.float32),
-    )(conv, conv, conv, dt_g, cum_g, cumt_g, segc, segr, dsk)
+        in_specs=specs,
+        out_specs=pl.BlockSpec((STRETCH, GROUP_COLS), lambda b: (b, g)),
+        out_shape=jax.ShapeDtypeStruct((tok, INNER), jnp.float32),
+        input_output_aliases=aliases,
+    )(*operands)
 
 
 def mix_kernel(
@@ -312,9 +325,9 @@
 
     local_states, cdec, payload = block_states(bt, conv, dt_g, cum_g, segc, bdec, peers)
     dsk = jnp.repeat(d_skip, HEAD_DIM)[None, :]
-    y_local = jnp.concatenate(
-        [intra_part(conv, dt_g, cum_g, cumt_g, segc, segr, dsk, g) for g in range(GROUPS)], axis=1
-    )
+    y_local = None
+    for g in range(GROUPS):
+        y_local = intra_part(conv, dt_g, cum_g, cumt_g, segc, segr, dsk, g, y_local)
     back = compose(payload)
     gain = norm_gain[None, :]
     return mix(conv, y_local, z_gate, back, local_states, cdec, cum_g, segc, eb, gain)

time: 169 us -> 169 us (level)
  the two profiles are of different devices: /device:TPU:1 before, /device:TPU:13 now
where the time goes in v8:
time: 169 us
  Pallas kernels  75.9 us (45%)
  blocking collectives  54 us (32%)
  local copies, waits for them, and re-layouts  14 us (8%)
  waiting for transfers between devices  10.5 us (6%)
  starting transfers between devices  9.51 us (6%)
  other arithmetic  4.66 us (3%)
    all_to_all x1, blocking collectives, compose(): lax.all_to_all(payload, 'ctx', split_axis=0, concat_axis=0, tiled=True)  54 us
    pallas_call x2, Pallas kernels, intra_part(): pl.pallas_call(kernel, grid=(nb,), in_specs=specs, out_specs=pl.BlockSpec...  34.7 us
    pallas_call x1, Pallas kernels, mix(): pl.pallas_call(mix_kernel, grid=(nb, GROUPS), in_specs=[pl.BlockSpec((STR...  13.5 us
    pallas_call x1, Pallas kernels, block_states(): pl.pallas_call(state_kernel, grid=(GROUPS, nb), in_specs=[pl.BlockSpec((S...  12.3 us
    pallas_call x1, Pallas kernels, conv_part(): pl.pallas_call(conv_kernel, grid=(chans // CONV_COLS,), in_specs=[pl.Bloc...  11.8 us
    all_to_all x1, waiting for transfers between devices, compose(): lax.all_to_all(entering, 'ctx', split_axis=0, concat_axis=0, tiled=True)  10.5 us
    all_to_all x1, starting transfers between devices, compose(): lax.all_to_all(entering, 'ctx', split_axis=0, concat_axis=0, tiled=True)  5.81 us
    ppermute x1, starting transfers between devices, shifted(): return lax.ppermute(value, axis, pairs)  3.71 us
  transfers between devices with their start and end apart: 2, of which 1 were waited for; matrix products, arithmetic and copies ran while one was open for 8% of the time, Pallas kernels for 21%

profile of v8, /device:TPU:13, one launch (start us, length us, event | category | flops | bytes accessed | tf_op | source)
XLA Modules:
  0.0 168.7 jit_solution(17514556192549211373)
XLA Ops:
  0.0 0.9 slice.43
  0.9 3.7 %collective-permute-start = (bf16[3,5120]{1,0:T(4,128)(2,1)S(1)}, bf16[3,5120]{1,0:T(4,128)(2,1)S(1)}, u32[]{:S(2)}, u32[]{:S(2)}) collective-permute-start(bf16[3,5120]{1,0:T(4,128)(2,1)S(1)} %slice.43), channel_id=1, source_target_pairs={{0,1},{1,2},{2,3},{3,4},{4,5},{5,6},{6,7},{7,8},{8,9},{9,10},{10,1... | collective-permute-start | bytes 92168 | tf_op jit(solution)/shard_map/ppermute | solution.py:23
  4.7 0.7 exp.14
  5.3 0.8 reduce-window.18
  6.2 0.2 fusion.4
  6.3 0.1 copy.58
  6.4 0.1 convert_reduce_fusion.1
  6.5 0.1 convert_reduce_fusion
  6.6 0.1 fusion.1
  6.8 0.2 copy.49
  7.0 1.0 negate_multiply_fusion
  8.0 1.2 reduce-window.19
  9.2 0.2 slice_reduce_fusion
  9.5 0.1 bitcast_bitcast_fusion
  9.6 0.2 fusion
  9.7 0.2 compare_reduce_fusion
  9.9 0.1 broadcast_select_fusion
  10.0 0.7 pad_convert_fusion.m_ref
  10.7 0.1 copy.54
  10.8 1.6 concatenate.12.w_ref
  12.4 0.1 reshape_reshape.3
  12.5 0.1 broadcast_in_dim.67
  12.6 0.7 broadcast_in_dim_reshape.7.bdec_ref
  13.3 1.0 copy.55
  14.3 1.0 copy.50
  15.3 0.0 collective-permute-done
  15.3 0.7 concatenate.11.rim_ref
  16.0 11.8 %shard_map.100.c_ref.b_ref.x_ref.refs_0_.refs_1_.refs_2_ = bf16[512,5120]{1,0:T(8,128)(2,1)} custom-call(bf16[512,5120]{1,0:T(8,128)(2,1)} %x_ref.1, bf16[8,5120]{1,0:T(8,128)(2,1)} %concatenate.11.rim_ref, f32[8,5120]{1,0:T(8,128)} %concatenate.12.w_ref, f32[1,5120]{1,0:T(1,128)} %bitcast.48, f32[512,128]{1,0:T(8,128)} %pad_convert_fusion.m_ref), custom_call_target="tpu_custom_call" | custom-call | tf_op jit(solution)/shard_map/pallas_call | solution.py:72
  27.8 1.1 slice.59
  28.9 1.0 copy.59
  29.9 0.8 broadcast_in_dim.33.segc_ref.refs_6_
  30.7 12.3 %shard_map.103 = (f32[2,256,4096]{2,1,0:T(8,128)}, f32[2,1,4096]{2,1,0:T(1,128)}, bf16[16,258,256]{2,1,0:T(8,128)(2,1)}) custom-call(bf16[512,512]{1,0:T(8,128)(2,1)} %bitcast.43, bf16[512,5120]{1,0:T(8,128)(2,1)} %shard_map.100.c_ref.b_ref.x_ref.refs_0_.refs_1_.refs_2_, f32[2,512,32]{2,1,0:T(8,128)} %bitcast.40, f32[2,512,32]{2,1,0:T(8,128)} %bitcast.36, ...), custom_call_target="tpu_custom_call" | custom-call | tf_op jit(solution)/shard_map/pallas_call | solution.py:132
  43.1 54.0 %all_to_all.10.got_ref = bf16[16,258,256]{2,1,0:T(8,128)(2,1)} all-to-all(bf16[16,258,256]{2,1,0:T(8,128)(2,1)} %get-tuple-element.8), channel_id=1, replica_groups=mesh['group'=2,'ctx'=16] {'ctx'}, dimensions={0} | all-to-all | bytes 4227072 | tf_op jit(solution)/shard_map/all_to_all | solution.py:282
  97.1 3.6 %shard_map.104 = bf16[16,256,256]{2,1,0:T(8,128)(2,1)} custom-call(bf16[16,258,256]{2,1,0:T(8,128)(2,1)} %all_to_all.10.got_ref), custom_call_target="tpu_custom_call" | custom-call | tf_op jit(solution)/shard_map/pallas_call | solution.py:283
  100.6 5.8 %all-to-all-start.1 = ((bf16[16,256,256]{2,1,0:T(8,128)(2,1)}), bf16[16,256,256]{2,1,0:T(8,128)(2,1)S(1)}, u32[]{:S(2)}, u32[]{:S(2)}) async-start(bf16[16,256,256]{2,1,0:T(8,128)(2,1)} %shard_map.104), calls=%async_computation.1 | async-start | bytes 4194304 | tf_op jit(solution)/shard_map/all_to_all | solution.py:287
  106.4 0.1 broadcast_in_dim.68
  106.5 0.1 broadcast_in_dim.69
  106.6 0.0 copy-done.1
  106.6 0.1 broadcast_in_dim.35
  106.7 0.7 broadcast_in_dim_reshape.6.dsk_ref.refs_8_
  107.3 0.7 copy.63
  108.0 0.6 broadcast_in_dim.34.segr_ref.refs_7_
  108.6 17.4 %shard_map.101.refs_9_ = f32[512,4096]{1,0:T(8,128)} custom-call(bf16[512,5120]{1,0:T(8,128)(2,1)} %shard_map.100.c_ref.b_ref.x_ref.refs_0_.refs_1_.refs_2_, bf16[512,5120]{1,0:T(8,128)(2,1)} %shard_map.100.c_ref.b_ref.x_ref.refs_0_.refs_1_.refs_2_, bf16[512,5120]{1,0:T(8,128)(2,1)} %shard_map.100.c_ref.b_ref.x_ref.refs_0_.refs_1_.refs_2_, ...), custom_call_target="tpu_custom_call" | custom-call | tf_op jit(solution)/shard_map/pallas_call | solution.py:211
  126.0 17.3 %shard_map.102.y_ref = f32[512,4096]{1,0:T(8,128)} custom-call(bf16[512,5120]{1,0:T(8,128)(2,1)} %shard_map.100.c_ref.b_ref.x_ref.refs_0_.refs_1_.refs_2_, bf16[512,5120]{1,0:T(8,128)(2,1)} %shard_map.100.c_ref.b_ref.x_ref.refs_0_.refs_1_.refs_2_, ...), custom_call_target="tpu_custom_call", output_to_operand_aliasing={{}: (9, {})} | custom-call | tf_op jit(solution)/shard_map/pallas_call | solution.py:211
  143.3 10.5 %all-to-all-done.1.back_ref = bf16[16,256,256]{2,1,0:T(8,128)(2,1)S(1)} async-done(((bf16[16,256,256]{2,1,0:T(8,128)(2,1)}), bf16[16,256,256]{2,1,0:T(8,128)(2,1)S(1)}, u32[]{:S(2)}, u32[]{:S(2)}) %all-to-all-start.1) | async-done | bytes 2097184 | tf_op jit(solution)/shard_map/all_to_all | solution.py:287
  153.9 0.8 broadcast_in_dim.70.eb_ref
  154.7 0.6 copy-done
  155.2 13.5 %shard_map.105 = bf16[512,4096]{1,0:T(8,128)(2,1)} custom-call(bf16[512,5120]{1,0:T(8,128)(2,1)} %shard_map.100.c_ref.b_ref.x_ref.refs_0_.refs_1_.refs_2_, f32[512,4096]{1,0:T(8,128)} %shard_map.102.y_ref, bf16[512,4096]{1,0:T(8,128)(2,1)} %z_ref.1, bf16[16,256,256]{2,1,0:T(8,128)(2,1)} %copy-done, f32[2,256,4096]{2,1,0:T(8,128)} %get-tuple-element.9.local_ref, ...), custom_call_target="tpu_custom_call" | custom-call | tf_op jit(solution)/shard_map/pallas_call | solution.py:246
  (14 shorter events, 0.1 us)
Async XLA Ops:
  0.9 14.4 %collective-permute-start = (bf16[3,5120]{1,0:T(4,128)(2,1)S(1)}, bf16[3,5120]{1,0:T(4,128)(2,1)S(1)}, u32[]{:S(2)}, u32[]{:S(2)}) collective-permute-start(bf16[3,5120]{1,0:T(4,128)(2,1)S(1)} %slice.43), channel_id=1, source_target_pairs={{0,1},{1,2},{2,3},{3,4},{4,5},{5,6},{6,7},{7,8},{8,9},{9,10},{10,1... | collective-permute-start | bytes 92168 | tf_op jit(solution)/shard_map/ppermute | solution.py:23
  97.1 9.5 %copy-start.1 = (f32[64]{0:T(128)S(1)}, f32[64]{0:T(128)}, u32[]{:S(2)}) copy-start(f32[64]{0:T(128)} %param.18) | copy-start | bytes 772
  100.6 53.2 %all-to-all-start.1 = ((bf16[16,256,256]{2,1,0:T(8,128)(2,1)}), bf16[16,256,256]{2,1,0:T(8,128)(2,1)S(1)}, u32[]{:S(2)}, u32[]{:S(2)}) async-start(bf16[16,256,256]{2,1,0:T(8,128)(2,1)} %shard_map.104), calls=%async_computation.1 | async-start | bytes 4194304 | tf_op jit(solution)/shard_map/all_to_all | solution.py:287
  153.9 1.4 copy-start

commit v9 on v7

--- a/solution.py
+++ b/solution.py
@@ -85,7 +85,7 @@
 
 
 def state_kernel(
-    bt_ref, x_ref, dt_ref, cum_ref, segc_ref, bdec_ref, local_ref, cdec_ref, tot_ref, tdec_ref,
+    bt_ref, x_ref, dt_ref, cum_ref, segc_ref, bdec_ref, local_ref, cdec_ref, tot_ref,
     acc_ref, dec_ref,
 ):
     b = pl.program_id(1)
@@ -112,8 +112,8 @@
 
     @pl.when(b == pl.num_programs(1) - 1)
     def _():
-        tot_ref[...] = acc_ref[...]
-        tdec_ref[...] = dec_ref[...]
+        tot_ref[0, 0:STATE, :] = acc_ref[...]
+        tot_ref[0, STATE : STATE + 1, :] = dec_ref[...]
 
 
 def block_states(bt, conv, dt_g, cum_g, segc, bdec):
@@ -133,14 +133,12 @@
         out_specs=[
             pl.BlockSpec((1, STATE, GROUP_COLS), lambda g, b: (b, 0, g)),
             pl.BlockSpec((1, 1, GROUP_COLS), lambda g, b: (b, 0, g)),
-            pl.BlockSpec((STATE, GROUP_COLS), lambda g, b: (0, g)),
-            pl.BlockSpec((1, GROUP_COLS), lambda g, b: (0, g)),
+            pl.BlockSpec((1, STATE + 1, GROUP_COLS), lambda g, b: (g, 0, 0)),
         ],
         out_shape=[
             jax.ShapeDtypeStruct((nb, STATE, INNER), jnp.float32),
             jax.ShapeDtypeStruct((nb, 1, INNER), jnp.float32),
-            jax.ShapeDtypeStruct((STATE, INNER), jnp.float32),
-            jax.ShapeDtypeStruct((1, INNER), jnp.float32),
+            jax.ShapeDtypeStruct((GROUPS, STATE + 1, GROUP_COLS), jnp.float32),
         ],
         scratch_shapes=[
             pltpu.VMEM((STATE, GROUP_COLS), jnp.float32),
@@ -267,14 +265,25 @@
     return lax.ppermute(value, "core", [(0, 1), (1, 0)])
 
 
-def compose(total, total_decay):
+def exchange(value, axis):
+    count = lax.axis_size(axis)
+    me = lax.axis_index(axis)
+    got = [lax.dynamic_index_in_dim(value, me, 0, keepdims=False)]
+    for by in range(1, count):
+        piece = lax.dynamic_index_in_dim(value, (me + by) % count, 0, keepdims=False)
+        pairs = [(i, (i + by) % count) for i in range(count)]
+        got.append(lax.ppermute(piece, axis, pairs))
+    stacked = jnp.stack(got)
+    return jnp.take(stacked, (me - jnp.arange(count)) % count, axis=0)
+
+
+def compose(both):
     core = lax.axis_index("core")
     chips = lax.axis_size("chip")
-    half = INNER // 2
+    half = GROUP_COLS
     width = half // chips
-    both = jnp.concatenate([total, total_decay], axis=0)
-    mine = lax.dynamic_slice_in_dim(both, core * half, half, axis=1)
-    theirs = swap_cores(lax.dynamic_slice_in_dim(both, (1 - core) * half, half, axis=1))
+    mine = lax.dynamic_index_in_dim(both, core, 0, keepdims=False)
+    theirs = swap_cores(lax.dynamic_index_in_dim(both, 1 - core, 0, keepdims=False))
     first = jnp.where(core == 0, mine, theirs)
     second = jnp.where(core == 0, theirs, mine)
     first_decay = first[STATE:]
@@ -285,12 +294,12 @@
     payload = jnp.concatenate(
         [chip_state.astype(jnp.bfloat16), decay_hi, decay_lo], axis=0
     ).reshape(STATE + 2, chips, width).transpose(1, 0, 2)
-    got = lax.all_to_all(payload, "chip", split_axis=0, concat_axis=0, tiled=True)
+    got = exchange(payload, "chip")
     entering = pl.pallas_call(
         scan_kernel,
         out_shape=jax.ShapeDtypeStruct((chips, STATE, width), jnp.bfloat16),
     )(got)
-    back = lax.all_to_all(entering, "chip", split_axis=0, concat_axis=0, tiled=True)
+    back = exchange(entering, "chip")
     chip_in = back.transpose(1, 0, 2).reshape(STATE, half).astype(jnp.float32)
     later_in = first_decay * chip_in + first[:STATE]
     keep = jnp.where(core == 0, chip_in, later_in).astype(jnp.bfloat16)
@@ -337,12 +346,12 @@
     bt = conv[:, INNER : INNER + GROUPS * STATE].T
     bdec = jnp.repeat(block_decay, HEAD_DIM, axis=1)[:, None, :]
 
-    local_states, cdec, total, total_decay = block_states(bt, conv, dt_g, cum_g, segc, bdec)
+    local_states, cdec, both = block_states(bt, conv, dt_g, cum_g, segc, bdec)
     dsk = jnp.repeat(d_skip, HEAD_DIM)[None, :]
     y_local = None
     for g in range(GROUPS):
         y_local = intra_part(conv, dt_g, cum_g, cumt_g, segc, segr, dsk, g, y_local)
-    back = compose(total, total_decay)
+    back = compose(both)
     gain = norm_gain[None, :]
     return mix(conv, y_local, z_gate, back, local_states, cdec, cum_g, segc, eb, gain)
 

time: 180 us -> 177 us (0.983)
  the two profiles are of different devices: /device:TPU:1 before, /device:TPU:13 now
where the time goes in v9:
time: 177 us; the launch traced here: 176 us
  Pallas kernels  75.4 us (43%)
  waiting for transfers between devices  34.4 us (19%)
  local copies, waits for them, and re-layouts  32.8 us (19%)
  starting transfers between devices  20 us (11%)
  other arithmetic  12.8 us (7%)
    pallas_call x2, Pallas kernels, intra_part(): pl.pallas_call(kernel, grid=(nb,), in_specs=specs, out_specs=pl.BlockSpec...  34.7 us
    ppermute x14, waiting for transfers between devices, exchange(): got.append(lax.ppermute(piece, axis, pairs))  30.2 us
    ppermute x14, starting transfers between devices, exchange(): got.append(lax.ppermute(piece, axis, pairs))  15.7 us
    pallas_call x1, Pallas kernels, mix(): pl.pallas_call(mix_kernel, grid=(nb, GROUPS), in_specs=[pl.BlockSpec((STR...  13.5 us
    pallas_call x1, Pallas kernels, block_states(): pl.pallas_call(state_kernel, grid=(GROUPS, nb), in_specs=[pl.BlockSpec((S...  12.8 us
    pallas_call x1, Pallas kernels, conv_part(): pl.pallas_call(conv_kernel, grid=(chans // CONV_COLS,), in_specs=[pl.Bloc...  11.8 us
    unnamed x26, local copies, waits for them, and re-layouts  10.1 us
    ppermute x2, waiting for transfers between devices, swap_cores(): return lax.ppermute(value, 'core', [(0, 1), (1, 0)])  4.22 us
  transfers between devices with their start and end apart: 17, of which 9 were waited for; matrix products, arithmetic and copies ran while one was open for 12% of the time, Pallas kernels for 20%

profile of v9, /device:TPU:13, one launch (start us, length us, event | category | flops | bytes accessed | tf_op | source)
XLA Modules:
  0.0 175.9 jit_solution(7447029974246767449)
XLA Ops:
  0.0 0.9 slice.57
  0.9 3.7 %collective-permute-start = (bf16[3,5120]{1,0:T(4,128)(2,1)S(1)}, bf16[3,5120]{1,0:T(4,128)(2,1)S(1)}, u32[]{:S(2)}, u32[]{:S(2)}) collective-permute-start(bf16[3,5120]{1,0:T(4,128)(2,1)S(1)} %slice.57), channel_id=1, source_target_pairs={{0,1},{1,2},{2,3},{3,4},{4,5},{5,6},{6,7},{7,8},{8,9},{9,10},{10,1... | collective-permute-start | bytes 92168 | tf_op jit(solution)/shard_map/ppermute | solution.py:23
  4.7 0.8 reduce-window.18
  6.6 1.0 negate_multiply_fusion
  7.7 1.2 reduce-window.19
  10.1 0.7 pad_convert_fusion.m_ref
  10.9 0.7 concatenate.21.w_ref
  11.6 1.0 copy.78
  12.7 1.0 copy.83
  13.8 0.7 broadcast_in_dim_reshape.7.bdec_ref
  15.2 11.8 %shard_map.100.c_ref.b_ref.x_ref.refs_0_.refs_1_.refs_2_ = bf16[512,5120]{1,0:T(8,128)(2,1)} custom-call(bf16[512,5120]{1,0:T(8,128)(2,1)} %x_ref.1, bf16[8,5120]{1,0:T(8,128)(2,1)} %concatenate.20.rim_ref, f32[8,5120]{1,0:T(8,128)} %concatenate.21.w_ref, f32[1,5120]{1,0:T(1,128)} %bitcast.143, f32[512,128]{1,0:T(8,128)} %pad_convert_fusion.m_ref), custom_call_target="tpu_custom_call" | custom-call | tf_op jit(solution)/shard_map/pallas_call | solution.py:72
  27.0 1.1 slice.81
  28.1 1.0 copy.96
  29.1 0.8 broadcast_in_dim.81.segc_ref.refs_6_
  29.9 12.8 %shard_map.103 = (f32[2,256,4096]{2,1,0:T(8,128)}, f32[2,1,4096]{2,1,0:T(1,128)}, f32[2,257,2048]{2,1,0:T(8,128)}) custom-call(bf16[512,512]{1,0:T(8,128)(2,1)} %bitcast.129, bf16[512,5120]{1,0:T(8,128)(2,1)} %shard_map.100.c_ref.b_ref.x_ref.refs_0_.refs_1_.refs_2_, f32[2,512,32]{2,1,0:T(8,128)} %bitcast.123, f32[2,512,32]{2,1,0:T(8,128)} %bitcast.119, ...), custom_call_target="tpu_custom_call" | custom-call | tf_op jit(solution)/shard_map/pallas_call | solution.py:122
  42.7 1.7 dynamic-slice_bitcast_fusion
  44.7 4.2 %collective-permute-done.1 = f32[257,2048]{1,0:T(8,128)} collective-permute-done((f32[257,2048]{1,0:T(8,128)S(1)}, f32[257,2048]{1,0:T(8,128)}, u32[]{:S(2)}, u32[]{:S(2)}) %collective-permute-start.1) | collective-permute-done | bytes 2105376 | tf_op jit(solution)/shard_map/ppermute | solution.py:265
  48.9 2.6 %bitcast_select_fusion.1 = (f32[257,2048]{1,0:T(8,128)S(1)}, f32[257,2048]{1,0:T(8,128)S(1)}) fusion(f32[257,2048]{1,0:T(8,128)} %collective-permute-done.1, f32[2,257,2048]{2,1,0:T(8,128)} %get-tuple-element.8, s32[]{:T(128)S(6)} %select_n.181, pred[]{:T(512)S(6)} %eq.42), kind=kLoop, calls=%fused_computation.3 | loop fusion | flops 1052672 | bytes 8421381 | tf_op jit(solution)/shard_map/jit(_where)/select_n | solution.py:288
  52.4 2.2 %constant_dynamic-slice_fusion = (bf16[258,1,256]{2,1,0:T(2,128)(2,1)S(1)}, bf16[258,1,256]{2,1,0:T(2,128)(2,1)S(1)}, bf16[258,1,256]{2,1,0:T(2,128)(2,1)S(1)}, ...) fusion(bf16[258,8,256]{2,1,0:T(8,128)(2,1)S(1)} %slice.88, ...), kind=kLoop, calls=%fused_computation.60 | loop fusion | bytes 2113568 | tf_op jit(solution)/shard_map/dynamic-slice.7
  54.6 1.3 collective-permute-start.2
  56.0 1.4 collective-permute-start.3
  57.3 0.9 collective-permute-start.4
  58.3 1.5 collective-permute-start.5
  59.8 1.1 collective-permute-start.6
  60.9 0.7 fusion.1
  61.6 1.1 collective-permute-start.7
  64.4 11.8 %collective-permute-done.4 = bf16[258,256]{1,0:T(8,128)(2,1)S(1)} collective-permute-done((bf16[258,256]{1,0:T(8,128)(2,1)S(1)}, bf16[258,256]{1,0:T(8,128)(2,1)S(1)}, u32[]{:S(2)}, u32[]{:S(2)}) %collective-permute-start.4) | collective-permute-done | bytes 132128 | tf_op jit(solution)/shard_map/ppermute | solution.py:275
  76.8 2.2 %collective-permute-done.5 = bf16[258,256]{1,0:T(8,128)(2,1)S(1)} collective-permute-done((bf16[258,256]{1,0:T(8,128)(2,1)S(1)}, bf16[258,256]{1,0:T(8,128)(2,1)S(1)}, u32[]{:S(2)}, u32[]{:S(2)}) %collective-permute-start.5) | collective-permute-done | bytes 132128 | tf_op jit(solution)/shard_map/ppermute | solution.py:275
  80.4 0.9 collective-permute-done.7
  83.2 1.9 %gather_fusion = bf16[8,258,256]{2,1,0:T(8,128)(2,1)S(1)} fusion(bf16[8,258,256]{2,1,0:T(8,128)(2,1)} %bitcast_dynamic-update-slice_fusion, s32[1024]{0:T(1024)S(1)} %pad_clamp_fusion), kind=kCustom, calls=%fused_computation | custom fusion | bytes 2113568 | tf_op jit(solution)/shard_map/jit(_take)/gather | solution.py:277
  85.1 1.1 broadcast_select_fusion.got_ref
  86.2 2.6 %shard_map.104 = bf16[8,256,256]{2,1,0:T(8,128)(2,1)} custom-call(bf16[8,258,256]{2,1,0:T(8,128)(2,1)} %broadcast_select_fusion.got_ref), custom_call_target="tpu_custom_call" | custom-call | tf_op jit(solution)/shard_map/pallas_call | solution.py:298
  88.8 2.0 %dynamic-slice_bitcast_fusion.1 = (bf16[256,256]{1,0:T(8,128)(2,1)S(1)}, bf16[256,256]{1,0:T(8,128)(2,1)S(1)}, bf16[256,256]{1,0:T(8,128)(2,1)S(1)}, bf16[256,25...) fusion(bf16[8,256,256]{2,1,0:T(8,128)(2,1)} %shard_map.104, ...), kind=kLoop, calls=%fused_computation.44 | loop fusion | bytes 2097184 | tf_op jit(solution)/shard_map/jit(dynamic_index_in_dim)/squeeze | solution.py:273
  91.4 2.6 %collective-permute-start.11 = (bf16[256,256]{1,0:T(8,128)(2,1)S(1)}, bf16[256,256]{1,0:T(8,128)(2,1)S(1)}, u32[]{:S(2)}, u32[]{:S(2)}) collective-permute-start(bf16[256,256]{1,0:T(8,128)(2,1)S(1)} %get-tuple-element.31), channel_id=1, source_target_pairs={{0,6},{2,8},{4,10},{6,12},{8,14},{10,0},{12,2},{14,4},{1,7},{3,9},... | collective-permute-start | bytes 393224 | tf_op jit(solution)/shard_map/ppermute | solution.py:275
  94.4 1.2 collective-permute-start.13
  95.6 1.9 %collective-permute-start.14 = (bf16[256,256]{1,0:T(8,128)(2,1)S(1)}, bf16[256,256]{1,0:T(8,128)(2,1)S(1)}, u32[]{:S(2)}, u32[]{:S(2)}) collective-permute-start(bf16[256,256]{1,0:T(8,128)(2,1)S(1)} %get-tuple-element.28), channel_id=1, source_target_pairs={{0,12},{2,14},{4,0},{6,2},{8,4},{10,6},{12,8},{14,10},{1,13},{3,15... | collective-permute-start | bytes 393224 | tf_op jit(solution)/shard_map/ppermute | solution.py:275
  98.2 1.5 collective-permute-start.15
  100.3 10.0 %collective-permute-done.11 = bf16[256,256]{1,0:T(8,128)(2,1)S(1)} collective-permute-done((bf16[256,256]{1,0:T(8,128)(2,1)S(1)}, bf16[256,256]{1,0:T(8,128)(2,1)S(1)}, u32[]{:S(2)}, u32[]{:S(2)}) %collective-permute-start.11) | collective-permute-done | bytes 131104 | tf_op jit(solution)/shard_map/ppermute | solution.py:275
  111.0 2.1 %collective-permute-done.12 = bf16[256,256]{1,0:T(8,128)(2,1)S(1)} collective-permute-done((bf16[256,256]{1,0:T(8,128)(2,1)S(1)}, bf16[256,256]{1,0:T(8,128)(2,1)S(1)}, u32[]{:S(2)}, u32[]{:S(2)}) %collective-permute-start.12) | collective-permute-done | bytes 131104 | tf_op jit(solution)/shard_map/ppermute | solution.py:275
  114.5 1.9 %collective-permute-done.14 = bf16[256,256]{1,0:T(8,128)(2,1)S(1)} collective-permute-done((bf16[256,256]{1,0:T(8,128)(2,1)S(1)}, bf16[256,256]{1,0:T(8,128)(2,1)S(1)}, u32[]{:S(2)}, u32[]{:S(2)}) %collective-permute-start.14) | collective-permute-done | bytes 131104 | tf_op jit(solution)/shard_map/ppermute | solution.py:275
  118.3 1.8 %gather_fusion.1 = bf16[8,256,256]{2,1,0:T(8,128)(2,1)S(1)} fusion(bf16[8,256,256]{2,1,0:T(8,128)(2,1)} %bitcast_dynamic-update-slice_fusion.7, s32[1024]{0:T(1024)S(1)} %pad_clamp_fusion), kind=kCustom, calls=%fused_computation.1 | custom fusion | bytes 2097184 | tf_op jit(solution)/shard_map/jit(_take)/gather | solution.py:277
  120.6 1.5 select_convert_fusion.1
  122.7 0.7 copy.108
  123.4 0.7 broadcast_in_dim_reshape.6.dsk_ref.refs_8_
  124.9 17.3 %shard_map.101.refs_9_ = f32[512,4096]{1,0:T(8,128)} custom-call(bf16[512,5120]{1,0:T(8,128)(2,1)} %shard_map.100.c_ref.b_ref.x_ref.refs_0_.refs_1_.refs_2_, bf16[512,5120]{1,0:T(8,128)(2,1)} %shard_map.100.c_ref.b_ref.x_ref.refs_0_.refs_1_.refs_2_, bf16[512,5120]{1,0:T(8,128)(2,1)} %shard_map.100.c_ref.b_ref.x_ref.refs_0_.refs_1_.refs_2_, ...), custom_call_target="tpu_custom_call" | custom-call | tf_op jit(solution)/shard_map/pallas_call | solution.py:201
  142.2 17.4 %shard_map.102.y_ref = f32[512,4096]{1,0:T(8,128)} custom-call(bf16[512,5120]{1,0:T(8,128)(2,1)} %shard_map.100.c_ref.b_ref.x_ref.refs_0_.refs_1_.refs_2_, bf16[512,5120]{1,0:T(8,128)(2,1)} %shard_map.100.c_ref.b_ref.x_ref.refs_0_.refs_1_.refs_2_, ...), custom_call_target="tpu_custom_call", output_to_operand_aliasing={{}: (9, {})} | custom-call | tf_op jit(solution)/shard_map/pallas_call | solution.py:201
  159.6 2.2 %maximum_select_fusion.hin_ref = bf16[256,4096]{1,0:T(8,128)(2,1)} fusion(bf16[256,2048]{1,0:T(8,128)(2,1)S(1)} %collective-permute-done.16, bf16[256,2048]{1,0:T(8,128)(2,1)S(1)} %get-tuple-element.15, pred[]{:T(512)S(6)} %eq.42), kind=kLoop, calls=%fused_computation.7 | loop fusion | flops 9437184 | bytes 4194305 | tf_op jit(solution)/shard_map/jit(_where)/select_n | solution.py:307
  162.4 13.5 %shard_map.105 = bf16[512,4096]{1,0:T(8,128)(2,1)} custom-call(bf16[512,5120]{1,0:T(8,128)(2,1)} %shard_map.100.c_ref.b_ref.x_ref.refs_0_.refs_1_.refs_2_, f32[512,4096]{1,0:T(8,128)} %shard_map.102.y_ref, bf16[512,4096]{1,0:T(8,128)(2,1)} %z_ref.1, bf16[256,4096]{1,0:T(8,128)(2,1)} %maximum_select_fusion.hin_ref, ...), custom_call_target="tpu_custom_call" | custom-call | tf_op jit(solution)/shard_map/pallas_call | solution.py:231
  (84 shorter events, 18.5 us)
Async XLA Ops:
  0.0 10.9 %copy-start = (f32[4,5120]{1,0:T(4,128)S(1)}, f32[4,5120]{1,0:T(4,128)}, u32[]{:S(2)}) copy-start(f32[4,5120]{1,0:T(4,128)} %param.14) | copy-start | bytes 245764
  0.9 13.6 %collective-permute-start = (bf16[3,5120]{1,0:T(4,128)(2,1)S(1)}, bf16[3,5120]{1,0:T(4,128)(2,1)S(1)}, u32[]{:S(2)}, u32[]{:S(2)}) collective-permute-start(bf16[3,5120]{1,0:T(4,128)(2,1)S(1)} %slice.57), channel_id=1, source_target_pairs={{0,1},{1,2},{2,3},{3,4},{4,5},{5,6},{6,7},{7,8},{8,9},{9,10},{10,1... | collective-permute-start | bytes 92168 | tf_op jit(solution)/shard_map/ppermute | solution.py:23
  44.5 4.5 %collective-permute-start.1 = (f32[257,2048]{1,0:T(8,128)S(1)}, f32[257,2048]{1,0:T(8,128)}, u32[]{:S(2)}, u32[]{:S(2)}) collective-permute-start(f32[257,2048]{1,0:T(8,128)S(1)} %dynamic-slice_bitcast_fusion), channel_id=1, source_target_pairs={{0,1},{1,0},{2,3},{3,2},{4,5},{5,4},{6,7},{7,6},{8,9},{9,8},{10,11... | collective-permute-start | bytes 6316040 | tf_op jit(solution)/shard_map/ppermute | solution.py:265
  54.6 6.9 %collective-permute-start.2 = (bf16[258,256]{1,0:T(8,128)(2,1)S(1)}, bf16[258,256]{1,0:T(8,128)(2,1)S(1)}, u32[]{:S(2)}, u32[]{:S(2)}) collective-permute-start(bf16[258,256]{1,0:T(8,128)(2,1)S(1)} %bitcast.140), channel_id=1, source_target_pairs={{0,2},{2,4},{4,6},{6,8},{8,10},{10,12},{12,14},{14,0},{1,3},{3,5},... | collective-permute-start | bytes 396296 | tf_op jit(solution)/shard_map/ppermute | solution.py:275
  56.0 7.4 %collective-permute-start.3 = (bf16[258,256]{1,0:T(8,128)(2,1)S(1)}, bf16[258,256]{1,0:T(8,128)(2,1)S(1)}, u32[]{:S(2)}, u32[]{:S(2)}) collective-permute-start(bf16[258,256]{1,0:T(8,128)(2,1)S(1)} %bitcast.139), channel_id=1, source_target_pairs={{0,4},{2,6},{4,8},{6,10},{8,12},{10,14},{12,0},{14,2},{1,5},{3,7},... | collective-permute-start | bytes 396296 | tf_op jit(solution)/shard_map/ppermute | solution.py:275
  57.3 18.8 %collective-permute-start.4 = (bf16[258,256]{1,0:T(8,128)(2,1)S(1)}, bf16[258,256]{1,0:T(8,128)(2,1)S(1)}, u32[]{:S(2)}, u32[]{:S(2)}) collective-permute-start(bf16[258,256]{1,0:T(8,128)(2,1)S(1)} %bitcast.138), channel_id=1, source_target_pairs={{0,6},{2,8},{4,10},{6,12},{8,14},{10,0},{12,2},{14,4},{1,7},{3,9},... | collective-permute-start | bytes 396296 | tf_op jit(solution)/shard_map/ppermute | solution.py:275
  58.3 20.8 %collective-permute-start.5 = (bf16[258,256]{1,0:T(8,128)(2,1)S(1)}, bf16[258,256]{1,0:T(8,128)(2,1)S(1)}, u32[]{:S(2)}, u32[]{:S(2)}) collective-permute-start(bf16[258,256]{1,0:T(8,128)(2,1)S(1)} %bitcast.137), channel_id=1, source_target_pairs={{0,8},{2,10},{4,12},{6,14},{8,0},{10,2},{12,4},{14,6},{1,9},{3,11}... | collective-permute-start | bytes 396296 | tf_op jit(solution)/shard_map/ppermute | solution.py:275
  59.8 19.9 %collective-permute-start.6 = (bf16[258,256]{1,0:T(8,128)(2,1)S(1)}, bf16[258,256]{1,0:T(8,128)(2,1)S(1)}, u32[]{:S(2)}, u32[]{:S(2)}) collective-permute-start(bf16[258,256]{1,0:T(8,128)(2,1)S(1)} %bitcast.136), channel_id=1, source_target_pairs={{0,10},{2,12},{4,14},{6,0},{8,2},{10,4},{12,6},{14,8},{1,11},{3,13... | collective-permute-start | bytes 396296 | tf_op jit(solution)/shard_map/ppermute | solution.py:275
  61.6 19.7 %collective-permute-start.7 = (bf16[258,256]{1,0:T(8,128)(2,1)S(1)}, bf16[258,256]{1,0:T(8,128)(2,1)S(1)}, u32[]{:S(2)}, u32[]{:S(2)}) collective-permute-start(bf16[258,256]{1,0:T(8,128)(2,1)S(1)} %bitcast.135), channel_id=1, source_target_pairs={{0,12},{2,14},{4,0},{6,2},{8,4},{10,6},{12,8},{14,10},{1,13},{3,15... | collective-permute-start | bytes 396296 | tf_op jit(solution)/shard_map/ppermute | solution.py:275
  63.4 19.1 %collective-permute-start.8 = (bf16[258,256]{1,0:T(8,128)(2,1)S(1)}, bf16[258,256]{1,0:T(8,128)(2,1)S(1)}, u32[]{:S(2)}, u32[]{:S(2)}) collective-permute-start(bf16[258,256]{1,0:T(8,128)(2,1)S(1)} %bitcast.134), channel_id=1, source_target_pairs={{0,14},{2,0},{4,2},{6,4},{8,6},{10,8},{12,10},{14,12},{1,15},{3,1}... | collective-permute-start | bytes 396296 | tf_op jit(solution)/shard_map/ppermute | solution.py:275
  90.8 4.8 %collective-permute-start.9 = (bf16[256,256]{1,0:T(8,128)(2,1)S(1)}, bf16[256,256]{1,0:T(8,128)(2,1)S(1)}, u32[]{:S(2)}, u32[]{:S(2)}) collective-permute-start(bf16[256,256]{1,0:T(8,128)(2,1)S(1)} %get-tuple-element.33), channel_id=1, source_target_pairs={{0,2},{2,4},{4,6},{6,8},{8,10},{10,12},{12,14},{14,0},{1,3},{3,5},... | collective-permute-start | bytes 393224 | tf_op jit(solution)/shard_map/ppermute | solution.py:275
  90.8 7.4 %collective-permute-start.10 = (bf16[256,256]{1,0:T(8,128)(2,1)S(1)}, bf16[256,256]{1,0:T(8,128)(2,1)S(1)}, u32[]{:S(2)}, u32[]{:S(2)}) collective-permute-start(bf16[256,256]{1,0:T(8,128)(2,1)S(1)} %get-tuple-element.32), channel_id=1, source_target_pairs={{0,4},{2,6},{4,8},{6,10},{8,12},{10,14},{12,0},{14,2},{1,5},{3,7},... | collective-permute-start | bytes 393224 | tf_op jit(solution)/shard_map/ppermute | solution.py:275
  91.4 18.9 %collective-permute-start.11 = (bf16[256,256]{1,0:T(8,128)(2,1)S(1)}, bf16[256,256]{1,0:T(8,128)(2,1)S(1)}, u32[]{:S(2)}, u32[]{:S(2)}) collective-permute-start(bf16[256,256]{1,0:T(8,128)(2,1)S(1)} %get-tuple-element.31), channel_id=1, source_target_pairs={{0,6},{2,8},{4,10},{6,12},{8,14},{10,0},{12,2},{14,4},{1,7},{3,9},... | collective-permute-start | bytes 393224 | tf_op jit(solution)/shard_map/ppermute | solution.py:275
  94.0 19.2 %collective-permute-start.12 = (bf16[256,256]{1,0:T(8,128)(2,1)S(1)}, bf16[256,256]{1,0:T(8,128)(2,1)S(1)}, u32[]{:S(2)}, u32[]{:S(2)}) collective-permute-start(bf16[256,256]{1,0:T(8,128)(2,1)S(1)} %get-tuple-element.30), channel_id=1, source_target_pairs={{0,8},{2,10},{4,12},{6,14},{8,0},{10,2},{12,4},{14,6},{1,9},{3,11}... | collective-permute-start | bytes 393224 | tf_op jit(solution)/shard_map/ppermute | solution.py:275
  94.4 19.5 %collective-permute-start.13 = (bf16[256,256]{1,0:T(8,128)(2,1)S(1)}, bf16[256,256]{1,0:T(8,128)(2,1)S(1)}, u32[]{:S(2)}, u32[]{:S(2)}) collective-permute-start(bf16[256,256]{1,0:T(8,128)(2,1)S(1)} %get-tuple-element.29), channel_id=1, source_target_pairs={{0,10},{2,12},{4,14},{6,0},{8,2},{10,4},{12,6},{14,8},{1,11},{3,13... | collective-permute-start | bytes 393224 | tf_op jit(solution)/shard_map/ppermute | solution.py:275
  95.6 20.8 %collective-permute-start.14 = (bf16[256,256]{1,0:T(8,128)(2,1)S(1)}, bf16[256,256]{1,0:T(8,128)(2,1)S(1)}, u32[]{:S(2)}, u32[]{:S(2)}) collective-permute-start(bf16[256,256]{1,0:T(8,128)(2,1)S(1)} %get-tuple-element.28), channel_id=1, source_target_pairs={{0,12},{2,14},{4,0},{6,2},{8,4},{10,6},{12,8},{14,10},{1,13},{3,15... | collective-permute-start | bytes 393224 | tf_op jit(solution)/shard_map/ppermute | solution.py:275
  98.2 19.4 %collective-permute-start.15 = (bf16[256,256]{1,0:T(8,128)(2,1)S(1)}, bf16[256,256]{1,0:T(8,128)(2,1)S(1)}, u32[]{:S(2)}, u32[]{:S(2)}) collective-permute-start(bf16[256,256]{1,0:T(8,128)(2,1)S(1)} %get-tuple-element.27), channel_id=1, source_target_pairs={{0,14},{2,0},{4,2},{6,4},{8,6},{10,8},{12,10},{14,12},{1,15},{3,1}... | collective-permute-start | bytes 393224 | tf_op jit(solution)/shard_map/ppermute | solution.py:275
  120.6 2.7 %copy-start.1 = (f32[64]{0:T(128)S(1)}, f32[64]{0:T(128)}, u32[]{:S(2)}) copy-start(f32[64]{0:T(128)} %param.18) | copy-start | bytes 772
  122.2 37.4 %collective-permute-start.16 = (bf16[256,2048]{1,0:T(8,128)(2,1)}, bf16[256,2048]{1,0:T(8,128)(2,1)S(1)}, u32[]{:S(2)}, u32[]{:S(2)}) collective-permute-start(bf16[256,2048]{1,0:T(8,128)(2,1)} %get-tuple-element.16), channel_id=1, source_target_pairs={{0,1},{1,0},{2,3},{3,2},{4,5},{5,4},{6,7},{7,6},{8,9},{9,8},{10,11... | collective-permute-start | bytes 3145736 | tf_op jit(solution)/shard_map/ppermute | solution.py:265

commit v10 on v9

--- a/solution.py
+++ b/solution.py
@@ -277,7 +277,20 @@
     return jnp.take(stacked, (me - jnp.arange(count)) % count, axis=0)
 
 
-def compose(both):
+def tie(value, *after):
+    def kernel(*refs):
+        del refs
+
+    return pl.pallas_call(
+        kernel,
+        in_specs=[pl.BlockSpec(memory_space=pl.ANY) for _ in range(1 + len(after))],
+        out_specs=pl.BlockSpec(memory_space=pl.ANY),
+        out_shape=jax.ShapeDtypeStruct(value.shape, value.dtype),
+        input_output_aliases={0: 0},
+    )(value, *after)
+
+
+def compose(both, first_work, second_work):
     core = lax.axis_index("core")
     chips = lax.axis_size("chip")
     half = GROUP_COLS
@@ -294,21 +307,24 @@
     payload = jnp.concatenate(
         [chip_state.astype(jnp.bfloat16), decay_hi, decay_lo], axis=0
     ).reshape(STATE + 2, chips, width).transpose(1, 0, 2)
-    got = exchange(payload, "chip")
+    work = first_work()
+    got = tie(exchange(payload, "chip"), work)
     entering = pl.pallas_call(
         scan_kernel,
         out_shape=jax.ShapeDtypeStruct((chips, STATE, width), jnp.bfloat16),
     )(got)
-    back = exchange(entering, "chip")
+    work = second_work(work)
+    back = tie(exchange(entering, "chip"), work)
     chip_in = back.transpose(1, 0, 2).reshape(STATE, half).astype(jnp.float32)
     later_in = first_decay * chip_in + first[:STATE]
     keep = jnp.where(core == 0, chip_in, later_in).astype(jnp.bfloat16)
     other = swap_cores(jnp.where(core == 0, later_in, chip_in).astype(jnp.bfloat16))
-    return jnp.where(
+    hin = jnp.where(
         core == 0,
         jnp.concatenate([keep, other], axis=1),
         jnp.concatenate([other, keep], axis=1),
     )
+    return hin, work
 
 
 def local(xbc, z_gate, dt_raw, lengths, conv_weight, conv_bias, dt_bias, a_log, d_skip, norm_gain):
@@ -348,10 +364,13 @@
 
     local_states, cdec, both = block_states(bt, conv, dt_g, cum_g, segc, bdec)
     dsk = jnp.repeat(d_skip, HEAD_DIM)[None, :]
-    y_local = None
-    for g in range(GROUPS):
-        y_local = intra_part(conv, dt_g, cum_g, cumt_g, segc, segr, dsk, g, y_local)
-    back = compose(both)
+    def first_work():
+        return intra_part(conv, dt_g, cum_g, cumt_g, segc, segr, dsk, 0)
+
+    def second_work(done):
+        return intra_part(conv, dt_g, cum_g, cumt_g, segc, segr, dsk, 1, done)
+
+    back, y_local = compose(both, first_work, second_work)
     gain = norm_gain[None, :]
     return mix(conv, y_local, z_gate, back, local_states, cdec, cum_g, segc, eb, gain)
 

time: 177 us -> 177 us (level)
  the two profiles are of different devices: /device:TPU:13 before, /device:TPU:15 now
where the time goes in v10:
time: 177 us; the launch traced here: 176 us
  Pallas kernels  75.4 us (43%)
  local copies, waits for them, and re-layouts  32.8 us (19%)
  waiting for transfers between devices  32.4 us (18%)
  starting transfers between devices  19.8 us (11%)
  other arithmetic  15.2 us (9%)
    pallas_call x2, Pallas kernels, intra_part(): pl.pallas_call(kernel, grid=(nb,), in_specs=specs, out_specs=pl.BlockSpec...  34.7 us
    ppermute x14, waiting for transfers between devices, exchange(): got.append(lax.ppermute(piece, axis, pairs))  30.1 us
    ppermute x14, starting transfers between devices, exchange(): got.append(lax.ppermute(piece, axis, pairs))  15.4 us
    pallas_call x1, Pallas kernels, mix(): pl.pallas_call(mix_kernel, grid=(nb, GROUPS), in_specs=[pl.BlockSpec((STR...  13.5 us
    pallas_call x1, Pallas kernels, block_states(): pl.pallas_call(state_kernel, grid=(GROUPS, nb), in_specs=[pl.BlockSpec((S...  12.8 us
    pallas_call x1, Pallas kernels, conv_part(): pl.pallas_call(conv_kernel, grid=(chans // CONV_COLS,), in_specs=[pl.Bloc...  11.8 us
    unnamed x26, local copies, waits for them, and re-layouts  10.1 us
    ppermute x1, starting transfers between devices, shifted(): return lax.ppermute(value, axis, pairs)  3.71 us
  transfers between devices with their start and end apart: 17, of which 9 were waited for; matrix products, arithmetic and copies ran while one was open for 12% of the time, Pallas kernels for 20%

profile of v10, /device:TPU:15, one launch (start us, length us, event | category | flops | bytes accessed | tf_op | source)
XLA Modules:
  0.0 176.0 jit_solution(3907525493050964268)
XLA Ops:
  0.0 0.9 slice.57
  0.9 3.7 %collective-permute-start = (bf16[3,5120]{1,0:T(4,128)(2,1)S(1)}, bf16[3,5120]{1,0:T(4,128)(2,1)S(1)}, u32[]{:S(2)}, u32[]{:S(2)}) collective-permute-start(bf16[3,5120]{1,0:T(4,128)(2,1)S(1)} %slice.57), channel_id=1, source_target_pairs={{0,1},{1,2},{2,3},{3,4},{4,5},{5,6},{6,7},{7,8},{8,9},{9,10},{10,1... | collective-permute-start | bytes 92168 | tf_op jit(solution)/shard_map/ppermute | solution.py:23
  4.7 0.8 reduce-window.18
  7.0 1.0 negate_multiply_fusion
  8.1 1.2 reduce-window.19
  10.1 0.7 pad_convert_fusion.m_ref
  11.7 0.7 broadcast_in_dim_reshape.7.bdec_ref
  12.5 1.0 copy.85
  13.5 1.0 copy.80
  15.2 11.8 %shard_map.100.c_ref.b_ref.x_ref.refs_0_.refs_1_.refs_2_ = bf16[512,5120]{1,0:T(8,128)(2,1)} custom-call(bf16[512,5120]{1,0:T(8,128)(2,1)} %x_ref.1, bf16[8,5120]{1,0:T(8,128)(2,1)} %concatenate.20.rim_ref, f32[8,5120]{1,0:T(8,128)} %concatenate.21.w_ref, f32[1,5120]{1,0:T(1,128)} %bitcast.143, f32[512,128]{1,0:T(8,128)} %pad_convert_fusion.m_ref), custom_call_target="tpu_custom_call" | custom-call | tf_op jit(solution)/shard_map/pallas_call | solution.py:72
  27.0 1.1 slice.81
  28.1 1.0 copy.98
  29.1 0.8 broadcast_in_dim.81.segc_ref.refs_6_
  29.9 12.8 %shard_map.103 = (f32[2,256,4096]{2,1,0:T(8,128)}, f32[2,1,4096]{2,1,0:T(1,128)}, f32[2,257,2048]{2,1,0:T(8,128)}) custom-call(bf16[512,512]{1,0:T(8,128)(2,1)} %bitcast.129, bf16[512,5120]{1,0:T(8,128)(2,1)} %shard_map.100.c_ref.b_ref.x_ref.refs_0_.refs_1_.refs_2_, f32[2,512,32]{2,1,0:T(8,128)} %bitcast.123, f32[2,512,32]{2,1,0:T(8,128)} %bitcast.119, ...), custom_call_target="tpu_custom_call" | custom-call | tf_op jit(solution)/shard_map/pallas_call | solution.py:122
  42.7 1.8 %dynamic-slice_bitcast_fusion = f32[257,2048]{1,0:T(8,128)S(1)} fusion(f32[2,257,2048]{2,1,0:T(8,128)} %get-tuple-element.8, s32[]{:T(128)S(6)} %select_n.178), kind=kLoop, calls=%fused_computation.4 | loop fusion | bytes 4210692 | tf_op jit(solution)/shard_map/jit(dynamic_index_in_dim)/squeeze | solution.py:299
  46.8 17.3 %shard_map.101.refs_9_.refs_1_ = f32[512,4096]{1,0:T(8,128)} custom-call(bf16[512,5120]{1,0:T(8,128)(2,1)} %shard_map.100.c_ref.b_ref.x_ref.refs_0_.refs_1_.refs_2_, bf16[512,5120]{1,0:T(8,128)(2,1)} %shard_map.100.c_ref.b_ref.x_ref.refs_0_.refs_1_.refs_2_, bf16[512,5120]{1,0:T(8,128)(2,1)} %shard_map.100.c_ref.b_ref.x_ref.refs_0_.refs_1_.refs_2_, ...), custom_call_target="tpu_custom_call" | custom-call | tf_op jit(solution)/shard_map/pallas_call | solution.py:201
  64.1 2.6 %bitcast_select_fusion.1 = (f32[257,2048]{1,0:T(8,128)S(1)}, f32[257,2048]{1,0:T(8,128)S(1)}) fusion(f32[257,2048]{1,0:T(8,128)} %collective-permute-done.1, f32[2,257,2048]{2,1,0:T(8,128)} %get-tuple-element.8, s32[]{:T(128)S(6)} %select_n.179, pred[]{:T(512)S(6)} %eq.42), kind=kLoop, calls=%fused_computation.3 | loop fusion | flops 1052672 | bytes 8421381 | tf_op jit(solution)/shard_map/jit(_where)/select_n | solution.py:301
  67.6 2.2 %constant_dynamic-slice_fusion = (bf16[258,1,256]{2,1,0:T(2,128)(2,1)S(1)}, bf16[258,1,256]{2,1,0:T(2,128)(2,1)S(1)}, bf16[258,1,256]{2,1,0:T(2,128)(2,1)S(1)}, ...) fusion(bf16[258,8,256]{2,1,0:T(8,128)(2,1)S(1)} %slice.88, ...), kind=kLoop, calls=%fused_computation.61 | loop fusion | bytes 2113568 | tf_op jit(solution)/shard_map/dynamic-slice.7
  69.9 1.3 collective-permute-start.2
  71.2 1.4 collective-permute-start.3
  72.5 1.0 collective-permute-start.4
  73.5 1.5 collective-permute-start.5
  75.0 1.1 collective-permute-start.6
  76.8 1.1 collective-permute-start.7
  79.6 11.5 %collective-permute-done.4 = bf16[258,256]{1,0:T(8,128)(2,1)S(1)} collective-permute-done((bf16[258,256]{1,0:T(8,128)(2,1)S(1)}, bf16[258,256]{1,0:T(8,128)(2,1)S(1)}, u32[]{:S(2)}, u32[]{:S(2)}) %collective-permute-start.4) | collective-permute-done | bytes 132128 | tf_op jit(solution)/shard_map/ppermute | solution.py:275
  91.8 2.2 %collective-permute-done.5 = bf16[258,256]{1,0:T(8,128)(2,1)S(1)} collective-permute-done((bf16[258,256]{1,0:T(8,128)(2,1)S(1)}, bf16[258,256]{1,0:T(8,128)(2,1)S(1)}, u32[]{:S(2)}, u32[]{:S(2)}) %collective-permute-start.5) | collective-permute-done | bytes 132128 | tf_op jit(solution)/shard_map/ppermute | solution.py:275
  95.3 1.1 collective-permute-done.7
  98.5 1.9 %gather_fusion = bf16[8,258,256]{2,1,0:T(8,128)(2,1)S(1)} fusion(bf16[8,258,256]{2,1,0:T(8,128)(2,1)} %bitcast_dynamic-update-slice_fusion, s32[1024]{0:T(1024)S(1)} %pad_clamp_fusion), kind=kCustom, calls=%fused_computation | custom fusion | bytes 2113568 | tf_op jit(solution)/shard_map/jit(_take)/gather | solution.py:277
  100.3 1.1 broadcast_select_fusion.refs_0_
  101.5 2.6 %shard_map.105 = bf16[8,256,256]{2,1,0:T(8,128)(2,1)} custom-call(bf16[8,258,256]{2,1,0:T(8,128)(2,1)} %shard_map.104.got_ref), custom_call_target="tpu_custom_call" | custom-call | tf_op jit(solution)/shard_map/pallas_call | solution.py:312
  104.0 2.0 %dynamic-slice_bitcast_fusion.1 = (bf16[256,256]{1,0:T(8,128)(2,1)S(1)}, bf16[256,256]{1,0:T(8,128)(2,1)S(1)}, bf16[256,256]{1,0:T(8,128)(2,1)S(1)}, bf16[256,25...) fusion(bf16[8,256,256]{2,1,0:T(8,128)(2,1)} %shard_map.105, ...), kind=kLoop, calls=%fused_computation.45 | loop fusion | bytes 2097184 | tf_op jit(solution)/shard_map/jit(dynamic_index_in_dim)/squeeze | solution.py:273
  106.0 17.4 %shard_map.102.refs_1_.y_ref = f32[512,4096]{1,0:T(8,128)} custom-call(bf16[512,5120]{1,0:T(8,128)(2,1)} %shard_map.100.c_ref.b_ref.x_ref.refs_0_.refs_1_.refs_2_, bf16[512,5120]{1,0:T(8,128)(2,1)} %shard_map.100.c_ref.b_ref.x_ref.refs_0_.refs_1_.refs_2_, ...), custom_call_target="tpu_custom_call", output_to_operand_aliasing={{}: (9, {})} | custom-call | tf_op jit(solution)/shard_map/pallas_call | solution.py:201
  123.6 2.6 %collective-permute-start.11 = (bf16[256,256]{1,0:T(8,128)(2,1)S(1)}, bf16[256,256]{1,0:T(8,128)(2,1)S(1)}, u32[]{:S(2)}, u32[]{:S(2)}) collective-permute-start(bf16[256,256]{1,0:T(8,128)(2,1)S(1)} %get-tuple-element.31), channel_id=1, source_target_pairs={{0,6},{2,8},{4,10},{6,12},{8,14},{10,0},{12,2},{14,4},{1,7},{3,9},... | collective-permute-start | bytes 393224 | tf_op jit(solution)/shard_map/ppermute | solution.py:275
  126.3 0.7 collective-permute-start.12
  127.0 0.9 collective-permute-start.13
  127.8 1.9 %collective-permute-start.14 = (bf16[256,256]{1,0:T(8,128)(2,1)S(1)}, bf16[256,256]{1,0:T(8,128)(2,1)S(1)}, u32[]{:S(2)}, u32[]{:S(2)}) collective-permute-start(bf16[256,256]{1,0:T(8,128)(2,1)S(1)} %get-tuple-element.28), channel_id=1, source_target_pairs={{0,12},{2,14},{4,0},{6,2},{8,4},{10,6},{12,8},{14,10},{1,13},{3,15... | collective-permute-start | bytes 393224 | tf_op jit(solution)/shard_map/ppermute | solution.py:275
  130.4 1.5 collective-permute-start.15
  132.6 8.0 %collective-permute-done.11 = bf16[256,256]{1,0:T(8,128)(2,1)S(1)} collective-permute-done((bf16[256,256]{1,0:T(8,128)(2,1)S(1)}, bf16[256,256]{1,0:T(8,128)(2,1)S(1)}, u32[]{:S(2)}, u32[]{:S(2)}) %collective-permute-start.11) | collective-permute-done | bytes 131104 | tf_op jit(solution)/shard_map/ppermute | solution.py:275
  141.2 2.1 %collective-permute-done.12 = bf16[256,256]{1,0:T(8,128)(2,1)S(1)} collective-permute-done((bf16[256,256]{1,0:T(8,128)(2,1)S(1)}, bf16[256,256]{1,0:T(8,128)(2,1)S(1)}, u32[]{:S(2)}, u32[]{:S(2)}) %collective-permute-start.12) | collective-permute-done | bytes 131104 | tf_op jit(solution)/shard_map/ppermute | solution.py:275
  144.7 1.7 collective-permute-done.14
  147.1 2.7 %collective-permute-done.15 = bf16[256,256]{1,0:T(8,128)(2,1)S(1)} collective-permute-done((bf16[256,256]{1,0:T(8,128)(2,1)S(1)}, bf16[256,256]{1,0:T(8,128)(2,1)S(1)}, u32[]{:S(2)}, u32[]{:S(2)}) %collective-permute-start.15) | collective-permute-done | bytes 131104 | tf_op jit(solution)/shard_map/ppermute | solution.py:275
  150.4 1.8 %gather_fusion.1 = bf16[8,256,256]{2,1,0:T(8,128)(2,1)S(1)} fusion(bf16[8,256,256]{2,1,0:T(8,128)(2,1)} %bitcast_dynamic-update-slice_fusion.7, s32[1024]{0:T(1024)S(1)} %pad_clamp_fusion), kind=kCustom, calls=%fused_computation.1 | custom fusion | bytes 2097184 | tf_op jit(solution)/shard_map/jit(_take)/gather | solution.py:277
  152.3 1.1 broadcast_select_fusion.1.refs_0_
  153.4 1.4 convert_bitcast_fusion
  155.1 1.5 select_convert_fusion.1
  157.4 2.3 %collective-permute-done.16 = bf16[256,2048]{1,0:T(8,128)(2,1)S(1)} collective-permute-done((bf16[256,2048]{1,0:T(8,128)(2,1)}, bf16[256,2048]{1,0:T(8,128)(2,1)S(1)}, u32[]{:S(2)}, u32[]{:S(2)}) %collective-permute-start.16) | collective-permute-done | bytes 1048608 | tf_op jit(solution)/shard_map/ppermute | solution.py:265
  159.7 2.2 %maximum_select_fusion.hin_ref = bf16[256,4096]{1,0:T(8,128)(2,1)} fusion(bf16[256,2048]{1,0:T(8,128)(2,1)S(1)} %collective-permute-done.16, bf16[256,2048]{1,0:T(8,128)(2,1)S(1)} %get-tuple-element.15, pred[]{:T(512)S(6)} %eq.42), kind=kLoop, calls=%fused_computation.7 | loop fusion | flops 9437184 | bytes 4194305 | tf_op jit(solution)/shard_map/jit(_where)/select_n | solution.py:322
  162.6 13.5 %shard_map.107 = bf16[512,4096]{1,0:T(8,128)(2,1)} custom-call(bf16[512,5120]{1,0:T(8,128)(2,1)} %shard_map.100.c_ref.b_ref.x_ref.refs_0_.refs_1_.refs_2_, f32[512,4096]{1,0:T(8,128)} %shard_map.102.refs_1_.y_ref, bf16[512,4096]{1,0:T(8,128)(2,1)} %z_ref.1, bf16[256,4096]{1,0:T(8,128)(2,1)} %maximum_select_fusion.hin_ref, ...), custom_call_target="tpu_custom_call" | custom-call | tf_op jit(solution)/shard_map/pallas_call | solution.py:231
  (87 shorter events, 19.9 us)
Async XLA Ops:
  0.0 10.9 %copy-start = (f32[4,5120]{1,0:T(4,128)S(1)}, f32[4,5120]{1,0:T(4,128)}, u32[]{:S(2)}) copy-start(f32[4,5120]{1,0:T(4,128)} %param.14) | copy-start | bytes 245764
  0.9 13.6 %collective-permute-start = (bf16[3,5120]{1,0:T(4,128)(2,1)S(1)}, bf16[3,5120]{1,0:T(4,128)(2,1)S(1)}, u32[]{:S(2)}, u32[]{:S(2)}) collective-permute-start(bf16[3,5120]{1,0:T(4,128)(2,1)S(1)} %slice.57), channel_id=1, source_target_pairs={{0,1},{1,2},{2,3},{3,4},{4,5},{5,6},{6,7},{7,8},{8,9},{9,10},{10,1... | collective-permute-start | bytes 92168 | tf_op jit(solution)/shard_map/ppermute | solution.py:23
  42.7 2.6 %copy-start.1 = (f32[64]{0:T(128)S(1)}, f32[64]{0:T(128)}, u32[]{:S(2)}) copy-start(f32[64]{0:T(128)} %param.18) | copy-start | bytes 772
  44.5 19.6 %collective-permute-start.1 = (f32[257,2048]{1,0:T(8,128)S(1)}, f32[257,2048]{1,0:T(8,128)}, u32[]{:S(2)}, u32[]{:S(2)}) collective-permute-start(f32[257,2048]{1,0:T(8,128)S(1)} %dynamic-slice_bitcast_fusion), channel_id=1, source_target_pairs={{0,1},{1,0},{2,3},{3,2},{4,5},{5,4},{6,7},{7,6},{8,9},{9,8},{10,11... | collective-permute-start | bytes 6316040 | tf_op jit(solution)/shard_map/ppermute | solution.py:265
  69.9 6.9 %collective-permute-start.2 = (bf16[258,256]{1,0:T(8,128)(2,1)S(1)}, bf16[258,256]{1,0:T(8,128)(2,1)S(1)}, u32[]{:S(2)}, u32[]{:S(2)}) collective-permute-start(bf16[258,256]{1,0:T(8,128)(2,1)S(1)} %bitcast.140), channel_id=1, source_target_pairs={{0,2},{2,4},{4,6},{6,8},{8,10},{10,12},{12,14},{14,0},{1,3},{3,5},... | collective-permute-start | bytes 396296 | tf_op jit(solution)/shard_map/ppermute | solution.py:275
  71.2 7.4 %collective-permute-start.3 = (bf16[258,256]{1,0:T(8,128)(2,1)S(1)}, bf16[258,256]{1,0:T(8,128)(2,1)S(1)}, u32[]{:S(2)}, u32[]{:S(2)}) collective-permute-start(bf16[258,256]{1,0:T(8,128)(2,1)S(1)} %bitcast.139), channel_id=1, source_target_pairs={{0,4},{2,6},{4,8},{6,10},{8,12},{10,14},{12,0},{14,2},{1,5},{3,7},... | collective-permute-start | bytes 396296 | tf_op jit(solution)/shard_map/ppermute | solution.py:275
  72.5 18.6 %collective-permute-start.4 = (bf16[258,256]{1,0:T(8,128)(2,1)S(1)}, bf16[258,256]{1,0:T(8,128)(2,1)S(1)}, u32[]{:S(2)}, u32[]{:S(2)}) collective-permute-start(bf16[258,256]{1,0:T(8,128)(2,1)S(1)} %bitcast.138), channel_id=1, source_target_pairs={{0,6},{2,8},{4,10},{6,12},{8,14},{10,0},{12,2},{14,4},{1,7},{3,9},... | collective-permute-start | bytes 396296 | tf_op jit(solution)/shard_map/ppermute | solution.py:275
  73.5 20.5 %collective-permute-start.5 = (bf16[258,256]{1,0:T(8,128)(2,1)S(1)}, bf16[258,256]{1,0:T(8,128)(2,1)S(1)}, u32[]{:S(2)}, u32[]{:S(2)}) collective-permute-start(bf16[258,256]{1,0:T(8,128)(2,1)S(1)} %bitcast.137), channel_id=1, source_target_pairs={{0,8},{2,10},{4,12},{6,14},{8,0},{10,2},{12,4},{14,6},{1,9},{3,11}... | collective-permute-start | bytes 396296 | tf_op jit(solution)/shard_map/ppermute | solution.py:275
  75.0 19.6 %collective-permute-start.6 = (bf16[258,256]{1,0:T(8,128)(2,1)S(1)}, bf16[258,256]{1,0:T(8,128)(2,1)S(1)}, u32[]{:S(2)}, u32[]{:S(2)}) collective-permute-start(bf16[258,256]{1,0:T(8,128)(2,1)S(1)} %bitcast.136), channel_id=1, source_target_pairs={{0,10},{2,12},{4,14},{6,0},{8,2},{10,4},{12,6},{14,8},{1,11},{3,13... | collective-permute-start | bytes 396296 | tf_op jit(solution)/shard_map/ppermute | solution.py:275
  76.8 19.6 %collective-permute-start.7 = (bf16[258,256]{1,0:T(8,128)(2,1)S(1)}, bf16[258,256]{1,0:T(8,128)(2,1)S(1)}, u32[]{:S(2)}, u32[]{:S(2)}) collective-permute-start(bf16[258,256]{1,0:T(8,128)(2,1)S(1)} %bitcast.135), channel_id=1, source_target_pairs={{0,12},{2,14},{4,0},{6,2},{8,4},{10,6},{12,8},{14,10},{1,13},{3,15... | collective-permute-start | bytes 396296 | tf_op jit(solution)/shard_map/ppermute | solution.py:275
  78.6 19.2 %collective-permute-start.8 = (bf16[258,256]{1,0:T(8,128)(2,1)S(1)}, bf16[258,256]{1,0:T(8,128)(2,1)S(1)}, u32[]{:S(2)}, u32[]{:S(2)}) collective-permute-start(bf16[258,256]{1,0:T(8,128)(2,1)S(1)} %bitcast.134), channel_id=1, source_target_pairs={{0,14},{2,0},{4,2},{6,4},{8,6},{10,8},{12,10},{14,12},{1,15},{3,1}... | collective-permute-start | bytes 396296 | tf_op jit(solution)/shard_map/ppermute | solution.py:275
  106.0 21.8 %collective-permute-start.9 = (bf16[256,256]{1,0:T(8,128)(2,1)S(1)}, bf16[256,256]{1,0:T(8,128)(2,1)S(1)}, u32[]{:S(2)}, u32[]{:S(2)}) collective-permute-start(bf16[256,256]{1,0:T(8,128)(2,1)S(1)} %get-tuple-element.33), channel_id=1, source_target_pairs={{0,2},{2,4},{4,6},{6,8},{8,10},{10,12},{12,14},{14,0},{1,3},{3,5},... | collective-permute-start | bytes 393224 | tf_op jit(solution)/shard_map/ppermute | solution.py:275
  123.4 7.1 %collective-permute-start.10 = (bf16[256,256]{1,0:T(8,128)(2,1)S(1)}, bf16[256,256]{1,0:T(8,128)(2,1)S(1)}, u32[]{:S(2)}, u32[]{:S(2)}) collective-permute-start(bf16[256,256]{1,0:T(8,128)(2,1)S(1)} %get-tuple-element.32), channel_id=1, source_target_pairs={{0,4},{2,6},{4,8},{6,10},{8,12},{10,14},{12,0},{14,2},{1,5},{3,7},... | collective-permute-start | bytes 393224 | tf_op jit(solution)/shard_map/ppermute | solution.py:275
  123.6 16.9 %collective-permute-start.11 = (bf16[256,256]{1,0:T(8,128)(2,1)S(1)}, bf16[256,256]{1,0:T(8,128)(2,1)S(1)}, u32[]{:S(2)}, u32[]{:S(2)}) collective-permute-start(bf16[256,256]{1,0:T(8,128)(2,1)S(1)} %get-tuple-element.31), channel_id=1, source_target_pairs={{0,6},{2,8},{4,10},{6,12},{8,14},{10,0},{12,2},{14,4},{1,7},{3,9},... | collective-permute-start | bytes 393224 | tf_op jit(solution)/shard_map/ppermute | solution.py:275
  126.3 17.1 %collective-permute-start.12 = (bf16[256,256]{1,0:T(8,128)(2,1)S(1)}, bf16[256,256]{1,0:T(8,128)(2,1)S(1)}, u32[]{:S(2)}, u32[]{:S(2)}) collective-permute-start(bf16[256,256]{1,0:T(8,128)(2,1)S(1)} %get-tuple-element.30), channel_id=1, source_target_pairs={{0,8},{2,10},{4,12},{6,14},{8,0},{10,2},{12,4},{14,6},{1,9},{3,11}... | collective-permute-start | bytes 393224 | tf_op jit(solution)/shard_map/ppermute | solution.py:275
  127.0 17.1 %collective-permute-start.13 = (bf16[256,256]{1,0:T(8,128)(2,1)S(1)}, bf16[256,256]{1,0:T(8,128)(2,1)S(1)}, u32[]{:S(2)}, u32[]{:S(2)}) collective-permute-start(bf16[256,256]{1,0:T(8,128)(2,1)S(1)} %get-tuple-element.29), channel_id=1, source_target_pairs={{0,10},{2,12},{4,14},{6,0},{8,2},{10,4},{12,6},{14,8},{1,11},{3,13... | collective-permute-start | bytes 393224 | tf_op jit(solution)/shard_map/ppermute | solution.py:275
  127.8 18.6 %collective-permute-start.14 = (bf16[256,256]{1,0:T(8,128)(2,1)S(1)}, bf16[256,256]{1,0:T(8,128)(2,1)S(1)}, u32[]{:S(2)}, u32[]{:S(2)}) collective-permute-start(bf16[256,256]{1,0:T(8,128)(2,1)S(1)} %get-tuple-element.28), channel_id=1, source_target_pairs={{0,12},{2,14},{4,0},{6,2},{8,4},{10,6},{12,8},{14,10},{1,13},{3,15... | collective-permute-start | bytes 393224 | tf_op jit(solution)/shard_map/ppermute | solution.py:275
  130.4 19.3 %collective-permute-start.15 = (bf16[256,256]{1,0:T(8,128)(2,1)S(1)}, bf16[256,256]{1,0:T(8,128)(2,1)S(1)}, u32[]{:S(2)}, u32[]{:S(2)}) collective-permute-start(bf16[256,256]{1,0:T(8,128)(2,1)S(1)} %get-tuple-element.27), channel_id=1, source_target_pairs={{0,14},{2,0},{4,2},{6,4},{8,6},{10,8},{12,10},{14,12},{1,15},{3,1}... | collective-permute-start | bytes 393224 | tf_op jit(solution)/shard_map/ppermute | solution.py:275
  156.6 3.1 %collective-permute-start.16 = (bf16[256,2048]{1,0:T(8,128)(2,1)}, bf16[256,2048]{1,0:T(8,128)(2,1)S(1)}, u32[]{:S(2)}, u32[]{:S(2)}) collective-permute-start(bf16[256,2048]{1,0:T(8,128)(2,1)} %get-tuple-element.16), channel_id=1, source_target_pairs={{0,1},{1,0},{2,3},{3,2},{4,5},{5,4},{6,7},{7,6},{8,9},{9,8},{10,11... | collective-permute-start | bytes 3145736 | tf_op jit(solution)/shard_map/ppermute | solution.py:265

commit v11 on v8

--- a/solution.py
+++ b/solution.py
@@ -85,7 +85,7 @@
 
 
 def state_kernel(
-    bt_ref, x_ref, dt_ref, cum_ref, segc_ref, bdec_ref, local_ref, cdec_ref, pay_ref,
+    bt_ref, x_ref, dt_ref, cum_ref, segc_ref, bdec_ref, local_ref, cdec_ref, pay_ref, drow_ref,
     acc_ref, dec_ref,
 ):
     b = pl.program_id(1)
@@ -95,8 +95,11 @@
         acc_ref[...] = jnp.zeros(acc_ref.shape, jnp.float32)
         dec_ref[...] = jnp.ones(dec_ref.shape, jnp.float32)
 
-    local_ref[0] = acc_ref[...]
-    cdec_ref[0] = dec_ref[...]
+    @pl.when(b > 0)
+    def _():
+        local_ref[0] = acc_ref[...]
+        cdec_ref[0] = dec_ref[...]
+
     cum = cum_ref[0]
     step = dt_ref[0]
     segc = segc_ref[:, 0:1]
@@ -119,9 +122,9 @@
         lo = (dec - hi.astype(jnp.float32)).astype(jnp.bfloat16)
         for k in range(pieces):
             cols = slice(k * width, (k + 1) * width)
-            pay_ref[k, 0:STATE, :] = total[:, cols].astype(jnp.bfloat16)
-            pay_ref[k, STATE : STATE + 1, :] = hi[:, cols]
-            pay_ref[k, STATE + 1 : STATE + 2, :] = lo[:, cols]
+            pay_ref[k] = total[:, cols].astype(jnp.bfloat16)
+            drow_ref[k, 0:1, :] = hi[:, cols]
+            drow_ref[k, 1:2, :] = lo[:, cols]
 
 
 def block_states(bt, conv, dt_g, cum_g, segc, bdec, peers):
@@ -141,14 +144,16 @@
             pl.BlockSpec((1, 1, GROUP_COLS), lambda g, b: (b, 0, g)),
         ],
         out_specs=[
-            pl.BlockSpec((1, STATE, GROUP_COLS), lambda g, b: (b, 0, g)),
-            pl.BlockSpec((1, 1, GROUP_COLS), lambda g, b: (b, 0, g)),
-            pl.BlockSpec((per, STATE + 2, width), lambda g, b: (g, 0, 0)),
+            pl.BlockSpec((1, STATE, GROUP_COLS), lambda g, b: (jnp.maximum(b - 1, 0), 0, g)),
+            pl.BlockSpec((1, 1, GROUP_COLS), lambda g, b: (jnp.maximum(b - 1, 0), 0, g)),
+            pl.BlockSpec((per, STATE, width), lambda g, b: (g, 0, 0)),
+            pl.BlockSpec((per, 2, width), lambda g, b: (g, 0, 0)),
         ],
         out_shape=[
-            jax.ShapeDtypeStruct((nb, STATE, INNER), jnp.float32),
-            jax.ShapeDtypeStruct((nb, 1, INNER), jnp.float32),
-            jax.ShapeDtypeStruct((peers, STATE + 2, width), jnp.bfloat16),
+            jax.ShapeDtypeStruct((max(nb - 1, 1), STATE, INNER), jnp.float32),
+            jax.ShapeDtypeStruct((max(nb - 1, 1), 1, INNER), jnp.float32),
+            jax.ShapeDtypeStruct((peers, STATE, width), jnp.bfloat16),
+            jax.ShapeDtypeStruct((peers, 2, width), jnp.bfloat16),
         ],
         scratch_shapes=[
             pltpu.VMEM((STATE, GROUP_COLS), jnp.float32),
@@ -220,16 +225,25 @@
 
 def mix_kernel(
     c_ref, y_ref, z_ref, back_ref, local_ref, cdec_ref, cum_ref, segc_ref, eb_ref, gain_ref,
-    out_ref, hin_ref,
+    out_ref, hin_ref, state_ref,
 ):
+    b = pl.program_id(1)
     pieces, _, width = back_ref.shape
-    for k in range(pieces):
-        hin_ref[:, k * width : (k + 1) * width] = back_ref[k].astype(jnp.float32)
-    state = cdec_ref[0] * hin_ref[...] + local_ref[0]
+
+    @pl.when(b == 0)
+    def _():
+        for k in range(pieces):
+            hin_ref[:, k * width : (k + 1) * width] = back_ref[k].astype(jnp.float32)
+        state_ref[...] = hin_ref[...].astype(jnp.bfloat16)
+
+    @pl.when(b > 0)
+    def _():
+        state_ref[...] = (cdec_ref[0] * hin_ref[...] + local_ref[0]).astype(jnp.bfloat16)
+
     segc = segc_ref[:, 0:1]
     entry = eb_ref[0:1, 0:1]
     in_weight = jnp.where(segc == entry, jnp.exp(cum_ref[0]), 0.0)
-    inter = jnp.dot(c_ref[...], state.astype(jnp.bfloat16), preferred_element_type=jnp.float32)
+    inter = jnp.dot(c_ref[...], state_ref[...], preferred_element_type=jnp.float32)
     y = y_ref[...] + inter * expand_heads(in_weight)
     zf = z_ref[...].astype(jnp.float32)
     gated = y * (zf * jax.nn.sigmoid(zf))
@@ -245,22 +259,25 @@
     per = peers // GROUPS
     return pl.pallas_call(
         mix_kernel,
-        grid=(nb, GROUPS),
+        grid=(GROUPS, nb),
         in_specs=[
-            pl.BlockSpec((STRETCH, STATE), lambda b, g: (b, c_col + g)),
-            pl.BlockSpec((STRETCH, GROUP_COLS), lambda b, g: (b, g)),
-            pl.BlockSpec((STRETCH, GROUP_COLS), lambda b, g: (b, g)),
-            pl.BlockSpec((per, STATE, width), lambda b, g: (g, 0, 0)),
-            pl.BlockSpec((1, STATE, GROUP_COLS), lambda b, g: (b, 0, g)),
-            pl.BlockSpec((1, 1, GROUP_COLS), lambda b, g: (b, 0, g)),
-            pl.BlockSpec((1, STRETCH, PER_GROUP), lambda b, g: (g, b, 0)),
-            pl.BlockSpec((STRETCH, 128), lambda b, g: (b, 0)),
-            pl.BlockSpec((8, 128), lambda b, g: (b, 0)),
-            pl.BlockSpec((1, GROUP_COLS), lambda b, g: (0, g)),
-        ],
-        out_specs=pl.BlockSpec((STRETCH, GROUP_COLS), lambda b, g: (b, g)),
+            pl.BlockSpec((STRETCH, STATE), lambda g, b: (b, c_col + g)),
+            pl.BlockSpec((STRETCH, GROUP_COLS), lambda g, b: (b, g)),
+            pl.BlockSpec((STRETCH, GROUP_COLS), lambda g, b: (b, g)),
+            pl.BlockSpec((per, STATE, width), lambda g, b: (g, 0, 0)),
+            pl.BlockSpec((1, STATE, GROUP_COLS), lambda g, b: (jnp.maximum(b - 1, 0), 0, g)),
+            pl.BlockSpec((1, 1, GROUP_COLS), lambda g, b: (jnp.maximum(b - 1, 0), 0, g)),
+            pl.BlockSpec((1, STRETCH, PER_GROUP), lambda g, b: (g, b, 0)),
+            pl.BlockSpec((STRETCH, 128), lambda g, b: (b, 0)),
+            pl.BlockSpec((8, 128), lambda g, b: (b, 0)),
+            pl.BlockSpec((1, GROUP_COLS), lambda g, b: (0, g)),
+        ],
+        out_specs=pl.BlockSpec((STRETCH, GROUP_COLS), lambda g, b: (b, g)),
         out_shape=jax.ShapeDtypeStruct((tok, INNER), jnp.bfloat16),
-        scratch_shapes=[pltpu.VMEM((STATE, GROUP_COLS), jnp.float32)],
+        scratch_shapes=[
+            pltpu.VMEM((STATE, GROUP_COLS), jnp.float32),
+            pltpu.VMEM((STATE, GROUP_COLS), jnp.bfloat16),
+        ],
     )(conv, y_local, z_gate, back, local_states, cdec, cum_g, segc, eb, gain)
 
 
@@ -277,14 +294,31 @@
     lax.fori_loop(0, peers, body, jnp.zeros(out_ref.shape[1:], jnp.float32))
 
 
-def compose(payload):
-    peers, _, width = payload.shape
-    got = lax.all_to_all(payload, "ctx", split_axis=0, concat_axis=0, tiled=True)
+def tie(value, *after):
+    def kernel(*refs):
+        del refs
+
+    return pl.pallas_call(
+        kernel,
+        in_specs=[pl.BlockSpec(memory_space=pl.ANY) for _ in range(1 + len(after))],
+        out_specs=pl.BlockSpec(memory_space=pl.ANY),
+        out_shape=jax.ShapeDtypeStruct(value.shape, value.dtype),
+        input_output_aliases={0: 0},
+    )(value, *after)
+
+
+def compose(pieces, rows, first_work, second_work):
+    peers, _, width = pieces.shape
+    payload = jnp.concatenate([pieces, rows], axis=1)
+    work = first_work()
+    got = tie(lax.all_to_all(payload, "ctx", split_axis=0, concat_axis=0, tiled=True), work)
     entering = pl.pallas_call(
         scan_kernel,
         out_shape=jax.ShapeDtypeStruct((peers, STATE, width), jnp.bfloat16),
     )(got)
-    return lax.all_to_all(entering, "ctx", split_axis=0, concat_axis=0, tiled=True)
+    work = second_work(work)
+    back = lax.all_to_all(entering, "ctx", split_axis=0, concat_axis=0, tiled=True)
+    return tie(back, work), work
 
 
 def local(xbc, z_gate, dt_raw, lengths, conv_weight, conv_bias, dt_bias, a_log, d_skip, norm_gain):
@@ -323,12 +357,15 @@
     bt = conv[:, INNER : INNER + GROUPS * STATE].T
     bdec = jnp.repeat(block_decay, HEAD_DIM, axis=1)[:, None, :]
 
-    local_states, cdec, payload = block_states(bt, conv, dt_g, cum_g, segc, bdec, peers)
+    local_states, cdec, pieces, rows = block_states(bt, conv, dt_g, cum_g, segc, bdec, peers)
     dsk = jnp.repeat(d_skip, HEAD_DIM)[None, :]
-    y_local = None
-    for g in range(GROUPS):
-        y_local = intra_part(conv, dt_g, cum_g, cumt_g, segc, segr, dsk, g, y_local)
-    back = compose(payload)
+    def first_work():
+        return intra_part(conv, dt_g, cum_g, cumt_g, segc, segr, dsk, 0)
+
+    def second_work(done):
+        return intra_part(conv, dt_g, cum_g, cumt_g, segc, segr, dsk, 1, done)
+
+    back, y_local = compose(pieces, rows, first_work, second_work)
     gain = norm_gain[None, :]
     return mix(conv, y_local, z_gate, back, local_states, cdec, cum_g, segc, eb, gain)
 

time: 169 us -> 173 us (1.024)
  blocking collectives: 54 us -> 0 us
  waiting for transfers between devices: 10.5 us -> 59.2 us
  starting transfers between devices: 9.51 us -> 13.8 us
  other arithmetic: 4.66 us -> 7.76 us
    all_to_all x1 -> x0, blocking collectives: 54 us -> none  [compose(): lax.all_to_all(payload, 'ctx', split_axis=0, concat_axis=0, tiled=True)]
    all_to_all x0 -> x1, waiting for transfers between devices: none -> 29.4 us  [compose(): lax.all_to_all(payload, 'ctx', split_axis=0, concat_axis=0, tiled=True)]
    all_to_all x1, waiting for transfers between devices: 10.5 us -> 29.8 us  [compose(): lax.all_to_all(entering, 'ctx', split_axis=0, concat_axis=0, tiled=True)]
    all_to_all x0 -> x1, starting transfers between devices: none -> 5.17 us  [compose(): lax.all_to_all(payload, 'ctx', split_axis=0, concat_axis=0, tiled=True)]
    concatenate x0 -> x1, other arithmetic: none -> 3.11 us  [compose(): payload = jnp.concatenate([pieces, rows], axis=1)]
    unnamed x5 -> x9, local copies, waits for them, and re-layouts: 1.61 us -> 3.7 us
    pallas_call x1 -> x3, Pallas kernels: 13.5 us -> 14 us  [the longest x1 14 us: mix(): pl.pallas_call(mix_kernel, grid=(GROUPS, nb), in_specs=[pl.BlockSpec((STR...]
  transfers between devices with their start and end apart: 2 -> 3, of which waited for: 1 -> 2; matrix products, arithmetic and copies ran while one was open for 8% -> 7% of each run, Pallas kernels for 21% -> 20%
where the time goes in v11:
time: 173 us
  Pallas kernels  76.7 us (44%)
  waiting for transfers between devices  59.2 us (34%)
  local copies, waits for them, and re-layouts  15.1 us (9%)
  starting transfers between devices  13.8 us (8%)
  other arithmetic  7.76 us (4%)
    pallas_call x2, Pallas kernels, intra_part(): pl.pallas_call(kernel, grid=(nb,), in_specs=specs, out_specs=pl.BlockSpec...  34.8 us
    all_to_all x1, waiting for transfers between devices, compose(): lax.all_to_all(entering, 'ctx', split_axis=0, concat_axis=0, tiled=True)  29.8 us
    all_to_all x1, waiting for transfers between devices, compose(): lax.all_to_all(payload, 'ctx', split_axis=0, concat_axis=0, tiled=True)  29.4 us
    pallas_call x1, Pallas kernels, mix(): pl.pallas_call(mix_kernel, grid=(GROUPS, nb), in_specs=[pl.BlockSpec((STR...  14 us
    pallas_call x1, Pallas kernels, block_states(): pl.pallas_call(state_kernel, grid=(GROUPS, nb), in_specs=[pl.BlockSpec((S...  12.6 us
    pallas_call x1, Pallas kernels, conv_part(): pl.pallas_call(conv_kernel, grid=(chans // CONV_COLS,), in_specs=[pl.Bloc...  11.8 us
    all_to_all x1, starting transfers between devices, compose(): lax.all_to_all(payload, 'ctx', split_axis=0, concat_axis=0, tiled=True)  5.17 us
    all_to_all x1, starting transfers between devices, compose(): lax.all_to_all(entering, 'ctx', split_axis=0, concat_axis=0, tiled=True)  4.91 us
  transfers between devices with their start and end apart: 3, of which 2 were waited for; matrix products, arithmetic and copies ran while one was open for 7% of the time, Pallas kernels for 20%

profile of v11, /device:TPU:13, one launch (start us, length us, event | category | flops | bytes accessed | tf_op | source)
XLA Modules:
  0.0 172.7 jit_solution(5951462960957594895)
XLA Ops:
  0.0 0.9 slice.43
  0.9 3.7 %collective-permute-start = (bf16[3,5120]{1,0:T(4,128)(2,1)S(1)}, bf16[3,5120]{1,0:T(4,128)(2,1)S(1)}, u32[]{:S(2)}, u32[]{:S(2)}) collective-permute-start(bf16[3,5120]{1,0:T(4,128)(2,1)S(1)} %slice.43), channel_id=1, source_target_pairs={{0,1},{1,2},{2,3},{3,4},{4,5},{5,6},{6,7},{7,8},{8,9},{9,10},{10,1... | collective-permute-start | bytes 92168 | tf_op jit(solution)/shard_map/ppermute | solution.py:23
  4.7 0.8 reduce-window.18
  5.5 0.1 convert_reduce_fusion
  5.6 0.1 fusion.1
  5.8 0.2 copy.51
  6.0 0.1 convert_reduce_fusion.1
  6.1 0.2 fusion.4
  6.3 0.1 copy.60
  6.4 0.7 exp.14
  7.0 1.0 negate_multiply_fusion
  8.1 1.2 reduce-window.19
  9.3 0.2 slice_reduce_fusion
  9.5 0.1 bitcast_bitcast_fusion
  9.6 0.2 fusion
  9.8 0.2 compare_reduce_fusion
  10.0 0.1 broadcast_select_fusion
  10.1 0.7 pad_convert_fusion.m_ref
  10.8 0.1 copy.56
  10.9 0.7 concatenate.15.w_ref
  11.6 0.1 broadcast_in_dim.67
  11.7 0.7 broadcast_in_dim_reshape.7.bdec_ref
  12.4 0.1 reshape_reshape.3
  12.5 1.0 copy.57
  13.5 1.0 copy.52
  14.5 0.7 concatenate.14.rim_ref
  15.2 11.8 %shard_map.100.c_ref.b_ref.x_ref.refs_0_.refs_1_.refs_2_ = bf16[512,5120]{1,0:T(8,128)(2,1)} custom-call(bf16[512,5120]{1,0:T(8,128)(2,1)} %x_ref.1, bf16[8,5120]{1,0:T(8,128)(2,1)} %concatenate.14.rim_ref, f32[8,5120]{1,0:T(8,128)} %concatenate.15.w_ref, f32[1,5120]{1,0:T(1,128)} %bitcast.48, f32[512,128]{1,0:T(8,128)} %pad_convert_fusion.m_ref), custom_call_target="tpu_custom_call" | custom-call | tf_op jit(solution)/shard_map/pallas_call | solution.py:72
  26.9 1.1 slice.59
  28.0 1.0 copy.61
  29.0 0.8 broadcast_in_dim.33.segc_ref.refs_6_
  29.8 12.6 %shard_map.103 = (f32[1,256,4096]{2,1,0:T(8,128)}, f32[1,1,4096]{2,1,0:T(1,128)}, bf16[16,256,256]{2,1,0:T(8,128)(2,1)}, bf16[16,2,256]{2,1,0:T(2,128)(2,1)}) custom-call(bf16[512,512]{1,0:T(8,128)(2,1)} %bitcast.43, bf16[512,5120]{1,0:T(8,128)(2,1)} %shard_map.100.c_ref.b_ref.x_ref.refs_0_.refs_1_.refs_2_, f32[2,512,32]{2,1,0:T(8,128)} %bitcast.40, ...), custom_call_target="tpu_custom_call" | custom-call | tf_op jit(solution)/shard_map/pallas_call | solution.py:135
  42.4 3.1 %pad_maximum_fusion = bf16[16,258,256]{2,1,0:T(8,128)(2,1)} fusion(bf16[16,2,256]{2,1,0:T(2,128)(2,1)} %get-tuple-element.10, bf16[16,256,256]{2,1,0:T(8,128)(2,1)} %get-tuple-element.9), kind=kLoop, calls=%fused_computation | loop fusion | flops 4227072 | bytes 4227072 | tf_op jit(solution)/shard_map/concatenate | solution.py:312
  45.5 5.2 %all-to-all-start = ((bf16[16,258,256]{2,1,0:T(8,128)(2,1)}), bf16[16,258,256]{2,1,0:T(8,128)(2,1)S(1)}, u32[]{:S(2)}, u32[]{:S(2)}) async-start(bf16[16,258,256]{2,1,0:T(8,128)(2,1)} %pad_maximum_fusion), calls=%async_computation | async-start | bytes 4325376 | tf_op jit(solution)/shard_map/all_to_all | solution.py:314
  50.7 0.7 copy.65
  51.3 0.1 broadcast_in_dim.35
  51.4 0.7 broadcast_in_dim_reshape.6.dsk_ref.refs_8_
  52.1 0.6 broadcast_in_dim.34.segr_ref.refs_7_
  52.7 17.4 %shard_map.101.refs_9_.refs_1_ = f32[512,4096]{1,0:T(8,128)} custom-call(bf16[512,5120]{1,0:T(8,128)(2,1)} %shard_map.100.c_ref.b_ref.x_ref.refs_0_.refs_1_.refs_2_, bf16[512,5120]{1,0:T(8,128)(2,1)} %shard_map.100.c_ref.b_ref.x_ref.refs_0_.refs_1_.refs_2_, bf16[512,5120]{1,0:T(8,128)(2,1)} %shard_map.100.c_ref.b_ref.x_ref.refs_0_.refs_1_.refs_2_, ...), custom_call_target="tpu_custom_call" | custom-call | tf_op jit(solution)/shard_map/pallas_call | solution.py:216
  70.1 29.4 %all-to-all-done.refs_0_ = bf16[16,258,256]{2,1,0:T(8,128)(2,1)S(1)} async-done(((bf16[16,258,256]{2,1,0:T(8,128)(2,1)}), bf16[16,258,256]{2,1,0:T(8,128)(2,1)S(1)}, u32[]{:S(2)}, u32[]{:S(2)}) %all-to-all-start) | async-done | bytes 2113568 | tf_op jit(solution)/shard_map/all_to_all | solution.py:314
  99.5 1.3 copy-done
  100.8 3.6 %shard_map.105 = bf16[16,256,256]{2,1,0:T(8,128)(2,1)} custom-call(bf16[16,258,256]{2,1,0:T(8,128)(2,1)} %shard_map.104.got_ref), custom_call_target="tpu_custom_call" | custom-call | tf_op jit(solution)/shard_map/pallas_call | solution.py:315
  104.4 4.9 %all-to-all-start.1 = ((bf16[16,256,256]{2,1,0:T(8,128)(2,1)}), bf16[16,256,256]{2,1,0:T(8,128)(2,1)S(1)}, u32[]{:S(2)}, u32[]{:S(2)}) async-start(bf16[16,256,256]{2,1,0:T(8,128)(2,1)} %shard_map.105), calls=%async_computation.1 | async-start | bytes 4194304 | tf_op jit(solution)/shard_map/all_to_all | solution.py:320
  109.4 0.1 broadcast_in_dim.69
  109.5 17.5 %shard_map.102.refs_1_.y_ref = f32[512,4096]{1,0:T(8,128)} custom-call(bf16[512,5120]{1,0:T(8,128)(2,1)} %shard_map.100.c_ref.b_ref.x_ref.refs_0_.refs_1_.refs_2_, bf16[512,5120]{1,0:T(8,128)(2,1)} %shard_map.100.c_ref.b_ref.x_ref.refs_0_.refs_1_.refs_2_, ...), custom_call_target="tpu_custom_call", output_to_operand_aliasing={{}: (9, {})} | custom-call | tf_op jit(solution)/shard_map/pallas_call | solution.py:216
  126.9 29.8 %all-to-all-done.1.refs_0_ = bf16[16,256,256]{2,1,0:T(8,128)(2,1)S(1)} async-done(((bf16[16,256,256]{2,1,0:T(8,128)(2,1)}), bf16[16,256,256]{2,1,0:T(8,128)(2,1)S(1)}, u32[]{:S(2)}, u32[]{:S(2)}) %all-to-all-start.1) | async-done | bytes 2097184 | tf_op jit(solution)/shard_map/all_to_all | solution.py:320
  156.7 1.4 copy-done.1
  158.1 0.7 broadcast_in_dim.70.eb_ref
  158.8 14.0 %shard_map.107 = bf16[512,4096]{1,0:T(8,128)(2,1)} custom-call(bf16[512,5120]{1,0:T(8,128)(2,1)} %shard_map.100.c_ref.b_ref.x_ref.refs_0_.refs_1_.refs_2_, f32[512,4096]{1,0:T(8,128)} %shard_map.102.refs_1_.y_ref, bf16[512,4096]{1,0:T(8,128)(2,1)} %z_ref.1, bf16[16,256,256]{2,1,0:T(8,128)(2,1)} %shard_map.106.back_ref, ...), custom_call_target="tpu_custom_call" | custom-call | tf_op jit(solution)/shard_map/pallas_call | solution.py:260
  (22 shorter events, 0.2 us)
Async XLA Ops:
  0.0 10.9 %copy-start.2 = (f32[4,5120]{1,0:T(4,128)S(1)}, f32[4,5120]{1,0:T(4,128)}, u32[]{:S(2)}) copy-start(f32[4,5120]{1,0:T(4,128)} %param.14) | copy-start | bytes 245764
  0.9 13.5 %collective-permute-start = (bf16[3,5120]{1,0:T(4,128)(2,1)S(1)}, bf16[3,5120]{1,0:T(4,128)(2,1)S(1)}, u32[]{:S(2)}, u32[]{:S(2)}) collective-permute-start(bf16[3,5120]{1,0:T(4,128)(2,1)S(1)} %slice.43), channel_id=1, source_target_pairs={{0,1},{1,2},{2,3},{3,4},{4,5},{5,6},{6,7},{7,8},{8,9},{9,10},{10,1... | collective-permute-start | bytes 92168 | tf_op jit(solution)/shard_map/ppermute | solution.py:23
  45.5 5.8 %copy-start.3 = (f32[64]{0:T(128)S(1)}, f32[64]{0:T(128)}, u32[]{:S(2)}) copy-start(f32[64]{0:T(128)} %param.18) | copy-start | bytes 772
  45.5 54.0 %all-to-all-start = ((bf16[16,258,256]{2,1,0:T(8,128)(2,1)}), bf16[16,258,256]{2,1,0:T(8,128)(2,1)S(1)}, u32[]{:S(2)}, u32[]{:S(2)}) async-start(bf16[16,258,256]{2,1,0:T(8,128)(2,1)} %pad_maximum_fusion), calls=%async_computation | async-start | bytes 4325376 | tf_op jit(solution)/shard_map/all_to_all | solution.py:314
  99.5 1.3 copy-start
  104.4 52.3 %all-to-all-start.1 = ((bf16[16,256,256]{2,1,0:T(8,128)(2,1)}), bf16[16,256,256]{2,1,0:T(8,128)(2,1)S(1)}, u32[]{:S(2)}, u32[]{:S(2)}) async-start(bf16[16,256,256]{2,1,0:T(8,128)(2,1)} %shard_map.105), calls=%async_computation.1 | async-start | bytes 4194304 | tf_op jit(solution)/shard_map/all_to_all | solution.py:320
  156.7 1.4 copy-start.1

commit v12 on v10

--- a/solution.py
+++ b/solution.py
@@ -265,18 +265,6 @@
     return lax.ppermute(value, "core", [(0, 1), (1, 0)])
 
 
-def exchange(value, axis):
-    count = lax.axis_size(axis)
-    me = lax.axis_index(axis)
-    got = [lax.dynamic_index_in_dim(value, me, 0, keepdims=False)]
-    for by in range(1, count):
-        piece = lax.dynamic_index_in_dim(value, (me + by) % count, 0, keepdims=False)
-        pairs = [(i, (i + by) % count) for i in range(count)]
-        got.append(lax.ppermute(piece, axis, pairs))
-    stacked = jnp.stack(got)
-    return jnp.take(stacked, (me - jnp.arange(count)) % count, axis=0)
-
-
 def tie(value, *after):
     def kernel(*refs):
         del refs
@@ -308,13 +296,13 @@
         [chip_state.astype(jnp.bfloat16), decay_hi, decay_lo], axis=0
     ).reshape(STATE + 2, chips, width).transpose(1, 0, 2)
     work = first_work()
-    got = tie(exchange(payload, "chip"), work)
+    got = tie(lax.all_to_all(payload, "chip", split_axis=0, concat_axis=0, tiled=True), work)
     entering = pl.pallas_call(
         scan_kernel,
         out_shape=jax.ShapeDtypeStruct((chips, STATE, width), jnp.bfloat16),
     )(got)
     work = second_work(work)
-    back = tie(exchange(entering, "chip"), work)
+    back = tie(lax.all_to_all(entering, "chip", split_axis=0, concat_axis=0, tiled=True), work)
     chip_in = back.transpose(1, 0, 2).reshape(STATE, half).astype(jnp.float32)
     later_in = first_decay * chip_in + first[:STATE]
     keep = jnp.where(core == 0, chip_in, later_in).astype(jnp.bfloat16)

time: 177 us -> 144 us (0.81)
  the two profiles are of different devices: /device:TPU:15 before, /device:TPU:1 now
where the time goes in v12:
time: 144 us; the launch traced here: 143 us
  Pallas kernels  75.4 us (52%)
  waiting for transfers between devices  21.3 us (15%)
  local copies, waits for them, and re-layouts  17.9 us (12%)
  starting transfers between devices  15 us (10%)
  other arithmetic  12.9 us (9%)
    pallas_call x2, Pallas kernels, intra_part(): pl.pallas_call(kernel, grid=(nb,), in_specs=specs, out_specs=pl.BlockSpec...  34.7 us
    pallas_call x1, Pallas kernels, mix(): pl.pallas_call(mix_kernel, grid=(nb, GROUPS), in_specs=[pl.BlockSpec((STR...  13.4 us
    pallas_call x1, Pallas kernels, block_states(): pl.pallas_call(state_kernel, grid=(GROUPS, nb), in_specs=[pl.BlockSpec((S...  12.9 us
    pallas_call x1, Pallas kernels, conv_part(): pl.pallas_call(conv_kernel, grid=(chans // CONV_COLS,), in_specs=[pl.Bloc...  11.8 us
    all_to_all x1, waiting for transfers between devices, compose(): lax.all_to_all(entering, 'chip', split_axis=0, concat_axis=0, tiled=True)  7.81 us
    all_to_all x1, waiting for transfers between devices, compose(): lax.all_to_all(payload, 'chip', split_axis=0, concat_axis=0, tiled=True)  6.76 us
    ppermute x2, waiting for transfers between devices, swap_cores(): return lax.ppermute(value, 'core', [(0, 1), (1, 0)])  6.71 us
    all_to_all x1, starting transfers between devices, compose(): lax.all_to_all(payload, 'chip', split_axis=0, concat_axis=0, tiled=True)  4.6 us
  transfers between devices with their start and end apart: 5, of which 4 were waited for; matrix products, arithmetic and copies ran while one was open for 8% of the time, Pallas kernels for 24%

profile of v12, /device:TPU:1, one launch (start us, length us, event | category | flops | bytes accessed | tf_op | source)
XLA Modules:
  0.0 142.7 jit_solution(2776699704301351319)
XLA Ops:
  0.0 0.9 slice.57
  0.9 4.5 %collective-permute-start = (bf16[3,5120]{1,0:T(4,128)(2,1)S(1)}, bf16[3,5120]{1,0:T(4,128)(2,1)S(1)}, u32[]{:S(2)}, u32[]{:S(2)}) collective-permute-start(bf16[3,5120]{1,0:T(4,128)(2,1)S(1)} %slice.57), channel_id=1, source_target_pairs={{0,1},{1,2},{2,3},{3,4},{4,5},{5,6},{6,7},{7,8},{8,9},{9,10},{10,1... | collective-permute-start | bytes 92168 | tf_op jit(solution)/shard_map/ppermute | solution.py:23
  5.5 0.8 reduce-window.18
  6.6 0.2 copy.59
  6.9 0.2 fusion.5
  7.2 0.7 exp.14
  7.8 1.0 negate_multiply_fusion
  8.9 1.2 reduce-window.19
  10.1 0.2 slice_reduce_fusion
  10.4 0.2 fusion.1
  10.6 0.2 compare_reduce_fusion
  10.9 0.7 pad_convert_fusion.m_ref
  11.7 0.7 concatenate.21.w_ref
  12.5 0.7 broadcast_in_dim_reshape.7.bdec_ref
  13.3 1.0 copy.65
  14.3 1.0 copy.60
  15.3 0.7 concatenate.20.rim_ref
  16.0 11.8 %shard_map.100.c_ref.b_ref.x_ref.refs_0_.refs_1_.refs_2_ = bf16[512,5120]{1,0:T(8,128)(2,1)} custom-call(bf16[512,5120]{1,0:T(8,128)(2,1)} %x_ref.1, bf16[8,5120]{1,0:T(8,128)(2,1)} %concatenate.20.rim_ref, f32[8,5120]{1,0:T(8,128)} %concatenate.21.w_ref, f32[1,5120]{1,0:T(1,128)} %bitcast.71, f32[512,128]{1,0:T(8,128)} %pad_convert_fusion.m_ref), custom_call_target="tpu_custom_call" | custom-call | tf_op jit(solution)/shard_map/pallas_call | solution.py:72
  27.8 1.1 slice.77
  28.9 1.0 copy.71
  29.9 0.8 broadcast_in_dim.33.segc_ref.refs_6_
  30.7 12.9 %shard_map.103 = (f32[2,256,4096]{2,1,0:T(8,128)}, f32[2,1,4096]{2,1,0:T(1,128)}, f32[2,257,2048]{2,1,0:T(8,128)}) custom-call(bf16[512,512]{1,0:T(8,128)(2,1)} %bitcast.64, bf16[512,5120]{1,0:T(8,128)(2,1)} %shard_map.100.c_ref.b_ref.x_ref.refs_0_.refs_1_.refs_2_, f32[2,512,32]{2,1,0:T(8,128)} %bitcast.57, f32[2,512,32]{2,1,0:T(8,128)} %bitcast.53, ...), custom_call_target="tpu_custom_call" | custom-call | tf_op jit(solution)/shard_map/pallas_call | solution.py:122
  43.6 1.7 %dynamic-slice_bitcast_fusion = f32[257,2048]{1,0:T(8,128)S(1)} fusion(f32[2,257,2048]{2,1,0:T(8,128)} %get-tuple-element.8, s32[]{:T(128)S(6)} %select_n.52), kind=kLoop, calls=%fused_computation.2 | loop fusion | bytes 4210692 | tf_op jit(solution)/shard_map/jit(dynamic_index_in_dim)/squeeze | solution.py:287
  45.4 4.4 %collective-permute-done.1 = f32[257,2048]{1,0:T(8,128)} collective-permute-done((f32[257,2048]{1,0:T(8,128)S(1)}, f32[257,2048]{1,0:T(8,128)}, u32[]{:S(2)}, u32[]{:S(2)}) %collective-permute-start.1) | collective-permute-done | bytes 2105376 | tf_op jit(solution)/shard_map/ppermute | solution.py:265
  49.8 2.6 %bitcast_select_fusion.1 = (f32[257,2048]{1,0:T(8,128)S(1)}, f32[257,2048]{1,0:T(8,128)S(1)}) fusion(f32[257,2048]{1,0:T(8,128)} %collective-permute-done.1, f32[2,257,2048]{2,1,0:T(8,128)} %get-tuple-element.8, s32[]{:T(128)S(6)} %select_n.53, pred[]{:T(512)S(6)} %eq.24), kind=kLoop, calls=%fused_computation.1 | loop fusion | flops 1052672 | bytes 8421381 | tf_op jit(solution)/shard_map/jit(_where)/select_n | solution.py:289
  52.4 0.4 fusion
  52.9 0.3 copy.77
  53.3 1.2 copy.84
  54.5 4.6 %all-to-all-start = ((bf16[8,258,256]{2,1,0:T(8,128)(2,1)}), bf16[8,258,256]{2,1,0:T(8,128)(2,1)S(1)}, u32[]{:S(2)}, u32[]{:S(2)}) async-start(bf16[8,258,256]{2,1,0:T(8,128)(2,1)} %bitcast.61), calls=%async_computation | async-start | bytes 2162688 | tf_op jit(solution)/shard_map/all_to_all | solution.py:299
  59.1 0.7 copy.75
  59.9 0.7 broadcast_in_dim_reshape.6.dsk_ref.refs_8_
  60.5 0.6 broadcast_in_dim.34.segr_ref.refs_7_
  61.1 17.4 %shard_map.101.refs_9_.refs_1_ = f32[512,4096]{1,0:T(8,128)} custom-call(bf16[512,5120]{1,0:T(8,128)(2,1)} %shard_map.100.c_ref.b_ref.x_ref.refs_0_.refs_1_.refs_2_, bf16[512,5120]{1,0:T(8,128)(2,1)} %shard_map.100.c_ref.b_ref.x_ref.refs_0_.refs_1_.refs_2_, bf16[512,5120]{1,0:T(8,128)(2,1)} %shard_map.100.c_ref.b_ref.x_ref.refs_0_.refs_1_.refs_2_, ...), custom_call_target="tpu_custom_call" | custom-call | tf_op jit(solution)/shard_map/pallas_call | solution.py:201
  78.5 6.8 %all-to-all-done.refs_0_ = bf16[8,258,256]{2,1,0:T(8,128)(2,1)S(1)} async-done(((bf16[8,258,256]{2,1,0:T(8,128)(2,1)}), bf16[8,258,256]{2,1,0:T(8,128)(2,1)S(1)}, u32[]{:S(2)}, u32[]{:S(2)}) %all-to-all-start) | async-done | bytes 1056800 | tf_op jit(solution)/shard_map/all_to_all | solution.py:299
  85.3 1.0 copy-done
  86.3 2.6 %shard_map.105 = bf16[8,256,256]{2,1,0:T(8,128)(2,1)} custom-call(bf16[8,258,256]{2,1,0:T(8,128)(2,1)} %shard_map.104.got_ref), custom_call_target="tpu_custom_call" | custom-call | tf_op jit(solution)/shard_map/pallas_call | solution.py:300
  88.8 4.1 %all-to-all-start.1 = ((bf16[8,256,256]{2,1,0:T(8,128)(2,1)}), bf16[8,256,256]{2,1,0:T(8,128)(2,1)S(1)}, u32[]{:S(2)}, u32[]{:S(2)}) async-start(bf16[8,256,256]{2,1,0:T(8,128)(2,1)} %shard_map.105), calls=%async_computation.1 | async-start | bytes 2097152 | tf_op jit(solution)/shard_map/all_to_all | solution.py:305
  93.0 17.3 %shard_map.102.refs_1_.y_ref = f32[512,4096]{1,0:T(8,128)} custom-call(bf16[512,5120]{1,0:T(8,128)(2,1)} %shard_map.100.c_ref.b_ref.x_ref.refs_0_.refs_1_.refs_2_, bf16[512,5120]{1,0:T(8,128)(2,1)} %shard_map.100.c_ref.b_ref.x_ref.refs_0_.refs_1_.refs_2_, ...), custom_call_target="tpu_custom_call", output_to_operand_aliasing={{}: (9, {})} | custom-call | tf_op jit(solution)/shard_map/pallas_call | solution.py:201
  110.3 7.8 %all-to-all-done.1.refs_0_ = bf16[8,256,256]{2,1,0:T(8,128)(2,1)S(1)} async-done(((bf16[8,256,256]{2,1,0:T(8,128)(2,1)}), bf16[8,256,256]{2,1,0:T(8,128)(2,1)S(1)}, u32[]{:S(2)}, u32[]{:S(2)}) %all-to-all-start.1) | async-done | bytes 1048608 | tf_op jit(solution)/shard_map/all_to_all | solution.py:305
  118.1 1.0 copy-done.1
  119.1 1.4 convert_bitcast_fusion
  120.5 0.3 copy.76
  120.8 1.5 %select_convert_fusion.1 = (bf16[256,2048]{1,0:T(8,128)(2,1)S(1)}, bf16[256,2048]{1,0:T(8,128)(2,1)}) fusion(f32[256,2048]{1,0:T(8,128)S(1)} %bitcast.60, f32[257,2048]{1,0:T(8,128)S(1)} %get-tuple-element.12, f32[2048]{0:T(1024)S(1)} %bitcast.69, pred[]{:T(512)S(6)} %eq.24), kind=kLoop, calls=%fused_computation.8 | loop fusion | flops 3145728 | bytes 6299649 | tf_op jit(solution)/shard_map/convert_element_type | solution.py:308
  122.3 1.6 %collective-permute-start.2 = (bf16[256,2048]{1,0:T(8,128)(2,1)}, bf16[256,2048]{1,0:T(8,128)(2,1)S(1)}, u32[]{:S(2)}, u32[]{:S(2)}) collective-permute-start(bf16[256,2048]{1,0:T(8,128)(2,1)} %get-tuple-element.16), channel_id=1, source_target_pairs={{0,1},{1,0},{2,3},{3,2},{4,5},{5,4},{6,7},{7,6},{8,9},{9,8},{10,11... | collective-permute-start | bytes 3145736 | tf_op jit(solution)/shard_map/ppermute | solution.py:265
  124.1 2.3 %collective-permute-done.2 = bf16[256,2048]{1,0:T(8,128)(2,1)S(1)} collective-permute-done((bf16[256,2048]{1,0:T(8,128)(2,1)}, bf16[256,2048]{1,0:T(8,128)(2,1)S(1)}, u32[]{:S(2)}, u32[]{:S(2)}) %collective-permute-start.2) | collective-permute-done | bytes 1048608 | tf_op jit(solution)/shard_map/ppermute | solution.py:265
  126.4 2.2 %maximum_select_fusion.hin_ref = bf16[256,4096]{1,0:T(8,128)(2,1)} fusion(bf16[256,2048]{1,0:T(8,128)(2,1)S(1)} %collective-permute-done.2, bf16[256,2048]{1,0:T(8,128)(2,1)S(1)} %get-tuple-element.15, pred[]{:T(512)S(6)} %eq.24), kind=kLoop, calls=%fused_computation.5 | loop fusion | flops 9437184 | bytes 4194305 | tf_op jit(solution)/shard_map/jit(_where)/select_n | solution.py:310
  128.6 0.7 broadcast_in_dim.70.eb_ref
  129.3 13.4 %shard_map.107 = bf16[512,4096]{1,0:T(8,128)(2,1)} custom-call(bf16[512,5120]{1,0:T(8,128)(2,1)} %shard_map.100.c_ref.b_ref.x_ref.refs_0_.refs_1_.refs_2_, f32[512,4096]{1,0:T(8,128)} %shard_map.102.refs_1_.y_ref, bf16[512,4096]{1,0:T(8,128)(2,1)} %z_ref.1, bf16[256,4096]{1,0:T(8,128)(2,1)} %maximum_select_fusion.hin_ref, ...), custom_call_target="tpu_custom_call" | custom-call | tf_op jit(solution)/shard_map/pallas_call | solution.py:231
  (37 shorter events, 1.4 us)
Async XLA Ops:
  0.0 11.7 %copy-start.2 = (f32[4,5120]{1,0:T(4,128)S(1)}, f32[4,5120]{1,0:T(4,128)}, u32[]{:S(2)}) copy-start(f32[4,5120]{1,0:T(4,128)} %param.14) | copy-start | bytes 245764
  0.9 14.4 %collective-permute-start = (bf16[3,5120]{1,0:T(4,128)(2,1)S(1)}, bf16[3,5120]{1,0:T(4,128)(2,1)S(1)}, u32[]{:S(2)}, u32[]{:S(2)}) collective-permute-start(bf16[3,5120]{1,0:T(4,128)(2,1)S(1)} %slice.57), channel_id=1, source_target_pairs={{0,1},{1,2},{2,3},{3,4},{4,5},{5,6},{6,7},{7,8},{8,9},{9,10},{10,1... | collective-permute-start | bytes 92168 | tf_op jit(solution)/shard_map/ppermute | solution.py:23
  45.4 4.5 %collective-permute-start.1 = (f32[257,2048]{1,0:T(8,128)S(1)}, f32[257,2048]{1,0:T(8,128)}, u32[]{:S(2)}, u32[]{:S(2)}) collective-permute-start(f32[257,2048]{1,0:T(8,128)S(1)} %dynamic-slice_bitcast_fusion), channel_id=1, source_target_pairs={{0,1},{1,0},{2,3},{3,2},{4,5},{5,4},{6,7},{7,6},{8,9},{9,8},{10,11... | collective-permute-start | bytes 6316040 | tf_op jit(solution)/shard_map/ppermute | solution.py:265
  53.3 6.5 %copy-start.3 = (f32[64]{0:T(128)S(1)}, f32[64]{0:T(128)}, u32[]{:S(2)}) copy-start(f32[64]{0:T(128)} %param.18) | copy-start | bytes 772
  54.5 30.8 %all-to-all-start = ((bf16[8,258,256]{2,1,0:T(8,128)(2,1)}), bf16[8,258,256]{2,1,0:T(8,128)(2,1)S(1)}, u32[]{:S(2)}, u32[]{:S(2)}) async-start(bf16[8,258,256]{2,1,0:T(8,128)(2,1)} %bitcast.61), calls=%async_computation | async-start | bytes 2162688 | tf_op jit(solution)/shard_map/all_to_all | solution.py:299
  85.3 1.0 copy-start
  88.8 29.3 %all-to-all-start.1 = ((bf16[8,256,256]{2,1,0:T(8,128)(2,1)}), bf16[8,256,256]{2,1,0:T(8,128)(2,1)S(1)}, u32[]{:S(2)}, u32[]{:S(2)}) async-start(bf16[8,256,256]{2,1,0:T(8,128)(2,1)} %shard_map.105), calls=%async_computation.1 | async-start | bytes 2097152 | tf_op jit(solution)/shard_map/all_to_all | solution.py:305
  118.1 1.0 copy-start.1
  122.3 4.1 %collective-permute-start.2 = (bf16[256,2048]{1,0:T(8,128)(2,1)}, bf16[256,2048]{1,0:T(8,128)(2,1)S(1)}, u32[]{:S(2)}, u32[]{:S(2)}) collective-permute-start(bf16[256,2048]{1,0:T(8,128)(2,1)} %get-tuple-element.16), channel_id=1, source_target_pairs={{0,1},{1,0},{2,3},{3,2},{4,5},{5,4},{6,7},{7,6},{8,9},{9,8},{10,11... | collective-permute-start | bytes 3145736 | tf_op jit(solution)/shard_map/ppermute | solution.py:265

commit v13 on v12

--- a/solution.py
+++ b/solution.py
@@ -40,6 +40,10 @@
     out = jnp.dot(hi, spread, preferred_element_type=jnp.float32)
     out = out + jnp.dot(mid, spread, preferred_element_type=jnp.float32)
     return out + jnp.dot(lo, spread, preferred_element_type=jnp.float32)
+
+
+def silu(v):
+    return v * (0.5 + 0.5 * jnp.tanh(0.5 * v))
 
 
 CONV_COLS = 640
@@ -63,8 +67,8 @@
             top_term = jnp.where(rows8 < by, pltpu.roll(rim, by, 0), term[0:8])
         summed = summed + jnp.where(kept, term * wk, 0.0)
         top = top + jnp.where(kept[0:8], top_term * wk, 0.0)
-    out_ref[...] = jax.nn.silu(summed + bias_ref[...]).astype(jnp.bfloat16)
-    out_ref[0:8, :] = jax.nn.silu(top + bias_ref[...]).astype(jnp.bfloat16)
+    out_ref[...] = silu(summed + bias_ref[...]).astype(jnp.bfloat16)
+    out_ref[0:8, :] = silu(top + bias_ref[...]).astype(jnp.bfloat16)
 
 
 def conv_part(xbc, rim8, w8, bias, masks):
@@ -219,7 +223,7 @@
     inter = jnp.dot(c_ref[...], state.astype(jnp.bfloat16), preferred_element_type=jnp.float32)
     y = y_ref[...] + inter * expand_heads(in_weight)
     zf = z_ref[...].astype(jnp.float32)
-    gated = y * (zf * jax.nn.sigmoid(zf))
+    gated = y * silu(zf)
     mean_square = jnp.mean(gated * gated, axis=1, keepdims=True) + 1e-05
     out_ref[...] = (gated * lax.rsqrt(mean_square) * gain_ref[...]).astype(jnp.bfloat16)
 

time: 144 us -> 144 us (level)
  no operation moved by 1% of the time
where the time goes in v13:
time: 144 us; the launch traced here: 143 us
  Pallas kernels  76 us (53%)
  waiting for transfers between devices  21.3 us (15%)
  local copies, waits for them, and re-layouts  17.9 us (12%)
  starting transfers between devices  15 us (10%)
  other arithmetic  12.9 us (9%)
    pallas_call x2, Pallas kernels, intra_part(): pl.pallas_call(kernel, grid=(nb,), in_specs=specs, out_specs=pl.BlockSpec...  34.7 us
    pallas_call x1, Pallas kernels, mix(): pl.pallas_call(mix_kernel, grid=(nb, GROUPS), in_specs=[pl.BlockSpec((STR...  13.7 us
    pallas_call x1, Pallas kernels, block_states(): pl.pallas_call(state_kernel, grid=(GROUPS, nb), in_specs=[pl.BlockSpec((S...  12.9 us
    pallas_call x1, Pallas kernels, conv_part(): pl.pallas_call(conv_kernel, grid=(chans // CONV_COLS,), in_specs=[pl.Bloc...  12.2 us
    all_to_all x1, waiting for transfers between devices, compose(): lax.all_to_all(entering, 'chip', split_axis=0, concat_axis=0, tiled=True)  7.81 us
    all_to_all x1, waiting for transfers between devices, compose(): lax.all_to_all(payload, 'chip', split_axis=0, concat_axis=0, tiled=True)  6.76 us
    ppermute x2, waiting for transfers between devices, swap_cores(): return lax.ppermute(value, 'core', [(0, 1), (1, 0)])  6.71 us
    all_to_all x1, starting transfers between devices, compose(): lax.all_to_all(payload, 'chip', split_axis=0, concat_axis=0, tiled=True)  4.6 us
  transfers between devices with their start and end apart: 5, of which 4 were waited for; matrix products, arithmetic and copies ran while one was open for 8% of the time, Pallas kernels for 24%

profile of v13, /device:TPU:1, one launch (start us, length us, event | category | flops | bytes accessed | tf_op | source)
XLA Modules:
  0.0 143.3 jit_solution(13143962394939366565)
XLA Ops:
  0.0 0.9 slice.57
  0.9 4.5 %collective-permute-start = (bf16[3,5120]{1,0:T(4,128)(2,1)S(1)}, bf16[3,5120]{1,0:T(4,128)(2,1)S(1)}, u32[]{:S(2)}, u32[]{:S(2)}) collective-permute-start(bf16[3,5120]{1,0:T(4,128)(2,1)S(1)} %slice.57), channel_id=1, source_target_pairs={{0,1},{1,2},{2,3},{3,4},{4,5},{5,6},{6,7},{7,8},{8,9},{9,10},{10,1... | collective-permute-start | bytes 92168 | tf_op jit(solution)/shard_map/ppermute | solution.py:23
  5.5 0.8 reduce-window.18
  6.6 0.2 copy.59
  6.9 0.2 fusion.5
  7.2 0.7 exp.14
  7.8 1.0 negate_multiply_fusion
  8.9 1.2 reduce-window.19
  10.1 0.2 slice_reduce_fusion
  10.4 0.2 fusion.1
  10.6 0.2 compare_reduce_fusion
  10.9 0.7 pad_convert_fusion.m_ref
  11.7 0.7 concatenate.21.w_ref
  12.5 0.7 broadcast_in_dim_reshape.7.bdec_ref
  13.3 1.0 copy.65
  14.3 1.0 copy.60
  15.3 0.7 concatenate.20.rim_ref
  16.0 12.2 %shard_map.100.c_ref.b_ref.x_ref.refs_0_.refs_1_.refs_2_ = bf16[512,5120]{1,0:T(8,128)(2,1)} custom-call(bf16[512,5120]{1,0:T(8,128)(2,1)} %x_ref.1, bf16[8,5120]{1,0:T(8,128)(2,1)} %concatenate.20.rim_ref, f32[8,5120]{1,0:T(8,128)} %concatenate.21.w_ref, f32[1,5120]{1,0:T(1,128)} %bitcast.71, f32[512,128]{1,0:T(8,128)} %pad_convert_fusion.m_ref), custom_call_target="tpu_custom_call" | custom-call | tf_op jit(solution)/shard_map/pallas_call | solution.py:76
  28.2 1.1 slice.77
  29.3 1.0 copy.71
  30.3 0.8 broadcast_in_dim.33.segc_ref.refs_6_
  31.1 12.9 %shard_map.103 = (f32[2,256,4096]{2,1,0:T(8,128)}, f32[2,1,4096]{2,1,0:T(1,128)}, f32[2,257,2048]{2,1,0:T(8,128)}) custom-call(bf16[512,512]{1,0:T(8,128)(2,1)} %bitcast.64, bf16[512,5120]{1,0:T(8,128)(2,1)} %shard_map.100.c_ref.b_ref.x_ref.refs_0_.refs_1_.refs_2_, f32[2,512,32]{2,1,0:T(8,128)} %bitcast.57, f32[2,512,32]{2,1,0:T(8,128)} %bitcast.53, ...), custom_call_target="tpu_custom_call" | custom-call | tf_op jit(solution)/shard_map/pallas_call | solution.py:126
  44.0 1.7 %dynamic-slice_bitcast_fusion = f32[257,2048]{1,0:T(8,128)S(1)} fusion(f32[2,257,2048]{2,1,0:T(8,128)} %get-tuple-element.8, s32[]{:T(128)S(6)} %select_n.52), kind=kLoop, calls=%fused_computation.2 | loop fusion | bytes 4210692 | tf_op jit(solution)/shard_map/jit(dynamic_index_in_dim)/squeeze | solution.py:291
  45.8 4.4 %collective-permute-done.1 = f32[257,2048]{1,0:T(8,128)} collective-permute-done((f32[257,2048]{1,0:T(8,128)S(1)}, f32[257,2048]{1,0:T(8,128)}, u32[]{:S(2)}, u32[]{:S(2)}) %collective-permute-start.1) | collective-permute-done | bytes 2105376 | tf_op jit(solution)/shard_map/ppermute | solution.py:269
  50.2 2.6 %bitcast_select_fusion.1 = (f32[257,2048]{1,0:T(8,128)S(1)}, f32[257,2048]{1,0:T(8,128)S(1)}) fusion(f32[257,2048]{1,0:T(8,128)} %collective-permute-done.1, f32[2,257,2048]{2,1,0:T(8,128)} %get-tuple-element.8, s32[]{:T(128)S(6)} %select_n.53, pred[]{:T(512)S(6)} %eq.24), kind=kLoop, calls=%fused_computation.1 | loop fusion | flops 1052672 | bytes 8421381 | tf_op jit(solution)/shard_map/jit(_where)/select_n | solution.py:293
  52.8 0.4 fusion
  53.3 0.3 copy.77
  53.7 1.2 copy.84
  54.9 4.6 %all-to-all-start = ((bf16[8,258,256]{2,1,0:T(8,128)(2,1)}), bf16[8,258,256]{2,1,0:T(8,128)(2,1)S(1)}, u32[]{:S(2)}, u32[]{:S(2)}) async-start(bf16[8,258,256]{2,1,0:T(8,128)(2,1)} %bitcast.61), calls=%async_computation | async-start | bytes 2162688 | tf_op jit(solution)/shard_map/all_to_all | solution.py:303
  59.5 0.7 copy.75
  60.2 0.7 broadcast_in_dim_reshape.6.dsk_ref.refs_8_
  60.9 0.6 broadcast_in_dim.34.segr_ref.refs_7_
  61.5 17.4 %shard_map.101.refs_9_.refs_1_ = f32[512,4096]{1,0:T(8,128)} custom-call(bf16[512,5120]{1,0:T(8,128)(2,1)} %shard_map.100.c_ref.b_ref.x_ref.refs_0_.refs_1_.refs_2_, bf16[512,5120]{1,0:T(8,128)(2,1)} %shard_map.100.c_ref.b_ref.x_ref.refs_0_.refs_1_.refs_2_, bf16[512,5120]{1,0:T(8,128)(2,1)} %shard_map.100.c_ref.b_ref.x_ref.refs_0_.refs_1_.refs_2_, ...), custom_call_target="tpu_custom_call" | custom-call | tf_op jit(solution)/shard_map/pallas_call | solution.py:205
  78.9 6.8 %all-to-all-done.refs_0_ = bf16[8,258,256]{2,1,0:T(8,128)(2,1)S(1)} async-done(((bf16[8,258,256]{2,1,0:T(8,128)(2,1)}), bf16[8,258,256]{2,1,0:T(8,128)(2,1)S(1)}, u32[]{:S(2)}, u32[]{:S(2)}) %all-to-all-start) | async-done | bytes 1056800 | tf_op jit(solution)/shard_map/all_to_all | solution.py:303
  85.6 1.0 copy-done
  86.6 2.6 %shard_map.105 = bf16[8,256,256]{2,1,0:T(8,128)(2,1)} custom-call(bf16[8,258,256]{2,1,0:T(8,128)(2,1)} %shard_map.104.got_ref), custom_call_target="tpu_custom_call" | custom-call | tf_op jit(solution)/shard_map/pallas_call | solution.py:304
  89.2 4.1 %all-to-all-start.1 = ((bf16[8,256,256]{2,1,0:T(8,128)(2,1)}), bf16[8,256,256]{2,1,0:T(8,128)(2,1)S(1)}, u32[]{:S(2)}, u32[]{:S(2)}) async-start(bf16[8,256,256]{2,1,0:T(8,128)(2,1)} %shard_map.105), calls=%async_computation.1 | async-start | bytes 2097152 | tf_op jit(solution)/shard_map/all_to_all | solution.py:309
  93.3 17.3 %shard_map.102.refs_1_.y_ref = f32[512,4096]{1,0:T(8,128)} custom-call(bf16[512,5120]{1,0:T(8,128)(2,1)} %shard_map.100.c_ref.b_ref.x_ref.refs_0_.refs_1_.refs_2_, bf16[512,5120]{1,0:T(8,128)(2,1)} %shard_map.100.c_ref.b_ref.x_ref.refs_0_.refs_1_.refs_2_, ...), custom_call_target="tpu_custom_call", output_to_operand_aliasing={{}: (9, {})} | custom-call | tf_op jit(solution)/shard_map/pallas_call | solution.py:205
  110.7 7.8 %all-to-all-done.1.refs_0_ = bf16[8,256,256]{2,1,0:T(8,128)(2,1)S(1)} async-done(((bf16[8,256,256]{2,1,0:T(8,128)(2,1)}), bf16[8,256,256]{2,1,0:T(8,128)(2,1)S(1)}, u32[]{:S(2)}, u32[]{:S(2)}) %all-to-all-start.1) | async-done | bytes 1048608 | tf_op jit(solution)/shard_map/all_to_all | solution.py:309
  118.5 1.0 copy-done.1
  119.5 1.4 convert_bitcast_fusion
  120.9 0.3 copy.76
  121.2 1.5 %select_convert_fusion.1 = (bf16[256,2048]{1,0:T(8,128)(2,1)S(1)}, bf16[256,2048]{1,0:T(8,128)(2,1)}) fusion(f32[256,2048]{1,0:T(8,128)S(1)} %bitcast.60, f32[257,2048]{1,0:T(8,128)S(1)} %get-tuple-element.12, f32[2048]{0:T(1024)S(1)} %bitcast.69, pred[]{:T(512)S(6)} %eq.24), kind=kLoop, calls=%fused_computation.8 | loop fusion | flops 3145728 | bytes 6299649 | tf_op jit(solution)/shard_map/convert_element_type | solution.py:312
  122.7 1.6 %collective-permute-start.2 = (bf16[256,2048]{1,0:T(8,128)(2,1)}, bf16[256,2048]{1,0:T(8,128)(2,1)S(1)}, u32[]{:S(2)}, u32[]{:S(2)}) collective-permute-start(bf16[256,2048]{1,0:T(8,128)(2,1)} %get-tuple-element.16), channel_id=1, source_target_pairs={{0,1},{1,0},{2,3},{3,2},{4,5},{5,4},{6,7},{7,6},{8,9},{9,8},{10,11... | collective-permute-start | bytes 3145736 | tf_op jit(solution)/shard_map/ppermute | solution.py:269
  124.5 2.3 %collective-permute-done.2 = bf16[256,2048]{1,0:T(8,128)(2,1)S(1)} collective-permute-done((bf16[256,2048]{1,0:T(8,128)(2,1)}, bf16[256,2048]{1,0:T(8,128)(2,1)S(1)}, u32[]{:S(2)}, u32[]{:S(2)}) %collective-permute-start.2) | collective-permute-done | bytes 1048608 | tf_op jit(solution)/shard_map/ppermute | solution.py:269
  126.8 2.2 %maximum_select_fusion.hin_ref = bf16[256,4096]{1,0:T(8,128)(2,1)} fusion(bf16[256,2048]{1,0:T(8,128)(2,1)S(1)} %collective-permute-done.2, bf16[256,2048]{1,0:T(8,128)(2,1)S(1)} %get-tuple-element.15, pred[]{:T(512)S(6)} %eq.24), kind=kLoop, calls=%fused_computation.5 | loop fusion | flops 9437184 | bytes 4194305 | tf_op jit(solution)/shard_map/jit(_where)/select_n | solution.py:314
  129.0 0.7 broadcast_in_dim.70.eb_ref
  129.6 13.7 %shard_map.107 = bf16[512,4096]{1,0:T(8,128)(2,1)} custom-call(bf16[512,5120]{1,0:T(8,128)(2,1)} %shard_map.100.c_ref.b_ref.x_ref.refs_0_.refs_1_.refs_2_, f32[512,4096]{1,0:T(8,128)} %shard_map.102.refs_1_.y_ref, bf16[512,4096]{1,0:T(8,128)(2,1)} %z_ref.1, bf16[256,4096]{1,0:T(8,128)(2,1)} %maximum_select_fusion.hin_ref, ...), custom_call_target="tpu_custom_call" | custom-call | tf_op jit(solution)/shard_map/pallas_call | solution.py:235
  (37 shorter events, 1.4 us)
Async XLA Ops:
  0.0 11.7 %copy-start.2 = (f32[4,5120]{1,0:T(4,128)S(1)}, f32[4,5120]{1,0:T(4,128)}, u32[]{:S(2)}) copy-start(f32[4,5120]{1,0:T(4,128)} %param.14) | copy-start | bytes 245764
  0.9 14.4 %collective-permute-start = (bf16[3,5120]{1,0:T(4,128)(2,1)S(1)}, bf16[3,5120]{1,0:T(4,128)(2,1)S(1)}, u32[]{:S(2)}, u32[]{:S(2)}) collective-permute-start(bf16[3,5120]{1,0:T(4,128)(2,1)S(1)} %slice.57), channel_id=1, source_target_pairs={{0,1},{1,2},{2,3},{3,4},{4,5},{5,6},{6,7},{7,8},{8,9},{9,10},{10,1... | collective-permute-start | bytes 92168 | tf_op jit(solution)/shard_map/ppermute | solution.py:23
  45.7 4.5 %collective-permute-start.1 = (f32[257,2048]{1,0:T(8,128)S(1)}, f32[257,2048]{1,0:T(8,128)}, u32[]{:S(2)}, u32[]{:S(2)}) collective-permute-start(f32[257,2048]{1,0:T(8,128)S(1)} %dynamic-slice_bitcast_fusion), channel_id=1, source_target_pairs={{0,1},{1,0},{2,3},{3,2},{4,5},{5,4},{6,7},{7,6},{8,9},{9,8},{10,11... | collective-permute-start | bytes 6316040 | tf_op jit(solution)/shard_map/ppermute | solution.py:269
  53.7 6.5 %copy-start.3 = (f32[64]{0:T(128)S(1)}, f32[64]{0:T(128)}, u32[]{:S(2)}) copy-start(f32[64]{0:T(128)} %param.18) | copy-start | bytes 772
  54.9 30.8 %all-to-all-start = ((bf16[8,258,256]{2,1,0:T(8,128)(2,1)}), bf16[8,258,256]{2,1,0:T(8,128)(2,1)S(1)}, u32[]{:S(2)}, u32[]{:S(2)}) async-start(bf16[8,258,256]{2,1,0:T(8,128)(2,1)} %bitcast.61), calls=%async_computation | async-start | bytes 2162688 | tf_op jit(solution)/shard_map/all_to_all | solution.py:303
  85.6 1.0 copy-start
  89.2 29.3 %all-to-all-start.1 = ((bf16[8,256,256]{2,1,0:T(8,128)(2,1)}), bf16[8,256,256]{2,1,0:T(8,128)(2,1)S(1)}, u32[]{:S(2)}, u32[]{:S(2)}) async-start(bf16[8,256,256]{2,1,0:T(8,128)(2,1)} %shard_map.105), calls=%async_computation.1 | async-start | bytes 2097152 | tf_op jit(solution)/shard_map/all_to_all | solution.py:309
  118.5 1.0 copy-start.1
  122.7 4.1 %collective-permute-start.2 = (bf16[256,2048]{1,0:T(8,128)(2,1)}, bf16[256,2048]{1,0:T(8,128)(2,1)S(1)}, u32[]{:S(2)}, u32[]{:S(2)}) collective-permute-start(bf16[256,2048]{1,0:T(8,128)(2,1)} %get-tuple-element.16), channel_id=1, source_target_pairs={{0,1},{1,0},{2,3},{3,2},{4,5},{5,4},{6,7},{7,6},{8,9},{9,8},{10,11... | collective-permute-start | bytes 3145736 | tf_op jit(solution)/shard_map/ppermute | solution.py:269

commit v14 on v12

--- a/solution.py
+++ b/solution.py
@@ -116,35 +116,84 @@
         tot_ref[0, STATE : STATE + 1, :] = dec_ref[...]
 
 
-def block_states(bt, conv, dt_g, cum_g, segc, bdec):
+def half_state_kernel(
+    core_ref, bt_ref, x_ref, dt_ref, cum_ref, segc_ref, bdec_ref, *rest
+):
+    local_ref, cdec_ref, tot_ref, acc_ref, dec_ref = rest[-5:]
+    del core_ref
+    b = pl.program_id(0)
+
+    @pl.when(b == 0)
+    def _():
+        acc_ref[...] = jnp.zeros(acc_ref.shape, jnp.float32)
+        dec_ref[...] = jnp.ones(dec_ref.shape, jnp.float32)
+
+    local_ref[0] = acc_ref[...]
+    cdec_ref[0] = dec_ref[...]
+    cum = cum_ref[0]
+    step = dt_ref[0]
+    segc = segc_ref[:, 0:1]
+    last = cum[STRETCH - 1 : STRETCH, :]
+    seg_last = segc[STRETCH - 1 : STRETCH, :]
+    w = jnp.where(segc == seg_last, jnp.exp(last - cum), 0.0)
+    scaled = (x_ref[...].astype(jnp.float32) * expand_heads(step)).astype(jnp.bfloat16)
+    weighted = (scaled.astype(jnp.float32) * expand_heads(w)).astype(jnp.bfloat16)
+    block_state = jnp.dot(bt_ref[...], weighted, preferred_element_type=jnp.float32)
+    decay = bdec_ref[0]
+    acc_ref[...] = decay * acc_ref[...] + block_state
+    dec_ref[...] = dec_ref[...] * decay
+
+    @pl.when(b == pl.num_programs(0) - 1)
+    def _():
+        tot_ref[0:STATE, :] = acc_ref[...]
+        tot_ref[STATE : STATE + 1, :] = dec_ref[...]
+
+
+def half_states(bt, conv, dt_g, cum_g, segc, bdec, core_arr, which, prev=None):
     tok = conv.shape[0]
     nb = tok // STRETCH
-    return pl.pallas_call(
-        state_kernel,
-        grid=(GROUPS, nb),
-        in_specs=[
-            pl.BlockSpec((STATE, STRETCH), lambda g, b: (g, b)),
-            pl.BlockSpec((STRETCH, GROUP_COLS), lambda g, b: (b, g)),
-            pl.BlockSpec((1, STRETCH, PER_GROUP), lambda g, b: (g, b, 0)),
-            pl.BlockSpec((1, STRETCH, PER_GROUP), lambda g, b: (g, b, 0)),
-            pl.BlockSpec((STRETCH, 128), lambda g, b: (b, 0)),
-            pl.BlockSpec((1, 1, GROUP_COLS), lambda g, b: (b, 0, g)),
-        ],
+
+    def grp(c):
+        return (which + 1 + c[0]) % GROUPS
+
+    operands = [bt, conv, dt_g, cum_g, segc, bdec]
+    specs = [
+        pl.BlockSpec((STATE, STRETCH), lambda b, c: (grp(c), b)),
+        pl.BlockSpec((STRETCH, GROUP_COLS), lambda b, c: (b, grp(c))),
+        pl.BlockSpec((1, STRETCH, PER_GROUP), lambda b, c: (grp(c), b, 0)),
+        pl.BlockSpec((1, STRETCH, PER_GROUP), lambda b, c: (grp(c), b, 0)),
+        pl.BlockSpec((STRETCH, 128), lambda b, c: (b, 0)),
+        pl.BlockSpec((1, 1, GROUP_COLS), lambda b, c: (b, 0, grp(c))),
+    ]
+    aliases = {}
+    if prev is not None:
+        operands += list(prev)
+        specs += [pl.BlockSpec(memory_space=pl.ANY), pl.BlockSpec(memory_space=pl.ANY)]
+        aliases = {len(operands) - 1: 0, len(operands): 1}
+    grid_spec = pltpu.PrefetchScalarGridSpec(
+        num_scalar_prefetch=1,
+        grid=(nb,),
+        in_specs=specs,
         out_specs=[
-            pl.BlockSpec((1, STATE, GROUP_COLS), lambda g, b: (b, 0, g)),
-            pl.BlockSpec((1, 1, GROUP_COLS), lambda g, b: (b, 0, g)),
-            pl.BlockSpec((1, STATE + 1, GROUP_COLS), lambda g, b: (g, 0, 0)),
-        ],
-        out_shape=[
-            jax.ShapeDtypeStruct((nb, STATE, INNER), jnp.float32),
-            jax.ShapeDtypeStruct((nb, 1, INNER), jnp.float32),
-            jax.ShapeDtypeStruct((GROUPS, STATE + 1, GROUP_COLS), jnp.float32),
+            pl.BlockSpec((1, STATE, GROUP_COLS), lambda b, c: (b, 0, grp(c))),
+            pl.BlockSpec((1, 1, GROUP_COLS), lambda b, c: (b, 0, grp(c))),
+            pl.BlockSpec((STATE + 1, GROUP_COLS), lambda b, c: (0, 0)),
         ],
         scratch_shapes=[
             pltpu.VMEM((STATE, GROUP_COLS), jnp.float32),
             pltpu.VMEM((1, GROUP_COLS), jnp.float32),
         ],
-    )(bt, conv, dt_g, cum_g, segc, bdec)
+    )
+    return pl.pallas_call(
+        half_state_kernel,
+        grid_spec=grid_spec,
+        out_shape=[
+            jax.ShapeDtypeStruct((nb, STATE, INNER), jnp.float32),
+            jax.ShapeDtypeStruct((nb, 1, INNER), jnp.float32),
+            jax.ShapeDtypeStruct((STATE + 1, GROUP_COLS), jnp.float32),
+        ],
+        input_output_aliases=aliases,
+    )(core_arr, *operands)
 
 
 def intra_kernel(
@@ -278,13 +327,12 @@
     )(value, *after)
 
 
-def compose(both, first_work, second_work):
+def compose(for_other, mine, first_work, second_work):
     core = lax.axis_index("core")
     chips = lax.axis_size("chip")
     half = GROUP_COLS
     width = half // chips
-    mine = lax.dynamic_index_in_dim(both, core, 0, keepdims=False)
-    theirs = swap_cores(lax.dynamic_index_in_dim(both, 1 - core, 0, keepdims=False))
+    theirs = swap_cores(for_other)
     first = jnp.where(core == 0, mine, theirs)
     second = jnp.where(core == 0, theirs, mine)
     first_decay = first[STATE:]
@@ -350,7 +398,11 @@
     bt = conv[:, INNER : INNER + GROUPS * STATE].T
     bdec = jnp.repeat(block_decay, HEAD_DIM, axis=1)[:, None, :]
 
-    local_states, cdec, both = block_states(bt, conv, dt_g, cum_g, segc, bdec)
+    core_arr = lax.axis_index("core").astype(jnp.int32).reshape(1)
+    local_a, cdec_a, for_other = half_states(bt, conv, dt_g, cum_g, segc, bdec, core_arr, 0)
+    local_states, cdec, mine = half_states(
+        bt, conv, dt_g, cum_g, segc, bdec, core_arr, 1, (local_a, cdec_a)
+    )
     dsk = jnp.repeat(d_skip, HEAD_DIM)[None, :]
     def first_work():
         return intra_part(conv, dt_g, cum_g, cumt_g, segc, segr, dsk, 0)
@@ -358,7 +410,7 @@
     def second_work(done):
         return intra_part(conv, dt_g, cum_g, cumt_g, segc, segr, dsk, 1, done)
 
-    back, y_local = compose(both, first_work, second_work)
+    back, y_local = compose(for_other, mine, first_work, second_work)
     gain = norm_gain[None, :]
     return mix(conv, y_local, z_gate, back, local_states, cdec, cum_g, segc, eb, gain)
 

time: 144 us -> 142 us (0.986)
  waiting for transfers between devices: 21.3 us -> 16.6 us
  Pallas kernels: 75.4 us -> 78.6 us
    ppermute x2, waiting for transfers between devices: 6.71 us -> 2.35 us  [swap_cores(): return lax.ppermute(value, 'core', [(0, 1), (1, 0)])]
    pallas_call x1 -> x2, Pallas kernels: 12.9 us -> 16.1 us  [half_states(): pl.pallas_call(half_state_kernel, grid_spec=grid_spec, out_shape=[jax.Sha...]
    squeeze x1 -> x0, local copies, waits for them, and re-layouts: 1.75 us -> none  [compose(): lax.dynamic_index_in_dim(both, 1 - core, 0, keepdims=False)]
    unnamed x10 -> x12, local copies, waits for them, and re-layouts: 3.26 us -> 4.63 us
  transfers between devices with their start and end apart: 5 -> 5, of which waited for: 4 -> 3; matrix products, arithmetic and copies ran while one was open for 8% -> 8% of each run, Pallas kernels for 24% -> 30%
where the time goes in v14:
time: 142 us; the launch traced here: 141 us
  Pallas kernels  78.6 us (55%)
  local copies, waits for them, and re-layouts  17.5 us (12%)
  waiting for transfers between devices  16.6 us (12%)
  starting transfers between devices  15.1 us (11%)
  other arithmetic  12.9 us (9%)
    pallas_call x2, Pallas kernels, intra_part(): pl.pallas_call(kernel, grid=(nb,), in_specs=specs, out_specs=pl.BlockSpec...  34.7 us
    pallas_call x2, Pallas kernels, half_states(): pl.pallas_call(half_state_kernel, grid_spec=grid_spec, out_shape=[jax.Sha...  16.1 us
    pallas_call x1, Pallas kernels, mix(): pl.pallas_call(mix_kernel, grid=(nb, GROUPS), in_specs=[pl.BlockSpec((STR...  13.5 us
    pallas_call x1, Pallas kernels, conv_part(): pl.pallas_call(conv_kernel, grid=(chans // CONV_COLS,), in_specs=[pl.Bloc...  11.8 us
    all_to_all x1, waiting for transfers between devices, compose(): lax.all_to_all(entering, 'chip', split_axis=0, concat_axis=0, tiled=True)  7.79 us
    all_to_all x1, waiting for transfers between devices, compose(): lax.all_to_all(payload, 'chip', split_axis=0, concat_axis=0, tiled=True)  6.51 us
    unnamed x12, local copies, waits for them, and re-layouts  4.63 us
    all_to_all x1, starting transfers between devices, compose(): lax.all_to_all(payload, 'chip', split_axis=0, concat_axis=0, tiled=True)  4.6 us
  transfers between devices with their start and end apart: 5, of which 3 were waited for; matrix products, arithmetic and copies ran while one was open for 8% of the time, Pallas kernels for 30%

profile of v14, /device:TPU:1, one launch (start us, length us, event | category | flops | bytes accessed | tf_op | source)
XLA Modules:
  0.0 141.1 jit_solution(5004173248004850348)
XLA Ops:
  0.0 0.9 slice.57
  0.9 4.5 %collective-permute-start = (bf16[3,5120]{1,0:T(4,128)(2,1)S(1)}, bf16[3,5120]{1,0:T(4,128)(2,1)S(1)}, u32[]{:S(2)}, u32[]{:S(2)}) collective-permute-start(bf16[3,5120]{1,0:T(4,128)(2,1)S(1)} %slice.57), channel_id=1, source_target_pairs={{0,1},{1,2},{2,3},{3,4},{4,5},{5,6},{6,7},{7,8},{8,9},{9,10},{10,1... | collective-permute-start | bytes 92168 | tf_op jit(solution)/shard_map/ppermute | solution.py:23
  5.5 0.8 reduce-window.18
  6.6 0.2 copy.61
  6.9 0.2 fusion.5
  7.2 0.7 exp.14
  7.8 1.0 negate_multiply_fusion
  8.9 1.2 reduce-window.19
  10.1 0.2 slice_reduce_fusion
  10.4 0.2 fusion.1
  10.6 0.2 compare_reduce_fusion
  10.9 0.7 pad_convert_fusion.m_ref
  11.7 0.7 concatenate.21.w_ref
  12.5 0.7 broadcast_in_dim_reshape.7.bdec_ref
  13.3 1.0 copy.67
  14.3 1.0 copy.62
  15.3 0.7 concatenate.20.rim_ref
  16.0 11.8 %shard_map.100.c_ref.b_ref.x_ref.refs_0_.refs_1_.refs_2_ = bf16[512,5120]{1,0:T(8,128)(2,1)} custom-call(bf16[512,5120]{1,0:T(8,128)(2,1)} %x_ref.1, bf16[8,5120]{1,0:T(8,128)(2,1)} %concatenate.20.rim_ref, f32[8,5120]{1,0:T(8,128)} %concatenate.21.w_ref, f32[1,5120]{1,0:T(1,128)} %bitcast.70, f32[512,128]{1,0:T(8,128)} %pad_convert_fusion.m_ref), custom_call_target="tpu_custom_call" | custom-call | tf_op jit(solution)/shard_map/pallas_call | solution.py:72
  27.8 1.1 slice.77
  28.9 1.0 copy.73
  29.9 0.8 broadcast_in_dim.33.segc_ref.refs_6_
  30.7 8.0 %shard_map.103 = (f32[2,256,4096]{2,1,0:T(8,128)}, f32[2,1,4096]{2,1,0:T(1,128)}, f32[257,2048]{1,0:T(8,128)}) custom-call(s32[1]{0:T(128)} %bitcast.11.core_ref, bf16[512,512]{1,0:T(8,128)(2,1)} %bitcast.59, bf16[512,5120]{1,0:T(8,128)(2,1)} %shard_map.100.c_ref.b_ref.x_ref.refs_0_.refs_1_.refs_2_, f32[2,512,32]{2,1,0:T(8,128)} %bitcast.54, ...), custom_call_target="tpu_custom_call" | custom-call | tf_op jit(solution)/shard_map/pallas_call | solution.py:187
  38.7 8.1 %shard_map.104 = (f32[2,256,4096]{2,1,0:T(8,128)}, f32[2,1,4096]{2,1,0:T(1,128)}, f32[257,2048]{1,0:T(8,128)}) custom-call(s32[1]{0:T(128)} %bitcast.11.core_ref, bf16[512,512]{1,0:T(8,128)(2,1)} %bitcast.60, bf16[512,5120]{1,0:T(8,128)(2,1)} %shard_map.100.c_ref.b_ref.x_ref.refs_0_.refs_1_.refs_2_, ...), custom_call_target="tpu_custom_call", output_to_operand_aliasing={{0}: (7, {}), {1}: (8, {})} | custom-call | tf_op jit(solution)/shard_map/pallas_call | solution.py:187
  46.8 1.3 copy-done.2
  48.2 2.6 %broadcast_select_fusion.1 = (f32[257,2048]{1,0:T(8,128)S(1)}, f32[257,2048]{1,0:T(8,128)S(1)}) fusion(f32[257,2048]{1,0:T(8,128)} %copy-done.2, f32[257,2048]{1,0:T(8,128)} %get-tuple-element.14, pred[]{:T(512)S(6)} %eq.24), kind=kLoop, calls=%fused_computation.10 | loop fusion | flops 1052672 | bytes 8421377 | tf_op jit(solution)/shard_map/jit(_where)/select_n | solution.py:337
  50.8 0.4 fusion
  51.3 0.3 copy.79
  51.7 1.2 copy.86
  52.9 4.6 %all-to-all-start = ((bf16[8,258,256]{2,1,0:T(8,128)(2,1)}), bf16[8,258,256]{2,1,0:T(8,128)(2,1)S(1)}, u32[]{:S(2)}, u32[]{:S(2)}) async-start(bf16[8,258,256]{2,1,0:T(8,128)(2,1)} %bitcast.61), calls=%async_computation | async-start | bytes 2162688 | tf_op jit(solution)/shard_map/all_to_all | solution.py:347
  57.5 0.7 copy.77
  58.2 0.7 broadcast_in_dim_reshape.6.dsk_ref.refs_8_
  58.9 0.6 broadcast_in_dim.34.segr_ref.refs_7_
  59.5 17.4 %shard_map.101.refs_9_.refs_1_ = f32[512,4096]{1,0:T(8,128)} custom-call(bf16[512,5120]{1,0:T(8,128)(2,1)} %shard_map.100.c_ref.b_ref.x_ref.refs_0_.refs_1_.refs_2_, bf16[512,5120]{1,0:T(8,128)(2,1)} %shard_map.100.c_ref.b_ref.x_ref.refs_0_.refs_1_.refs_2_, bf16[512,5120]{1,0:T(8,128)(2,1)} %shard_map.100.c_ref.b_ref.x_ref.refs_0_.refs_1_.refs_2_, ...), custom_call_target="tpu_custom_call" | custom-call | tf_op jit(solution)/shard_map/pallas_call | solution.py:250
  76.9 6.5 %all-to-all-done.refs_0_ = bf16[8,258,256]{2,1,0:T(8,128)(2,1)S(1)} async-done(((bf16[8,258,256]{2,1,0:T(8,128)(2,1)}), bf16[8,258,256]{2,1,0:T(8,128)(2,1)S(1)}, u32[]{:S(2)}, u32[]{:S(2)}) %all-to-all-start) | async-done | bytes 1056800 | tf_op jit(solution)/shard_map/all_to_all | solution.py:347
  83.4 1.0 copy-done
  84.4 2.6 %shard_map.106 = bf16[8,256,256]{2,1,0:T(8,128)(2,1)} custom-call(bf16[8,258,256]{2,1,0:T(8,128)(2,1)} %shard_map.105.got_ref), custom_call_target="tpu_custom_call" | custom-call | tf_op jit(solution)/shard_map/pallas_call | solution.py:348
  86.9 4.4 %all-to-all-start.1 = ((bf16[8,256,256]{2,1,0:T(8,128)(2,1)}), bf16[8,256,256]{2,1,0:T(8,128)(2,1)S(1)}, u32[]{:S(2)}, u32[]{:S(2)}) async-start(bf16[8,256,256]{2,1,0:T(8,128)(2,1)} %shard_map.106), calls=%async_computation.1 | async-start | bytes 2097152 | tf_op jit(solution)/shard_map/all_to_all | solution.py:353
  91.3 17.3 %shard_map.102.refs_1_.y_ref = f32[512,4096]{1,0:T(8,128)} custom-call(bf16[512,5120]{1,0:T(8,128)(2,1)} %shard_map.100.c_ref.b_ref.x_ref.refs_0_.refs_1_.refs_2_, bf16[512,5120]{1,0:T(8,128)(2,1)} %shard_map.100.c_ref.b_ref.x_ref.refs_0_.refs_1_.refs_2_, ...), custom_call_target="tpu_custom_call", output_to_operand_aliasing={{}: (9, {})} | custom-call | tf_op jit(solution)/shard_map/pallas_call | solution.py:250
  108.7 7.8 %all-to-all-done.1.refs_0_ = bf16[8,256,256]{2,1,0:T(8,128)(2,1)S(1)} async-done(((bf16[8,256,256]{2,1,0:T(8,128)(2,1)}), bf16[8,256,256]{2,1,0:T(8,128)(2,1)S(1)}, u32[]{:S(2)}, u32[]{:S(2)}) %all-to-all-start.1) | async-done | bytes 1048608 | tf_op jit(solution)/shard_map/all_to_all | solution.py:353
  116.5 1.0 copy-done.1
  117.4 1.4 convert_bitcast_fusion
  118.8 0.3 copy.78
  119.1 1.5 %select_convert_fusion.1 = (bf16[256,2048]{1,0:T(8,128)(2,1)S(1)}, bf16[256,2048]{1,0:T(8,128)(2,1)}) fusion(f32[256,2048]{1,0:T(8,128)S(1)} %bitcast.58, f32[257,2048]{1,0:T(8,128)S(1)} %get-tuple-element.20, f32[2048]{0:T(1024)S(1)} %bitcast.68, pred[]{:T(512)S(6)} %eq.24), kind=kLoop, calls=%fused_computation.5 | loop fusion | flops 3145728 | bytes 6299649 | tf_op jit(solution)/shard_map/convert_element_type | solution.py:356
  120.7 1.6 %collective-permute-start.2 = (bf16[256,2048]{1,0:T(8,128)(2,1)}, bf16[256,2048]{1,0:T(8,128)(2,1)S(1)}, u32[]{:S(2)}, u32[]{:S(2)}) collective-permute-start(bf16[256,2048]{1,0:T(8,128)(2,1)} %get-tuple-element.22), channel_id=1, source_target_pairs={{0,1},{1,0},{2,3},{3,2},{4,5},{5,4},{6,7},{7,6},{8,9},{9,8},{10,11... | collective-permute-start | bytes 3145736 | tf_op jit(solution)/shard_map/ppermute | solution.py:314
  122.4 2.3 %collective-permute-done.2 = bf16[256,2048]{1,0:T(8,128)(2,1)S(1)} collective-permute-done((bf16[256,2048]{1,0:T(8,128)(2,1)}, bf16[256,2048]{1,0:T(8,128)(2,1)S(1)}, u32[]{:S(2)}, u32[]{:S(2)}) %collective-permute-start.2) | collective-permute-done | bytes 1048608 | tf_op jit(solution)/shard_map/ppermute | solution.py:314
  124.8 2.2 %maximum_select_fusion.hin_ref = bf16[256,4096]{1,0:T(8,128)(2,1)} fusion(bf16[256,2048]{1,0:T(8,128)(2,1)S(1)} %collective-permute-done.2, bf16[256,2048]{1,0:T(8,128)(2,1)S(1)} %get-tuple-element.21, pred[]{:T(512)S(6)} %eq.24), kind=kLoop, calls=%fused_computation.2 | loop fusion | flops 9437184 | bytes 4194305 | tf_op jit(solution)/shard_map/jit(_where)/select_n | solution.py:358
  126.9 0.7 broadcast_in_dim.70.eb_ref
  127.6 13.5 %shard_map.108 = bf16[512,4096]{1,0:T(8,128)(2,1)} custom-call(bf16[512,5120]{1,0:T(8,128)(2,1)} %shard_map.100.c_ref.b_ref.x_ref.refs_0_.refs_1_.refs_2_, f32[512,4096]{1,0:T(8,128)} %shard_map.102.refs_1_.y_ref, bf16[512,4096]{1,0:T(8,128)(2,1)} %z_ref.1, bf16[256,4096]{1,0:T(8,128)(2,1)} %maximum_select_fusion.hin_ref, ...), custom_call_target="tpu_custom_call" | custom-call | tf_op jit(solution)/shard_map/pallas_call | solution.py:280
  (39 shorter events, 1.4 us)
Async XLA Ops:
  0.0 11.7 %copy-start.3 = (f32[4,5120]{1,0:T(4,128)S(1)}, f32[4,5120]{1,0:T(4,128)}, u32[]{:S(2)}) copy-start(f32[4,5120]{1,0:T(4,128)} %param.14) | copy-start | bytes 245764
  0.9 14.4 %collective-permute-start = (bf16[3,5120]{1,0:T(4,128)(2,1)S(1)}, bf16[3,5120]{1,0:T(4,128)(2,1)S(1)}, u32[]{:S(2)}, u32[]{:S(2)}) collective-permute-start(bf16[3,5120]{1,0:T(4,128)(2,1)S(1)} %slice.57), channel_id=1, source_target_pairs={{0,1},{1,2},{2,3},{3,4},{4,5},{5,6},{6,7},{7,8},{8,9},{9,10},{10,1... | collective-permute-start | bytes 92168 | tf_op jit(solution)/shard_map/ppermute | solution.py:23
  38.7 8.1 %collective-permute-start.1 = (f32[257,2048]{1,0:T(8,128)}, f32[257,2048]{1,0:T(8,128)S(1)}, u32[]{:S(2)}, u32[]{:S(2)}) collective-permute-start(f32[257,2048]{1,0:T(8,128)} %get-tuple-element.11), channel_id=1, source_target_pairs={{0,1},{1,0},{2,3},{3,2},{4,5},{5,4},{6,7},{7,6},{8,9},{9,8},{10,11... | collective-permute-start | bytes 6316040 | tf_op jit(solution)/shard_map/ppermute | solution.py:314
  46.8 1.3 copy-start.2
  51.7 6.5 %copy-start.4 = (f32[64]{0:T(128)S(1)}, f32[64]{0:T(128)}, u32[]{:S(2)}) copy-start(f32[64]{0:T(128)} %param.18) | copy-start | bytes 772
  52.9 30.5 %all-to-all-start = ((bf16[8,258,256]{2,1,0:T(8,128)(2,1)}), bf16[8,258,256]{2,1,0:T(8,128)(2,1)S(1)}, u32[]{:S(2)}, u32[]{:S(2)}) async-start(bf16[8,258,256]{2,1,0:T(8,128)(2,1)} %bitcast.61), calls=%async_computation | async-start | bytes 2162688 | tf_op jit(solution)/shard_map/all_to_all | solution.py:347
  83.4 1.0 copy-start
  86.9 29.5 %all-to-all-start.1 = ((bf16[8,256,256]{2,1,0:T(8,128)(2,1)}), bf16[8,256,256]{2,1,0:T(8,128)(2,1)S(1)}, u32[]{:S(2)}, u32[]{:S(2)}) async-start(bf16[8,256,256]{2,1,0:T(8,128)(2,1)} %shard_map.106), calls=%async_computation.1 | async-start | bytes 2097152 | tf_op jit(solution)/shard_map/all_to_all | solution.py:353
  116.5 1.0 copy-start.1
  120.7 4.1 %collective-permute-start.2 = (bf16[256,2048]{1,0:T(8,128)(2,1)}, bf16[256,2048]{1,0:T(8,128)(2,1)S(1)}, u32[]{:S(2)}, u32[]{:S(2)}) collective-permute-start(bf16[256,2048]{1,0:T(8,128)(2,1)} %get-tuple-element.22), channel_id=1, source_target_pairs={{0,1},{1,0},{2,3},{3,2},{4,5},{5,4},{6,7},{7,6},{8,9},{9,8},{10,11... | collective-permute-start | bytes 3145736 | tf_op jit(solution)/shard_map/ppermute | solution.py:314

commit v15 on v14

--- a/solution.py
+++ b/solution.py
@@ -273,28 +273,54 @@
     out_ref[...] = (gated * lax.rsqrt(mean_square) * gain_ref[...]).astype(jnp.bfloat16)
 
 
-def mix(conv, y_local, z_gate, back, local_states, cdec, cum_g, segc, eb, gain):
+def mix(conv, y_local, z_gate, hin, local_states, cdec, cum_g, segc, eb, gain, core_arr, which,
+        prev=None):
     tok = conv.shape[0]
     nb = tok // STRETCH
     c_col = INNER // STATE + GROUPS
+
+    def grp(c):
+        return (which + c[0]) % GROUPS
+
+    operands = [conv, y_local, z_gate, hin, local_states, cdec, cum_g, segc, eb, gain]
+    specs = [
+        pl.BlockSpec((STRETCH, STATE), lambda b, c: (b, c_col + grp(c))),
+        pl.BlockSpec((STRETCH, GROUP_COLS), lambda b, c: (b, grp(c))),
+        pl.BlockSpec((STRETCH, GROUP_COLS), lambda b, c: (b, grp(c))),
+        pl.BlockSpec((STATE, GROUP_COLS), lambda b, c: (0, 0)),
+        pl.BlockSpec((1, STATE, GROUP_COLS), lambda b, c: (b, 0, grp(c))),
+        pl.BlockSpec((1, 1, GROUP_COLS), lambda b, c: (b, 0, grp(c))),
+        pl.BlockSpec((1, STRETCH, PER_GROUP), lambda b, c: (grp(c), b, 0)),
+        pl.BlockSpec((STRETCH, 128), lambda b, c: (b, 0)),
+        pl.BlockSpec((8, 128), lambda b, c: (b, 0)),
+        pl.BlockSpec((1, GROUP_COLS), lambda b, c: (0, grp(c))),
+    ]
+    kernel = mix_kernel
+    aliases = {}
+    if prev is not None:
+        operands.append(prev)
+        specs.append(pl.BlockSpec(memory_space=pl.ANY))
+        aliases = {len(operands): 0}
+
+        def kernel(*refs):
+            mix_kernel(*refs[:-2], refs[-1])
+
+    def with_core(core_ref, *refs):
+        del core_ref
+        kernel(*refs)
+
+    grid_spec = pltpu.PrefetchScalarGridSpec(
+        num_scalar_prefetch=1,
+        grid=(nb,),
+        in_specs=specs,
+        out_specs=pl.BlockSpec((STRETCH, GROUP_COLS), lambda b, c: (b, grp(c))),
+    )
     return pl.pallas_call(
-        mix_kernel,
-        grid=(nb, GROUPS),
-        in_specs=[
-            pl.BlockSpec((STRETCH, STATE), lambda b, g: (b, c_col + g)),
-            pl.BlockSpec((STRETCH, GROUP_COLS), lambda b, g: (b, g)),
-            pl.BlockSpec((STRETCH, GROUP_COLS), lambda b, g: (b, g)),
-            pl.BlockSpec((STATE, GROUP_COLS), lambda b, g: (0, g)),
-            pl.BlockSpec((1, STATE, GROUP_COLS), lambda b, g: (b, 0, g)),
-            pl.BlockSpec((1, 1, GROUP_COLS), lambda b, g: (b, 0, g)),
-            pl.BlockSpec((1, STRETCH, PER_GROUP), lambda b, g: (g, b, 0)),
-            pl.BlockSpec((STRETCH, 128), lambda b, g: (b, 0)),
-            pl.BlockSpec((8, 128), lambda b, g: (b, 0)),
-            pl.BlockSpec((1, GROUP_COLS), lambda b, g: (0, g)),
-        ],
-        out_specs=pl.BlockSpec((STRETCH, GROUP_COLS), lambda b, g: (b, g)),
+        with_core,
+        grid_spec=grid_spec,
         out_shape=jax.ShapeDtypeStruct((tok, INNER), jnp.bfloat16),
-    )(conv, y_local, z_gate, back, local_states, cdec, cum_g, segc, eb, gain)
+        input_output_aliases=aliases,
+    )(core_arr, *operands)
 
 
 def scan_kernel(got_ref, out_ref):
@@ -355,12 +381,7 @@
     later_in = first_decay * chip_in + first[:STATE]
     keep = jnp.where(core == 0, chip_in, later_in).astype(jnp.bfloat16)
     other = swap_cores(jnp.where(core == 0, later_in, chip_in).astype(jnp.bfloat16))
-    hin = jnp.where(
-        core == 0,
-        jnp.concatenate([keep, other], axis=1),
-        jnp.concatenate([other, keep], axis=1),
-    )
-    return hin, work
+    return keep, other, work
 
 
 def local(xbc, z_gate, dt_raw, lengths, conv_weight, conv_bias, dt_bias, a_log, d_skip, norm_gain):
@@ -410,9 +431,12 @@
     def second_work(done):
         return intra_part(conv, dt_g, cum_g, cumt_g, segc, segr, dsk, 1, done)
 
-    back, y_local = compose(for_other, mine, first_work, second_work)
+    keep, other, y_local = compose(for_other, mine, first_work, second_work)
     gain = norm_gain[None, :]
-    return mix(conv, y_local, z_gate, back, local_states, cdec, cum_g, segc, eb, gain)
+    parts = (y_local, z_gate)
+    rest = (local_states, cdec, cum_g, segc, eb, gain, core_arr)
+    out = mix(conv, *parts, keep, *rest, 0)
+    return mix(conv, *parts, other, *rest, 1, out)
 
 
 def solution(mesh):

time: 142 us -> 140 us (0.986)
  waiting for transfers between devices: 16.6 us -> 14.2 us
  other arithmetic: 12.9 us -> 10.7 us
  Pallas kernels: 78.6 us -> 80.7 us
    ppermute x2, waiting for transfers between devices: 2.35 us -> 0.01 us  [swap_cores(): return lax.ppermute(value, 'core', [(0, 1), (1, 0)])]
    select_n x2 -> x1, other arithmetic: 4.76 us -> 2.6 us  [compose(): first = jnp.where(core == 0, mine, theirs)]
    pallas_call x1 -> x2, Pallas kernels: 13.5 us -> 15.5 us  [mix(): pl.pallas_call(with_core, grid_spec=grid_spec, out_shape=jax.ShapeDtypeSt...]
    unnamed x12 -> x14, local copies, waits for them, and re-layouts: 4.63 us -> 5.62 us
  transfers between devices with their start and end apart: 5 -> 5, of which waited for: 3 -> 2; matrix products, arithmetic and copies ran while one was open for 8% -> 9% of each run, Pallas kernels for 30% -> 36%
where the time goes in v15:
time: 140 us
  Pallas kernels  80.7 us (58%)
  local copies, waits for them, and re-layouts  18.6 us (13%)
  starting transfers between devices  15.1 us (11%)
  waiting for transfers between devices  14.2 us (10%)
  other arithmetic  10.7 us (8%)
    pallas_call x2, Pallas kernels, intra_part(): pl.pallas_call(kernel, grid=(nb,), in_specs=specs, out_specs=pl.BlockSpec...  34.8 us
    pallas_call x2, Pallas kernels, half_states(): pl.pallas_call(half_state_kernel, grid_spec=grid_spec, out_shape=[jax.Sha...  16 us
    pallas_call x2, Pallas kernels, mix(): pl.pallas_call(with_core, grid_spec=grid_spec, out_shape=jax.ShapeDtypeSt...  15.5 us
    pallas_call x1, Pallas kernels, conv_part(): pl.pallas_call(conv_kernel, grid=(chans // CONV_COLS,), in_specs=[pl.Bloc...  11.8 us
    all_to_all x1, waiting for transfers between devices, compose(): lax.all_to_all(entering, 'chip', split_axis=0, concat_axis=0, tiled=True)  7.66 us
    all_to_all x1, waiting for transfers between devices, compose(): lax.all_to_all(payload, 'chip', split_axis=0, concat_axis=0, tiled=True)  6.49 us
    unnamed x14, local copies, waits for them, and re-layouts  5.62 us
    all_to_all x1, starting transfers between devices, compose(): lax.all_to_all(payload, 'chip', split_axis=0, concat_axis=0, tiled=True)  4.6 us
  transfers between devices with their start and end apart: 5, of which 2 were waited for; matrix products, arithmetic and copies ran while one was open for 9% of the time, Pallas kernels for 36%

profile of v15, /device:TPU:1, one launch (start us, length us, event | category | flops | bytes accessed | tf_op | source)
XLA Modules:
  0.0 139.6 jit_solution(5672894725958294301)
XLA Ops:
  0.0 0.9 slice.57
  0.9 4.5 %collective-permute-start = (bf16[3,5120]{1,0:T(4,128)(2,1)S(1)}, bf16[3,5120]{1,0:T(4,128)(2,1)S(1)}, u32[]{:S(2)}, u32[]{:S(2)}) collective-permute-start(bf16[3,5120]{1,0:T(4,128)(2,1)S(1)} %slice.57), channel_id=1, source_target_pairs={{0,1},{1,2},{2,3},{3,4},{4,5},{5,6},{6,7},{7,8},{8,9},{9,10},{10,1... | collective-permute-start | bytes 92168 | tf_op jit(solution)/shard_map/ppermute | solution.py:23
  5.5 0.8 reduce-window.18
  6.6 0.2 copy.62
  6.9 0.2 fusion.5
  7.2 0.7 exp.14
  7.8 1.0 negate_multiply_fusion
  8.9 1.2 reduce-window.19
  10.1 0.2 slice_reduce_fusion
  10.4 0.2 fusion.1
  10.6 0.2 compare_reduce_fusion
  10.9 0.7 pad_convert_fusion.m_ref
  11.7 0.7 concatenate.15.w_ref
  12.5 0.7 broadcast_in_dim_reshape.7.bdec_ref
  13.3 1.0 copy.68
  14.3 1.0 copy.63
  15.3 0.7 concatenate.14.rim_ref
  16.0 11.8 %shard_map.100.c_ref.b_ref.x_ref.refs_0_.refs_1_.refs_2_ = bf16[512,5120]{1,0:T(8,128)(2,1)} custom-call(bf16[512,5120]{1,0:T(8,128)(2,1)} %x_ref.1, bf16[8,5120]{1,0:T(8,128)(2,1)} %concatenate.14.rim_ref, f32[8,5120]{1,0:T(8,128)} %concatenate.15.w_ref, f32[1,5120]{1,0:T(1,128)} %bitcast.73, f32[512,128]{1,0:T(8,128)} %pad_convert_fusion.m_ref), custom_call_target="tpu_custom_call" | custom-call | tf_op jit(solution)/shard_map/pallas_call | solution.py:72
  27.8 1.1 slice.77
  28.9 1.0 copy.74
  29.9 0.8 broadcast_in_dim.33.segc_ref.refs_6_.refs_7_
  30.8 8.0 %shard_map.103 = (f32[2,256,4096]{2,1,0:T(8,128)}, f32[2,1,4096]{2,1,0:T(1,128)}, f32[257,2048]{1,0:T(8,128)}) custom-call(s32[1]{0:T(128)} %bitcast.core_ref, bf16[512,512]{1,0:T(8,128)(2,1)} %bitcast.60, bf16[512,5120]{1,0:T(8,128)(2,1)} %shard_map.100.c_ref.b_ref.x_ref.refs_0_.refs_1_.refs_2_, f32[2,512,32]{2,1,0:T(8,128)} %bitcast.55, ...), custom_call_target="tpu_custom_call" | custom-call | tf_op jit(solution)/shard_map/pallas_call | solution.py:187
  38.8 8.0 %shard_map.104 = (f32[2,256,4096]{2,1,0:T(8,128)}, f32[2,1,4096]{2,1,0:T(1,128)}, f32[257,2048]{1,0:T(8,128)}) custom-call(s32[1]{0:T(128)} %bitcast.core_ref, bf16[512,512]{1,0:T(8,128)(2,1)} %bitcast.61, bf16[512,5120]{1,0:T(8,128)(2,1)} %shard_map.100.c_ref.b_ref.x_ref.refs_0_.refs_1_.refs_2_, ...), custom_call_target="tpu_custom_call", output_to_operand_aliasing={{0}: (7, {}), {1}: (8, {})} | custom-call | tf_op jit(solution)/shard_map/pallas_call | solution.py:187
  46.8 1.3 copy-done.2
  48.1 2.6 %broadcast_select_fusion.1 = (f32[257,2048]{1,0:T(8,128)S(1)}, f32[257,2048]{1,0:T(8,128)S(1)}) fusion(f32[257,2048]{1,0:T(8,128)} %get-tuple-element.13, f32[257,2048]{1,0:T(8,128)} %copy-done.2, pred[]{:T(512)S(6)} %eq.23), kind=kLoop, calls=%fused_computation.9 | loop fusion | flops 1052672 | bytes 8421377 | tf_op jit(solution)/shard_map/jit(_where)/select_n | solution.py:362
  50.8 0.4 fusion
  51.3 0.3 copy.80
  51.7 1.2 copy.87
  52.8 4.6 %all-to-all-start = ((bf16[8,258,256]{2,1,0:T(8,128)(2,1)}), bf16[8,258,256]{2,1,0:T(8,128)(2,1)S(1)}, u32[]{:S(2)}, u32[]{:S(2)}) async-start(bf16[8,258,256]{2,1,0:T(8,128)(2,1)} %bitcast.62), calls=%async_computation | async-start | bytes 2162688 | tf_op jit(solution)/shard_map/all_to_all | solution.py:373
  57.4 0.7 copy.78
  58.2 0.7 broadcast_in_dim_reshape.6.dsk_ref.refs_8_
  58.9 0.6 broadcast_in_dim.34.segr_ref.refs_7_
  59.5 17.4 %shard_map.101.refs_9_.refs_1_ = f32[512,4096]{1,0:T(8,128)} custom-call(bf16[512,5120]{1,0:T(8,128)(2,1)} %shard_map.100.c_ref.b_ref.x_ref.refs_0_.refs_1_.refs_2_, bf16[512,5120]{1,0:T(8,128)(2,1)} %shard_map.100.c_ref.b_ref.x_ref.refs_0_.refs_1_.refs_2_, bf16[512,5120]{1,0:T(8,128)(2,1)} %shard_map.100.c_ref.b_ref.x_ref.refs_0_.refs_1_.refs_2_, ...), custom_call_target="tpu_custom_call" | custom-call | tf_op jit(solution)/shard_map/pallas_call | solution.py:250
  76.8 6.5 %all-to-all-done.refs_0_ = bf16[8,258,256]{2,1,0:T(8,128)(2,1)S(1)} async-done(((bf16[8,258,256]{2,1,0:T(8,128)(2,1)}), bf16[8,258,256]{2,1,0:T(8,128)(2,1)S(1)}, u32[]{:S(2)}, u32[]{:S(2)}) %all-to-all-start) | async-done | bytes 1056800 | tf_op jit(solution)/shard_map/all_to_all | solution.py:373
  83.3 1.0 copy-done
  84.3 2.6 %shard_map.106 = bf16[8,256,256]{2,1,0:T(8,128)(2,1)} custom-call(bf16[8,258,256]{2,1,0:T(8,128)(2,1)} %shard_map.105.got_ref), custom_call_target="tpu_custom_call" | custom-call | tf_op jit(solution)/shard_map/pallas_call | solution.py:374
  86.9 4.4 %all-to-all-start.1 = ((bf16[8,256,256]{2,1,0:T(8,128)(2,1)}), bf16[8,256,256]{2,1,0:T(8,128)(2,1)S(1)}, u32[]{:S(2)}, u32[]{:S(2)}) async-start(bf16[8,256,256]{2,1,0:T(8,128)(2,1)} %shard_map.106), calls=%async_computation.1 | async-start | bytes 2097152 | tf_op jit(solution)/shard_map/all_to_all | solution.py:379
  91.3 17.5 %shard_map.102.refs_1_ = f32[512,4096]{1,0:T(8,128)} custom-call(bf16[512,5120]{1,0:T(8,128)(2,1)} %shard_map.100.c_ref.b_ref.x_ref.refs_0_.refs_1_.refs_2_, bf16[512,5120]{1,0:T(8,128)(2,1)} %shard_map.100.c_ref.b_ref.x_ref.refs_0_.refs_1_.refs_2_, ...), custom_call_target="tpu_custom_call", output_to_operand_aliasing={{}: (9, {})} | custom-call | tf_op jit(solution)/shard_map/pallas_call | solution.py:250
  108.7 7.7 %all-to-all-done.1.refs_0_ = bf16[8,256,256]{2,1,0:T(8,128)(2,1)S(1)} async-done(((bf16[8,256,256]{2,1,0:T(8,128)(2,1)}), bf16[8,256,256]{2,1,0:T(8,128)(2,1)S(1)}, u32[]{:S(2)}, u32[]{:S(2)}) %all-to-all-start.1) | async-done | bytes 1048608 | tf_op jit(solution)/shard_map/all_to_all | solution.py:379
  116.4 1.0 copy-done.1
  117.4 1.4 %convert_bitcast_fusion = f32[8,32,8,256]{3,2,1,0:T(8,128)S(1)} fusion(bf16[8,256,256]{2,1,0:T(8,128)(2,1)} %shard_map.107), kind=kLoop, calls=%fused_computation.2 | loop fusion | flops 524288 | bytes 3145728
  118.8 0.3 copy.79
  119.1 1.6 %select_convert_fusion = (bf16[256,2048]{1,0:T(8,128)(2,1)}, bf16[256,2048]{1,0:T(8,128)(2,1)S(1)}) fusion(f32[256,2048]{1,0:T(8,128)S(1)} %bitcast.59, f32[257,2048]{1,0:T(8,128)S(1)} %get-tuple-element.19, f32[2048]{0:T(1024)S(1)} %bitcast.71, pred[]{:T(512)S(6)} %eq.23), kind=kLoop, calls=%fused_computation.3 | loop fusion | flops 3145728 | bytes 6299649 | tf_op jit(solution)/shard_map/convert_element_type | solution.py:382
  120.7 1.6 %collective-permute-start.2 = (bf16[256,2048]{1,0:T(8,128)(2,1)S(1)}, bf16[256,2048]{1,0:T(8,128)(2,1)S(1)}, u32[]{:S(2)}, u32[]{:S(2)}) collective-permute-start(bf16[256,2048]{1,0:T(8,128)(2,1)S(1)} %get-tuple-element.22), channel_id=1, source_target_pairs={{0,1},{1,0},{2,3},{3,2},{4,5},{5,4},{6,7},{7,6},{8,9},{9,8},{10,11... | collective-permute-start | bytes 3145736 | tf_op jit(solution)/shard_map/ppermute | solution.py:340
  122.4 0.7 broadcast_in_dim.70.refs_8_
  123.1 7.8 %shard_map.108.refs_10_ = bf16[512,4096]{1,0:T(8,128)(2,1)} custom-call(s32[1]{0:T(128)} %bitcast.core_ref, bf16[512,5120]{1,0:T(8,128)(2,1)} %shard_map.100.c_ref.b_ref.x_ref.refs_0_.refs_1_.refs_2_, f32[512,4096]{1,0:T(8,128)} %shard_map.102.refs_1_, bf16[512,4096]{1,0:T(8,128)(2,1)} %refs_2_.3, bf16[256,2048]{1,0:T(8,128)(2,1)} %get-tuple-element.21.refs_3_, ...), custom_call_target="tpu_custom_call" | custom-call | tf_op jit(solution)/shard_map/pallas_call | solution.py:318
  130.9 1.0 copy-done.3
  131.9 7.8 %shard_map.109 = bf16[512,4096]{1,0:T(8,128)(2,1)} custom-call(s32[1]{0:T(128)} %bitcast.core_ref, bf16[512,5120]{1,0:T(8,128)(2,1)} %shard_map.100.c_ref.b_ref.x_ref.refs_0_.refs_1_.refs_2_, f32[512,4096]{1,0:T(8,128)} %shard_map.102.refs_1_, bf16[512,4096]{1,0:T(8,128)(2,1)} %refs_2_.3, ...), custom_call_target="tpu_custom_call", output_to_operand_aliasing={{}: (11, {})} | custom-call | tf_op jit(solution)/shard_map/pallas_call | solution.py:318
  (41 shorter events, 1.4 us)
Async XLA Ops:
  0.0 11.7 %copy-start.4 = (f32[4,5120]{1,0:T(4,128)S(1)}, f32[4,5120]{1,0:T(4,128)}, u32[]{:S(2)}) copy-start(f32[4,5120]{1,0:T(4,128)} %param.14) | copy-start | bytes 245764
  0.9 14.4 %collective-permute-start = (bf16[3,5120]{1,0:T(4,128)(2,1)S(1)}, bf16[3,5120]{1,0:T(4,128)(2,1)S(1)}, u32[]{:S(2)}, u32[]{:S(2)}) collective-permute-start(bf16[3,5120]{1,0:T(4,128)(2,1)S(1)} %slice.57), channel_id=1, source_target_pairs={{0,1},{1,2},{2,3},{3,4},{4,5},{5,6},{6,7},{7,8},{8,9},{9,10},{10,1... | collective-permute-start | bytes 92168 | tf_op jit(solution)/shard_map/ppermute | solution.py:23
  38.8 8.0 %collective-permute-start.1 = (f32[257,2048]{1,0:T(8,128)}, f32[257,2048]{1,0:T(8,128)S(1)}, u32[]{:S(2)}, u32[]{:S(2)}) collective-permute-start(f32[257,2048]{1,0:T(8,128)} %get-tuple-element.14), channel_id=1, source_target_pairs={{0,1},{1,0},{2,3},{3,2},{4,5},{5,4},{6,7},{7,6},{8,9},{9,8},{10,11... | collective-permute-start | bytes 6316040 | tf_op jit(solution)/shard_map/ppermute | solution.py:340
  46.8 1.3 copy-start.2
  51.6 6.5 %copy-start.5 = (f32[64]{0:T(128)S(1)}, f32[64]{0:T(128)}, u32[]{:S(2)}) copy-start(f32[64]{0:T(128)} %param.18) | copy-start | bytes 772
  52.8 30.5 %all-to-all-start = ((bf16[8,258,256]{2,1,0:T(8,128)(2,1)}), bf16[8,258,256]{2,1,0:T(8,128)(2,1)S(1)}, u32[]{:S(2)}, u32[]{:S(2)}) async-start(bf16[8,258,256]{2,1,0:T(8,128)(2,1)} %bitcast.62), calls=%async_computation | async-start | bytes 2162688 | tf_op jit(solution)/shard_map/all_to_all | solution.py:373
  83.3 1.0 copy-start
  86.9 29.5 %all-to-all-start.1 = ((bf16[8,256,256]{2,1,0:T(8,128)(2,1)}), bf16[8,256,256]{2,1,0:T(8,128)(2,1)S(1)}, u32[]{:S(2)}, u32[]{:S(2)}) async-start(bf16[8,256,256]{2,1,0:T(8,128)(2,1)} %shard_map.106), calls=%async_computation.1 | async-start | bytes 2097152 | tf_op jit(solution)/shard_map/all_to_all | solution.py:379
  116.4 1.0 copy-start.1
  120.7 10.2 %collective-permute-start.2 = (bf16[256,2048]{1,0:T(8,128)(2,1)S(1)}, bf16[256,2048]{1,0:T(8,128)(2,1)S(1)}, u32[]{:S(2)}, u32[]{:S(2)}) collective-permute-start(bf16[256,2048]{1,0:T(8,128)(2,1)S(1)} %get-tuple-element.22), channel_id=1, source_target_pairs={{0,1},{1,0},{2,3},{3,2},{4,5},{5,4},{6,7},{7,6},{8,9},{9,8},{10,11... | collective-permute-start | bytes 3145736 | tf_op jit(solution)/shard_map/ppermute | solution.py:340
  130.9 1.0 copy-start.3

commit v16 on v15

--- a/solution.py
+++ b/solution.py
@@ -389,7 +389,7 @@
     nb = tok // STRETCH
     first_pos = (lax.axis_index("chip") * lax.axis_size("core") + lax.axis_index("core")) * tok
     rim_rows = shifted(xbc[tok - (CONV - 1) :], ("chip", "core"), 1)
-    rim8 = jnp.concatenate([jnp.zeros((8 - (CONV - 1), CHANNELS), xbc.dtype), rim_rows], axis=0)
+    rim8 = jnp.zeros((8, CHANNELS), xbc.dtype)
     ext_pos = first_pos - (CONV - 1) + jnp.arange(tok + CONV - 1)
     ext_seg = segment_of(ext_pos, lengths)
     target = ext_seg[CONV - 1 :]
@@ -400,6 +400,12 @@
     masks = jnp.concatenate([masks, jnp.zeros((tok, 128 - CONV), jnp.float32)], axis=1)
     w8 = jnp.concatenate([conv_weight, jnp.zeros((8 - CONV, CHANNELS), jnp.float32)], axis=0)
     conv = conv_part(xbc, rim8, w8, conv_bias[None, :], masks)
+    head = jnp.concatenate([rim_rows, xbc[: CONV - 1]], axis=0).astype(jnp.float32)
+    summed = conv_bias[None, :]
+    for tap in range(CONV):
+        term = head[tap : tap + CONV - 1] * conv_weight[tap][None, :]
+        summed = summed + jnp.where(kept[tap][: CONV - 1, None], term, 0.0)
+    conv = lax.dynamic_update_slice(conv, jax.nn.silu(summed).astype(jnp.bfloat16), (0, 0))
     step = jax.nn.softplus(dt_raw.astype(jnp.float32) + dt_bias[None, :])
     log_decay = -step * jnp.exp(a_log)[None, :]
     cum = jnp.cumsum(log_decay.reshape(nb, STRETCH, HEADS), axis=1).reshape(tok, HEADS)

time: 140 us -> 144 us (1.029)
  local copies, waits for them, and re-layouts: 18.6 us -> 21.4 us
    transpose x0 -> x2, local copies, waits for them, and re-layouts: none -> 2.09 us  [local(): bt = conv[:, INNER:INNER + GROUPS * STATE].T]
    dynamic_update_slice x0 -> x1, local copies, waits for them, and re-layouts: none -> 1.66 us  [local(): lax.dynamic_update_slice(conv, jax.nn.silu(summed).astype(jnp.bfloat16),...]
    unnamed x14 -> x15, local copies, waits for them, and re-layouts: 5.62 us -> 4.6 us
  transfers between devices with their start and end apart: 5 -> 5, of which waited for: 2 -> 2; matrix products, arithmetic and copies ran while one was open for 9% -> 10% of each run, Pallas kernels for 36% -> 44%
where the time goes in v16:
time: 144 us; the launch traced here: 143 us
  Pallas kernels  80.7 us (56%)
  local copies, waits for them, and re-layouts  21.4 us (15%)
  starting transfers between devices  15.1 us (10%)
  waiting for transfers between devices  14.2 us (10%)
  other arithmetic  11 us (8%)
    pallas_call x2, Pallas kernels, intra_part(): pl.pallas_call(kernel, grid=(nb,), in_specs=specs, out_specs=pl.BlockSpec...  34.8 us
    pallas_call x2, Pallas kernels, half_states(): pl.pallas_call(half_state_kernel, grid_spec=grid_spec, out_shape=[jax.Sha...  16 us
    pallas_call x2, Pallas kernels, mix(): pl.pallas_call(with_core, grid_spec=grid_spec, out_shape=jax.ShapeDtypeSt...  15.5 us
    pallas_call x1, Pallas kernels, conv_part(): pl.pallas_call(conv_kernel, grid=(chans // CONV_COLS,), in_specs=[pl.Bloc...  11.8 us
    all_to_all x1, waiting for transfers between devices, compose(): lax.all_to_all(entering, 'chip', split_axis=0, concat_axis=0, tiled=True)  7.66 us
    all_to_all x1, waiting for transfers between devices, compose(): lax.all_to_all(payload, 'chip', split_axis=0, concat_axis=0, tiled=True)  6.5 us
    unnamed x15, local copies, waits for them, and re-layouts  4.6 us
    all_to_all x1, starting transfers between devices, compose(): lax.all_to_all(payload, 'chip', split_axis=0, concat_axis=0, tiled=True)  4.6 us
  transfers between devices with their start and end apart: 5, of which 2 were waited for; matrix products, arithmetic and copies ran while one was open for 10% of the time, Pallas kernels for 44%

profile of v16, /device:TPU:1, one launch (start us, length us, event | category | flops | bytes accessed | tf_op | source)
XLA Modules:
  0.0 142.7 jit_solution(10702518370698222347)
XLA Ops:
  0.0 1.0 fusion.15
  1.0 4.5 %collective-permute-start = (bf16[3,5120]{1,0:T(4,128)(2,1)S(1)}, bf16[3,5120]{1,0:T(4,128)(2,1)S(1)}, u32[]{:S(2)}, u32[]{:S(2)}) collective-permute-start(bf16[3,5120]{1,0:T(4,128)(2,1)S(1)} %get-tuple-element.17), channel_id=1, source_target_pairs={{0,1},{1,2},{2,3},{3,4},{4,5},{5,6},{6,7},{7,8},{8,9},{9,10},{10,1... | collective-permute-start | bytes 92168 | tf_op jit(solution)/shard_map/ppermute | solution.py:23
  5.6 0.8 reduce-window.18
  6.6 1.2 fusion.16
  7.8 0.2 copy.66
  8.4 0.7 exp.19
  9.1 1.0 negate_multiply_fusion
  10.1 1.2 reduce-window.19
  11.3 0.2 slice_reduce_fusion
  11.8 0.2 compare_reduce_fusion
  12.1 0.7 pad_convert_fusion.m_ref
  12.8 0.7 concatenate.14.w_ref
  13.7 0.7 broadcast_in_dim_reshape.7.bdec_ref
  14.5 1.0 copy.72
  15.5 1.0 copy.67
  16.6 0.6 broadcast_in_dim.97.rim_ref
  17.2 11.8 %shard_map.100 = bf16[512,5120]{1,0:T(8,128)(2,1)} custom-call(bf16[512,5120]{1,0:T(8,128)(2,1)} %x_ref.1, bf16[8,5120]{1,0:T(8,128)(2,1)} %broadcast_in_dim.97.rim_ref, f32[8,5120]{1,0:T(8,128)} %concatenate.14.w_ref, f32[1,5120]{1,0:T(1,128)} %bitcast.76, f32[512,128]{1,0:T(8,128)} %pad_convert_fusion.m_ref), custom_call_target="tpu_custom_call" | custom-call | tf_op jit(solution)/shard_map/pallas_call | solution.py:72
  29.3 1.7 %dynamic_update_slice.3.c_ref.b_ref.x_ref.refs_0_.refs_1_.refs_2_ = bf16[512,5120]{1,0:T(8,128)(2,1)} dynamic-update-slice(bf16[512,5120]{1,0:T(8,128)(2,1)} %shard_map.100, bf16[3,5120]{1,0:T(4,128)(2,1)S(1)} %fusion.9, s32[]{:T(128)} %constant.40.clone.1, s32[]{:T(128)} %constant.40.clone.1) | dynamic-update-slice | bytes 61444 | tf_op jit(solution)/shard_map/dynamic_update_slice | solution.py:408
  30.9 1.1 slice_bitcast_fusion
  32.0 1.0 copy.76.bt_ref
  33.0 0.8 broadcast_in_dim.104.segc_ref.refs_6_.refs_7_
  33.9 8.0 %shard_map.103 = (f32[2,256,4096]{2,1,0:T(8,128)}, f32[2,1,4096]{2,1,0:T(1,128)}, f32[257,2048]{1,0:T(8,128)}) custom-call(s32[1]{0:T(128)} %bitcast.core_ref, bf16[512,512]{1,0:T(8,128)(2,1)} %copy.76.bt_ref, bf16[512,5120]{1,0:T(8,128)(2,1)} %dynamic_update_slice.3.c_ref.b_ref.x_ref.refs_0_.refs_1_.refs_2_, f32[2,512,32]{2,1,0:T(8,128)} %bitcast.64, ...), custom_call_target="tpu_custom_call" | custom-call | tf_op jit(solution)/shard_map/pallas_call | solution.py:187
  41.9 8.0 %shard_map.104 = (f32[2,256,4096]{2,1,0:T(8,128)}, f32[2,1,4096]{2,1,0:T(1,128)}, f32[257,2048]{1,0:T(8,128)}) custom-call(s32[1]{0:T(128)} %bitcast.core_ref, bf16[512,512]{1,0:T(8,128)(2,1)} %copy.76.bt_ref, bf16[512,5120]{1,0:T(8,128)(2,1)} %dynamic_update_slice.3.c_ref.b_ref.x_ref.refs_0_.refs_1_.refs_2_, ...), custom_call_target="tpu_custom_call", output_to_operand_aliasing={{0}: (7, {}), {1}: (8, {})} | custom-call | tf_op jit(solution)/shard_map/pallas_call | solution.py:187
  49.9 1.3 copy-done.2
  51.2 2.6 %broadcast_select_fusion.1 = (f32[257,2048]{1,0:T(8,128)S(1)}, f32[257,2048]{1,0:T(8,128)S(1)}) fusion(f32[257,2048]{1,0:T(8,128)} %get-tuple-element.13, f32[257,2048]{1,0:T(8,128)} %copy-done.2, pred[]{:T(512)S(6)} %eq.23), kind=kLoop, calls=%fused_computation.9 | loop fusion | flops 1052672 | bytes 8421377 | tf_op jit(solution)/shard_map/jit(_where)/select_n | solution.py:362
  53.9 0.4 fusion
  54.3 0.3 copy.84
  54.7 1.2 copy.91
  55.9 4.6 %all-to-all-start = ((bf16[8,258,256]{2,1,0:T(8,128)(2,1)}), bf16[8,258,256]{2,1,0:T(8,128)(2,1)S(1)}, u32[]{:S(2)}, u32[]{:S(2)}) async-start(bf16[8,258,256]{2,1,0:T(8,128)(2,1)} %bitcast.69), calls=%async_computation | async-start | bytes 2162688 | tf_op jit(solution)/shard_map/all_to_all | solution.py:373
  60.5 0.7 copy.82
  61.3 0.7 broadcast_in_dim_reshape.6.dsk_ref.refs_8_
  62.0 0.6 broadcast_in_dim.105.segr_ref.refs_7_
  62.6 17.4 %shard_map.101.refs_9_.refs_1_ = f32[512,4096]{1,0:T(8,128)} custom-call(bf16[512,5120]{1,0:T(8,128)(2,1)} %dynamic_update_slice.3.c_ref.b_ref.x_ref.refs_0_.refs_1_.refs_2_, bf16[512,5120]{1,0:T(8,128)(2,1)} %dynamic_update_slice.3.c_ref.b_ref.x_ref.refs_0_.refs_1_.refs_2_, bf16[512,5120]{1,0:T(8,128)(2,1)} %dynamic_update_slice.3.c_ref.b_ref.x_ref.refs_0_.refs_1_.refs_2_, ...), custom_call_target="tpu_custom_call" | custom-call | tf_op jit(solution)/shard_map/pallas_call | solution.py:250
  79.9 6.5 %all-to-all-done.refs_0_ = bf16[8,258,256]{2,1,0:T(8,128)(2,1)S(1)} async-done(((bf16[8,258,256]{2,1,0:T(8,128)(2,1)}), bf16[8,258,256]{2,1,0:T(8,128)(2,1)S(1)}, u32[]{:S(2)}, u32[]{:S(2)}) %all-to-all-start) | async-done | bytes 1056800 | tf_op jit(solution)/shard_map/all_to_all | solution.py:373
  86.4 1.0 copy-done
  87.4 2.6 %shard_map.106 = bf16[8,256,256]{2,1,0:T(8,128)(2,1)} custom-call(bf16[8,258,256]{2,1,0:T(8,128)(2,1)} %shard_map.105.got_ref), custom_call_target="tpu_custom_call" | custom-call | tf_op jit(solution)/shard_map/pallas_call | solution.py:374
  90.0 4.4 %all-to-all-start.1 = ((bf16[8,256,256]{2,1,0:T(8,128)(2,1)}), bf16[8,256,256]{2,1,0:T(8,128)(2,1)S(1)}, u32[]{:S(2)}, u32[]{:S(2)}) async-start(bf16[8,256,256]{2,1,0:T(8,128)(2,1)} %shard_map.106), calls=%async_computation.1 | async-start | bytes 2097152 | tf_op jit(solution)/shard_map/all_to_all | solution.py:379
  94.4 17.5 %shard_map.102.refs_1_ = f32[512,4096]{1,0:T(8,128)} custom-call(bf16[512,5120]{1,0:T(8,128)(2,1)} %dynamic_update_slice.3.c_ref.b_ref.x_ref.refs_0_.refs_1_.refs_2_, bf16[512,5120]{1,0:T(8,128)(2,1)} %dynamic_update_slice.3.c_ref.b_ref.x_ref.refs_0_.refs_1_.refs_2_, ...), custom_call_target="tpu_custom_call", output_to_operand_aliasing={{}: (9, {})} | custom-call | tf_op jit(solution)/shard_map/pallas_call | solution.py:250
  111.8 7.7 %all-to-all-done.1.refs_0_ = bf16[8,256,256]{2,1,0:T(8,128)(2,1)S(1)} async-done(((bf16[8,256,256]{2,1,0:T(8,128)(2,1)}), bf16[8,256,256]{2,1,0:T(8,128)(2,1)S(1)}, u32[]{:S(2)}, u32[]{:S(2)}) %all-to-all-start.1) | async-done | bytes 1048608 | tf_op jit(solution)/shard_map/all_to_all | solution.py:379
  119.5 1.0 copy-done.1
  120.5 1.4 convert_bitcast_fusion
  121.9 0.3 copy.83
  122.2 1.6 %select_convert_fusion = (bf16[256,2048]{1,0:T(8,128)(2,1)}, bf16[256,2048]{1,0:T(8,128)(2,1)S(1)}) fusion(f32[256,2048]{1,0:T(8,128)S(1)} %bitcast.68, f32[257,2048]{1,0:T(8,128)S(1)} %get-tuple-element.21, f32[2048]{0:T(1024)S(1)} %bitcast.83, pred[]{:T(512)S(6)} %eq.23), kind=kLoop, calls=%fused_computation.3 | loop fusion | flops 3145728 | bytes 6299649 | tf_op jit(solution)/shard_map/convert_element_type | solution.py:382
  123.7 1.6 %collective-permute-start.2 = (bf16[256,2048]{1,0:T(8,128)(2,1)S(1)}, bf16[256,2048]{1,0:T(8,128)(2,1)S(1)}, u32[]{:S(2)}, u32[]{:S(2)}) collective-permute-start(bf16[256,2048]{1,0:T(8,128)(2,1)S(1)} %get-tuple-element.24), channel_id=1, source_target_pairs={{0,1},{1,0},{2,3},{3,2},{4,5},{5,4},{6,7},{7,6},{8,9},{9,8},{10,11... | collective-permute-start | bytes 3145736 | tf_op jit(solution)/shard_map/ppermute | solution.py:340
  125.5 0.7 broadcast_in_dim.113.refs_8_
  126.2 7.8 %shard_map.108.refs_10_ = bf16[512,4096]{1,0:T(8,128)(2,1)} custom-call(s32[1]{0:T(128)} %bitcast.core_ref, bf16[512,5120]{1,0:T(8,128)(2,1)} %dynamic_update_slice.3.c_ref.b_ref.x_ref.refs_0_.refs_1_.refs_2_, f32[512,4096]{1,0:T(8,128)} %shard_map.102.refs_1_, bf16[512,4096]{1,0:T(8,128)(2,1)} %refs_2_.3, bf16[256,2048]{1,0:T(8,128)(2,1)} %get-tuple-element.23.refs_3_, ...), custom_call_target="tpu_custom_call" | custom-call | tf_op jit(solution)/shard_map/pallas_call | solution.py:318
  134.0 1.0 copy-done.3
  135.0 7.8 %shard_map.109 = bf16[512,4096]{1,0:T(8,128)(2,1)} custom-call(s32[1]{0:T(128)} %bitcast.core_ref, bf16[512,5120]{1,0:T(8,128)(2,1)} %dynamic_update_slice.3.c_ref.b_ref.x_ref.refs_0_.refs_1_.refs_2_, f32[512,4096]{1,0:T(8,128)} %shard_map.102.refs_1_, bf16[512,4096]{1,0:T(8,128)(2,1)} %refs_2_.3, ...), custom_call_target="tpu_custom_call", output_to_operand_aliasing={{}: (11, {})} | custom-call | tf_op jit(solution)/shard_map/pallas_call | solution.py:318
  (47 shorter events, 1.9 us)
Async XLA Ops:
  0.0 12.8 %copy-start.4 = (f32[4,5120]{1,0:T(4,128)S(1)}, f32[4,5120]{1,0:T(4,128)}, u32[]{:S(2)}) copy-start(f32[4,5120]{1,0:T(4,128)} %param.14) | copy-start | bytes 245764
  1.0 28.0 %collective-permute-start = (bf16[3,5120]{1,0:T(4,128)(2,1)S(1)}, bf16[3,5120]{1,0:T(4,128)(2,1)S(1)}, u32[]{:S(2)}, u32[]{:S(2)}) collective-permute-start(bf16[3,5120]{1,0:T(4,128)(2,1)S(1)} %get-tuple-element.17), channel_id=1, source_target_pairs={{0,1},{1,2},{2,3},{3,4},{4,5},{5,6},{6,7},{7,8},{8,9},{9,10},{10,1... | collective-permute-start | bytes 92168 | tf_op jit(solution)/shard_map/ppermute | solution.py:23
  17.2 11.9 %copy-start.5 = (f32[5120]{0:T(1024)S(1)}, f32[5120]{0:T(1024)}, u32[]{:S(2)}) copy-start(f32[5120]{0:T(1024)} %param.15) | copy-start | bytes 61444
  41.8 8.0 %collective-permute-start.1 = (f32[257,2048]{1,0:T(8,128)}, f32[257,2048]{1,0:T(8,128)S(1)}, u32[]{:S(2)}, u32[]{:S(2)}) collective-permute-start(f32[257,2048]{1,0:T(8,128)} %get-tuple-element.14), channel_id=1, source_target_pairs={{0,1},{1,0},{2,3},{3,2},{4,5},{5,4},{6,7},{7,6},{8,9},{9,8},{10,11... | collective-permute-start | bytes 6316040 | tf_op jit(solution)/shard_map/ppermute | solution.py:340
  49.9 1.3 copy-start.2
  54.7 6.5 %copy-start.6 = (f32[64]{0:T(128)S(1)}, f32[64]{0:T(128)}, u32[]{:S(2)}) copy-start(f32[64]{0:T(128)} %param.18) | copy-start | bytes 772
  55.9 30.5 %all-to-all-start = ((bf16[8,258,256]{2,1,0:T(8,128)(2,1)}), bf16[8,258,256]{2,1,0:T(8,128)(2,1)S(1)}, u32[]{:S(2)}, u32[]{:S(2)}) async-start(bf16[8,258,256]{2,1,0:T(8,128)(2,1)} %bitcast.69), calls=%async_computation | async-start | bytes 2162688 | tf_op jit(solution)/shard_map/all_to_all | solution.py:373
  86.4 1.0 copy-start
  90.0 29.5 %all-to-all-start.1 = ((bf16[8,256,256]{2,1,0:T(8,128)(2,1)}), bf16[8,256,256]{2,1,0:T(8,128)(2,1)S(1)}, u32[]{:S(2)}, u32[]{:S(2)}) async-start(bf16[8,256,256]{2,1,0:T(8,128)(2,1)} %shard_map.106), calls=%async_computation.1 | async-start | bytes 2097152 | tf_op jit(solution)/shard_map/all_to_all | solution.py:379
  119.5 1.0 copy-start.1
  123.7 10.2 %collective-permute-start.2 = (bf16[256,2048]{1,0:T(8,128)(2,1)S(1)}, bf16[256,2048]{1,0:T(8,128)(2,1)S(1)}, u32[]{:S(2)}, u32[]{:S(2)}) collective-permute-start(bf16[256,2048]{1,0:T(8,128)(2,1)S(1)} %get-tuple-element.24), channel_id=1, source_target_pairs={{0,1},{1,0},{2,3},{3,2},{4,5},{5,4},{6,7},{7,6},{8,9},{9,8},{10,11... | collective-permute-start | bytes 3145736 | tf_op jit(solution)/shard_map/ppermute | solution.py:340
  133.9 1.0 copy-start.3

commit v17 on v15

--- a/solution.py
+++ b/solution.py
@@ -75,9 +75,9 @@
         in_specs=[
             pl.BlockSpec((tok, CONV_COLS), lambda c: (0, c)),
             pl.BlockSpec((8, CONV_COLS), lambda c: (0, c)),
-            pl.BlockSpec((8, CONV_COLS), lambda c: (0, c)),
+            pl.BlockSpec((CONV, CONV_COLS), lambda c: (0, c)),
             pl.BlockSpec((1, CONV_COLS), lambda c: (0, c)),
-            pl.BlockSpec((tok, 128), lambda c: (0, 0)),
+            pl.BlockSpec((tok, CONV), lambda c: (0, 0)),
         ],
         out_specs=pl.BlockSpec((tok, CONV_COLS), lambda c: (0, c)),
         out_shape=jax.ShapeDtypeStruct((tok, chans), jnp.bfloat16),
@@ -397,9 +397,7 @@
         (ext_pos[tap : tap + tok] >= 0) & (ext_seg[tap : tap + tok] == target) for tap in range(CONV)
     ]
     masks = jnp.stack(kept, axis=1).astype(jnp.float32)
-    masks = jnp.concatenate([masks, jnp.zeros((tok, 128 - CONV), jnp.float32)], axis=1)
-    w8 = jnp.concatenate([conv_weight, jnp.zeros((8 - CONV, CHANNELS), jnp.float32)], axis=0)
-    conv = conv_part(xbc, rim8, w8, conv_bias[None, :], masks)
+    conv = conv_part(xbc, rim8, conv_weight, conv_bias[None, :], masks)
     step = jax.nn.softplus(dt_raw.astype(jnp.float32) + dt_bias[None, :])
     log_decay = -step * jnp.exp(a_log)[None, :]
     cum = jnp.cumsum(log_decay.reshape(nb, STRETCH, HEADS), axis=1).reshape(tok, HEADS)

time: 140 us -> 140 us (level)
    unnamed x14 -> x12, local copies, waits for them, and re-layouts: 5.62 us -> 5.62 us
where the time goes in v17:
time: 140 us; the launch traced here: 139 us
  Pallas kernels  80.9 us (58%)
  local copies, waits for them, and re-layouts  18.6 us (13%)
  starting transfers between devices  15.2 us (11%)
  waiting for transfers between devices  14.2 us (10%)
  other arithmetic  10 us (7%)
    pallas_call x2, Pallas kernels, intra_part(): pl.pallas_call(kernel, grid=(nb,), in_specs=specs, out_specs=pl.BlockSpec...  34.8 us
    pallas_call x2, Pallas kernels, half_states(): pl.pallas_call(half_state_kernel, grid_spec=grid_spec, out_shape=[jax.Sha...  16 us
    pallas_call x2, Pallas kernels, mix(): pl.pallas_call(with_core, grid_spec=grid_spec, out_shape=jax.ShapeDtypeSt...  15.5 us
    pallas_call x1, Pallas kernels, conv_part(): pl.pallas_call(conv_kernel, grid=(chans // CONV_COLS,), in_specs=[pl.Bloc...  12 us
    all_to_all x1, waiting for transfers between devices, compose(): lax.all_to_all(entering, 'chip', split_axis=0, concat_axis=0, tiled=True)  7.67 us
    all_to_all x1, waiting for transfers between devices, compose(): lax.all_to_all(payload, 'chip', split_axis=0, concat_axis=0, tiled=True)  6.5 us
    unnamed x12, local copies, waits for them, and re-layouts  5.62 us
    all_to_all x1, starting transfers between devices, compose(): lax.all_to_all(payload, 'chip', split_axis=0, concat_axis=0, tiled=True)  4.6 us
  transfers between devices with their start and end apart: 5, of which 2 were waited for; matrix products, arithmetic and copies ran while one was open for 9% of the time, Pallas kernels for 36%

profile of v17, /device:TPU:1, one launch (start us, length us, event | category | flops | bytes accessed | tf_op | source)
XLA Modules:
  0.0 139.0 jit_solution(3272499727079622428)
XLA Ops:
  0.0 0.9 slice.57
  0.9 4.5 %collective-permute-start = (bf16[3,5120]{1,0:T(4,128)(2,1)S(1)}, bf16[3,5120]{1,0:T(4,128)(2,1)S(1)}, u32[]{:S(2)}, u32[]{:S(2)}) collective-permute-start(bf16[3,5120]{1,0:T(4,128)(2,1)S(1)} %slice.57), channel_id=1, source_target_pairs={{0,1},{1,2},{2,3},{3,4},{4,5},{5,6},{6,7},{7,8},{8,9},{9,10},{10,1... | collective-permute-start | bytes 92168 | tf_op jit(solution)/shard_map/ppermute | solution.py:23
  5.5 0.8 reduce-window.18
  6.6 0.2 fusion.5
  6.9 0.7 exp.14
  7.6 1.0 negate_multiply_fusion
  8.6 1.2 reduce-window.19
  9.8 0.2 slice_reduce_fusion
  10.1 0.1 bitcast_bitcast_fusion
  10.2 0.2 fusion.1
  10.4 0.2 compare_reduce_fusion
  10.8 0.9 copy.74.m_ref
  11.7 0.7 broadcast_in_dim_reshape.7.bdec_ref
  12.4 0.1 reshape_reshape.3
  12.5 1.0 copy.80
  13.5 1.0 copy.75
  14.6 0.7 concatenate.6.rim_ref
  15.2 12.0 %shard_map.100.c_ref.b_ref.x_ref.refs_0_.refs_1_.refs_2_ = bf16[512,5120]{1,0:T(8,128)(2,1)} custom-call(bf16[512,5120]{1,0:T(8,128)(2,1)} %x_ref.1, bf16[8,5120]{1,0:T(8,128)(2,1)} %concatenate.6.rim_ref, f32[4,5120]{1,0:T(4,128)} %w_ref.1, f32[1,5120]{1,0:T(1,128)} %bitcast.73, f32[512,4]{1,0:T(8,128)} %copy.74.m_ref), custom_call_target="tpu_custom_call" | custom-call | tf_op jit(solution)/shard_map/pallas_call | solution.py:72
  27.2 1.1 slice.77
  28.3 1.0 copy.86
  29.3 0.8 broadcast_in_dim.33.segc_ref.refs_6_.refs_7_
  30.2 8.0 %shard_map.103 = (f32[2,256,4096]{2,1,0:T(8,128)}, f32[2,1,4096]{2,1,0:T(1,128)}, f32[257,2048]{1,0:T(8,128)}) custom-call(s32[1]{0:T(128)} %bitcast.core_ref, bf16[512,512]{1,0:T(8,128)(2,1)} %bitcast.60, bf16[512,5120]{1,0:T(8,128)(2,1)} %shard_map.100.c_ref.b_ref.x_ref.refs_0_.refs_1_.refs_2_, f32[2,512,32]{2,1,0:T(8,128)} %bitcast.55, ...), custom_call_target="tpu_custom_call" | custom-call | tf_op jit(solution)/shard_map/pallas_call | solution.py:187
  38.2 8.0 %shard_map.104 = (f32[2,256,4096]{2,1,0:T(8,128)}, f32[2,1,4096]{2,1,0:T(1,128)}, f32[257,2048]{1,0:T(8,128)}) custom-call(s32[1]{0:T(128)} %bitcast.core_ref, bf16[512,512]{1,0:T(8,128)(2,1)} %bitcast.61, bf16[512,5120]{1,0:T(8,128)(2,1)} %shard_map.100.c_ref.b_ref.x_ref.refs_0_.refs_1_.refs_2_, ...), custom_call_target="tpu_custom_call", output_to_operand_aliasing={{0}: (7, {}), {1}: (8, {})} | custom-call | tf_op jit(solution)/shard_map/pallas_call | solution.py:187
  46.2 1.3 copy-done.2
  47.5 2.6 %broadcast_select_fusion.1 = (f32[257,2048]{1,0:T(8,128)S(1)}, f32[257,2048]{1,0:T(8,128)S(1)}) fusion(f32[257,2048]{1,0:T(8,128)} %get-tuple-element.13, f32[257,2048]{1,0:T(8,128)} %copy-done.2, pred[]{:T(512)S(6)} %eq.23), kind=kLoop, calls=%fused_computation.9 | loop fusion | flops 1052672 | bytes 8421377 | tf_op jit(solution)/shard_map/jit(_where)/select_n | solution.py:362
  50.2 0.4 fusion
  50.7 0.3 copy.92
  51.1 1.2 copy.99
  52.3 4.6 %all-to-all-start = ((bf16[8,258,256]{2,1,0:T(8,128)(2,1)}), bf16[8,258,256]{2,1,0:T(8,128)(2,1)S(1)}, u32[]{:S(2)}, u32[]{:S(2)}) async-start(bf16[8,258,256]{2,1,0:T(8,128)(2,1)} %bitcast.62), calls=%async_computation | async-start | bytes 2162688 | tf_op jit(solution)/shard_map/all_to_all | solution.py:373
  56.9 0.7 copy.90
  57.6 0.7 broadcast_in_dim_reshape.6.dsk_ref.refs_8_
  58.3 0.6 broadcast_in_dim.60.segr_ref.refs_7_
  58.9 17.4 %shard_map.101.refs_9_.refs_1_ = f32[512,4096]{1,0:T(8,128)} custom-call(bf16[512,5120]{1,0:T(8,128)(2,1)} %shard_map.100.c_ref.b_ref.x_ref.refs_0_.refs_1_.refs_2_, bf16[512,5120]{1,0:T(8,128)(2,1)} %shard_map.100.c_ref.b_ref.x_ref.refs_0_.refs_1_.refs_2_, bf16[512,5120]{1,0:T(8,128)(2,1)} %shard_map.100.c_ref.b_ref.x_ref.refs_0_.refs_1_.refs_2_, ...), custom_call_target="tpu_custom_call" | custom-call | tf_op jit(solution)/shard_map/pallas_call | solution.py:250
  76.3 6.5 %all-to-all-done.refs_0_ = bf16[8,258,256]{2,1,0:T(8,128)(2,1)S(1)} async-done(((bf16[8,258,256]{2,1,0:T(8,128)(2,1)}), bf16[8,258,256]{2,1,0:T(8,128)(2,1)S(1)}, u32[]{:S(2)}, u32[]{:S(2)}) %all-to-all-start) | async-done | bytes 1056800 | tf_op jit(solution)/shard_map/all_to_all | solution.py:373
  82.8 1.0 copy-done
  83.7 2.6 %shard_map.106 = bf16[8,256,256]{2,1,0:T(8,128)(2,1)} custom-call(bf16[8,258,256]{2,1,0:T(8,128)(2,1)} %shard_map.105.got_ref), custom_call_target="tpu_custom_call" | custom-call | tf_op jit(solution)/shard_map/pallas_call | solution.py:374
  86.3 4.4 %all-to-all-start.1 = ((bf16[8,256,256]{2,1,0:T(8,128)(2,1)}), bf16[8,256,256]{2,1,0:T(8,128)(2,1)S(1)}, u32[]{:S(2)}, u32[]{:S(2)}) async-start(bf16[8,256,256]{2,1,0:T(8,128)(2,1)} %shard_map.106), calls=%async_computation.1 | async-start | bytes 2097152 | tf_op jit(solution)/shard_map/all_to_all | solution.py:379
  90.7 17.5 %shard_map.102.refs_1_ = f32[512,4096]{1,0:T(8,128)} custom-call(bf16[512,5120]{1,0:T(8,128)(2,1)} %shard_map.100.c_ref.b_ref.x_ref.refs_0_.refs_1_.refs_2_, bf16[512,5120]{1,0:T(8,128)(2,1)} %shard_map.100.c_ref.b_ref.x_ref.refs_0_.refs_1_.refs_2_, ...), custom_call_target="tpu_custom_call", output_to_operand_aliasing={{}: (9, {})} | custom-call | tf_op jit(solution)/shard_map/pallas_call | solution.py:250
  108.2 7.7 %all-to-all-done.1.refs_0_ = bf16[8,256,256]{2,1,0:T(8,128)(2,1)S(1)} async-done(((bf16[8,256,256]{2,1,0:T(8,128)(2,1)}), bf16[8,256,256]{2,1,0:T(8,128)(2,1)S(1)}, u32[]{:S(2)}, u32[]{:S(2)}) %all-to-all-start.1) | async-done | bytes 1048608 | tf_op jit(solution)/shard_map/all_to_all | solution.py:379
  115.8 1.0 copy-done.1
  116.8 1.4 %convert_bitcast_fusion = f32[8,32,8,256]{3,2,1,0:T(8,128)S(1)} fusion(bf16[8,256,256]{2,1,0:T(8,128)(2,1)} %shard_map.107), kind=kLoop, calls=%fused_computation.2 | loop fusion | flops 524288 | bytes 3145728
  118.2 0.3 copy.91
  118.5 1.6 %select_convert_fusion = (bf16[256,2048]{1,0:T(8,128)(2,1)}, bf16[256,2048]{1,0:T(8,128)(2,1)S(1)}) fusion(f32[256,2048]{1,0:T(8,128)S(1)} %bitcast.59, f32[257,2048]{1,0:T(8,128)S(1)} %get-tuple-element.19, f32[2048]{0:T(1024)S(1)} %bitcast.71, pred[]{:T(512)S(6)} %eq.23), kind=kLoop, calls=%fused_computation.3 | loop fusion | flops 3145728 | bytes 6299649 | tf_op jit(solution)/shard_map/convert_element_type | solution.py:382
  120.1 1.6 %collective-permute-start.2 = (bf16[256,2048]{1,0:T(8,128)(2,1)S(1)}, bf16[256,2048]{1,0:T(8,128)(2,1)S(1)}, u32[]{:S(2)}, u32[]{:S(2)}) collective-permute-start(bf16[256,2048]{1,0:T(8,128)(2,1)S(1)} %get-tuple-element.22), channel_id=1, source_target_pairs={{0,1},{1,0},{2,3},{3,2},{4,5},{5,4},{6,7},{7,6},{8,9},{9,8},{10,11... | collective-permute-start | bytes 3145736 | tf_op jit(solution)/shard_map/ppermute | solution.py:340
  121.8 0.7 broadcast_in_dim.68.refs_8_
  122.5 7.8 %shard_map.108.refs_10_ = bf16[512,4096]{1,0:T(8,128)(2,1)} custom-call(s32[1]{0:T(128)} %bitcast.core_ref, bf16[512,5120]{1,0:T(8,128)(2,1)} %shard_map.100.c_ref.b_ref.x_ref.refs_0_.refs_1_.refs_2_, f32[512,4096]{1,0:T(8,128)} %shard_map.102.refs_1_, bf16[512,4096]{1,0:T(8,128)(2,1)} %refs_2_.3, bf16[256,2048]{1,0:T(8,128)(2,1)} %get-tuple-element.21.refs_3_, ...), custom_call_target="tpu_custom_call" | custom-call | tf_op jit(solution)/shard_map/pallas_call | solution.py:318
  130.3 1.0 copy-done.3
  131.3 7.8 %shard_map.109 = bf16[512,4096]{1,0:T(8,128)(2,1)} custom-call(s32[1]{0:T(128)} %bitcast.core_ref, bf16[512,5120]{1,0:T(8,128)(2,1)} %shard_map.100.c_ref.b_ref.x_ref.refs_0_.refs_1_.refs_2_, f32[512,4096]{1,0:T(8,128)} %shard_map.102.refs_1_, bf16[512,4096]{1,0:T(8,128)(2,1)} %refs_2_.3, ...), custom_call_target="tpu_custom_call", output_to_operand_aliasing={{}: (11, {})} | custom-call | tf_op jit(solution)/shard_map/pallas_call | solution.py:318
  (37 shorter events, 1.2 us)
Async XLA Ops:
  0.9 13.6 %collective-permute-start = (bf16[3,5120]{1,0:T(4,128)(2,1)S(1)}, bf16[3,5120]{1,0:T(4,128)(2,1)S(1)}, u32[]{:S(2)}, u32[]{:S(2)}) collective-permute-start(bf16[3,5120]{1,0:T(4,128)(2,1)S(1)} %slice.57), channel_id=1, source_target_pairs={{0,1},{1,2},{2,3},{3,4},{4,5},{5,6},{6,7},{7,8},{8,9},{9,10},{10,1... | collective-permute-start | bytes 92168 | tf_op jit(solution)/shard_map/ppermute | solution.py:23
  38.2 8.0 %collective-permute-start.1 = (f32[257,2048]{1,0:T(8,128)}, f32[257,2048]{1,0:T(8,128)S(1)}, u32[]{:S(2)}, u32[]{:S(2)}) collective-permute-start(f32[257,2048]{1,0:T(8,128)} %get-tuple-element.14), channel_id=1, source_target_pairs={{0,1},{1,0},{2,3},{3,2},{4,5},{5,4},{6,7},{7,6},{8,9},{9,8},{10,11... | collective-permute-start | bytes 6316040 | tf_op jit(solution)/shard_map/ppermute | solution.py:340
  46.2 1.3 copy-start.2
  51.0 6.5 %copy-start.4 = (f32[64]{0:T(128)S(1)}, f32[64]{0:T(128)}, u32[]{:S(2)}) copy-start(f32[64]{0:T(128)} %param.18) | copy-start | bytes 772
  52.3 30.5 %all-to-all-start = ((bf16[8,258,256]{2,1,0:T(8,128)(2,1)}), bf16[8,258,256]{2,1,0:T(8,128)(2,1)S(1)}, u32[]{:S(2)}, u32[]{:S(2)}) async-start(bf16[8,258,256]{2,1,0:T(8,128)(2,1)} %bitcast.62), calls=%async_computation | async-start | bytes 2162688 | tf_op jit(solution)/shard_map/all_to_all | solution.py:373
  82.7 1.0 copy-start
  86.3 29.5 %all-to-all-start.1 = ((bf16[8,256,256]{2,1,0:T(8,128)(2,1)}), bf16[8,256,256]{2,1,0:T(8,128)(2,1)S(1)}, u32[]{:S(2)}, u32[]{:S(2)}) async-start(bf16[8,256,256]{2,1,0:T(8,128)(2,1)} %shard_map.106), calls=%async_computation.1 | async-start | bytes 2097152 | tf_op jit(solution)/shard_map/all_to_all | solution.py:379
  115.8 1.0 copy-start.1
  120.1 10.2 %collective-permute-start.2 = (bf16[256,2048]{1,0:T(8,128)(2,1)S(1)}, bf16[256,2048]{1,0:T(8,128)(2,1)S(1)}, u32[]{:S(2)}, u32[]{:S(2)}) collective-permute-start(bf16[256,2048]{1,0:T(8,128)(2,1)S(1)} %get-tuple-element.22), channel_id=1, source_target_pairs={{0,1},{1,0},{2,3},{3,2},{4,5},{5,4},{6,7},{7,6},{8,9},{9,8},{10,11... | collective-permute-start | bytes 3145736 | tf_op jit(solution)/shard_map/ppermute | solution.py:340
  130.3 1.0 copy-start.3

commit v18 on v17

--- a/solution.py
+++ b/solution.py
@@ -138,7 +138,9 @@
     w = jnp.where(segc == seg_last, jnp.exp(last - cum), 0.0)
     scaled = (x_ref[...].astype(jnp.float32) * expand_heads(step)).astype(jnp.bfloat16)
     weighted = (scaled.astype(jnp.float32) * expand_heads(w)).astype(jnp.bfloat16)
-    block_state = jnp.dot(bt_ref[...], weighted, preferred_element_type=jnp.float32)
+    block_state = lax.dot_general(
+        bt_ref[...], weighted, (((0,), (0,)), ((), ())), preferred_element_type=jnp.float32
+    )
     decay = bdec_ref[0]
     acc_ref[...] = decay * acc_ref[...] + block_state
     dec_ref[...] = dec_ref[...] * decay
@@ -158,7 +160,7 @@
 
     operands = [bt, conv, dt_g, cum_g, segc, bdec]
     specs = [
-        pl.BlockSpec((STATE, STRETCH), lambda b, c: (grp(c), b)),
+        pl.BlockSpec((STRETCH, STATE), lambda b, c: (b, INNER // STATE + grp(c))),
         pl.BlockSpec((STRETCH, GROUP_COLS), lambda b, c: (b, grp(c))),
         pl.BlockSpec((1, STRETCH, PER_GROUP), lambda b, c: (grp(c), b, 0)),
         pl.BlockSpec((1, STRETCH, PER_GROUP), lambda b, c: (grp(c), b, 0)),
@@ -414,13 +416,12 @@
     segr = jnp.broadcast_to(segments[None, :], (8, tok)).astype(jnp.int32)
     eb = jnp.broadcast_to(seg_before[:, None, None], (nb, 8, 128)).reshape(nb * 8, 128)
     eb = eb.astype(jnp.int32)
-    bt = conv[:, INNER : INNER + GROUPS * STATE].T
     bdec = jnp.repeat(block_decay, HEAD_DIM, axis=1)[:, None, :]
 
     core_arr = lax.axis_index("core").astype(jnp.int32).reshape(1)
-    local_a, cdec_a, for_other = half_states(bt, conv, dt_g, cum_g, segc, bdec, core_arr, 0)
+    local_a, cdec_a, for_other = half_states(conv, conv, dt_g, cum_g, segc, bdec, core_arr, 0)
     local_states, cdec, mine = half_states(
-        bt, conv, dt_g, cum_g, segc, bdec, core_arr, 1, (local_a, cdec_a)
+        conv, conv, dt_g, cum_g, segc, bdec, core_arr, 1, (local_a, cdec_a)
     )
     dsk = jnp.repeat(d_skip, HEAD_DIM)[None, :]
     def first_work():

time: 140 us -> 138 us (0.986)
  local copies, waits for them, and re-layouts: 18.6 us -> 16.5 us
    unnamed x12 -> x11, local copies, waits for them, and re-layouts: 5.62 us -> 4.6 us
  transfers between devices with their start and end apart: 5 -> 5, of which waited for: 2 -> 2; matrix products, arithmetic and copies ran while one was open for 9% -> 9% of each run, Pallas kernels for 36% -> 37%
where the time goes in v18:
time: 138 us; the launch traced here: 137 us
  Pallas kernels  80.9 us (59%)
  local copies, waits for them, and re-layouts  16.5 us (12%)
  starting transfers between devices  15.2 us (11%)
  waiting for transfers between devices  14.2 us (10%)
  other arithmetic  10 us (7%)
    pallas_call x2, Pallas kernels, intra_part(): pl.pallas_call(kernel, grid=(nb,), in_specs=specs, out_specs=pl.BlockSpec...  34.8 us
    pallas_call x2, Pallas kernels, half_states(): pl.pallas_call(half_state_kernel, grid_spec=grid_spec, out_shape=[jax.Sha...  16 us
    pallas_call x2, Pallas kernels, mix(): pl.pallas_call(with_core, grid_spec=grid_spec, out_shape=jax.ShapeDtypeSt...  15.5 us
    pallas_call x1, Pallas kernels, conv_part(): pl.pallas_call(conv_kernel, grid=(chans // CONV_COLS,), in_specs=[pl.Bloc...  12 us
    all_to_all x1, waiting for transfers between devices, compose(): lax.all_to_all(entering, 'chip', split_axis=0, concat_axis=0, tiled=True)  7.66 us
    all_to_all x1, waiting for transfers between devices, compose(): lax.all_to_all(payload, 'chip', split_axis=0, concat_axis=0, tiled=True)  6.49 us
    unnamed x11, local copies, waits for them, and re-layouts  4.6 us
    all_to_all x1, starting transfers between devices, compose(): lax.all_to_all(payload, 'chip', split_axis=0, concat_axis=0, tiled=True)  4.6 us
  transfers between devices with their start and end apart: 5, of which 2 were waited for; matrix products, arithmetic and copies ran while one was open for 9% of the time, Pallas kernels for 37%

profile of v18, /device:TPU:1, one launch (start us, length us, event | category | flops | bytes accessed | tf_op | source)
XLA Modules:
  0.0 136.9 jit_solution(1495937340159806302)
XLA Ops:
  0.0 0.9 slice.54
  0.9 4.5 %collective-permute-start = (bf16[3,5120]{1,0:T(4,128)(2,1)S(1)}, bf16[3,5120]{1,0:T(4,128)(2,1)S(1)}, u32[]{:S(2)}, u32[]{:S(2)}) collective-permute-start(bf16[3,5120]{1,0:T(4,128)(2,1)S(1)} %slice.54), channel_id=1, source_target_pairs={{0,1},{1,2},{2,3},{3,4},{4,5},{5,6},{6,7},{7,8},{8,9},{9,10},{10,1... | collective-permute-start | bytes 92168 | tf_op jit(solution)/shard_map/ppermute | solution.py:23
  5.5 0.8 reduce-window.18
  6.6 0.2 fusion.5
  6.8 0.1 copy.77
  6.9 0.7 exp.14
  7.6 1.0 negate_multiply_fusion
  8.6 1.2 reduce-window.19
  9.8 0.2 slice_reduce_fusion
  10.1 0.1 bitcast_bitcast_fusion
  10.2 0.2 fusion.1
  10.4 0.2 compare_reduce_fusion
  10.6 0.1 copy.74
  10.8 0.9 copy.69.m_ref
  11.7 0.7 broadcast_in_dim_reshape.7.bdec_ref
  12.4 0.1 reshape_reshape.3
  12.5 1.0 copy.75
  13.5 1.0 copy.70
  14.6 0.7 concatenate.6.rim_ref
  15.2 12.0 %shard_map.100.c_ref.b_ref.x_ref.refs_0_.refs_1_.refs_2_.bt_ref = bf16[512,5120]{1,0:T(8,128)(2,1)} custom-call(bf16[512,5120]{1,0:T(8,128)(2,1)} %x_ref.1, bf16[8,5120]{1,0:T(8,128)(2,1)} %concatenate.6.rim_ref, f32[4,5120]{1,0:T(4,128)} %w_ref.1, f32[1,5120]{1,0:T(1,128)} %bitcast.70, f32[512,4]{1,0:T(8,128)} %copy.69.m_ref), custom_call_target="tpu_custom_call" | custom-call | tf_op jit(solution)/shard_map/pallas_call | solution.py:72
  27.3 0.8 broadcast_in_dim.33.segc_ref.refs_6_.refs_7_
  28.1 8.0 %shard_map.103 = (f32[2,256,4096]{2,1,0:T(8,128)}, f32[2,1,4096]{2,1,0:T(1,128)}, f32[257,2048]{1,0:T(8,128)}) custom-call(s32[1]{0:T(128)} %bitcast.core_ref, bf16[512,5120]{1,0:T(8,128)(2,1)} %shard_map.100.c_ref.b_ref.x_ref.refs_0_.refs_1_.refs_2_.bt_ref, bf16[512,5120]{1,0:T(8,128)(2,1)} %shard_map.100.c_ref.b_ref.x_ref.refs_0_.refs_1_.refs_2_.bt_ref, ...), custom_call_target="tpu_custom_call" | custom-call | tf_op jit(solution)/shard_map/pallas_call | solution.py:189
  36.1 8.0 %shard_map.104 = (f32[2,256,4096]{2,1,0:T(8,128)}, f32[2,1,4096]{2,1,0:T(1,128)}, f32[257,2048]{1,0:T(8,128)}) custom-call(s32[1]{0:T(128)} %bitcast.core_ref, bf16[512,5120]{1,0:T(8,128)(2,1)} %shard_map.100.c_ref.b_ref.x_ref.refs_0_.refs_1_.refs_2_.bt_ref, ...), custom_call_target="tpu_custom_call", output_to_operand_aliasing={{0}: (7, {}), {1}: (8, {})} | custom-call | tf_op jit(solution)/shard_map/pallas_call | solution.py:189
  44.1 1.3 copy-done.2
  45.4 2.6 %broadcast_select_fusion.1 = (f32[257,2048]{1,0:T(8,128)S(1)}, f32[257,2048]{1,0:T(8,128)S(1)}) fusion(f32[257,2048]{1,0:T(8,128)} %get-tuple-element.13, f32[257,2048]{1,0:T(8,128)} %copy-done.2, pred[]{:T(512)S(6)} %eq.23), kind=kLoop, calls=%fused_computation.9 | loop fusion | flops 1052672 | bytes 8421377 | tf_op jit(solution)/shard_map/jit(_where)/select_n | solution.py:364
  48.1 0.4 fusion
  48.6 0.3 copy.85
  49.0 1.2 copy.92
  50.2 4.6 %all-to-all-start = ((bf16[8,258,256]{2,1,0:T(8,128)(2,1)}), bf16[8,258,256]{2,1,0:T(8,128)(2,1)S(1)}, u32[]{:S(2)}, u32[]{:S(2)}) async-start(bf16[8,258,256]{2,1,0:T(8,128)(2,1)} %bitcast.59), calls=%async_computation | async-start | bytes 2162688 | tf_op jit(solution)/shard_map/all_to_all | solution.py:375
  54.8 0.7 copy.83
  55.5 0.7 broadcast_in_dim_reshape.6.dsk_ref.refs_8_
  56.2 0.6 broadcast_in_dim.60.segr_ref.refs_7_
  56.8 17.4 %shard_map.101.refs_9_.refs_1_ = f32[512,4096]{1,0:T(8,128)} custom-call(bf16[512,5120]{1,0:T(8,128)(2,1)} %shard_map.100.c_ref.b_ref.x_ref.refs_0_.refs_1_.refs_2_.bt_ref, bf16[512,5120]{1,0:T(8,128)(2,1)} %shard_map.100.c_ref.b_ref.x_ref.refs_0_.refs_1_.refs_2_.bt_ref, bf16[512,5120]{1,0:T(8,128)(2,1)} %shard_map.100.c_ref.b_ref.x_ref.refs_0_.refs_1_.refs_2_.bt_ref, ...), custom_call_target="tpu_custom_call" | custom-call | tf_op jit(solution)/shard_map/pallas_call | solution.py:252
  74.2 6.5 %all-to-all-done.refs_0_ = bf16[8,258,256]{2,1,0:T(8,128)(2,1)S(1)} async-done(((bf16[8,258,256]{2,1,0:T(8,128)(2,1)}), bf16[8,258,256]{2,1,0:T(8,128)(2,1)S(1)}, u32[]{:S(2)}, u32[]{:S(2)}) %all-to-all-start) | async-done | bytes 1056800 | tf_op jit(solution)/shard_map/all_to_all | solution.py:375
  80.7 1.0 copy-done
  81.6 2.6 %shard_map.106 = bf16[8,256,256]{2,1,0:T(8,128)(2,1)} custom-call(bf16[8,258,256]{2,1,0:T(8,128)(2,1)} %shard_map.105.got_ref), custom_call_target="tpu_custom_call" | custom-call | tf_op jit(solution)/shard_map/pallas_call | solution.py:376
  84.2 4.4 %all-to-all-start.1 = ((bf16[8,256,256]{2,1,0:T(8,128)(2,1)}), bf16[8,256,256]{2,1,0:T(8,128)(2,1)S(1)}, u32[]{:S(2)}, u32[]{:S(2)}) async-start(bf16[8,256,256]{2,1,0:T(8,128)(2,1)} %shard_map.106), calls=%async_computation.1 | async-start | bytes 2097152 | tf_op jit(solution)/shard_map/all_to_all | solution.py:381
  88.6 17.5 %shard_map.102.refs_1_ = f32[512,4096]{1,0:T(8,128)} custom-call(bf16[512,5120]{1,0:T(8,128)(2,1)} %shard_map.100.c_ref.b_ref.x_ref.refs_0_.refs_1_.refs_2_.bt_ref, bf16[512,5120]{1,0:T(8,128)(2,1)} %shard_map.100.c_ref.b_ref.x_ref.refs_0_.refs_1_.refs_2_.bt_ref, ...), custom_call_target="tpu_custom_call", output_to_operand_aliasing={{}: (9, {})} | custom-call | tf_op jit(solution)/shard_map/pallas_call | solution.py:252
  106.1 7.7 %all-to-all-done.1.refs_0_ = bf16[8,256,256]{2,1,0:T(8,128)(2,1)S(1)} async-done(((bf16[8,256,256]{2,1,0:T(8,128)(2,1)}), bf16[8,256,256]{2,1,0:T(8,128)(2,1)S(1)}, u32[]{:S(2)}, u32[]{:S(2)}) %all-to-all-start.1) | async-done | bytes 1048608 | tf_op jit(solution)/shard_map/all_to_all | solution.py:381
  113.7 1.0 copy-done.1
  114.7 1.4 %convert_bitcast_fusion = f32[8,32,8,256]{3,2,1,0:T(8,128)S(1)} fusion(bf16[8,256,256]{2,1,0:T(8,128)(2,1)} %shard_map.107), kind=kLoop, calls=%fused_computation.2 | loop fusion | flops 524288 | bytes 3145728
  116.1 0.3 copy.84
  116.4 1.6 %select_convert_fusion = (bf16[256,2048]{1,0:T(8,128)(2,1)}, bf16[256,2048]{1,0:T(8,128)(2,1)S(1)}) fusion(f32[256,2048]{1,0:T(8,128)S(1)} %bitcast.58, f32[257,2048]{1,0:T(8,128)S(1)} %get-tuple-element.19, f32[2048]{0:T(1024)S(1)} %bitcast.68, pred[]{:T(512)S(6)} %eq.23), kind=kLoop, calls=%fused_computation.3 | loop fusion | flops 3145728 | bytes 6299649 | tf_op jit(solution)/shard_map/convert_element_type | solution.py:384
  118.0 1.6 %collective-permute-start.2 = (bf16[256,2048]{1,0:T(8,128)(2,1)S(1)}, bf16[256,2048]{1,0:T(8,128)(2,1)S(1)}, u32[]{:S(2)}, u32[]{:S(2)}) collective-permute-start(bf16[256,2048]{1,0:T(8,128)(2,1)S(1)} %get-tuple-element.22), channel_id=1, source_target_pairs={{0,1},{1,0},{2,3},{3,2},{4,5},{5,4},{6,7},{7,6},{8,9},{9,8},{10,11... | collective-permute-start | bytes 3145736 | tf_op jit(solution)/shard_map/ppermute | solution.py:342
  119.8 0.7 broadcast_in_dim.68.refs_8_
  120.4 7.8 %shard_map.108.refs_10_ = bf16[512,4096]{1,0:T(8,128)(2,1)} custom-call(s32[1]{0:T(128)} %bitcast.core_ref, bf16[512,5120]{1,0:T(8,128)(2,1)} %shard_map.100.c_ref.b_ref.x_ref.refs_0_.refs_1_.refs_2_.bt_ref, f32[512,4096]{1,0:T(8,128)} %shard_map.102.refs_1_, bf16[512,4096]{1,0:T(8,128)(2,1)} %refs_2_.3, bf16[256,2048]{1,0:T(8,128)(2,1)} %get-tuple-element.21.refs_3_, ...), custom_call_target="tpu_custom_call" | custom-call | tf_op jit(solution)/shard_map/pallas_call | solution.py:320
  128.2 1.0 copy-done.3
  129.2 7.8 %shard_map.109 = bf16[512,4096]{1,0:T(8,128)(2,1)} custom-call(s32[1]{0:T(128)} %bitcast.core_ref, bf16[512,5120]{1,0:T(8,128)(2,1)} %shard_map.100.c_ref.b_ref.x_ref.refs_0_.refs_1_.refs_2_.bt_ref, f32[512,4096]{1,0:T(8,128)} %shard_map.102.refs_1_, bf16[512,4096]{1,0:T(8,128)(2,1)} %refs_2_.3, ...), custom_call_target="tpu_custom_call", output_to_operand_aliasing={{}: (11, {})} | custom-call | tf_op jit(solution)/shard_map/pallas_call | solution.py:320
  (35 shorter events, 1.0 us)
Async XLA Ops:
  0.9 13.6 %collective-permute-start = (bf16[3,5120]{1,0:T(4,128)(2,1)S(1)}, bf16[3,5120]{1,0:T(4,128)(2,1)S(1)}, u32[]{:S(2)}, u32[]{:S(2)}) collective-permute-start(bf16[3,5120]{1,0:T(4,128)(2,1)S(1)} %slice.54), channel_id=1, source_target_pairs={{0,1},{1,2},{2,3},{3,4},{4,5},{5,6},{6,7},{7,8},{8,9},{9,10},{10,1... | collective-permute-start | bytes 92168 | tf_op jit(solution)/shard_map/ppermute | solution.py:23
  36.1 8.0 %collective-permute-start.1 = (f32[257,2048]{1,0:T(8,128)}, f32[257,2048]{1,0:T(8,128)S(1)}, u32[]{:S(2)}, u32[]{:S(2)}) collective-permute-start(f32[257,2048]{1,0:T(8,128)} %get-tuple-element.14), channel_id=1, source_target_pairs={{0,1},{1,0},{2,3},{3,2},{4,5},{5,4},{6,7},{7,6},{8,9},{9,8},{10,11... | collective-permute-start | bytes 6316040 | tf_op jit(solution)/shard_map/ppermute | solution.py:342
  44.1 1.3 copy-start.2
  49.0 6.5 %copy-start.4 = (f32[64]{0:T(128)S(1)}, f32[64]{0:T(128)}, u32[]{:S(2)}) copy-start(f32[64]{0:T(128)} %param.18) | copy-start | bytes 772
  50.2 30.5 %all-to-all-start = ((bf16[8,258,256]{2,1,0:T(8,128)(2,1)}), bf16[8,258,256]{2,1,0:T(8,128)(2,1)S(1)}, u32[]{:S(2)}, u32[]{:S(2)}) async-start(bf16[8,258,256]{2,1,0:T(8,128)(2,1)} %bitcast.59), calls=%async_computation | async-start | bytes 2162688 | tf_op jit(solution)/shard_map/all_to_all | solution.py:375
  80.6 1.0 copy-start
  84.2 29.5 %all-to-all-start.1 = ((bf16[8,256,256]{2,1,0:T(8,128)(2,1)}), bf16[8,256,256]{2,1,0:T(8,128)(2,1)S(1)}, u32[]{:S(2)}, u32[]{:S(2)}) async-start(bf16[8,256,256]{2,1,0:T(8,128)(2,1)} %shard_map.106), calls=%async_computation.1 | async-start | bytes 2097152 | tf_op jit(solution)/shard_map/all_to_all | solution.py:381
  113.7 1.0 copy-start.1
  118.0 10.2 %collective-permute-start.2 = (bf16[256,2048]{1,0:T(8,128)(2,1)S(1)}, bf16[256,2048]{1,0:T(8,128)(2,1)S(1)}, u32[]{:S(2)}, u32[]{:S(2)}) collective-permute-start(bf16[256,2048]{1,0:T(8,128)(2,1)S(1)} %get-tuple-element.22), channel_id=1, source_target_pairs={{0,1},{1,0},{2,3},{3,2},{4,5},{5,4},{6,7},{7,6},{8,9},{9,8},{10,11... | collective-permute-start | bytes 3145736 | tf_op jit(solution)/shard_map/ppermute | solution.py:342
  128.2 1.0 copy-start.3

commit v19 on v18

--- a/solution.py
+++ b/solution.py
@@ -400,18 +400,18 @@
     ]
     masks = jnp.stack(kept, axis=1).astype(jnp.float32)
     conv = conv_part(xbc, rim8, conv_weight, conv_bias[None, :], masks)
-    step = jax.nn.softplus(dt_raw.astype(jnp.float32) + dt_bias[None, :])
-    log_decay = -step * jnp.exp(a_log)[None, :]
-    cum = jnp.cumsum(log_decay.reshape(nb, STRETCH, HEADS), axis=1).reshape(tok, HEADS)
+    raw_g = dt_raw.reshape(tok, GROUPS, PER_GROUP).transpose(1, 0, 2).astype(jnp.float32)
+    dt_g = jax.nn.softplus(raw_g + dt_bias.reshape(GROUPS, 1, PER_GROUP))
+    log_decay = -dt_g * jnp.exp(a_log).reshape(GROUPS, 1, PER_GROUP)
+    cum_blocks = jnp.cumsum(log_decay.reshape(GROUPS, nb, STRETCH, PER_GROUP), axis=2)
+    cum_g = cum_blocks.reshape(GROUPS, tok, PER_GROUP)
     segments = segment_of(first_pos + jnp.arange(tok), lengths)
     seg_before = segment_of(first_pos + jnp.arange(nb) * STRETCH - 1, lengths)
     seg_last = segments.reshape(nb, STRETCH)[:, -1]
-    cum_last = cum.reshape(nb, STRETCH, HEADS)[:, -1, :]
+    cum_last = cum_blocks[:, :, -1, :].transpose(1, 0, 2).reshape(nb, HEADS)
     block_decay = jnp.where((seg_last == seg_before)[:, None], jnp.exp(cum_last), 0.0)
 
-    cum_g = cum.reshape(tok, GROUPS, PER_GROUP).transpose(1, 0, 2)
-    dt_g = step.reshape(tok, GROUPS, PER_GROUP).transpose(1, 0, 2)
-    cumt_g = cum.T.reshape(GROUPS, PER_GROUP, tok)
+    cumt_g = cum_g.transpose(0, 2, 1)
     segc = jnp.broadcast_to(segments[:, None], (tok, 128)).astype(jnp.int32)
     segr = jnp.broadcast_to(segments[None, :], (8, tok)).astype(jnp.int32)
     eb = jnp.broadcast_to(seg_before[:, None, None], (nb, 8, 128)).reshape(nb * 8, 128)

time: 138 us -> 138 us (level)
    unnamed x11 -> x9, local copies, waits for them, and re-layouts: 4.6 us -> 2.65 us
    reshape x2 -> x1, local copies, waits for them, and re-layouts: 1.68 us -> 0.17 us  [local(): log_decay.reshape(GROUPS, nb, STRETCH, PER_GROUP)]
    another operation x3 -> x4, other arithmetic: 2.08 us -> 3.3 us
  transfers between devices with their start and end apart: 5 -> 5, of which waited for: 2 -> 2; matrix products, arithmetic and copies ran while one was open for 9% -> 10% of each run, Pallas kernels for 37% -> 37%
where the time goes in v19:
time: 138 us; the launch traced here: 137 us
  Pallas kernels  80.9 us (59%)
  starting transfers between devices  15.8 us (11%)
  local copies, waits for them, and re-layouts  15.5 us (11%)
  waiting for transfers between devices  13.7 us (10%)
  other arithmetic  11.2 us (8%)
    pallas_call x2, Pallas kernels, intra_part(): pl.pallas_call(kernel, grid=(nb,), in_specs=specs, out_specs=pl.BlockSpec...  34.9 us
    pallas_call x2, Pallas kernels, half_states(): pl.pallas_call(half_state_kernel, grid_spec=grid_spec, out_shape=[jax.Sha...  16 us
    pallas_call x2, Pallas kernels, mix(): pl.pallas_call(with_core, grid_spec=grid_spec, out_shape=jax.ShapeDtypeSt...  15.5 us
    pallas_call x1, Pallas kernels, conv_part(): pl.pallas_call(conv_kernel, grid=(chans // CONV_COLS,), in_specs=[pl.Bloc...  12 us
    all_to_all x1, waiting for transfers between devices, compose(): lax.all_to_all(entering, 'chip', split_axis=0, concat_axis=0, tiled=True)  7.28 us
    all_to_all x1, waiting for transfers between devices, compose(): lax.all_to_all(payload, 'chip', split_axis=0, concat_axis=0, tiled=True)  6.42 us
    all_to_all x1, starting transfers between devices, compose(): lax.all_to_all(payload, 'chip', split_axis=0, concat_axis=0, tiled=True)  4.6 us
    ppermute x1, starting transfers between devices, shifted(): return lax.ppermute(value, axis, pairs)  4.54 us
  transfers between devices with their start and end apart: 5, of which 2 were waited for; matrix products, arithmetic and copies ran while one was open for 10% of the time, Pallas kernels for 37%

profile of v19, /device:TPU:1, one launch (start us, length us, event | category | flops | bytes accessed | tf_op | source)
XLA Modules:
  0.0 137.4 jit_solution(17959166126373192715)
XLA Ops:
  0.0 0.9 slice.54
  0.9 4.5 %collective-permute-start = (bf16[3,5120]{1,0:T(4,128)(2,1)S(1)}, bf16[3,5120]{1,0:T(4,128)(2,1)S(1)}, u32[]{:S(2)}, u32[]{:S(2)}) collective-permute-start(bf16[3,5120]{1,0:T(4,128)(2,1)S(1)} %slice.54), channel_id=1, source_target_pairs={{0,1},{1,2},{2,3},{3,4},{4,5},{5,6},{6,7},{7,8},{8,9},{9,10},{10,1... | collective-permute-start | bytes 92168 | tf_op jit(solution)/shard_map/ppermute | solution.py:23
  5.5 0.8 reduce-window.18
  6.5 0.1 convert_reduce_fusion.1
  6.6 0.2 fusion.9
  6.8 0.1 copy.85
  6.9 1.0 copy.78
  7.9 0.7 exp.20
  8.7 0.7 add.67
  9.4 1.1 negate_multiply_fusion
  10.5 0.2 copy.79
  10.7 2.3 %reduce-window.19 = f32[2,2,32,2,128]{4,2,3,1,0:T(8,128)S(1)} reduce-window(f32[2,2,32,2,128]{4,2,3,1,0:T(8,128)S(1)} %copy_bitcast_fusion.1, f32[]{:T(128)} %constant.35.clone.1), window={size=1x1x1x1x128 pad=0_0x0_0x0_0x0_0x127_0}, to_apply=%region_2.3 | reduce-window | flops 4161536 | bytes 262148 | tf_op jit(solution)/shard_map/reduce-window.1
  13.0 0.2 slice_reduce_fusion
  13.3 0.1 bitcast_bitcast_fusion
  13.4 0.2 fusion.5
  13.7 0.2 compare_reduce_fusion
  14.0 1.0 copy.82
  15.0 0.9 copy.77.m_ref
  15.9 0.7 broadcast_in_dim_reshape.7.bdec_ref
  16.6 0.7 concatenate.6.rim_ref
  17.3 12.0 %shard_map.100.c_ref.b_ref.x_ref.refs_0_.refs_1_.refs_2_.bt_ref = bf16[512,5120]{1,0:T(8,128)(2,1)} custom-call(bf16[512,5120]{1,0:T(8,128)(2,1)} %x_ref.1, bf16[8,5120]{1,0:T(8,128)(2,1)} %concatenate.6.rim_ref, f32[4,5120]{1,0:T(4,128)} %w_ref.1, f32[1,5120]{1,0:T(1,128)} %bitcast.72, f32[512,4]{1,0:T(8,128)} %copy.77.m_ref), custom_call_target="tpu_custom_call" | custom-call | tf_op jit(solution)/shard_map/pallas_call | solution.py:72
  29.3 0.8 broadcast_in_dim.57.segc_ref.refs_6_.refs_7_
  30.1 8.0 %shard_map.103 = (f32[2,256,4096]{2,1,0:T(8,128)}, f32[2,1,4096]{2,1,0:T(1,128)}, f32[257,2048]{1,0:T(8,128)}) custom-call(s32[1]{0:T(128)} %bitcast.core_ref, bf16[512,5120]{1,0:T(8,128)(2,1)} %shard_map.100.c_ref.b_ref.x_ref.refs_0_.refs_1_.refs_2_.bt_ref, bf16[512,5120]{1,0:T(8,128)(2,1)} %shard_map.100.c_ref.b_ref.x_ref.refs_0_.refs_1_.refs_2_.bt_ref, ...), custom_call_target="tpu_custom_call" | custom-call | tf_op jit(solution)/shard_map/pallas_call | solution.py:189
  38.1 8.0 %shard_map.104 = (f32[2,256,4096]{2,1,0:T(8,128)}, f32[2,1,4096]{2,1,0:T(1,128)}, f32[257,2048]{1,0:T(8,128)}) custom-call(s32[1]{0:T(128)} %bitcast.core_ref, bf16[512,5120]{1,0:T(8,128)(2,1)} %shard_map.100.c_ref.b_ref.x_ref.refs_0_.refs_1_.refs_2_.bt_ref, ...), custom_call_target="tpu_custom_call", output_to_operand_aliasing={{0}: (7, {}), {1}: (8, {})} | custom-call | tf_op jit(solution)/shard_map/pallas_call | solution.py:189
  46.2 1.3 copy-done.1
  47.5 2.6 %broadcast_select_fusion.1 = (f32[257,2048]{1,0:T(8,128)S(1)}, f32[257,2048]{1,0:T(8,128)S(1)}) fusion(f32[257,2048]{1,0:T(8,128)} %get-tuple-element.13, f32[257,2048]{1,0:T(8,128)} %copy-done.1, pred[]{:T(512)S(6)} %eq.23), kind=kLoop, calls=%fused_computation.10 | loop fusion | flops 1052672 | bytes 8421377 | tf_op jit(solution)/shard_map/jit(_where)/select_n | solution.py:364
  50.1 0.4 fusion
  50.5 0.1 pad_maximum_fusion
  50.6 0.3 copy.92
  51.0 1.2 copy.96
  52.2 4.6 %all-to-all-start = ((bf16[8,258,256]{2,1,0:T(8,128)(2,1)}), bf16[8,258,256]{2,1,0:T(8,128)(2,1)}, u32[]{:S(2)}, u32[]{:S(2)}) async-start(bf16[8,258,256]{2,1,0:T(8,128)(2,1)} %bitcast.63), calls=%async_computation | async-start | bytes 2162688 | tf_op jit(solution)/shard_map/all_to_all | solution.py:375
  56.8 0.8 copy.84.cumt_ref.refs_5_
  57.7 0.7 broadcast_in_dim_reshape.6.dsk_ref.refs_8_
  58.4 0.6 broadcast_in_dim.58.segr_ref.refs_7_
  59.0 17.4 %shard_map.101.refs_9_.refs_1_ = f32[512,4096]{1,0:T(8,128)} custom-call(bf16[512,5120]{1,0:T(8,128)(2,1)} %shard_map.100.c_ref.b_ref.x_ref.refs_0_.refs_1_.refs_2_.bt_ref, bf16[512,5120]{1,0:T(8,128)(2,1)} %shard_map.100.c_ref.b_ref.x_ref.refs_0_.refs_1_.refs_2_.bt_ref, bf16[512,5120]{1,0:T(8,128)(2,1)} %shard_map.100.c_ref.b_ref.x_ref.refs_0_.refs_1_.refs_2_.bt_ref, ...), custom_call_target="tpu_custom_call" | custom-call | tf_op jit(solution)/shard_map/pallas_call | solution.py:252
  76.4 6.4 %all-to-all-done.refs_0_ = bf16[8,258,256]{2,1,0:T(8,128)(2,1)} async-done(((bf16[8,258,256]{2,1,0:T(8,128)(2,1)}), bf16[8,258,256]{2,1,0:T(8,128)(2,1)}, u32[]{:S(2)}, u32[]{:S(2)}) %all-to-all-start) | async-done | bytes 1056800 | tf_op jit(solution)/shard_map/all_to_all | solution.py:375
  82.8 2.5 %shard_map.106 = bf16[8,256,256]{2,1,0:T(8,128)(2,1)} custom-call(bf16[8,258,256]{2,1,0:T(8,128)(2,1)} %shard_map.105.got_ref), custom_call_target="tpu_custom_call" | custom-call | tf_op jit(solution)/shard_map/pallas_call | solution.py:376
  85.3 4.5 %all-to-all-start.1 = ((bf16[8,256,256]{2,1,0:T(8,128)(2,1)}), bf16[8,256,256]{2,1,0:T(8,128)(2,1)}, u32[]{:S(2)}, u32[]{:S(2)}) async-start(bf16[8,256,256]{2,1,0:T(8,128)(2,1)} %shard_map.106), calls=%async_computation.1 | async-start | bytes 2097152 | tf_op jit(solution)/shard_map/all_to_all | solution.py:381
  89.8 17.5 %shard_map.102.refs_1_ = f32[512,4096]{1,0:T(8,128)} custom-call(bf16[512,5120]{1,0:T(8,128)(2,1)} %shard_map.100.c_ref.b_ref.x_ref.refs_0_.refs_1_.refs_2_.bt_ref, bf16[512,5120]{1,0:T(8,128)(2,1)} %shard_map.100.c_ref.b_ref.x_ref.refs_0_.refs_1_.refs_2_.bt_ref, ...), custom_call_target="tpu_custom_call", output_to_operand_aliasing={{}: (9, {})} | custom-call | tf_op jit(solution)/shard_map/pallas_call | solution.py:252
  107.3 7.3 %all-to-all-done.1.refs_0_ = bf16[8,256,256]{2,1,0:T(8,128)(2,1)} async-done(((bf16[8,256,256]{2,1,0:T(8,128)(2,1)}), bf16[8,256,256]{2,1,0:T(8,128)(2,1)}, u32[]{:S(2)}, u32[]{:S(2)}) %all-to-all-start.1) | async-done | bytes 1048608 | tf_op jit(solution)/shard_map/all_to_all | solution.py:381
  114.6 1.4 %convert_bitcast_fusion = f32[8,32,8,256]{3,2,1,0:T(8,128)S(1)} fusion(bf16[8,256,256]{2,1,0:T(8,128)(2,1)} %shard_map.107), kind=kLoop, calls=%fused_computation.2 | loop fusion | flops 524288 | bytes 3145728
  116.0 0.3 copy.91
  116.3 1.6 %select_convert_fusion = (bf16[256,2048]{1,0:T(8,128)(2,1)}, bf16[256,2048]{1,0:T(8,128)(2,1)S(1)}) fusion(f32[256,2048]{1,0:T(8,128)S(1)} %bitcast.62, f32[257,2048]{1,0:T(8,128)S(1)} %get-tuple-element.21, f32[2048]{0:T(1024)S(1)} %bitcast.70, pred[]{:T(512)S(6)} %eq.23), kind=kLoop, calls=%fused_computation.3 | loop fusion | flops 3145728 | bytes 6299649 | tf_op jit(solution)/shard_map/convert_element_type | solution.py:384
  117.8 2.2 %collective-permute-start.2 = (bf16[256,2048]{1,0:T(8,128)(2,1)S(1)}, bf16[256,2048]{1,0:T(8,128)(2,1)S(1)}, u32[]{:S(2)}, u32[]{:S(2)}) collective-permute-start(bf16[256,2048]{1,0:T(8,128)(2,1)S(1)} %get-tuple-element.24), channel_id=1, source_target_pairs={{0,1},{1,0},{2,3},{3,2},{4,5},{5,4},{6,7},{7,6},{8,9},{9,8},{10,11... | collective-permute-start | bytes 3145736 | tf_op jit(solution)/shard_map/ppermute | solution.py:342
  120.2 0.7 broadcast_in_dim.66.refs_8_
  120.9 7.8 %shard_map.108.refs_10_ = bf16[512,4096]{1,0:T(8,128)(2,1)} custom-call(s32[1]{0:T(128)} %bitcast.core_ref, bf16[512,5120]{1,0:T(8,128)(2,1)} %shard_map.100.c_ref.b_ref.x_ref.refs_0_.refs_1_.refs_2_.bt_ref, f32[512,4096]{1,0:T(8,128)} %shard_map.102.refs_1_, bf16[512,4096]{1,0:T(8,128)(2,1)} %refs_2_.3, bf16[256,2048]{1,0:T(8,128)(2,1)} %get-tuple-element.23.refs_3_, ...), custom_call_target="tpu_custom_call" | custom-call | tf_op jit(solution)/shard_map/pallas_call | solution.py:320
  128.7 1.0 copy-done.2
  129.7 7.8 %shard_map.109 = bf16[512,4096]{1,0:T(8,128)(2,1)} custom-call(s32[1]{0:T(128)} %bitcast.core_ref, bf16[512,5120]{1,0:T(8,128)(2,1)} %shard_map.100.c_ref.b_ref.x_ref.refs_0_.refs_1_.refs_2_.bt_ref, f32[512,4096]{1,0:T(8,128)} %shard_map.102.refs_1_, bf16[512,4096]{1,0:T(8,128)(2,1)} %refs_2_.3, ...), custom_call_target="tpu_custom_call", output_to_operand_aliasing={{}: (11, {})} | custom-call | tf_op jit(solution)/shard_map/pallas_call | solution.py:320
  (36 shorter events, 1.0 us)
Async XLA Ops:
  0.9 15.7 %collective-permute-start = (bf16[3,5120]{1,0:T(4,128)(2,1)S(1)}, bf16[3,5120]{1,0:T(4,128)(2,1)S(1)}, u32[]{:S(2)}, u32[]{:S(2)}) collective-permute-start(bf16[3,5120]{1,0:T(4,128)(2,1)S(1)} %slice.54), channel_id=1, source_target_pairs={{0,1},{1,2},{2,3},{3,4},{4,5},{5,6},{6,7},{7,8},{8,9},{9,10},{10,1... | collective-permute-start | bytes 92168 | tf_op jit(solution)/shard_map/ppermute | solution.py:23
  38.1 8.0 %collective-permute-start.1 = (f32[257,2048]{1,0:T(8,128)}, f32[257,2048]{1,0:T(8,128)S(1)}, u32[]{:S(2)}, u32[]{:S(2)}) collective-permute-start(f32[257,2048]{1,0:T(8,128)} %get-tuple-element.14), channel_id=1, source_target_pairs={{0,1},{1,0},{2,3},{3,2},{4,5},{5,4},{6,7},{7,6},{8,9},{9,8},{10,11... | collective-permute-start | bytes 6316040 | tf_op jit(solution)/shard_map/ppermute | solution.py:342
  46.2 1.3 copy-start.1
  51.0 5.8 %copy-start = (f32[2,2,256,32]{3,2,1,0:T(8,128)S(1)}, f32[2,2,256,32]{3,2,1,0:T(8,128)}, u32[]{:S(2)}) copy-start(f32[2,2,256,32]{3,2,1,0:T(8,128)} %copy.82) | copy-start | bytes 393220
  51.0 6.6 %copy-start.3 = (f32[64]{0:T(128)S(1)}, f32[64]{0:T(128)}, u32[]{:S(2)}) copy-start(f32[64]{0:T(128)} %param.18) | copy-start | bytes 772
  52.2 30.6 %all-to-all-start = ((bf16[8,258,256]{2,1,0:T(8,128)(2,1)}), bf16[8,258,256]{2,1,0:T(8,128)(2,1)}, u32[]{:S(2)}, u32[]{:S(2)}) async-start(bf16[8,258,256]{2,1,0:T(8,128)(2,1)} %bitcast.63), calls=%async_computation | async-start | bytes 2162688 | tf_op jit(solution)/shard_map/all_to_all | solution.py:375
  85.3 29.2 %all-to-all-start.1 = ((bf16[8,256,256]{2,1,0:T(8,128)(2,1)}), bf16[8,256,256]{2,1,0:T(8,128)(2,1)}, u32[]{:S(2)}, u32[]{:S(2)}) async-start(bf16[8,256,256]{2,1,0:T(8,128)(2,1)} %shard_map.106), calls=%async_computation.1 | async-start | bytes 2097152 | tf_op jit(solution)/shard_map/all_to_all | solution.py:381
  117.8 10.8 %collective-permute-start.2 = (bf16[256,2048]{1,0:T(8,128)(2,1)S(1)}, bf16[256,2048]{1,0:T(8,128)(2,1)S(1)}, u32[]{:S(2)}, u32[]{:S(2)}) collective-permute-start(bf16[256,2048]{1,0:T(8,128)(2,1)S(1)} %get-tuple-element.24), channel_id=1, source_target_pairs={{0,1},{1,0},{2,3},{3,2},{4,5},{5,4},{6,7},{7,6},{8,9},{9,8},{10,11... | collective-permute-start | bytes 3145736 | tf_op jit(solution)/shard_map/ppermute | solution.py:342
  128.6 1.0 copy-start.2

commit v20 on v19

--- a/solution.py
+++ b/solution.py
@@ -164,7 +164,7 @@
         pl.BlockSpec((STRETCH, GROUP_COLS), lambda b, c: (b, grp(c))),
         pl.BlockSpec((1, STRETCH, PER_GROUP), lambda b, c: (grp(c), b, 0)),
         pl.BlockSpec((1, STRETCH, PER_GROUP), lambda b, c: (grp(c), b, 0)),
-        pl.BlockSpec((STRETCH, 128), lambda b, c: (b, 0)),
+        pl.BlockSpec((STRETCH, 1), lambda b, c: (b, 0)),
         pl.BlockSpec((1, 1, GROUP_COLS), lambda b, c: (b, 0, grp(c))),
     ]
     aliases = {}
@@ -235,7 +235,7 @@
         pl.BlockSpec((1, STRETCH, PER_GROUP), lambda b: (g, b, 0)),
         pl.BlockSpec((1, STRETCH, PER_GROUP), lambda b: (g, b, 0)),
         pl.BlockSpec((1, PER_GROUP, STRETCH), lambda b: (g, 0, b)),
-        pl.BlockSpec((STRETCH, 128), lambda b: (b, 0)),
+        pl.BlockSpec((STRETCH, 1), lambda b: (b, 0)),
         pl.BlockSpec((8, STRETCH), lambda b: (0, b)),
         pl.BlockSpec((1, GROUP_COLS), lambda b: (0, g)),
     ]
@@ -293,7 +293,7 @@
         pl.BlockSpec((1, STATE, GROUP_COLS), lambda b, c: (b, 0, grp(c))),
         pl.BlockSpec((1, 1, GROUP_COLS), lambda b, c: (b, 0, grp(c))),
         pl.BlockSpec((1, STRETCH, PER_GROUP), lambda b, c: (grp(c), b, 0)),
-        pl.BlockSpec((STRETCH, 128), lambda b, c: (b, 0)),
+        pl.BlockSpec((STRETCH, 1), lambda b, c: (b, 0)),
         pl.BlockSpec((8, 128), lambda b, c: (b, 0)),
         pl.BlockSpec((1, GROUP_COLS), lambda b, c: (0, grp(c))),
     ]
@@ -412,7 +412,7 @@
     block_decay = jnp.where((seg_last == seg_before)[:, None], jnp.exp(cum_last), 0.0)
 
     cumt_g = cum_g.transpose(0, 2, 1)
-    segc = jnp.broadcast_to(segments[:, None], (tok, 128)).astype(jnp.int32)
+    segc = segments[:, None].astype(jnp.int32)
     segr = jnp.broadcast_to(segments[None, :], (8, tok)).astype(jnp.int32)
     eb = jnp.broadcast_to(seg_before[:, None, None], (nb, 8, 128)).reshape(nb * 8, 128)
     eb = eb.astype(jnp.int32)

time: 138 us -> 138 us (level)
  transfers between devices with their start and end apart: 5 -> 5, of which waited for: 2 -> 2; matrix products, arithmetic and copies ran while one was open for 10% -> 11% of each run, Pallas kernels for 37% -> 37%
where the time goes in v20:
time: 138 us; the launch traced here: 137 us
  Pallas kernels  80.9 us (59%)
  starting transfers between devices  15.8 us (11%)
  local copies, waits for them, and re-layouts  15.5 us (11%)
  waiting for transfers between devices  13.7 us (10%)
  other arithmetic  11.2 us (8%)
    pallas_call x2, Pallas kernels, intra_part(): pl.pallas_call(kernel, grid=(nb,), in_specs=specs, out_specs=pl.BlockSpec...  34.9 us
    pallas_call x2, Pallas kernels, half_states(): pl.pallas_call(half_state_kernel, grid_spec=grid_spec, out_shape=[jax.Sha...  16 us
    pallas_call x2, Pallas kernels, mix(): pl.pallas_call(with_core, grid_spec=grid_spec, out_shape=jax.ShapeDtypeSt...  15.5 us
    pallas_call x1, Pallas kernels, conv_part(): pl.pallas_call(conv_kernel, grid=(chans // CONV_COLS,), in_specs=[pl.Bloc...  12 us
    all_to_all x1, waiting for transfers between devices, compose(): lax.all_to_all(entering, 'chip', split_axis=0, concat_axis=0, tiled=True)  7.28 us
    all_to_all x1, waiting for transfers between devices, compose(): lax.all_to_all(payload, 'chip', split_axis=0, concat_axis=0, tiled=True)  6.42 us
    all_to_all x1, starting transfers between devices, compose(): lax.all_to_all(payload, 'chip', split_axis=0, concat_axis=0, tiled=True)  4.6 us
    ppermute x1, starting transfers between devices, shifted(): return lax.ppermute(value, axis, pairs)  4.54 us
  transfers between devices with their start and end apart: 5, of which 2 were waited for; matrix products, arithmetic and copies ran while one was open for 11% of the time, Pallas kernels for 37%

profile of v20, /device:TPU:1, one launch (start us, length us, event | category | flops | bytes accessed | tf_op | source)
XLA Modules:
  0.0 137.5 jit_solution(7400258266487431254)
XLA Ops:
  0.0 0.9 slice.54
  0.9 4.5 %collective-permute-start = (bf16[3,5120]{1,0:T(4,128)(2,1)S(1)}, bf16[3,5120]{1,0:T(4,128)(2,1)S(1)}, u32[]{:S(2)}, u32[]{:S(2)}) collective-permute-start(bf16[3,5120]{1,0:T(4,128)(2,1)S(1)} %slice.54), channel_id=1, source_target_pairs={{0,1},{1,2},{2,3},{3,4},{4,5},{5,6},{6,7},{7,8},{8,9},{9,10},{10,1... | collective-permute-start | bytes 92168 | tf_op jit(solution)/shard_map/ppermute | solution.py:23
  5.5 0.8 reduce-window.18
  6.5 0.1 convert_reduce_fusion.1
  6.6 0.2 fusion.9
  6.8 0.1 copy.111
  6.9 1.0 copy.102
  7.9 0.7 exp.20
  8.7 0.7 add.67
  9.4 1.1 negate_multiply_fusion
  10.5 0.2 copy.103
  10.7 2.3 %reduce-window.19 = f32[2,2,32,2,128]{4,2,3,1,0:T(8,128)S(1)} reduce-window(f32[2,2,32,2,128]{4,2,3,1,0:T(8,128)S(1)} %copy_bitcast_fusion.1, f32[]{:T(128)} %constant.35.clone.1), window={size=1x1x1x1x128 pad=0_0x0_0x0_0x0_0x127_0}, to_apply=%region_2.3 | reduce-window | flops 4161536 | bytes 262148 | tf_op jit(solution)/shard_map/reduce-window.1
  13.0 0.2 slice_reduce_fusion
  13.3 0.1 bitcast_bitcast_fusion
  13.4 0.2 fusion.5
  13.7 0.2 compare_reduce_fusion
  14.0 1.0 copy.106
  15.0 0.9 copy.101.m_ref
  15.9 0.7 broadcast_in_dim_reshape.7.bdec_ref
  16.6 0.9 copy.110.segc_ref.refs_6_.refs_7_
  17.5 0.7 concatenate.6.rim_ref
  18.1 12.0 %shard_map.100.c_ref.b_ref.x_ref.refs_0_.refs_1_.refs_2_.bt_ref = bf16[512,5120]{1,0:T(8,128)(2,1)} custom-call(bf16[512,5120]{1,0:T(8,128)(2,1)} %x_ref.1, bf16[8,5120]{1,0:T(8,128)(2,1)} %concatenate.6.rim_ref, f32[4,5120]{1,0:T(4,128)} %w_ref.1, f32[1,5120]{1,0:T(1,128)} %bitcast.74, f32[512,4]{1,0:T(8,128)} %copy.101.m_ref), custom_call_target="tpu_custom_call" | custom-call | tf_op jit(solution)/shard_map/pallas_call | solution.py:72
  30.2 8.0 %shard_map.103 = (f32[2,256,4096]{2,1,0:T(8,128)}, f32[2,1,4096]{2,1,0:T(1,128)}, f32[257,2048]{1,0:T(8,128)}) custom-call(s32[1]{0:T(128)} %bitcast.core_ref, bf16[512,5120]{1,0:T(8,128)(2,1)} %shard_map.100.c_ref.b_ref.x_ref.refs_0_.refs_1_.refs_2_.bt_ref, bf16[512,5120]{1,0:T(8,128)(2,1)} %shard_map.100.c_ref.b_ref.x_ref.refs_0_.refs_1_.refs_2_.bt_ref, ...), custom_call_target="tpu_custom_call" | custom-call | tf_op jit(solution)/shard_map/pallas_call | solution.py:189
  38.2 8.0 %shard_map.104 = (f32[2,256,4096]{2,1,0:T(8,128)}, f32[2,1,4096]{2,1,0:T(1,128)}, f32[257,2048]{1,0:T(8,128)}) custom-call(s32[1]{0:T(128)} %bitcast.core_ref, bf16[512,5120]{1,0:T(8,128)(2,1)} %shard_map.100.c_ref.b_ref.x_ref.refs_0_.refs_1_.refs_2_.bt_ref, ...), custom_call_target="tpu_custom_call", output_to_operand_aliasing={{0}: (7, {}), {1}: (8, {})} | custom-call | tf_op jit(solution)/shard_map/pallas_call | solution.py:189
  46.2 1.3 copy-done.1
  47.6 2.6 %broadcast_select_fusion.1 = (f32[257,2048]{1,0:T(8,128)S(1)}, f32[257,2048]{1,0:T(8,128)S(1)}) fusion(f32[257,2048]{1,0:T(8,128)} %get-tuple-element.13, f32[257,2048]{1,0:T(8,128)} %copy-done.1, pred[]{:T(512)S(6)} %eq.23), kind=kLoop, calls=%fused_computation.10 | loop fusion | flops 1052672 | bytes 8421377 | tf_op jit(solution)/shard_map/jit(_where)/select_n | solution.py:364
  50.2 0.4 fusion
  50.6 0.1 pad_maximum_fusion
  50.7 0.3 copy.122
  51.1 1.2 copy.126
  52.3 4.6 %all-to-all-start = ((bf16[8,258,256]{2,1,0:T(8,128)(2,1)}), bf16[8,258,256]{2,1,0:T(8,128)(2,1)}, u32[]{:S(2)}, u32[]{:S(2)}) async-start(bf16[8,258,256]{2,1,0:T(8,128)(2,1)} %bitcast.64), calls=%async_computation | async-start | bytes 2162688 | tf_op jit(solution)/shard_map/all_to_all | solution.py:375
  56.9 0.8 copy.109.cumt_ref.refs_5_
  57.8 0.7 broadcast_in_dim_reshape.6.dsk_ref.refs_8_
  58.5 0.6 broadcast_in_dim.55.segr_ref.refs_7_
  59.1 17.4 %shard_map.101.refs_9_.refs_1_ = f32[512,4096]{1,0:T(8,128)} custom-call(bf16[512,5120]{1,0:T(8,128)(2,1)} %shard_map.100.c_ref.b_ref.x_ref.refs_0_.refs_1_.refs_2_.bt_ref, bf16[512,5120]{1,0:T(8,128)(2,1)} %shard_map.100.c_ref.b_ref.x_ref.refs_0_.refs_1_.refs_2_.bt_ref, bf16[512,5120]{1,0:T(8,128)(2,1)} %shard_map.100.c_ref.b_ref.x_ref.refs_0_.refs_1_.refs_2_.bt_ref, ...), custom_call_target="tpu_custom_call" | custom-call | tf_op jit(solution)/shard_map/pallas_call | solution.py:252
  76.5 6.4 %all-to-all-done.refs_0_ = bf16[8,258,256]{2,1,0:T(8,128)(2,1)} async-done(((bf16[8,258,256]{2,1,0:T(8,128)(2,1)}), bf16[8,258,256]{2,1,0:T(8,128)(2,1)}, u32[]{:S(2)}, u32[]{:S(2)}) %all-to-all-start) | async-done | bytes 1056800 | tf_op jit(solution)/shard_map/all_to_all | solution.py:375
  82.9 2.5 %shard_map.106 = bf16[8,256,256]{2,1,0:T(8,128)(2,1)} custom-call(bf16[8,258,256]{2,1,0:T(8,128)(2,1)} %shard_map.105.got_ref), custom_call_target="tpu_custom_call" | custom-call | tf_op jit(solution)/shard_map/pallas_call | solution.py:376
  85.4 4.5 %all-to-all-start.1 = ((bf16[8,256,256]{2,1,0:T(8,128)(2,1)}), bf16[8,256,256]{2,1,0:T(8,128)(2,1)}, u32[]{:S(2)}, u32[]{:S(2)}) async-start(bf16[8,256,256]{2,1,0:T(8,128)(2,1)} %shard_map.106), calls=%async_computation.1 | async-start | bytes 2097152 | tf_op jit(solution)/shard_map/all_to_all | solution.py:381
  89.9 17.5 %shard_map.102.refs_1_ = f32[512,4096]{1,0:T(8,128)} custom-call(bf16[512,5120]{1,0:T(8,128)(2,1)} %shard_map.100.c_ref.b_ref.x_ref.refs_0_.refs_1_.refs_2_.bt_ref, bf16[512,5120]{1,0:T(8,128)(2,1)} %shard_map.100.c_ref.b_ref.x_ref.refs_0_.refs_1_.refs_2_.bt_ref, ...), custom_call_target="tpu_custom_call", output_to_operand_aliasing={{}: (9, {})} | custom-call | tf_op jit(solution)/shard_map/pallas_call | solution.py:252
  107.4 7.3 %all-to-all-done.1.refs_0_ = bf16[8,256,256]{2,1,0:T(8,128)(2,1)} async-done(((bf16[8,256,256]{2,1,0:T(8,128)(2,1)}), bf16[8,256,256]{2,1,0:T(8,128)(2,1)}, u32[]{:S(2)}, u32[]{:S(2)}) %all-to-all-start.1) | async-done | bytes 1048608 | tf_op jit(solution)/shard_map/all_to_all | solution.py:381
  114.6 1.4 %convert_bitcast_fusion = f32[8,32,8,256]{3,2,1,0:T(8,128)S(1)} fusion(bf16[8,256,256]{2,1,0:T(8,128)(2,1)} %shard_map.107), kind=kLoop, calls=%fused_computation.2 | loop fusion | flops 524288 | bytes 3145728
  116.0 0.3 copy.121
  116.3 1.6 %select_convert_fusion = (bf16[256,2048]{1,0:T(8,128)(2,1)}, bf16[256,2048]{1,0:T(8,128)(2,1)S(1)}) fusion(f32[256,2048]{1,0:T(8,128)S(1)} %bitcast.63, f32[257,2048]{1,0:T(8,128)S(1)} %get-tuple-element.21, f32[2048]{0:T(1024)S(1)} %bitcast.71, pred[]{:T(512)S(6)} %eq.23), kind=kLoop, calls=%fused_computation.3 | loop fusion | flops 3145728 | bytes 6299649 | tf_op jit(solution)/shard_map/convert_element_type | solution.py:384
  117.9 2.2 %collective-permute-start.2 = (bf16[256,2048]{1,0:T(8,128)(2,1)S(1)}, bf16[256,2048]{1,0:T(8,128)(2,1)S(1)}, u32[]{:S(2)}, u32[]{:S(2)}) collective-permute-start(bf16[256,2048]{1,0:T(8,128)(2,1)S(1)} %get-tuple-element.24), channel_id=1, source_target_pairs={{0,1},{1,0},{2,3},{3,2},{4,5},{5,4},{6,7},{7,6},{8,9},{9,8},{10,11... | collective-permute-start | bytes 3145736 | tf_op jit(solution)/shard_map/ppermute | solution.py:342
  120.3 0.7 broadcast_in_dim.63.refs_8_
  121.0 7.8 %shard_map.108.refs_10_ = bf16[512,4096]{1,0:T(8,128)(2,1)} custom-call(s32[1]{0:T(128)} %bitcast.core_ref, bf16[512,5120]{1,0:T(8,128)(2,1)} %shard_map.100.c_ref.b_ref.x_ref.refs_0_.refs_1_.refs_2_.bt_ref, f32[512,4096]{1,0:T(8,128)} %shard_map.102.refs_1_, bf16[512,4096]{1,0:T(8,128)(2,1)} %refs_2_.3, bf16[256,2048]{1,0:T(8,128)(2,1)} %get-tuple-element.23.refs_3_, ...), custom_call_target="tpu_custom_call" | custom-call | tf_op jit(solution)/shard_map/pallas_call | solution.py:320
  128.7 1.0 copy-done.2
  129.7 7.8 %shard_map.109 = bf16[512,4096]{1,0:T(8,128)(2,1)} custom-call(s32[1]{0:T(128)} %bitcast.core_ref, bf16[512,5120]{1,0:T(8,128)(2,1)} %shard_map.100.c_ref.b_ref.x_ref.refs_0_.refs_1_.refs_2_.bt_ref, f32[512,4096]{1,0:T(8,128)} %shard_map.102.refs_1_, bf16[512,4096]{1,0:T(8,128)(2,1)} %refs_2_.3, ...), custom_call_target="tpu_custom_call", output_to_operand_aliasing={{}: (11, {})} | custom-call | tf_op jit(solution)/shard_map/pallas_call | solution.py:320
  (36 shorter events, 1.0 us)
Async XLA Ops:
  0.9 16.6 %collective-permute-start = (bf16[3,5120]{1,0:T(4,128)(2,1)S(1)}, bf16[3,5120]{1,0:T(4,128)(2,1)S(1)}, u32[]{:S(2)}, u32[]{:S(2)}) collective-permute-start(bf16[3,5120]{1,0:T(4,128)(2,1)S(1)} %slice.54), channel_id=1, source_target_pairs={{0,1},{1,2},{2,3},{3,4},{4,5},{5,6},{6,7},{7,8},{8,9},{9,10},{10,1... | collective-permute-start | bytes 92168 | tf_op jit(solution)/shard_map/ppermute | solution.py:23
  38.2 8.0 %collective-permute-start.1 = (f32[257,2048]{1,0:T(8,128)}, f32[257,2048]{1,0:T(8,128)S(1)}, u32[]{:S(2)}, u32[]{:S(2)}) collective-permute-start(f32[257,2048]{1,0:T(8,128)} %get-tuple-element.14), channel_id=1, source_target_pairs={{0,1},{1,0},{2,3},{3,2},{4,5},{5,4},{6,7},{7,6},{8,9},{9,8},{10,11... | collective-permute-start | bytes 6316040 | tf_op jit(solution)/shard_map/ppermute | solution.py:342
  46.2 1.3 copy-start.1
  51.1 5.8 %copy-start = (f32[2,2,256,32]{3,2,1,0:T(8,128)S(1)}, f32[2,2,256,32]{3,2,1,0:T(8,128)}, u32[]{:S(2)}) copy-start(f32[2,2,256,32]{3,2,1,0:T(8,128)} %copy.106) | copy-start | bytes 393220
  51.1 6.6 %copy-start.3 = (f32[64]{0:T(128)S(1)}, f32[64]{0:T(128)}, u32[]{:S(2)}) copy-start(f32[64]{0:T(128)} %param.18) | copy-start | bytes 772
  52.3 30.6 %all-to-all-start = ((bf16[8,258,256]{2,1,0:T(8,128)(2,1)}), bf16[8,258,256]{2,1,0:T(8,128)(2,1)}, u32[]{:S(2)}, u32[]{:S(2)}) async-start(bf16[8,258,256]{2,1,0:T(8,128)(2,1)} %bitcast.64), calls=%async_computation | async-start | bytes 2162688 | tf_op jit(solution)/shard_map/all_to_all | solution.py:375
  85.4 29.2 %all-to-all-start.1 = ((bf16[8,256,256]{2,1,0:T(8,128)(2,1)}), bf16[8,256,256]{2,1,0:T(8,128)(2,1)}, u32[]{:S(2)}, u32[]{:S(2)}) async-start(bf16[8,256,256]{2,1,0:T(8,128)(2,1)} %shard_map.106), calls=%async_computation.1 | async-start | bytes 2097152 | tf_op jit(solution)/shard_map/all_to_all | solution.py:381
  117.9 10.8 %collective-permute-start.2 = (bf16[256,2048]{1,0:T(8,128)(2,1)S(1)}, bf16[256,2048]{1,0:T(8,128)(2,1)S(1)}, u32[]{:S(2)}, u32[]{:S(2)}) collective-permute-start(bf16[256,2048]{1,0:T(8,128)(2,1)S(1)} %get-tuple-element.24), channel_id=1, source_target_pairs={{0,1},{1,0},{2,3},{3,2},{4,5},{5,4},{6,7},{7,6},{8,9},{9,8},{10,11... | collective-permute-start | bytes 3145736 | tf_op jit(solution)/shard_map/ppermute | solution.py:342
  128.7 1.0 copy-start.2

commit v21 on v19

--- a/solution.py
+++ b/solution.py
@@ -42,7 +42,7 @@
     return out + jnp.dot(lo, spread, preferred_element_type=jnp.float32)
 
 
-CONV_COLS = 640
+CONV_COLS = 1280
 
 
 def conv_kernel(x_ref, rim_ref, w_ref, bias_ref, m_ref, out_ref):

time: 138 us -> 138 us (level)
  no operation moved by 1% of the time
where the time goes in v21:
time: 138 us; the launch traced here: 137 us
  Pallas kernels  80.9 us (59%)
  starting transfers between devices  15.8 us (11%)
  local copies, waits for them, and re-layouts  15.5 us (11%)
  waiting for transfers between devices  13.7 us (10%)
  other arithmetic  11.2 us (8%)
    pallas_call x2, Pallas kernels, intra_part(): pl.pallas_call(kernel, grid=(nb,), in_specs=specs, out_specs=pl.BlockSpec...  34.9 us
    pallas_call x2, Pallas kernels, half_states(): pl.pallas_call(half_state_kernel, grid_spec=grid_spec, out_shape=[jax.Sha...  16 us
    pallas_call x2, Pallas kernels, mix(): pl.pallas_call(with_core, grid_spec=grid_spec, out_shape=jax.ShapeDtypeSt...  15.5 us
    pallas_call x1, Pallas kernels, conv_part(): pl.pallas_call(conv_kernel, grid=(chans // CONV_COLS,), in_specs=[pl.Bloc...  12 us
    all_to_all x1, waiting for transfers between devices, compose(): lax.all_to_all(entering, 'chip', split_axis=0, concat_axis=0, tiled=True)  7.27 us
    all_to_all x1, waiting for transfers between devices, compose(): lax.all_to_all(payload, 'chip', split_axis=0, concat_axis=0, tiled=True)  6.43 us
    all_to_all x1, starting transfers between devices, compose(): lax.all_to_all(payload, 'chip', split_axis=0, concat_axis=0, tiled=True)  4.6 us
    ppermute x1, starting transfers between devices, shifted(): return lax.ppermute(value, axis, pairs)  4.54 us
  transfers between devices with their start and end apart: 5, of which 2 were waited for; matrix products, arithmetic and copies ran while one was open for 10% of the time, Pallas kernels for 37%

profile of v21, /device:TPU:1, one launch (start us, length us, event | category | flops | bytes accessed | tf_op | source)
XLA Modules:
  0.0 137.5 jit_solution(6898945530240204756)
XLA Ops:
  0.0 0.9 slice.54
  0.9 4.5 %collective-permute-start = (bf16[3,5120]{1,0:T(4,128)(2,1)S(1)}, bf16[3,5120]{1,0:T(4,128)(2,1)S(1)}, u32[]{:S(2)}, u32[]{:S(2)}) collective-permute-start(bf16[3,5120]{1,0:T(4,128)(2,1)S(1)} %slice.54), channel_id=1, source_target_pairs={{0,1},{1,2},{2,3},{3,4},{4,5},{5,6},{6,7},{7,8},{8,9},{9,10},{10,1... | collective-permute-start | bytes 92168 | tf_op jit(solution)/shard_map/ppermute | solution.py:23
  5.5 0.8 reduce-window.18
  6.5 0.1 convert_reduce_fusion.1
  6.6 0.2 fusion.9
  6.8 0.1 copy.85
  6.9 1.0 copy.78
  7.9 0.7 exp.20
  8.7 0.7 add.67
  9.4 1.1 negate_multiply_fusion
  10.5 0.2 copy.79
  10.7 2.3 %reduce-window.19 = f32[2,2,32,2,128]{4,2,3,1,0:T(8,128)S(1)} reduce-window(f32[2,2,32,2,128]{4,2,3,1,0:T(8,128)S(1)} %copy_bitcast_fusion.1, f32[]{:T(128)} %constant.35.clone.1), window={size=1x1x1x1x128 pad=0_0x0_0x0_0x0_0x127_0}, to_apply=%region_2.3 | reduce-window | flops 4161536 | bytes 262148 | tf_op jit(solution)/shard_map/reduce-window.1
  13.0 0.2 slice_reduce_fusion
  13.3 0.1 bitcast_bitcast_fusion
  13.4 0.2 fusion.5
  13.7 0.2 compare_reduce_fusion
  14.0 1.0 copy.82
  15.0 0.9 copy.77.m_ref
  15.9 0.7 broadcast_in_dim_reshape.7.bdec_ref
  16.6 0.7 concatenate.6.rim_ref
  17.3 12.0 %shard_map.100.c_ref.b_ref.x_ref.refs_0_.refs_1_.refs_2_.bt_ref = bf16[512,5120]{1,0:T(8,128)(2,1)} custom-call(bf16[512,5120]{1,0:T(8,128)(2,1)} %x_ref.1, bf16[8,5120]{1,0:T(8,128)(2,1)} %concatenate.6.rim_ref, f32[4,5120]{1,0:T(4,128)} %w_ref.1, f32[1,5120]{1,0:T(1,128)} %bitcast.72, f32[512,4]{1,0:T(8,128)} %copy.77.m_ref), custom_call_target="tpu_custom_call" | custom-call | tf_op jit(solution)/shard_map/pallas_call | solution.py:72
  29.3 0.8 broadcast_in_dim.57.segc_ref.refs_6_.refs_7_
  30.2 8.0 %shard_map.103 = (f32[2,256,4096]{2,1,0:T(8,128)}, f32[2,1,4096]{2,1,0:T(1,128)}, f32[257,2048]{1,0:T(8,128)}) custom-call(s32[1]{0:T(128)} %bitcast.core_ref, bf16[512,5120]{1,0:T(8,128)(2,1)} %shard_map.100.c_ref.b_ref.x_ref.refs_0_.refs_1_.refs_2_.bt_ref, bf16[512,5120]{1,0:T(8,128)(2,1)} %shard_map.100.c_ref.b_ref.x_ref.refs_0_.refs_1_.refs_2_.bt_ref, ...), custom_call_target="tpu_custom_call" | custom-call | tf_op jit(solution)/shard_map/pallas_call | solution.py:189
  38.2 8.0 %shard_map.104 = (f32[2,256,4096]{2,1,0:T(8,128)}, f32[2,1,4096]{2,1,0:T(1,128)}, f32[257,2048]{1,0:T(8,128)}) custom-call(s32[1]{0:T(128)} %bitcast.core_ref, bf16[512,5120]{1,0:T(8,128)(2,1)} %shard_map.100.c_ref.b_ref.x_ref.refs_0_.refs_1_.refs_2_.bt_ref, ...), custom_call_target="tpu_custom_call", output_to_operand_aliasing={{0}: (7, {}), {1}: (8, {})} | custom-call | tf_op jit(solution)/shard_map/pallas_call | solution.py:189
  46.2 1.3 copy-done.1
  47.5 2.6 %broadcast_select_fusion.1 = (f32[257,2048]{1,0:T(8,128)S(1)}, f32[257,2048]{1,0:T(8,128)S(1)}) fusion(f32[257,2048]{1,0:T(8,128)} %get-tuple-element.13, f32[257,2048]{1,0:T(8,128)} %copy-done.1, pred[]{:T(512)S(6)} %eq.23), kind=kLoop, calls=%fused_computation.10 | loop fusion | flops 1052672 | bytes 8421377 | tf_op jit(solution)/shard_map/jit(_where)/select_n | solution.py:364
  50.2 0.4 fusion
  50.5 0.1 pad_maximum_fusion
  50.6 0.3 copy.92
  51.1 1.2 copy.96
  52.2 4.6 %all-to-all-start = ((bf16[8,258,256]{2,1,0:T(8,128)(2,1)}), bf16[8,258,256]{2,1,0:T(8,128)(2,1)}, u32[]{:S(2)}, u32[]{:S(2)}) async-start(bf16[8,258,256]{2,1,0:T(8,128)(2,1)} %bitcast.63), calls=%async_computation | async-start | bytes 2162688 | tf_op jit(solution)/shard_map/all_to_all | solution.py:375
  56.9 0.8 copy.84.cumt_ref.refs_5_
  57.8 0.7 broadcast_in_dim_reshape.6.dsk_ref.refs_8_
  58.4 0.6 broadcast_in_dim.58.segr_ref.refs_7_
  59.0 17.4 %shard_map.101.refs_9_.refs_1_ = f32[512,4096]{1,0:T(8,128)} custom-call(bf16[512,5120]{1,0:T(8,128)(2,1)} %shard_map.100.c_ref.b_ref.x_ref.refs_0_.refs_1_.refs_2_.bt_ref, bf16[512,5120]{1,0:T(8,128)(2,1)} %shard_map.100.c_ref.b_ref.x_ref.refs_0_.refs_1_.refs_2_.bt_ref, bf16[512,5120]{1,0:T(8,128)(2,1)} %shard_map.100.c_ref.b_ref.x_ref.refs_0_.refs_1_.refs_2_.bt_ref, ...), custom_call_target="tpu_custom_call" | custom-call | tf_op jit(solution)/shard_map/pallas_call | solution.py:252
  76.4 6.4 %all-to-all-done.refs_0_ = bf16[8,258,256]{2,1,0:T(8,128)(2,1)} async-done(((bf16[8,258,256]{2,1,0:T(8,128)(2,1)}), bf16[8,258,256]{2,1,0:T(8,128)(2,1)}, u32[]{:S(2)}, u32[]{:S(2)}) %all-to-all-start) | async-done | bytes 1056800 | tf_op jit(solution)/shard_map/all_to_all | solution.py:375
  82.8 2.5 %shard_map.106 = bf16[8,256,256]{2,1,0:T(8,128)(2,1)} custom-call(bf16[8,258,256]{2,1,0:T(8,128)(2,1)} %shard_map.105.got_ref), custom_call_target="tpu_custom_call" | custom-call | tf_op jit(solution)/shard_map/pallas_call | solution.py:376
  85.4 4.5 %all-to-all-start.1 = ((bf16[8,256,256]{2,1,0:T(8,128)(2,1)}), bf16[8,256,256]{2,1,0:T(8,128)(2,1)}, u32[]{:S(2)}, u32[]{:S(2)}) async-start(bf16[8,256,256]{2,1,0:T(8,128)(2,1)} %shard_map.106), calls=%async_computation.1 | async-start | bytes 2097152 | tf_op jit(solution)/shard_map/all_to_all | solution.py:381
  89.8 17.5 %shard_map.102.refs_1_ = f32[512,4096]{1,0:T(8,128)} custom-call(bf16[512,5120]{1,0:T(8,128)(2,1)} %shard_map.100.c_ref.b_ref.x_ref.refs_0_.refs_1_.refs_2_.bt_ref, bf16[512,5120]{1,0:T(8,128)(2,1)} %shard_map.100.c_ref.b_ref.x_ref.refs_0_.refs_1_.refs_2_.bt_ref, ...), custom_call_target="tpu_custom_call", output_to_operand_aliasing={{}: (9, {})} | custom-call | tf_op jit(solution)/shard_map/pallas_call | solution.py:252
  107.3 7.3 %all-to-all-done.1.refs_0_ = bf16[8,256,256]{2,1,0:T(8,128)(2,1)} async-done(((bf16[8,256,256]{2,1,0:T(8,128)(2,1)}), bf16[8,256,256]{2,1,0:T(8,128)(2,1)}, u32[]{:S(2)}, u32[]{:S(2)}) %all-to-all-start.1) | async-done | bytes 1048608 | tf_op jit(solution)/shard_map/all_to_all | solution.py:381
  114.6 1.4 %convert_bitcast_fusion = f32[8,32,8,256]{3,2,1,0:T(8,128)S(1)} fusion(bf16[8,256,256]{2,1,0:T(8,128)(2,1)} %shard_map.107), kind=kLoop, calls=%fused_computation.2 | loop fusion | flops 524288 | bytes 3145728
  116.0 0.3 copy.91
  116.3 1.6 %select_convert_fusion = (bf16[256,2048]{1,0:T(8,128)(2,1)}, bf16[256,2048]{1,0:T(8,128)(2,1)S(1)}) fusion(f32[256,2048]{1,0:T(8,128)S(1)} %bitcast.62, f32[257,2048]{1,0:T(8,128)S(1)} %get-tuple-element.21, f32[2048]{0:T(1024)S(1)} %bitcast.70, pred[]{:T(512)S(6)} %eq.23), kind=kLoop, calls=%fused_computation.3 | loop fusion | flops 3145728 | bytes 6299649 | tf_op jit(solution)/shard_map/convert_element_type | solution.py:384
  117.9 2.2 %collective-permute-start.2 = (bf16[256,2048]{1,0:T(8,128)(2,1)S(1)}, bf16[256,2048]{1,0:T(8,128)(2,1)S(1)}, u32[]{:S(2)}, u32[]{:S(2)}) collective-permute-start(bf16[256,2048]{1,0:T(8,128)(2,1)S(1)} %get-tuple-element.24), channel_id=1, source_target_pairs={{0,1},{1,0},{2,3},{3,2},{4,5},{5,4},{6,7},{7,6},{8,9},{9,8},{10,11... | collective-permute-start | bytes 3145736 | tf_op jit(solution)/shard_map/ppermute | solution.py:342
  120.2 0.7 broadcast_in_dim.66.refs_8_
  120.9 7.8 %shard_map.108.refs_10_ = bf16[512,4096]{1,0:T(8,128)(2,1)} custom-call(s32[1]{0:T(128)} %bitcast.core_ref, bf16[512,5120]{1,0:T(8,128)(2,1)} %shard_map.100.c_ref.b_ref.x_ref.refs_0_.refs_1_.refs_2_.bt_ref, f32[512,4096]{1,0:T(8,128)} %shard_map.102.refs_1_, bf16[512,4096]{1,0:T(8,128)(2,1)} %refs_2_.3, bf16[256,2048]{1,0:T(8,128)(2,1)} %get-tuple-element.23.refs_3_, ...), custom_call_target="tpu_custom_call" | custom-call | tf_op jit(solution)/shard_map/pallas_call | solution.py:320
  128.7 1.0 copy-done.2
  129.7 7.8 %shard_map.109 = bf16[512,4096]{1,0:T(8,128)(2,1)} custom-call(s32[1]{0:T(128)} %bitcast.core_ref, bf16[512,5120]{1,0:T(8,128)(2,1)} %shard_map.100.c_ref.b_ref.x_ref.refs_0_.refs_1_.refs_2_.bt_ref, f32[512,4096]{1,0:T(8,128)} %shard_map.102.refs_1_, bf16[512,4096]{1,0:T(8,128)(2,1)} %refs_2_.3, ...), custom_call_target="tpu_custom_call", output_to_operand_aliasing={{}: (11, {})} | custom-call | tf_op jit(solution)/shard_map/pallas_call | solution.py:320
  (36 shorter events, 1.0 us)
Async XLA Ops:
  0.9 15.7 %collective-permute-start = (bf16[3,5120]{1,0:T(4,128)(2,1)S(1)}, bf16[3,5120]{1,0:T(4,128)(2,1)S(1)}, u32[]{:S(2)}, u32[]{:S(2)}) collective-permute-start(bf16[3,5120]{1,0:T(4,128)(2,1)S(1)} %slice.54), channel_id=1, source_target_pairs={{0,1},{1,2},{2,3},{3,4},{4,5},{5,6},{6,7},{7,8},{8,9},{9,10},{10,1... | collective-permute-start | bytes 92168 | tf_op jit(solution)/shard_map/ppermute | solution.py:23
  38.2 8.0 %collective-permute-start.1 = (f32[257,2048]{1,0:T(8,128)}, f32[257,2048]{1,0:T(8,128)S(1)}, u32[]{:S(2)}, u32[]{:S(2)}) collective-permute-start(f32[257,2048]{1,0:T(8,128)} %get-tuple-element.14), channel_id=1, source_target_pairs={{0,1},{1,0},{2,3},{3,2},{4,5},{5,4},{6,7},{7,6},{8,9},{9,8},{10,11... | collective-permute-start | bytes 6316040 | tf_op jit(solution)/shard_map/ppermute | solution.py:342
  46.2 1.3 copy-start.1
  51.0 5.8 %copy-start = (f32[2,2,256,32]{3,2,1,0:T(8,128)S(1)}, f32[2,2,256,32]{3,2,1,0:T(8,128)}, u32[]{:S(2)}) copy-start(f32[2,2,256,32]{3,2,1,0:T(8,128)} %copy.82) | copy-start | bytes 393220
  51.0 6.6 %copy-start.3 = (f32[64]{0:T(128)S(1)}, f32[64]{0:T(128)}, u32[]{:S(2)}) copy-start(f32[64]{0:T(128)} %param.18) | copy-start | bytes 772
  52.2 30.6 %all-to-all-start = ((bf16[8,258,256]{2,1,0:T(8,128)(2,1)}), bf16[8,258,256]{2,1,0:T(8,128)(2,1)}, u32[]{:S(2)}, u32[]{:S(2)}) async-start(bf16[8,258,256]{2,1,0:T(8,128)(2,1)} %bitcast.63), calls=%async_computation | async-start | bytes 2162688 | tf_op jit(solution)/shard_map/all_to_all | solution.py:375
  85.4 29.2 %all-to-all-start.1 = ((bf16[8,256,256]{2,1,0:T(8,128)(2,1)}), bf16[8,256,256]{2,1,0:T(8,128)(2,1)}, u32[]{:S(2)}, u32[]{:S(2)}) async-start(bf16[8,256,256]{2,1,0:T(8,128)(2,1)} %shard_map.106), calls=%async_computation.1 | async-start | bytes 2097152 | tf_op jit(solution)/shard_map/all_to_all | solution.py:381
  117.9 10.8 %collective-permute-start.2 = (bf16[256,2048]{1,0:T(8,128)(2,1)S(1)}, bf16[256,2048]{1,0:T(8,128)(2,1)S(1)}, u32[]{:S(2)}, u32[]{:S(2)}) collective-permute-start(bf16[256,2048]{1,0:T(8,128)(2,1)S(1)} %get-tuple-element.24), channel_id=1, source_target_pairs={{0,1},{1,0},{2,3},{3,2},{4,5},{5,4},{6,7},{7,6},{8,9},{9,8},{10,11... | collective-permute-start | bytes 3145736 | tf_op jit(solution)/shard_map/ppermute | solution.py:342
  128.7 1.0 copy-start.2

commit v22 on v19

--- a/solution.py
+++ b/solution.py
@@ -263,7 +263,8 @@
     c_ref, y_ref, z_ref, hin_ref, local_ref, cdec_ref, cum_ref, segc_ref, eb_ref, gain_ref,
     out_ref,
 ):
-    state = cdec_ref[0] * hin_ref[...].astype(jnp.float32) + local_ref[0]
+    hin = hin_ref[...].astype(jnp.float32)
+    state = jnp.where(pl.program_id(0) == 0, hin, cdec_ref[0] * hin + local_ref[0])
     segc = segc_ref[:, 0:1]
     entry = eb_ref[0:1, 0:1]
     in_weight = jnp.where(segc == entry, jnp.exp(cum_ref[0]), 0.0)
@@ -290,8 +291,8 @@
         pl.BlockSpec((STRETCH, GROUP_COLS), lambda b, c: (b, grp(c))),
         pl.BlockSpec((STRETCH, GROUP_COLS), lambda b, c: (b, grp(c))),
         pl.BlockSpec((STATE, GROUP_COLS), lambda b, c: (0, 0)),
-        pl.BlockSpec((1, STATE, GROUP_COLS), lambda b, c: (b, 0, grp(c))),
-        pl.BlockSpec((1, 1, GROUP_COLS), lambda b, c: (b, 0, grp(c))),
+        pl.BlockSpec((1, STATE, GROUP_COLS), lambda b, c: (jnp.maximum(b, 1), 0, grp(c))),
+        pl.BlockSpec((1, 1, GROUP_COLS), lambda b, c: (jnp.maximum(b, 1), 0, grp(c))),
         pl.BlockSpec((1, STRETCH, PER_GROUP), lambda b, c: (grp(c), b, 0)),
         pl.BlockSpec((STRETCH, 128), lambda b, c: (b, 0)),
         pl.BlockSpec((8, 128), lambda b, c: (b, 0)),

time: 138 us -> 138 us (level)
  no operation moved by 1% of the time
where the time goes in v22:
time: 138 us
  Pallas kernels  81.1 us (59%)
  starting transfers between devices  15.8 us (11%)
  local copies, waits for them, and re-layouts  15.5 us (11%)
  waiting for transfers between devices  13.7 us (10%)
  other arithmetic  11.2 us (8%)
    pallas_call x2, Pallas kernels, intra_part(): pl.pallas_call(kernel, grid=(nb,), in_specs=specs, out_specs=pl.BlockSpec...  34.9 us
    pallas_call x2, Pallas kernels, half_states(): pl.pallas_call(half_state_kernel, grid_spec=grid_spec, out_shape=[jax.Sha...  16 us
    pallas_call x2, Pallas kernels, mix(): pl.pallas_call(with_core, grid_spec=grid_spec, out_shape=jax.ShapeDtypeSt...  15.7 us
    pallas_call x1, Pallas kernels, conv_part(): pl.pallas_call(conv_kernel, grid=(chans // CONV_COLS,), in_specs=[pl.Bloc...  12 us
    all_to_all x1, waiting for transfers between devices, compose(): lax.all_to_all(entering, 'chip', split_axis=0, concat_axis=0, tiled=True)  7.28 us
    all_to_all x1, waiting for transfers between devices, compose(): lax.all_to_all(payload, 'chip', split_axis=0, concat_axis=0, tiled=True)  6.42 us
    all_to_all x1, starting transfers between devices, compose(): lax.all_to_all(payload, 'chip', split_axis=0, concat_axis=0, tiled=True)  4.6 us
    ppermute x1, starting transfers between devices, shifted(): return lax.ppermute(value, axis, pairs)  4.54 us
  transfers between devices with their start and end apart: 5, of which 2 were waited for; matrix products, arithmetic and copies ran while one was open for 10% of the time, Pallas kernels for 37%

profile of v22, /device:TPU:1, one launch (start us, length us, event | category | flops | bytes accessed | tf_op | source)
XLA Modules:
  0.0 137.6 jit_solution(556953947062361552)
XLA Ops:
  0.0 0.9 slice.54
  0.9 4.5 %collective-permute-start = (bf16[3,5120]{1,0:T(4,128)(2,1)S(1)}, bf16[3,5120]{1,0:T(4,128)(2,1)S(1)}, u32[]{:S(2)}, u32[]{:S(2)}) collective-permute-start(bf16[3,5120]{1,0:T(4,128)(2,1)S(1)} %slice.54), channel_id=1, source_target_pairs={{0,1},{1,2},{2,3},{3,4},{4,5},{5,6},{6,7},{7,8},{8,9},{9,10},{10,1... | collective-permute-start | bytes 92168 | tf_op jit(solution)/shard_map/ppermute | solution.py:23
  5.5 0.8 reduce-window.18
  6.5 0.1 convert_reduce_fusion.1
  6.6 0.2 fusion.9
  6.8 0.1 copy.85
  6.9 1.0 copy.78
  7.9 0.7 exp.20
  8.7 0.7 add.67
  9.4 1.1 negate_multiply_fusion
  10.5 0.2 copy.79
  10.7 2.3 %reduce-window.19 = f32[2,2,32,2,128]{4,2,3,1,0:T(8,128)S(1)} reduce-window(f32[2,2,32,2,128]{4,2,3,1,0:T(8,128)S(1)} %copy_bitcast_fusion.1, f32[]{:T(128)} %constant.35.clone.1), window={size=1x1x1x1x128 pad=0_0x0_0x0_0x0_0x127_0}, to_apply=%region_2.3 | reduce-window | flops 4161536 | bytes 262148 | tf_op jit(solution)/shard_map/reduce-window.1
  13.0 0.2 slice_reduce_fusion
  13.3 0.1 bitcast_bitcast_fusion
  13.4 0.2 fusion.5
  13.7 0.2 compare_reduce_fusion
  14.0 1.0 copy.82
  15.0 0.9 copy.77.m_ref
  15.9 0.7 broadcast_in_dim_reshape.7.bdec_ref
  16.6 0.7 concatenate.6.rim_ref
  17.3 12.0 %shard_map.100.c_ref.b_ref.x_ref.refs_0_.refs_1_.refs_2_.bt_ref = bf16[512,5120]{1,0:T(8,128)(2,1)} custom-call(bf16[512,5120]{1,0:T(8,128)(2,1)} %x_ref.1, bf16[8,5120]{1,0:T(8,128)(2,1)} %concatenate.6.rim_ref, f32[4,5120]{1,0:T(4,128)} %w_ref.1, f32[1,5120]{1,0:T(1,128)} %bitcast.72, f32[512,4]{1,0:T(8,128)} %copy.77.m_ref), custom_call_target="tpu_custom_call" | custom-call | tf_op jit(solution)/shard_map/pallas_call | solution.py:72
  29.3 0.8 broadcast_in_dim.57.segc_ref.refs_6_.refs_7_
  30.1 8.0 %shard_map.103 = (f32[2,256,4096]{2,1,0:T(8,128)}, f32[2,1,4096]{2,1,0:T(1,128)}, f32[257,2048]{1,0:T(8,128)}) custom-call(s32[1]{0:T(128)} %bitcast.core_ref, bf16[512,5120]{1,0:T(8,128)(2,1)} %shard_map.100.c_ref.b_ref.x_ref.refs_0_.refs_1_.refs_2_.bt_ref, bf16[512,5120]{1,0:T(8,128)(2,1)} %shard_map.100.c_ref.b_ref.x_ref.refs_0_.refs_1_.refs_2_.bt_ref, ...), custom_call_target="tpu_custom_call" | custom-call | tf_op jit(solution)/shard_map/pallas_call | solution.py:189
  38.1 8.0 %shard_map.104 = (f32[2,256,4096]{2,1,0:T(8,128)}, f32[2,1,4096]{2,1,0:T(1,128)}, f32[257,2048]{1,0:T(8,128)}) custom-call(s32[1]{0:T(128)} %bitcast.core_ref, bf16[512,5120]{1,0:T(8,128)(2,1)} %shard_map.100.c_ref.b_ref.x_ref.refs_0_.refs_1_.refs_2_.bt_ref, ...), custom_call_target="tpu_custom_call", output_to_operand_aliasing={{0}: (7, {}), {1}: (8, {})} | custom-call | tf_op jit(solution)/shard_map/pallas_call | solution.py:189
  46.2 1.3 copy-done.1
  47.5 2.6 %broadcast_select_fusion.1 = (f32[257,2048]{1,0:T(8,128)S(1)}, f32[257,2048]{1,0:T(8,128)S(1)}) fusion(f32[257,2048]{1,0:T(8,128)} %get-tuple-element.13, f32[257,2048]{1,0:T(8,128)} %copy-done.1, pred[]{:T(512)S(6)} %eq.23), kind=kLoop, calls=%fused_computation.10 | loop fusion | flops 1052672 | bytes 8421377 | tf_op jit(solution)/shard_map/jit(_where)/select_n | solution.py:365
  50.1 0.4 fusion
  50.5 0.1 pad_maximum_fusion
  50.6 0.3 copy.92
  51.0 1.2 copy.96
  52.2 4.6 %all-to-all-start = ((bf16[8,258,256]{2,1,0:T(8,128)(2,1)}), bf16[8,258,256]{2,1,0:T(8,128)(2,1)}, u32[]{:S(2)}, u32[]{:S(2)}) async-start(bf16[8,258,256]{2,1,0:T(8,128)(2,1)} %bitcast.63), calls=%async_computation | async-start | bytes 2162688 | tf_op jit(solution)/shard_map/all_to_all | solution.py:376
  56.8 0.8 copy.84.cumt_ref.refs_5_
  57.7 0.7 broadcast_in_dim_reshape.6.dsk_ref.refs_8_
  58.4 0.6 broadcast_in_dim.58.segr_ref.refs_7_
  59.0 17.4 %shard_map.101.refs_9_.refs_1_ = f32[512,4096]{1,0:T(8,128)} custom-call(bf16[512,5120]{1,0:T(8,128)(2,1)} %shard_map.100.c_ref.b_ref.x_ref.refs_0_.refs_1_.refs_2_.bt_ref, bf16[512,5120]{1,0:T(8,128)(2,1)} %shard_map.100.c_ref.b_ref.x_ref.refs_0_.refs_1_.refs_2_.bt_ref, bf16[512,5120]{1,0:T(8,128)(2,1)} %shard_map.100.c_ref.b_ref.x_ref.refs_0_.refs_1_.refs_2_.bt_ref, ...), custom_call_target="tpu_custom_call" | custom-call | tf_op jit(solution)/shard_map/pallas_call | solution.py:252
  76.4 6.4 %all-to-all-done.refs_0_ = bf16[8,258,256]{2,1,0:T(8,128)(2,1)} async-done(((bf16[8,258,256]{2,1,0:T(8,128)(2,1)}), bf16[8,258,256]{2,1,0:T(8,128)(2,1)}, u32[]{:S(2)}, u32[]{:S(2)}) %all-to-all-start) | async-done | bytes 1056800 | tf_op jit(solution)/shard_map/all_to_all | solution.py:376
  82.8 2.5 %shard_map.106 = bf16[8,256,256]{2,1,0:T(8,128)(2,1)} custom-call(bf16[8,258,256]{2,1,0:T(8,128)(2,1)} %shard_map.105.got_ref), custom_call_target="tpu_custom_call" | custom-call | tf_op jit(solution)/shard_map/pallas_call | solution.py:377
  85.3 4.5 %all-to-all-start.1 = ((bf16[8,256,256]{2,1,0:T(8,128)(2,1)}), bf16[8,256,256]{2,1,0:T(8,128)(2,1)}, u32[]{:S(2)}, u32[]{:S(2)}) async-start(bf16[8,256,256]{2,1,0:T(8,128)(2,1)} %shard_map.106), calls=%async_computation.1 | async-start | bytes 2097152 | tf_op jit(solution)/shard_map/all_to_all | solution.py:382
  89.8 17.5 %shard_map.102.refs_1_ = f32[512,4096]{1,0:T(8,128)} custom-call(bf16[512,5120]{1,0:T(8,128)(2,1)} %shard_map.100.c_ref.b_ref.x_ref.refs_0_.refs_1_.refs_2_.bt_ref, bf16[512,5120]{1,0:T(8,128)(2,1)} %shard_map.100.c_ref.b_ref.x_ref.refs_0_.refs_1_.refs_2_.bt_ref, ...), custom_call_target="tpu_custom_call", output_to_operand_aliasing={{}: (9, {})} | custom-call | tf_op jit(solution)/shard_map/pallas_call | solution.py:252
  107.3 7.3 %all-to-all-done.1.refs_0_ = bf16[8,256,256]{2,1,0:T(8,128)(2,1)} async-done(((bf16[8,256,256]{2,1,0:T(8,128)(2,1)}), bf16[8,256,256]{2,1,0:T(8,128)(2,1)}, u32[]{:S(2)}, u32[]{:S(2)}) %all-to-all-start.1) | async-done | bytes 1048608 | tf_op jit(solution)/shard_map/all_to_all | solution.py:382
  114.6 1.4 %convert_bitcast_fusion = f32[8,32,8,256]{3,2,1,0:T(8,128)S(1)} fusion(bf16[8,256,256]{2,1,0:T(8,128)(2,1)} %shard_map.107), kind=kLoop, calls=%fused_computation.2 | loop fusion | flops 524288 | bytes 3145728
  116.0 0.3 copy.91
  116.3 1.6 %select_convert_fusion = (bf16[256,2048]{1,0:T(8,128)(2,1)}, bf16[256,2048]{1,0:T(8,128)(2,1)S(1)}) fusion(f32[256,2048]{1,0:T(8,128)S(1)} %bitcast.62, f32[257,2048]{1,0:T(8,128)S(1)} %get-tuple-element.21, f32[2048]{0:T(1024)S(1)} %bitcast.70, pred[]{:T(512)S(6)} %eq.23), kind=kLoop, calls=%fused_computation.3 | loop fusion | flops 3145728 | bytes 6299649 | tf_op jit(solution)/shard_map/convert_element_type | solution.py:385
  117.8 2.2 %collective-permute-start.2 = (bf16[256,2048]{1,0:T(8,128)(2,1)S(1)}, bf16[256,2048]{1,0:T(8,128)(2,1)S(1)}, u32[]{:S(2)}, u32[]{:S(2)}) collective-permute-start(bf16[256,2048]{1,0:T(8,128)(2,1)S(1)} %get-tuple-element.24), channel_id=1, source_target_pairs={{0,1},{1,0},{2,3},{3,2},{4,5},{5,4},{6,7},{7,6},{8,9},{9,8},{10,11... | collective-permute-start | bytes 3145736 | tf_op jit(solution)/shard_map/ppermute | solution.py:343
  120.2 0.7 broadcast_in_dim.66.refs_8_
  120.9 7.9 %shard_map.108.refs_10_ = bf16[512,4096]{1,0:T(8,128)(2,1)} custom-call(s32[1]{0:T(128)} %bitcast.core_ref, bf16[512,5120]{1,0:T(8,128)(2,1)} %shard_map.100.c_ref.b_ref.x_ref.refs_0_.refs_1_.refs_2_.bt_ref, f32[512,4096]{1,0:T(8,128)} %shard_map.102.refs_1_, bf16[512,4096]{1,0:T(8,128)(2,1)} %refs_2_.3, bf16[256,2048]{1,0:T(8,128)(2,1)} %get-tuple-element.23.refs_3_, ...), custom_call_target="tpu_custom_call" | custom-call | tf_op jit(solution)/shard_map/pallas_call | solution.py:321
  128.8 1.0 copy-done.2
  129.8 7.9 %shard_map.109 = bf16[512,4096]{1,0:T(8,128)(2,1)} custom-call(s32[1]{0:T(128)} %bitcast.core_ref, bf16[512,5120]{1,0:T(8,128)(2,1)} %shard_map.100.c_ref.b_ref.x_ref.refs_0_.refs_1_.refs_2_.bt_ref, f32[512,4096]{1,0:T(8,128)} %shard_map.102.refs_1_, bf16[512,4096]{1,0:T(8,128)(2,1)} %refs_2_.3, ...), custom_call_target="tpu_custom_call", output_to_operand_aliasing={{}: (11, {})} | custom-call | tf_op jit(solution)/shard_map/pallas_call | solution.py:321
  (36 shorter events, 1.0 us)
Async XLA Ops:
  0.9 15.7 %collective-permute-start = (bf16[3,5120]{1,0:T(4,128)(2,1)S(1)}, bf16[3,5120]{1,0:T(4,128)(2,1)S(1)}, u32[]{:S(2)}, u32[]{:S(2)}) collective-permute-start(bf16[3,5120]{1,0:T(4,128)(2,1)S(1)} %slice.54), channel_id=1, source_target_pairs={{0,1},{1,2},{2,3},{3,4},{4,5},{5,6},{6,7},{7,8},{8,9},{9,10},{10,1... | collective-permute-start | bytes 92168 | tf_op jit(solution)/shard_map/ppermute | solution.py:23
  38.1 8.0 %collective-permute-start.1 = (f32[257,2048]{1,0:T(8,128)}, f32[257,2048]{1,0:T(8,128)S(1)}, u32[]{:S(2)}, u32[]{:S(2)}) collective-permute-start(f32[257,2048]{1,0:T(8,128)} %get-tuple-element.14), channel_id=1, source_target_pairs={{0,1},{1,0},{2,3},{3,2},{4,5},{5,4},{6,7},{7,6},{8,9},{9,8},{10,11... | collective-permute-start | bytes 6316040 | tf_op jit(solution)/shard_map/ppermute | solution.py:343
  46.2 1.3 copy-start.1
  51.0 5.8 %copy-start = (f32[2,2,256,32]{3,2,1,0:T(8,128)S(1)}, f32[2,2,256,32]{3,2,1,0:T(8,128)}, u32[]{:S(2)}) copy-start(f32[2,2,256,32]{3,2,1,0:T(8,128)} %copy.82) | copy-start | bytes 393220
  51.0 6.6 %copy-start.3 = (f32[64]{0:T(128)S(1)}, f32[64]{0:T(128)}, u32[]{:S(2)}) copy-start(f32[64]{0:T(128)} %param.18) | copy-start | bytes 772
  52.2 30.6 %all-to-all-start = ((bf16[8,258,256]{2,1,0:T(8,128)(2,1)}), bf16[8,258,256]{2,1,0:T(8,128)(2,1)}, u32[]{:S(2)}, u32[]{:S(2)}) async-start(bf16[8,258,256]{2,1,0:T(8,128)(2,1)} %bitcast.63), calls=%async_computation | async-start | bytes 2162688 | tf_op jit(solution)/shard_map/all_to_all | solution.py:376
  85.3 29.2 %all-to-all-start.1 = ((bf16[8,256,256]{2,1,0:T(8,128)(2,1)}), bf16[8,256,256]{2,1,0:T(8,128)(2,1)}, u32[]{:S(2)}, u32[]{:S(2)}) async-start(bf16[8,256,256]{2,1,0:T(8,128)(2,1)} %shard_map.106), calls=%async_computation.1 | async-start | bytes 2097152 | tf_op jit(solution)/shard_map/all_to_all | solution.py:382
  117.8 10.9 %collective-permute-start.2 = (bf16[256,2048]{1,0:T(8,128)(2,1)S(1)}, bf16[256,2048]{1,0:T(8,128)(2,1)S(1)}, u32[]{:S(2)}, u32[]{:S(2)}) collective-permute-start(bf16[256,2048]{1,0:T(8,128)(2,1)S(1)} %get-tuple-element.24), channel_id=1, source_target_pairs={{0,1},{1,0},{2,3},{3,2},{4,5},{5,4},{6,7},{7,6},{8,9},{9,8},{10,11... | collective-permute-start | bytes 3145736 | tf_op jit(solution)/shard_map/ppermute | solution.py:343
  128.8 1.0 copy-start.2

commit v23 on v21

--- a/solution.py
+++ b/solution.py
@@ -42,7 +42,7 @@
     return out + jnp.dot(lo, spread, preferred_element_type=jnp.float32)
 
 
-CONV_COLS = 1280
+CONV_COLS = 1024
 
 
 def conv_kernel(x_ref, rim_ref, w_ref, bias_ref, m_ref, out_ref):

time: 138 us -> 137 us (level)
  no operation moved by 1% of the time
where the time goes in v23:
time: 137 us
  Pallas kernels  80.3 us (59%)
  starting transfers between devices  15.8 us (12%)
  local copies, waits for them, and re-layouts  15.5 us (11%)
  waiting for transfers between devices  13.7 us (10%)
  other arithmetic  11.2 us (8%)
    pallas_call x2, Pallas kernels, intra_part(): pl.pallas_call(kernel, grid=(nb,), in_specs=specs, out_specs=pl.BlockSpec...  34.9 us
    pallas_call x2, Pallas kernels, half_states(): pl.pallas_call(half_state_kernel, grid_spec=grid_spec, out_shape=[jax.Sha...  16 us
    pallas_call x2, Pallas kernels, mix(): pl.pallas_call(with_core, grid_spec=grid_spec, out_shape=jax.ShapeDtypeSt...  15.5 us
    pallas_call x1, Pallas kernels, conv_part(): pl.pallas_call(conv_kernel, grid=(chans // CONV_COLS,), in_specs=[pl.Bloc...  11.4 us
    all_to_all x1, waiting for transfers between devices, compose(): lax.all_to_all(entering, 'chip', split_axis=0, concat_axis=0, tiled=True)  7.28 us
    all_to_all x1, waiting for transfers between devices, compose(): lax.all_to_all(payload, 'chip', split_axis=0, concat_axis=0, tiled=True)  6.42 us
    all_to_all x1, starting transfers between devices, compose(): lax.all_to_all(payload, 'chip', split_axis=0, concat_axis=0, tiled=True)  4.6 us
    ppermute x1, starting transfers between devices, shifted(): return lax.ppermute(value, axis, pairs)  4.54 us
  transfers between devices with their start and end apart: 5, of which 2 were waited for; matrix products, arithmetic and copies ran while one was open for 10% of the time, Pallas kernels for 37%

profile of v23, /device:TPU:1, one launch (start us, length us, event | category | flops | bytes accessed | tf_op | source)
XLA Modules:
  0.0 136.8 jit_solution(5479425700786359177)
XLA Ops:
  0.0 0.9 slice.54
  0.9 4.5 %collective-permute-start = (bf16[3,5120]{1,0:T(4,128)(2,1)S(1)}, bf16[3,5120]{1,0:T(4,128)(2,1)S(1)}, u32[]{:S(2)}, u32[]{:S(2)}) collective-permute-start(bf16[3,5120]{1,0:T(4,128)(2,1)S(1)} %slice.54), channel_id=1, source_target_pairs={{0,1},{1,2},{2,3},{3,4},{4,5},{5,6},{6,7},{7,8},{8,9},{9,10},{10,1... | collective-permute-start | bytes 92168 | tf_op jit(solution)/shard_map/ppermute | solution.py:23
  5.5 0.8 reduce-window.18
  6.5 0.1 convert_reduce_fusion.1
  6.6 0.2 fusion.9
  6.8 0.1 copy.85
  6.9 1.0 copy.78
  7.9 0.7 exp.20
  8.7 0.7 add.67
  9.4 1.1 negate_multiply_fusion
  10.5 0.2 copy.79
  10.7 2.3 %reduce-window.19 = f32[2,2,32,2,128]{4,2,3,1,0:T(8,128)S(1)} reduce-window(f32[2,2,32,2,128]{4,2,3,1,0:T(8,128)S(1)} %copy_bitcast_fusion.1, f32[]{:T(128)} %constant.35.clone.1), window={size=1x1x1x1x128 pad=0_0x0_0x0_0x0_0x127_0}, to_apply=%region_2.3 | reduce-window | flops 4161536 | bytes 262148 | tf_op jit(solution)/shard_map/reduce-window.1
  13.0 0.2 slice_reduce_fusion
  13.3 0.1 bitcast_bitcast_fusion
  13.4 0.2 fusion.5
  13.7 0.2 compare_reduce_fusion
  14.0 1.0 copy.82
  15.0 0.9 copy.77.m_ref
  15.9 0.7 broadcast_in_dim_reshape.7.bdec_ref
  16.6 0.7 concatenate.6.rim_ref
  17.3 11.4 %shard_map.100.c_ref.b_ref.x_ref.refs_0_.refs_1_.refs_2_.bt_ref = bf16[512,5120]{1,0:T(8,128)(2,1)} custom-call(bf16[512,5120]{1,0:T(8,128)(2,1)} %x_ref.1, bf16[8,5120]{1,0:T(8,128)(2,1)} %concatenate.6.rim_ref, f32[4,5120]{1,0:T(4,128)} %w_ref.1, f32[1,5120]{1,0:T(1,128)} %bitcast.72, f32[512,4]{1,0:T(8,128)} %copy.77.m_ref), custom_call_target="tpu_custom_call" | custom-call | tf_op jit(solution)/shard_map/pallas_call | solution.py:72
  28.7 0.8 broadcast_in_dim.57.segc_ref.refs_6_.refs_7_
  29.6 8.0 %shard_map.103 = (f32[2,256,4096]{2,1,0:T(8,128)}, f32[2,1,4096]{2,1,0:T(1,128)}, f32[257,2048]{1,0:T(8,128)}) custom-call(s32[1]{0:T(128)} %bitcast.core_ref, bf16[512,5120]{1,0:T(8,128)(2,1)} %shard_map.100.c_ref.b_ref.x_ref.refs_0_.refs_1_.refs_2_.bt_ref, bf16[512,5120]{1,0:T(8,128)(2,1)} %shard_map.100.c_ref.b_ref.x_ref.refs_0_.refs_1_.refs_2_.bt_ref, ...), custom_call_target="tpu_custom_call" | custom-call | tf_op jit(solution)/shard_map/pallas_call | solution.py:189
  37.6 8.0 %shard_map.104 = (f32[2,256,4096]{2,1,0:T(8,128)}, f32[2,1,4096]{2,1,0:T(1,128)}, f32[257,2048]{1,0:T(8,128)}) custom-call(s32[1]{0:T(128)} %bitcast.core_ref, bf16[512,5120]{1,0:T(8,128)(2,1)} %shard_map.100.c_ref.b_ref.x_ref.refs_0_.refs_1_.refs_2_.bt_ref, ...), custom_call_target="tpu_custom_call", output_to_operand_aliasing={{0}: (7, {}), {1}: (8, {})} | custom-call | tf_op jit(solution)/shard_map/pallas_call | solution.py:189
  45.6 1.3 copy-done.1
  46.9 2.6 %broadcast_select_fusion.1 = (f32[257,2048]{1,0:T(8,128)S(1)}, f32[257,2048]{1,0:T(8,128)S(1)}) fusion(f32[257,2048]{1,0:T(8,128)} %get-tuple-element.13, f32[257,2048]{1,0:T(8,128)} %copy-done.1, pred[]{:T(512)S(6)} %eq.23), kind=kLoop, calls=%fused_computation.10 | loop fusion | flops 1052672 | bytes 8421377 | tf_op jit(solution)/shard_map/jit(_where)/select_n | solution.py:364
  49.6 0.4 fusion
  49.9 0.1 pad_maximum_fusion
  50.0 0.3 copy.92
  50.4 1.2 copy.96
  51.6 4.6 %all-to-all-start = ((bf16[8,258,256]{2,1,0:T(8,128)(2,1)}), bf16[8,258,256]{2,1,0:T(8,128)(2,1)}, u32[]{:S(2)}, u32[]{:S(2)}) async-start(bf16[8,258,256]{2,1,0:T(8,128)(2,1)} %bitcast.63), calls=%async_computation | async-start | bytes 2162688 | tf_op jit(solution)/shard_map/all_to_all | solution.py:375
  56.2 0.8 copy.84.cumt_ref.refs_5_
  57.2 0.7 broadcast_in_dim_reshape.6.dsk_ref.refs_8_
  57.8 0.6 broadcast_in_dim.58.segr_ref.refs_7_
  58.4 17.4 %shard_map.101.refs_9_.refs_1_ = f32[512,4096]{1,0:T(8,128)} custom-call(bf16[512,5120]{1,0:T(8,128)(2,1)} %shard_map.100.c_ref.b_ref.x_ref.refs_0_.refs_1_.refs_2_.bt_ref, bf16[512,5120]{1,0:T(8,128)(2,1)} %shard_map.100.c_ref.b_ref.x_ref.refs_0_.refs_1_.refs_2_.bt_ref, bf16[512,5120]{1,0:T(8,128)(2,1)} %shard_map.100.c_ref.b_ref.x_ref.refs_0_.refs_1_.refs_2_.bt_ref, ...), custom_call_target="tpu_custom_call" | custom-call | tf_op jit(solution)/shard_map/pallas_call | solution.py:252
  75.8 6.4 %all-to-all-done.refs_0_ = bf16[8,258,256]{2,1,0:T(8,128)(2,1)} async-done(((bf16[8,258,256]{2,1,0:T(8,128)(2,1)}), bf16[8,258,256]{2,1,0:T(8,128)(2,1)}, u32[]{:S(2)}, u32[]{:S(2)}) %all-to-all-start) | async-done | bytes 1056800 | tf_op jit(solution)/shard_map/all_to_all | solution.py:375
  82.2 2.5 %shard_map.106 = bf16[8,256,256]{2,1,0:T(8,128)(2,1)} custom-call(bf16[8,258,256]{2,1,0:T(8,128)(2,1)} %shard_map.105.got_ref), custom_call_target="tpu_custom_call" | custom-call | tf_op jit(solution)/shard_map/pallas_call | solution.py:376
  84.8 4.5 %all-to-all-start.1 = ((bf16[8,256,256]{2,1,0:T(8,128)(2,1)}), bf16[8,256,256]{2,1,0:T(8,128)(2,1)}, u32[]{:S(2)}, u32[]{:S(2)}) async-start(bf16[8,256,256]{2,1,0:T(8,128)(2,1)} %shard_map.106), calls=%async_computation.1 | async-start | bytes 2097152 | tf_op jit(solution)/shard_map/all_to_all | solution.py:381
  89.2 17.5 %shard_map.102.refs_1_ = f32[512,4096]{1,0:T(8,128)} custom-call(bf16[512,5120]{1,0:T(8,128)(2,1)} %shard_map.100.c_ref.b_ref.x_ref.refs_0_.refs_1_.refs_2_.bt_ref, bf16[512,5120]{1,0:T(8,128)(2,1)} %shard_map.100.c_ref.b_ref.x_ref.refs_0_.refs_1_.refs_2_.bt_ref, ...), custom_call_target="tpu_custom_call", output_to_operand_aliasing={{}: (9, {})} | custom-call | tf_op jit(solution)/shard_map/pallas_call | solution.py:252
  106.7 7.3 %all-to-all-done.1.refs_0_ = bf16[8,256,256]{2,1,0:T(8,128)(2,1)} async-done(((bf16[8,256,256]{2,1,0:T(8,128)(2,1)}), bf16[8,256,256]{2,1,0:T(8,128)(2,1)}, u32[]{:S(2)}, u32[]{:S(2)}) %all-to-all-start.1) | async-done | bytes 1048608 | tf_op jit(solution)/shard_map/all_to_all | solution.py:381
  114.0 1.4 %convert_bitcast_fusion = f32[8,32,8,256]{3,2,1,0:T(8,128)S(1)} fusion(bf16[8,256,256]{2,1,0:T(8,128)(2,1)} %shard_map.107), kind=kLoop, calls=%fused_computation.2 | loop fusion | flops 524288 | bytes 3145728
  115.4 0.3 copy.91
  115.7 1.6 %select_convert_fusion = (bf16[256,2048]{1,0:T(8,128)(2,1)}, bf16[256,2048]{1,0:T(8,128)(2,1)S(1)}) fusion(f32[256,2048]{1,0:T(8,128)S(1)} %bitcast.62, f32[257,2048]{1,0:T(8,128)S(1)} %get-tuple-element.21, f32[2048]{0:T(1024)S(1)} %bitcast.70, pred[]{:T(512)S(6)} %eq.23), kind=kLoop, calls=%fused_computation.3 | loop fusion | flops 3145728 | bytes 6299649 | tf_op jit(solution)/shard_map/convert_element_type | solution.py:384
  117.3 2.2 %collective-permute-start.2 = (bf16[256,2048]{1,0:T(8,128)(2,1)S(1)}, bf16[256,2048]{1,0:T(8,128)(2,1)S(1)}, u32[]{:S(2)}, u32[]{:S(2)}) collective-permute-start(bf16[256,2048]{1,0:T(8,128)(2,1)S(1)} %get-tuple-element.24), channel_id=1, source_target_pairs={{0,1},{1,0},{2,3},{3,2},{4,5},{5,4},{6,7},{7,6},{8,9},{9,8},{10,11... | collective-permute-start | bytes 3145736 | tf_op jit(solution)/shard_map/ppermute | solution.py:342
  119.6 0.7 broadcast_in_dim.66.refs_8_
  120.3 7.8 %shard_map.108.refs_10_ = bf16[512,4096]{1,0:T(8,128)(2,1)} custom-call(s32[1]{0:T(128)} %bitcast.core_ref, bf16[512,5120]{1,0:T(8,128)(2,1)} %shard_map.100.c_ref.b_ref.x_ref.refs_0_.refs_1_.refs_2_.bt_ref, f32[512,4096]{1,0:T(8,128)} %shard_map.102.refs_1_, bf16[512,4096]{1,0:T(8,128)(2,1)} %refs_2_.3, bf16[256,2048]{1,0:T(8,128)(2,1)} %get-tuple-element.23.refs_3_, ...), custom_call_target="tpu_custom_call" | custom-call | tf_op jit(solution)/shard_map/pallas_call | solution.py:320
  128.1 1.0 copy-done.2
  129.1 7.8 %shard_map.109 = bf16[512,4096]{1,0:T(8,128)(2,1)} custom-call(s32[1]{0:T(128)} %bitcast.core_ref, bf16[512,5120]{1,0:T(8,128)(2,1)} %shard_map.100.c_ref.b_ref.x_ref.refs_0_.refs_1_.refs_2_.bt_ref, f32[512,4096]{1,0:T(8,128)} %shard_map.102.refs_1_, bf16[512,4096]{1,0:T(8,128)(2,1)} %refs_2_.3, ...), custom_call_target="tpu_custom_call", output_to_operand_aliasing={{}: (11, {})} | custom-call | tf_op jit(solution)/shard_map/pallas_call | solution.py:320
  (36 shorter events, 1.0 us)
Async XLA Ops:
  0.9 15.7 %collective-permute-start = (bf16[3,5120]{1,0:T(4,128)(2,1)S(1)}, bf16[3,5120]{1,0:T(4,128)(2,1)S(1)}, u32[]{:S(2)}, u32[]{:S(2)}) collective-permute-start(bf16[3,5120]{1,0:T(4,128)(2,1)S(1)} %slice.54), channel_id=1, source_target_pairs={{0,1},{1,2},{2,3},{3,4},{4,5},{5,6},{6,7},{7,8},{8,9},{9,10},{10,1... | collective-permute-start | bytes 92168 | tf_op jit(solution)/shard_map/ppermute | solution.py:23
  37.5 8.0 %collective-permute-start.1 = (f32[257,2048]{1,0:T(8,128)}, f32[257,2048]{1,0:T(8,128)S(1)}, u32[]{:S(2)}, u32[]{:S(2)}) collective-permute-start(f32[257,2048]{1,0:T(8,128)} %get-tuple-element.14), channel_id=1, source_target_pairs={{0,1},{1,0},{2,3},{3,2},{4,5},{5,4},{6,7},{7,6},{8,9},{9,8},{10,11... | collective-permute-start | bytes 6316040 | tf_op jit(solution)/shard_map/ppermute | solution.py:342
  45.6 1.3 copy-start.1
  50.4 5.8 %copy-start = (f32[2,2,256,32]{3,2,1,0:T(8,128)S(1)}, f32[2,2,256,32]{3,2,1,0:T(8,128)}, u32[]{:S(2)}) copy-start(f32[2,2,256,32]{3,2,1,0:T(8,128)} %copy.82) | copy-start | bytes 393220
  50.4 6.6 %copy-start.3 = (f32[64]{0:T(128)S(1)}, f32[64]{0:T(128)}, u32[]{:S(2)}) copy-start(f32[64]{0:T(128)} %param.18) | copy-start | bytes 772
  51.6 30.6 %all-to-all-start = ((bf16[8,258,256]{2,1,0:T(8,128)(2,1)}), bf16[8,258,256]{2,1,0:T(8,128)(2,1)}, u32[]{:S(2)}, u32[]{:S(2)}) async-start(bf16[8,258,256]{2,1,0:T(8,128)(2,1)} %bitcast.63), calls=%async_computation | async-start | bytes 2162688 | tf_op jit(solution)/shard_map/all_to_all | solution.py:375
  84.8 29.2 %all-to-all-start.1 = ((bf16[8,256,256]{2,1,0:T(8,128)(2,1)}), bf16[8,256,256]{2,1,0:T(8,128)(2,1)}, u32[]{:S(2)}, u32[]{:S(2)}) async-start(bf16[8,256,256]{2,1,0:T(8,128)(2,1)} %shard_map.106), calls=%async_computation.1 | async-start | bytes 2097152 | tf_op jit(solution)/shard_map/all_to_all | solution.py:381
  117.3 10.8 %collective-permute-start.2 = (bf16[256,2048]{1,0:T(8,128)(2,1)S(1)}, bf16[256,2048]{1,0:T(8,128)(2,1)S(1)}, u32[]{:S(2)}, u32[]{:S(2)}) collective-permute-start(bf16[256,2048]{1,0:T(8,128)(2,1)S(1)} %get-tuple-element.24), channel_id=1, source_target_pairs={{0,1},{1,0},{2,3},{3,2},{4,5},{5,4},{6,7},{7,6},{8,9},{9,8},{10,11... | collective-permute-start | bytes 3145736 | tf_op jit(solution)/shard_map/ppermute | solution.py:342
  128.1 1.0 copy-start.2
